TPU v7x, 32 devices: a whole 2x2x4 slice. The times are simulated.
32 devices in a mesh: basis: 2 (over x), eig: 8 (over z, y), chan: 2 (over core).
Axes of the slice: x: 2, y: 2, z: 4, core: 2. Of those that a mesh axis runs over, the one named last changes fastest.
Arguments:
- eigvecs: bfloat16 [512, 5120], P('eig', 'basis'), may hold values from -6 to 6
- boundary: bfloat16 [5120, 4096], P('basis', 'chan'), may hold values from -0.3125 to 0.3125
- block_sizes: int32 [16], replicated, may hold values from 256 to 768, as said below
- target_of_channel: int32 [4096], P('chan'), may hold values from 0 to 15, as said below
- poles: float32 [512], replicated, may hold values from -4 to 4, as said below
- energies: float32 [16], P('basis'), may hold values from -0.25 to 0.25
Outputs:
- rmatrix: float32 [16, 4096, 4096], P('basis', 'chan', 'eig')
Inputs may be any that keep to these rules, and one draw needn't show every extreme that they name: `poles`: every pole lies 0.5 or more away from zero, with both signs present. `block_sizes`: the sizes sum to 5120; every target state's block holds at least 256 basis rows. `target_of_channel`: every target state has exactly 256 channels.
All inputs are finite; a program needn't handle non-finite values.
Results may differ from a plain program's by a relative error of at most 0.0049.
Values may be sent and summed in bfloat16 or wider, within the bound.
No kernel may reach another device: no remote copies, remote signals or barrier semaphores. Data moves between devices by JAX's collectives and lax.ppermute only.
A program may use at most 128 MiB of HBM per device.

v0:
```python
import jax
import jax.numpy as jnp
from jax import lax
from jax.sharding import PartitionSpec as P


def per_device(eigvecs, boundary, block_sizes, target_of_channel, poles, energies):
    rows_here = eigvecs.shape[1]
    block_ends = jnp.cumsum(block_sizes)
    row_ids = lax.axis_index("basis") * rows_here + jnp.arange(rows_here, dtype=jnp.int32)
    owner_of = jnp.sum((block_ends[None, :] <= row_ids[:, None]).astype(jnp.int32), axis=1)
    member = owner_of[:, None] == target_of_channel[None, :]
    masked = jnp.where(member, boundary, jnp.zeros_like(boundary))
    partial_value = jnp.dot(eigvecs, masked, preferred_element_type=jnp.float32)
    amplitudes = lax.psum(partial_value, "basis").astype(jnp.bfloat16)
    all_channels = lax.all_gather(amplitudes, "chan", axis=1, tiled=True)
    own_width = amplitudes.shape[1]
    own_first = lax.axis_index("chan") * own_width
    col_width = all_channels.shape[1] // lax.axis_size("eig")
    col_first = lax.axis_index("eig") * col_width
    factor = poles.shape[0] ** (-0.5)
    weights = 1.0 / (poles[None, :] - energies[:, None])
    panel_in = lax.all_gather(all_channels, "eig", axis=0, tiled=True)
    left_panel = lax.dynamic_slice_in_dim(panel_in, own_first, own_width, 1)
    right_panel = lax.dynamic_slice_in_dim(panel_in, col_first, col_width, 1)
    scaled = (weights[:, :, None] * left_panel[None].astype(jnp.float32)).astype(jnp.bfloat16)
    summed = jnp.einsum("ekc,kd->ecd", scaled, right_panel, preferred_element_type=jnp.float32)
    return summed * factor


def solution(mesh):
    placed = (P("eig", "basis"), P("basis", "chan"), P(), P("chan"), P(), P("basis"))
    return jax.shard_map(
        per_device, mesh=mesh, in_specs=placed, out_specs=P("basis", "chan", "eig"), check_vma=False
    )
```

profile of v0, /device:TPU:0, one launch (start us, length us, event | category | flops | bytes accessed | tf_op | source)
XLA Modules:
  0.0 140.8 jit_solution(5083630222662826893)
XLA Ops:
  6.5 0.0 copy-start
  6.5 0.0 all-gather.2.cloned.1.call-start
  6.5 0.8 copy.11
  7.4 0.1 reduce
  7.5 0.1 convert_reduce_fusion
  7.6 0.0 copy-done
  7.6 0.0 copy-start.1
  7.6 0.0 copy-start.2
  7.6 6.4 %fusion.6 = f32[64,2048]{1,0:T(8,128)S(1)} fusion(bf16[64,2560]{1,0:T(8,128)(2,1)S(1)} %copy-done, bf16[2560,2048]{1,0:T(8,128)(2,1)} %param.7, s32[2048]{0:T(1024)} %param.9, s32[2560]{0:T(1024)S(1)} %convert_reduce_fusion), kind=kOutput, calls=%fused_computation.9 | convolution fusion | flops 681574400 | bytes 11356160 | tf_op jit(solution)/shard_map/dot_general | solution.py:14
  14.0 18.6 %all-reduce.1 = bf16[64,2048]{1,0:T(8,128)(2,1)S(1)} all-reduce(f32[64,2048]{1,0:T(8,128)S(1)} %fusion.6), channel_id=1, replica_groups=mesh['basis'=2,'eig'=8,'chan'=2] {'basis'}, use_global_device_ids=true, to_apply=%region_2.3 | all-reduce | flops 131072 | bytes 786432 | tf_op jit(solution)/shard_map/psum | solution.py:15
  32.6 2.3 %all_gather.6 = bf16[64,4096]{1,0:T(8,128)(2,1)} all-gather(bf16[64,2048]{1,0:T(8,128)(2,1)S(1)} %all-reduce.1), channel_id=1, replica_groups=mesh['basis'=2,'eig'=8,'chan'=2] {'chan'}, dimensions={1}, use_global_device_ids=true | all-gather | bytes 786432 | tf_op jit(solution)/shard_map/all_gather | solution.py:16
  34.9 0.0 all-gather.2.cloned.1.call-update
  35.0 0.0 copy-done.1
  35.0 0.0 copy-done.2
  35.0 0.1 subtract_divide_fusion
  35.1 73.2 %all-gather.2.cloned.1.call-done = bf16[512,4096]{1,0:T(8,128)(2,1)} async-done(((bf16[64,4096]{1,0:T(8,128)(2,1)}), bf16[512,4096]{1,0:T(8,128)(2,1)}) %all-gather.2.cloned.1.call-update) | async-done | bytes 4194320 | tf_op jit(solution)/shard_map/all_gather | solution.py:23
  108.2 4.1 %dynamic-slice_convert_fusion = f32[512,2048]{1,0:T(8,128)} fusion(bf16[512,4096]{1,0:T(8,128)(2,1)} %all-gather.2.cloned.1.call-done, s32[]{:T(128)S(6)} %select_n.11), kind=kLoop, calls=%fused_computation.10 | loop fusion | flops 1048576 | bytes 6291460 | tf_op jit(solution)/shard_map/convert_element_type | solution.py:26
  112.4 5.3 %copy.12 = f32[512,2048]{0,1:T(8,128)} copy(f32[512,2048]{1,0:T(8,128)} %dynamic-slice_convert_fusion) | data formatting | bytes 8388608 | tf_op jit(solution)/shard_map/convert_element_type | solution.py:26
  117.7 16.3 %convolution_multiply_fusion = f32[8,2048,512]{2,1,0:T(8,128)} fusion(f32[512,2048]{0,1:T(8,128)} %copy.12, f32[8,512]{1,0:T(8,128)S(1)} %subtract_divide_fusion, bf16[512,4096]{1,0:T(8,128)(2,1)} %all-gather.2.cloned.1.call-done, s32[]{:T(128)S(6)} %select_n.12), kind=kOutput, calls=%fused_computation.2 | convolution fusion | flops 8615100416 | bytes 38289412 | tf_op jit(solution)/shard_map/ekc,kd->ecd/dot_general | solution.py:27
  (2 shorter events, 0.0 us)
Async XLA Ops:
  6.5 1.1 copy-start
  6.5 101.7 %all-gather.2.cloned.1.call-start = ((), (), s32[]{:S(2)}) async-start(), calls=%async_computation | async-start | bytes 4718592 | tf_op jit(solution)/shard_map/all_gather | solution.py:23
  7.6 27.4 %copy-start.1 = (f32[512]{0:T(512)S(1)}, f32[512]{0:T(512)}, u32[]{:S(2)}) copy-start(f32[512]{0:T(512)} %param.10) | copy-start | bytes 6148
  7.6 27.4 %copy-start.2 = (f32[8]{0:T(128)S(1)}, f32[8]{0:T(128)}, u32[]{:S(2)}) copy-start(f32[8]{0:T(128)} %param.11) | copy-start | bytes 100
Sparse Core Ops, SparseCore 0:
  35.1 73.1 all-gather.1
where the time goes:
time: 141 us
  waiting for transfers between devices  73.2 us (52%)
  matrix products  22.7 us (16%)
  blocking collectives  20.9 us (15%)
  between operations  13.5 us (10%)
  local copies, waits for them, and re-layouts  6.14 us (4%)
  other arithmetic  4.47 us (3%)
    all_gather x1, waiting for transfers between devices, per_device(): panel_in = lax.all_gather(all_channels, 'eig', axis=0, tiled=True)  73.2 us
    psum x1, blocking collectives, per_device(): amplitudes = lax.psum(partial_value, 'basis').astype(jnp.bfloat16)  18.6 us
    dot_general x1, matrix products, per_device(): jnp.einsum('ekc,kd->ecd', scaled, right_panel, preferred_element_type=jnp...  16.3 us
    dot_general x1, matrix products, per_device(): partial_value = jnp.dot(eigvecs, masked, preferred_element_type=jnp.float32)  6.39 us
    convert_element_type x1, local copies, waits for them, and re-layouts, per_device(): left_panel[None].astype(jnp.float32)  5.34 us
    convert_element_type x1, other arithmetic, per_device(): left_panel[None].astype(jnp.float32)  4.13 us
  transfers between devices with their start and end apart: 1, of which 1 were waited for; matrix products, arithmetic and copies ran while one was open for 0% of the time, Pallas kernels for 0%

commit v1 on v0

v1 whole, which is shorter than its diff:
```python
import jax
import jax.numpy as jnp
from jax import lax
from jax.sharding import PartitionSpec as P


def per_device(eigvecs, boundary, block_sizes, target_of_channel, poles, energies):
    n_basis = lax.axis_size("basis")
    n_eig = lax.axis_size("eig")
    n_chan = lax.axis_size("chan")
    rows_here = eigvecs.shape[1]
    block_ends = jnp.cumsum(block_sizes)
    row_ids = lax.axis_index("basis") * rows_here + jnp.arange(rows_here, dtype=jnp.int32)
    owner_of = jnp.sum((block_ends[None, :] <= row_ids[:, None]).astype(jnp.int32), axis=1)
    member = owner_of[:, None] == target_of_channel[None, :]
    masked = jnp.where(member, boundary, jnp.zeros_like(boundary))
    partial_value = jnp.dot(eigvecs, masked, preferred_element_type=jnp.float32)
    summed_rows = lax.psum_scatter(partial_value, "basis", scatter_dimension=0, tiled=True)
    amp_rows = summed_rows.astype(jnp.bfloat16)
    left_panel = lax.all_gather(amp_rows, ("eig", "basis"), axis=0, tiled=True)
    own_width = left_panel.shape[1]
    col_width = own_width * n_chan // n_eig
    ratio = n_eig // n_chan
    eig_index = lax.axis_index("eig")
    piece = lax.dynamic_slice_in_dim(left_panel, (eig_index % ratio) * col_width, col_width, 1)
    pieces = lax.all_gather(piece, "chan", axis=0, tiled=False)
    right_panel = lax.dynamic_index_in_dim(pieces, eig_index // ratio, 0, keepdims=False)
    factor = poles.shape[0] ** (-0.5)
    weights = 1.0 / (poles[None, :] - energies[:, None])
    scaled = (weights[:, :, None] * left_panel[None].astype(jnp.float32)).astype(jnp.bfloat16)
    summed = jnp.einsum("ekc,kd->ecd", scaled, right_panel, preferred_element_type=jnp.float32)
    return summed * factor


def solution(mesh):
    placed = (P("eig", "basis"), P("basis", "chan"), P(), P("chan"), P(), P("basis"))
    return jax.shard_map(
        per_device, mesh=mesh, in_specs=placed, out_specs=P("basis", "chan", "eig"), check_vma=False
    )
```

time: 141 us -> 128 us (0.908)
  blocking collectives: 20.9 us -> 0 us
  waiting for transfers between devices: 73.2 us -> 82.7 us
  other arithmetic: 4.47 us -> 1.96 us
    psum x1 -> x0, blocking collectives: 18.6 us -> none  [per_device(): amplitudes = lax.psum(partial_value, 'basis').astype(jnp.bfloat16)]
    reduce_scatter x0 -> x1, waiting for transfers between devices: none -> 17.5 us  [per_device(): lax.psum_scatter(partial_value, 'basis', scatter_dimension=0, tiled=True)]
    all_gather x1 -> x2, waiting for transfers between devices: 73.2 us -> 65.2 us  [the longest x1 61.5 us: per_device(): left_panel = lax.all_gather(amp_rows, ('eig', 'basis'), axis=0, tiled=True)]
    convert_element_type x1, other arithmetic: 4.13 us -> 1.62 us  [per_device(): amp_rows = summed_rows.astype(jnp.bfloat16)]
    all_gather x1 -> x0, blocking collectives: 2.31 us -> none  [per_device(): all_channels = lax.all_gather(amplitudes, 'chan', axis=1, tiled=True)]
    dynamic_slice x0 -> x1, local copies, waits for them, and re-layouts: none -> 1.87 us  [per_device(): lax.dynamic_slice_in_dim(left_panel, eig_index % ratio * col_width, col_w...]
  transfers between devices with their start and end apart: 1 -> 3, of which waited for: 1 -> 3; matrix products, arithmetic and copies ran while one was open for 0% -> 3% of each run, Pallas kernels for 0% -> 0%
where the time goes in v1:
time: 128 us
  waiting for transfers between devices  82.7 us (65%)
  matrix products  23.5 us (18%)
  between operations  13.2 us (10%)
  local copies, waits for them, and re-layouts  6.8 us (5%)
  other arithmetic  1.96 us (2%)
    all_gather x1, waiting for transfers between devices, per_device(): left_panel = lax.all_gather(amp_rows, ('eig', 'basis'), axis=0, tiled=True)  61.5 us
    reduce_scatter x1, waiting for transfers between devices, per_device(): lax.psum_scatter(partial_value, 'basis', scatter_dimension=0, tiled=True)  17.5 us
    dot_general x1, matrix products, per_device(): jnp.einsum('ekc,kd->ecd', scaled, right_panel, preferred_element_type=jnp...  16.3 us
    dot_general x1, matrix products, per_device(): partial_value = jnp.dot(eigvecs, masked, preferred_element_type=jnp.float32)  7.18 us
    convert_element_type x1, local copies, waits for them, and re-layouts, per_device(): left_panel[None].astype(jnp.float32)  4.14 us
    all_gather x1, waiting for transfers between devices, per_device(): pieces = lax.all_gather(piece, 'chan', axis=0, tiled=False)  3.73 us
  transfers between devices with their start and end apart: 3, of which 3 were waited for; matrix products, arithmetic and copies ran while one was open for 3% of the time, Pallas kernels for 0%

profile of v1, /device:TPU:0, one launch (start us, length us, event | category | flops | bytes accessed | tf_op | source)
XLA Modules:
  0.0 128.2 jit_solution(8895201701488837647)
XLA Ops:
  6.5 0.0 copy-start
  6.5 0.0 reduce-scatter.2.cloned.1.call-start
  6.5 0.8 copy.11
  7.4 0.1 reduce
  7.5 0.1 convert_reduce_fusion
  7.6 0.0 copy-done
  7.6 0.0 copy-start.1
  7.6 0.0 copy-start.2
  7.6 7.2 %fusion.6 = f32[64,2048]{1,0:T(8,128)} fusion(bf16[64,2560]{1,0:T(8,128)(2,1)S(1)} %copy-done, bf16[2560,2048]{1,0:T(8,128)(2,1)} %param.7, s32[2048]{0:T(1024)} %param.9, s32[2560]{0:T(1024)S(1)} %convert_reduce_fusion), kind=kOutput, calls=%fused_computation.9 | convolution fusion | flops 681574400 | bytes 11356160 | tf_op jit(solution)/shard_map/dot_general | solution.py:17
  14.8 0.0 reduce-scatter.2.cloned.1.call-update
  14.8 0.0 all-gather.4.cloned.1.call-start
  14.9 17.5 %reduce-scatter.2.cloned.1.call-done = f32[32,2048]{1,0:T(8,128)} async-done(((f32[64,2048]{1,0:T(8,128)}), f32[32,2048]{1,0:T(8,128)}) %reduce-scatter.2.cloned.1.call-update) | async-done | bytes 262160 | tf_op jit(solution)/shard_map/reduce_scatter | solution.py:18
  32.3 1.6 %convert_element_type.14 = bf16[32,2048]{1,0:T(8,128)(2,1)} convert(f32[32,2048]{1,0:T(8,128)} %reduce-scatter.2.cloned.1.call-done) | non-fusion elementwise | flops 65536 | bytes 393216 | tf_op jit(solution)/shard_map/convert_element_type | solution.py:19
  34.0 0.0 all-gather.4.cloned.1.call-update
  34.0 0.0 all-gather.6.cloned.1.call-start
  34.1 61.5 %all-gather.4.cloned.1.call-done = bf16[512,2048]{1,0:T(8,128)(2,1)} async-done(((bf16[32,2048]{1,0:T(8,128)(2,1)}), bf16[512,2048]{1,0:T(8,128)(2,1)}) %all-gather.4.cloned.1.call-update) | async-done | bytes 2097168 | tf_op jit(solution)/shard_map/all_gather | solution.py:20
  95.5 1.9 %constant_dynamic-slice_fusion = bf16[512,512]{1,0:T(8,128)(2,1)} fusion(bf16[512,2048]{1,0:T(8,128)(2,1)} %all-gather.4.cloned.1.call-done, s32[]{:T(128)S(6)} %select_n.24), kind=kLoop, calls=%fused_computation.16 | loop fusion | bytes 1048580 | tf_op jit(solution)/shard_map/dynamic_slice | solution.py:25
  97.4 0.0 all-gather.6.cloned.1.call-update
  97.4 0.0 copy-done.1
  97.5 0.0 copy-done.2
  97.5 0.1 subtract_divide_fusion
  97.5 4.1 %copy.12 = f32[512,2048]{0,1:T(8,128)} copy(bf16[512,2048]{1,0:T(8,128)(2,1)} %all-gather.4.cloned.1.call-done) | data formatting | bytes 6291456 | tf_op jit(solution)/shard_map/convert_element_type | solution.py:30
  101.7 3.7 %all-gather.6.cloned.1.call-done = bf16[1024,512]{1,0:T(8,128)(2,1)} async-done(((bf16[512,512]{1,0:T(8,128)(2,1)}), bf16[1024,512]{1,0:T(8,128)(2,1)}) %all-gather.6.cloned.1.call-update) | async-done | bytes 1048592 | tf_op jit(solution)/shard_map/all_gather | solution.py:26
  105.4 16.3 %convolution_multiply_fusion = f32[8,2048,512]{2,1,0:T(8,128)} fusion(f32[512,2048]{0,1:T(8,128)} %copy.12, f32[8,512]{1,0:T(8,128)S(1)} %subtract_divide_fusion, bf16[2,512,512]{2,1,0:T(8,128)(2,1)} %bitcast.9, s32[]{:T(128)S(6)} %select_n.26), kind=kOutput, calls=%fused_computation.2 | convolution fusion | flops 8615100416 | bytes 38289412 | tf_op jit(solution)/shard_map/ekc,kd->ecd/dot_general | solution.py:31
  (2 shorter events, 0.0 us)
Async XLA Ops:
  6.5 1.1 copy-start
  6.5 25.8 %reduce-scatter.2.cloned.1.call-start = ((), (), s32[]{:S(2)}) async-start(), calls=%async_computation.1 | async-start | bytes 786432 | tf_op jit(solution)/shard_map/reduce_scatter | solution.py:18
  7.6 89.8 %copy-start.1 = (f32[512]{0:T(512)S(1)}, f32[512]{0:T(512)}, u32[]{:S(2)}) copy-start(f32[512]{0:T(512)} %param.10) | copy-start | bytes 6148
  7.6 89.8 %copy-start.2 = (f32[8]{0:T(128)S(1)}, f32[8]{0:T(128)}, u32[]{:S(2)}) copy-start(f32[8]{0:T(128)} %param.11) | copy-start | bytes 100
  14.8 80.7 %all-gather.4.cloned.1.call-start = ((), (), s32[]{:S(2)}) async-start(), calls=%async_computation.2 | async-start | bytes 2228224 | tf_op jit(solution)/shard_map/all_gather | solution.py:20
  34.0 71.4 %all-gather.6.cloned.1.call-start = ((), (), s32[]{:S(2)}) async-start(), calls=%async_computation.3 | async-start | bytes 1572864 | tf_op jit(solution)/shard_map/all_gather | solution.py:26
Sparse Core Ops, SparseCore 0:
  14.9 17.3 reduce-scatter.1
  35.1 60.3 all-gather.3
  97.5 7.8 all-gather.5

commit v2 on v0

v2 whole, which is shorter than its diff:
```python
import jax
import jax.numpy as jnp
import numpy as np
from jax import lax
from jax.sharding import PartitionSpec as P


def ring_order(mesh):
    n = mesh.shape["eig"]
    try:
        index = [0] * len(mesh.axis_names)
        where = mesh.axis_names.index("eig")
        coords = []
        for m in range(n):
            index[where] = m
            coords.append(tuple(int(v) for v in mesh.devices[tuple(index)].coords))
        varying = [a for a in range(len(coords[0])) if len({c[a] for c in coords}) > 1]
        if len(varying) != 2:
            return list(range(n))
        spans = [sorted({c[a] for c in coords}) for a in varying]
        if len(spans[0]) % 2 != 0:
            varying, spans = varying[::-1], spans[::-1]
        rows, cols = spans
        if len(rows) % 2 != 0 or len(cols) < 2 or len(rows) * len(cols) != n:
            return list(range(n))
        at = {(c[varying[0]], c[varying[1]]): m for m, c in enumerate(coords)}
        path = []
        for r_i, r in enumerate(rows):
            tail = cols[1:] if r_i % 2 == 0 else cols[1:][::-1]
            path += [at[(r, c)] for c in tail]
        path += [at[(r, cols[0])] for r in rows[::-1]]
        return path if sorted(path) == list(range(n)) else list(range(n))
    except Exception:
        return list(range(n))


def make_per_device(cycle):
    n_ring = len(cycle)
    position = [0] * n_ring
    for t, m in enumerate(cycle):
        position[m] = t
    fwd_pairs = [(cycle[t], cycle[(t + 1) % n_ring]) for t in range(n_ring)]
    bwd_pairs = [(cycle[t], cycle[(t - 1) % n_ring]) for t in range(n_ring)]
    n_fwd = n_ring // 2
    n_bwd = n_ring - 1 - n_fwd

    def per_device(eigvecs, boundary, block_sizes, target_of_channel, poles, energies):
        n_eig = lax.axis_size("eig")
        n_chan = lax.axis_size("chan")
        rows_here = eigvecs.shape[1]
        block_ends = jnp.cumsum(block_sizes)
        row_ids = lax.axis_index("basis") * rows_here + jnp.arange(rows_here, dtype=jnp.int32)
        owner_of = jnp.sum((block_ends[None, :] <= row_ids[:, None]).astype(jnp.int32), axis=1)
        member = owner_of[:, None] == target_of_channel[None, :]
        masked = jnp.where(member, boundary, jnp.zeros_like(boundary))
        partial_value = jnp.dot(eigvecs, masked, preferred_element_type=jnp.float32)
        n_basis = lax.axis_size("basis")
        total = partial_value
        for s in range(1, n_basis):
            shift = [(b, (b + s) % n_basis) for b in range(n_basis)]
            total = total + lax.ppermute(partial_value, "basis", shift)
        amp = total.astype(jnp.bfloat16)
        eig_index = lax.axis_index("eig")
        cycle_arr = jnp.array(cycle, dtype=jnp.int32)
        pos = jnp.array(position, dtype=jnp.int32)[eig_index]
        k_here = amp.shape[0]
        left_panel = jnp.zeros((k_here * n_ring, amp.shape[1]), amp.dtype)
        left_panel = lax.dynamic_update_slice_in_dim(left_panel, amp, eig_index * k_here, 0)
        fwd, bwd = amp, amp
        for s in range(max(n_fwd, n_bwd)):
            if s < n_fwd:
                fwd = lax.ppermute(fwd, "eig", fwd_pairs)
                origin = cycle_arr[(pos - s - 1) % n_ring]
                left_panel = lax.dynamic_update_slice_in_dim(left_panel, fwd, origin * k_here, 0)
            if s < n_bwd:
                bwd = lax.ppermute(bwd, "eig", bwd_pairs)
                origin = cycle_arr[(pos + s + 1) % n_ring]
                left_panel = lax.dynamic_update_slice_in_dim(left_panel, bwd, origin * k_here, 0)
        own_width = left_panel.shape[1]
        col_width = own_width * n_chan // n_eig
        ratio = n_eig // n_chan
        piece = lax.dynamic_slice_in_dim(left_panel, (eig_index % ratio) * col_width, col_width, 1)
        holder = eig_index // ratio
        if n_chan == 2:
            other = lax.ppermute(piece, "chan", [(0, 1), (1, 0)])
            right_panel = jnp.where(lax.axis_index("chan") == holder, piece, other)
        else:
            pieces = lax.all_gather(piece, "chan", axis=0, tiled=False)
            right_panel = lax.dynamic_index_in_dim(pieces, holder, 0, keepdims=False)
        factor = poles.shape[0] ** (-0.5)
        weights = 1.0 / (poles[None, :] - energies[:, None])
        scaled = (weights[:, :, None] * left_panel[None].astype(jnp.float32)).astype(jnp.bfloat16)
        summed = jnp.einsum("ekc,kd->ecd", scaled, right_panel, preferred_element_type=jnp.float32)
        return summed * factor

    return per_device


def solution(mesh):
    placed = (P("eig", "basis"), P("basis", "chan"), P(), P("chan"), P(), P("basis"))
    return jax.shard_map(
        make_per_device(ring_order(mesh)),
        mesh=mesh,
        in_specs=placed,
        out_specs=P("basis", "chan", "eig"),
        check_vma=False,
    )
```

time: 141 us -> 75.3 us (0.53)
  waiting for transfers between devices: 73.2 us -> 26.2 us
  blocking collectives: 20.9 us -> 0 us
  starting transfers between devices: 0.01 us -> 11.1 us
  between operations: 13.5 us -> 8.56 us
  other arithmetic: 4.47 us -> 1.13 us
    all_gather x1 -> x0, waiting for transfers between devices: 73.2 us -> none  [per_device(): panel_in = lax.all_gather(all_channels, 'eig', axis=0, tiled=True)]
    ppermute x0 -> x9, waiting for transfers between devices: none -> 26.2 us  [the longest x4 14.3 us: per_device(): fwd = lax.ppermute(fwd, 'eig', fwd_pairs)]
    psum x1 -> x0, blocking collectives: 18.6 us -> none  [per_device(): amplitudes = lax.psum(partial_value, 'basis').astype(jnp.bfloat16)]
    ppermute x0 -> x9, starting transfers between devices: none -> 11.1 us  [the longest x4 7.09 us: per_device(): fwd = lax.ppermute(fwd, 'eig', fwd_pairs)]
    convert_element_type x1 -> x0, other arithmetic: 4.13 us -> none  [per_device(): left_panel[None].astype(jnp.float32)]
    convert_element_type x1, local copies, waits for them, and re-layouts: 5.34 us -> 2.95 us  [per_device(): left_panel[None].astype(jnp.float32)]
    all_gather x1 -> x0, blocking collectives: 2.31 us -> none  [per_device(): all_channels = lax.all_gather(amplitudes, 'chan', axis=1, tiled=True)]
  transfers between devices with their start and end apart: 1 -> 9, of which waited for: 1 -> 4; matrix products, arithmetic and copies ran while one was open for 0% -> 6% of each run, Pallas kernels for 0% -> 0%
where the time goes in v2:
time: 75.3 us; the launch traced here: 75 us
  waiting for transfers between devices  26.2 us (35%)
  matrix products  22.6 us (30%)
  starting transfers between devices  11.1 us (15%)
  between operations  8.56 us (11%)
  local copies, waits for them, and re-layouts  5.46 us (7%)
  other arithmetic  1.13 us (2%)
    dot_general x1, matrix products, per_device(): jnp.einsum('ekc,kd->ecd', scaled, right_panel, preferred_element_type=jnp...  16.2 us
    ppermute x4, waiting for transfers between devices, per_device(): fwd = lax.ppermute(fwd, 'eig', fwd_pairs)  14.3 us
    ppermute x1, waiting for transfers between devices, per_device(): total = total + lax.ppermute(partial_value, 'basis', shift)  11.9 us
    ppermute x4, starting transfers between devices, per_device(): fwd = lax.ppermute(fwd, 'eig', fwd_pairs)  7.09 us
    dot_general x1, matrix products, per_device(): partial_value = jnp.dot(eigvecs, masked, preferred_element_type=jnp.float32)  6.4 us
    ppermute x1, starting transfers between devices, per_device(): total = total + lax.ppermute(partial_value, 'basis', shift)  3.03 us
    convert_element_type x1, local copies, waits for them, and re-layouts, per_device(): left_panel[None].astype(jnp.float32)  2.95 us
  transfers between devices with their start and end apart: 9, of which 4 were waited for; matrix products, arithmetic and copies ran while one was open for 6% of the time, Pallas kernels for 0%

profile of v2, /device:TPU:0, one launch (start us, length us, event | category | flops | bytes accessed | tf_op | source)
XLA Modules:
  0.0 75.0 jit_solution(12498795590492810445)
XLA Ops:
  0.0 0.8 %copy.13 = s32[16,1]{1,0:T(8,128)S(1)} copy(s32[16,1]{0,1:T(1,128)} %bitcast.21) | data formatting | bytes 128 | tf_op jit(solution)/shard_map/reshape.52
  0.8 0.1 reduce
  0.9 0.1 convert_reduce_fusion
  1.1 6.4 %fusion.6 = f32[64,2048]{1,0:T(8,128)S(1)} fusion(bf16[64,2560]{1,0:T(8,128)(2,1)S(1)} %copy-done, bf16[2560,2048]{1,0:T(8,128)(2,1)} %param.9, s32[2048]{0:T(1024)} %param.11, s32[2560]{0:T(1024)S(1)} %convert_reduce_fusion), kind=kOutput, calls=%fused_computation.9 | convolution fusion | flops 681574400 | bytes 11356160 | tf_op jit(solution)/shard_map/dot_general | solution.py:56
  7.5 0.0 copy-start.4
  7.5 0.0 copy-start.1
  7.5 3.0 %collective-permute-start = (f32[64,2048]{1,0:T(8,128)S(1)}, f32[64,2048]{1,0:T(8,128)S(1)}, u32[]{:S(2)}, u32[]{:S(2)}) collective-permute-start(f32[64,2048]{1,0:T(8,128)S(1)} %fusion.6), channel_id=1, source_target_pairs={{0,16},{16,0},{1,17},{17,1},{2,18},{18,2},{3,19},{19,3},{4,20},{20... | collective-permute-start | bytes 1572872 | tf_op jit(solution)/shard_map/ppermute | solution.py:61
  10.5 11.9 %collective-permute-done = f32[64,2048]{1,0:T(8,128)S(1)} collective-permute-done((f32[64,2048]{1,0:T(8,128)S(1)}, f32[64,2048]{1,0:T(8,128)S(1)}, u32[]{:S(2)}, u32[]{:S(2)}) %collective-permute-start) | collective-permute-done | bytes 524320 | tf_op jit(solution)/shard_map/ppermute | solution.py:61
  22.5 0.2 broadcast_in_dim.4
  22.7 0.8 %constant_dynamic-update-slice_fusion.7 = (bf16[512,2048]{1,0:T(8,128)(2,1)S(1)}, bf16[64,2048]{1,0:T(8,128)(2,1)}) fusion(bf16[512,2048]{1,0:T(8,128)(2,1)S(1)} %broadcast_in_dim.4, s32[]{:T(128)S(6)} %select_n.103, f32[64,2048]{1,0:T(8,128)S(1)} %fusion.6, f32[64,2048]{1,0:T(8,128)S(1)} %collective-permute-done), kind=kLoop, calls=%fused_computation.25 | loop fusion | flops 262144 | bytes 1572868 | tf_op jit(solution)/shard_map/dynamic_update_slice | solution.py:68
  23.5 1.8 %collective-permute-start.1 = (bf16[64,2048]{1,0:T(8,128)(2,1)}, bf16[64,2048]{1,0:T(8,128)(2,1)S(1)}, u32[]{:S(2)}, u32[]{:S(2)}) collective-permute-start(bf16[64,2048]{1,0:T(8,128)(2,1)} %get-tuple-element.6), channel_id=1, source_target_pairs={{4,8},{8,12},{12,14},{14,10},{10,6},{6,2},{2,0},{0,4},{5,9},{9,13}... | collective-permute-start | bytes 786440 | tf_op jit(solution)/shard_map/ppermute | solution.py:72
  25.3 0.2 collective-permute-start.2
  25.5 0.6 dynamic_slice.27
  30.2 0.7 fusion.11
  35.2 0.0 collective-permute-done.1
  35.2 1.9 %collective-permute-start.3 = (bf16[64,2048]{1,0:T(8,128)(2,1)S(1)}, bf16[64,2048]{1,0:T(8,128)(2,1)S(1)}, u32[]{:S(2)}, u32[]{:S(2)}) collective-permute-start(bf16[64,2048]{1,0:T(8,128)(2,1)S(1)} %collective-permute-done.1), channel_id=1, source_target_pairs={{4,8},{8,12},{12,14},{14,10},{10,6},{6,2},{2,0},{0,4},{5,9},{9,13}... | collective-permute-start | bytes 786440 | tf_op jit(solution)/shard_map/ppermute | solution.py:72
  37.0 0.0 collective-permute-done.2
  37.0 0.2 collective-permute-start.4
  37.3 0.0 copy-start.2
  37.3 0.0 copy-start.3
  37.3 4.8 %collective-permute-done.3 = bf16[64,2048]{1,0:T(8,128)(2,1)S(1)} collective-permute-done((bf16[64,2048]{1,0:T(8,128)(2,1)S(1)}, bf16[64,2048]{1,0:T(8,128)(2,1)S(1)}, u32[]{:S(2)}, u32[]{:S(2)}) %collective-permute-start.3) | collective-permute-done | bytes 262176 | tf_op jit(solution)/shard_map/ppermute | solution.py:72
  42.1 1.5 %collective-permute-start.5 = (bf16[64,2048]{1,0:T(8,128)(2,1)S(1)}, bf16[64,2048]{1,0:T(8,128)(2,1)S(1)}, u32[]{:S(2)}, u32[]{:S(2)}) collective-permute-start(bf16[64,2048]{1,0:T(8,128)(2,1)S(1)} %collective-permute-done.3), channel_id=1, source_target_pairs={{4,8},{8,12},{12,14},{14,10},{10,6},{6,2},{2,0},{0,4},{5,9},{9,13}... | collective-permute-start | bytes 786440 | tf_op jit(solution)/shard_map/ppermute | solution.py:72
  43.7 0.0 collective-permute-done.4
  43.7 0.5 collective-permute-start.6
  44.2 5.0 %collective-permute-done.5 = bf16[64,2048]{1,0:T(8,128)(2,1)S(1)} collective-permute-done((bf16[64,2048]{1,0:T(8,128)(2,1)S(1)}, bf16[64,2048]{1,0:T(8,128)(2,1)S(1)}, u32[]{:S(2)}, u32[]{:S(2)}) %collective-permute-start.5) | collective-permute-done | bytes 262176 | tf_op jit(solution)/shard_map/ppermute | solution.py:72
  49.2 1.8 %collective-permute-start.7 = (bf16[64,2048]{1,0:T(8,128)(2,1)S(1)}, bf16[64,2048]{1,0:T(8,128)(2,1)S(1)}, u32[]{:S(2)}, u32[]{:S(2)}) collective-permute-start(bf16[64,2048]{1,0:T(8,128)(2,1)S(1)} %collective-permute-done.5), channel_id=1, source_target_pairs={{4,8},{8,12},{12,14},{14,10},{10,6},{6,2},{2,0},{0,4},{5,9},{9,13}... | collective-permute-start | bytes 786440 | tf_op jit(solution)/shard_map/ppermute | solution.py:72
  51.1 0.0 collective-permute-done.6
  51.1 4.5 %collective-permute-done.7 = bf16[64,2048]{1,0:T(8,128)(2,1)S(1)} collective-permute-done((bf16[64,2048]{1,0:T(8,128)(2,1)S(1)}, bf16[64,2048]{1,0:T(8,128)(2,1)S(1)}, u32[]{:S(2)}, u32[]{:S(2)}) %collective-permute-start.7) | collective-permute-done | bytes 262176 | tf_op jit(solution)/shard_map/ppermute | solution.py:72
  55.7 0.1 collective-permute-start.8
  55.8 0.1 subtract_divide_fusion
  55.9 3.0 %copy.14 = f32[512,2048]{0,1:T(8,128)} copy(bf16[512,2048]{1,0:T(8,128)(2,1)S(1)} %constant_dynamic-update-slice_fusion) | data formatting | bytes 6291456 | tf_op jit(solution)/shard_map/convert_element_type | solution.py:92
  58.8 16.2 %convolution_multiply_fusion = f32[8,2048,512]{2,1,0:T(8,128)} fusion(f32[512,2048]{0,1:T(8,128)} %copy.14, f32[8,512]{1,0:T(8,128)S(1)} %subtract_divide_fusion, bf16[512,512]{1,0:T(8,128)(2,1)S(1)} %constant_dynamic-slice_fusion, bf16[512,512]{1,0:T(8,128)(2,1)S(1)} %collective-permute-done.8, pred[]{:T(512)S(6)} %eq.28), kind=kOutput, calls=%fused_computation.2 | convolution fusion | flops 8615362560 | bytes 38813696 | tf_op jit(solution)/shard_map/ekc,kd->ecd/dot_general | solution.py:93
  (17 shorter events, 0.3 us)
Async XLA Ops:
  0.0 1.1 %copy-start = (bf16[64,2560]{1,0:T(8,128)(2,1)S(1)}, bf16[64,2560]{1,0:T(8,128)(2,1)}, u32[]{:S(2)}) copy-start(bf16[64,2560]{1,0:T(8,128)(2,1)} %param.8) | copy-start | bytes 983044
  7.5 18.0 %copy-start.4 = (s32[8]{0:T(128)S(1)}, s32[8]{0:T(128)}, u32[]{:S(2)}) copy-start(s32[8]{0:T(128)} %constant.132.clone) | copy-start | bytes 100
  7.5 22.7 %copy-start.1 = (s32[8]{0:T(128)S(1)}, s32[8]{0:T(128)}, u32[]{:S(2)}) copy-start(s32[8]{0:T(128)} %constant.131.clone) | copy-start | bytes 100
  7.5 15.0 %collective-permute-start = (f32[64,2048]{1,0:T(8,128)S(1)}, f32[64,2048]{1,0:T(8,128)S(1)}, u32[]{:S(2)}, u32[]{:S(2)}) collective-permute-start(f32[64,2048]{1,0:T(8,128)S(1)} %fusion.6), channel_id=1, source_target_pairs={{0,16},{16,0},{1,17},{17,1},{2,18},{18,2},{3,19},{19,3},{4,20},{20... | collective-permute-start | bytes 1572872 | tf_op jit(solution)/shard_map/ppermute | solution.py:61
  23.5 11.7 %collective-permute-start.1 = (bf16[64,2048]{1,0:T(8,128)(2,1)}, bf16[64,2048]{1,0:T(8,128)(2,1)S(1)}, u32[]{:S(2)}, u32[]{:S(2)}) collective-permute-start(bf16[64,2048]{1,0:T(8,128)(2,1)} %get-tuple-element.6), channel_id=1, source_target_pairs={{4,8},{8,12},{12,14},{14,10},{10,6},{6,2},{2,0},{0,4},{5,9},{9,13}... | collective-permute-start | bytes 786440 | tf_op jit(solution)/shard_map/ppermute | solution.py:72
  25.3 11.7 %collective-permute-start.2 = (bf16[64,2048]{1,0:T(8,128)(2,1)}, bf16[64,2048]{1,0:T(8,128)(2,1)S(1)}, u32[]{:S(2)}, u32[]{:S(2)}) collective-permute-start(bf16[64,2048]{1,0:T(8,128)(2,1)} %get-tuple-element.6), channel_id=1, source_target_pairs={{4,0},{8,4},{12,8},{14,12},{10,14},{6,10},{2,6},{0,2},{5,1},{9,5},... | collective-permute-start | bytes 786440 | tf_op jit(solution)/shard_map/ppermute | solution.py:76
  35.2 7.0 %collective-permute-start.3 = (bf16[64,2048]{1,0:T(8,128)(2,1)S(1)}, bf16[64,2048]{1,0:T(8,128)(2,1)S(1)}, u32[]{:S(2)}, u32[]{:S(2)}) collective-permute-start(bf16[64,2048]{1,0:T(8,128)(2,1)S(1)} %collective-permute-done.1), channel_id=1, source_target_pairs={{4,8},{8,12},{12,14},{14,10},{10,6},{6,2},{2,0},{0,4},{5,9},{9,13}... | collective-permute-start | bytes 786440 | tf_op jit(solution)/shard_map/ppermute | solution.py:72
  37.0 6.6 %collective-permute-start.4 = (bf16[64,2048]{1,0:T(8,128)(2,1)S(1)}, bf16[64,2048]{1,0:T(8,128)(2,1)S(1)}, u32[]{:S(2)}, u32[]{:S(2)}) collective-permute-start(bf16[64,2048]{1,0:T(8,128)(2,1)S(1)} %collective-permute-done.2), channel_id=1, source_target_pairs={{4,0},{8,4},{12,8},{14,12},{10,14},{6,10},{2,6},{0,2},{5,1},{9,5},... | collective-permute-start | bytes 786440 | tf_op jit(solution)/shard_map/ppermute | solution.py:76
  37.3 18.5 %copy-start.2 = (f32[512]{0:T(512)S(1)}, f32[512]{0:T(512)}, u32[]{:S(2)}) copy-start(f32[512]{0:T(512)} %param.12) | copy-start | bytes 6148
  37.3 18.5 %copy-start.3 = (f32[8]{0:T(128)S(1)}, f32[8]{0:T(128)}, u32[]{:S(2)}) copy-start(f32[8]{0:T(128)} %param.13) | copy-start | bytes 100
  42.1 7.1 %collective-permute-start.5 = (bf16[64,2048]{1,0:T(8,128)(2,1)S(1)}, bf16[64,2048]{1,0:T(8,128)(2,1)S(1)}, u32[]{:S(2)}, u32[]{:S(2)}) collective-permute-start(bf16[64,2048]{1,0:T(8,128)(2,1)S(1)} %collective-permute-done.3), channel_id=1, source_target_pairs={{4,8},{8,12},{12,14},{14,10},{10,6},{6,2},{2,0},{0,4},{5,9},{9,13}... | collective-permute-start | bytes 786440 | tf_op jit(solution)/shard_map/ppermute | solution.py:72
  43.7 7.4 %collective-permute-start.6 = (bf16[64,2048]{1,0:T(8,128)(2,1)S(1)}, bf16[64,2048]{1,0:T(8,128)(2,1)S(1)}, u32[]{:S(2)}, u32[]{:S(2)}) collective-permute-start(bf16[64,2048]{1,0:T(8,128)(2,1)S(1)} %collective-permute-done.4), channel_id=1, source_target_pairs={{4,0},{8,4},{12,8},{14,12},{10,14},{6,10},{2,6},{0,2},{5,1},{9,5},... | collective-permute-start | bytes 786440 | tf_op jit(solution)/shard_map/ppermute | solution.py:76
  49.2 6.4 %collective-permute-start.7 = (bf16[64,2048]{1,0:T(8,128)(2,1)S(1)}, bf16[64,2048]{1,0:T(8,128)(2,1)S(1)}, u32[]{:S(2)}, u32[]{:S(2)}) collective-permute-start(bf16[64,2048]{1,0:T(8,128)(2,1)S(1)} %collective-permute-done.5), channel_id=1, source_target_pairs={{4,8},{8,12},{12,14},{14,10},{10,6},{6,2},{2,0},{0,4},{5,9},{9,13}... | collective-permute-start | bytes 786440 | tf_op jit(solution)/shard_map/ppermute | solution.py:72
  55.7 3.1 %collective-permute-start.8 = (bf16[512,512]{1,0:T(8,128)(2,1)S(1)}, bf16[512,512]{1,0:T(8,128)(2,1)S(1)}, u32[]{:S(2)}, u32[]{:S(2)}) collective-permute-start(bf16[512,512]{1,0:T(8,128)(2,1)S(1)} %constant_dynamic-slice_fusion), channel_id=1, source_target_pairs={{0,1},{1,0},{2,3},{3,2},{4,5},{5,4},{6,7},{7,6},{8,9},{9,8},{10,11... | collective-permute-start | bytes 1572872 | tf_op jit(solution)/shard_map/ppermute | solution.py:85

commit v3 on v2

--- a/solution.py
+++ b/solution.py
@@ -2,6 +2,8 @@
 import jax.numpy as jnp
 import numpy as np
 from jax import lax
+from jax.experimental import pallas as pl
+from jax.experimental.pallas import tpu as pltpu
 from jax.sharding import PartitionSpec as P
 
 
@@ -32,6 +34,37 @@
         return path if sorted(path) == list(range(n)) else list(range(n))
     except Exception:
         return list(range(n))
+
+
+def rmatrix_kernel(factor, w_ref, lt_ref, r_ref, o_ref):
+    e = pl.program_id(1)
+    w = w_ref[pl.ds(e, 1), :]
+    scaled = (lt_ref[...].astype(jnp.float32) * w).astype(jnp.bfloat16)
+    o_ref[0] = jnp.dot(scaled, r_ref[...], preferred_element_type=jnp.float32) * factor
+
+
+def rmatrix(weights, left_t, right_panel, factor):
+    n_e, k_all = weights.shape
+    width, _ = left_t.shape
+    cols = right_panel.shape[1]
+    tile = min(512, width)
+    return pl.pallas_call(
+        lambda *refs: rmatrix_kernel(factor, *refs),
+        grid=(width // tile, n_e),
+        in_specs=[
+            pl.BlockSpec((n_e, k_all), lambda c, e: (0, 0)),
+            pl.BlockSpec((tile, k_all), lambda c, e: (c, 0)),
+            pl.BlockSpec((k_all, cols), lambda c, e: (0, 0)),
+        ],
+        out_specs=pl.BlockSpec((1, tile, cols), lambda c, e: (e, c, 0)),
+        out_shape=jax.ShapeDtypeStruct((n_e, width, cols), jnp.float32),
+        compiler_params=pltpu.CompilerParams(dimension_semantics=("arbitrary", "arbitrary")),
+        cost_estimate=pl.CostEstimate(
+            flops=2 * n_e * width * k_all * cols,
+            bytes_accessed=4 * n_e * width * cols + 2 * width * k_all + 2 * k_all * cols,
+            transcendentals=0,
+        ),
+    )(weights, left_t, right_panel)
 
 
 def make_per_device(cycle):
@@ -89,9 +122,7 @@
             right_panel = lax.dynamic_index_in_dim(pieces, holder, 0, keepdims=False)
         factor = poles.shape[0] ** (-0.5)
         weights = 1.0 / (poles[None, :] - energies[:, None])
-        scaled = (weights[:, :, None] * left_panel[None].astype(jnp.float32)).astype(jnp.bfloat16)
-        summed = jnp.einsum("ekc,kd->ecd", scaled, right_panel, preferred_element_type=jnp.float32)
-        return summed * factor
+        return rmatrix(weights, left_panel.T, right_panel, factor)
 
     return per_device
 

time: 75.3 us -> 85.9 us (1.14)
  Pallas kernels: 0 us -> 25.6 us
  matrix products: 22.6 us -> 6.4 us
  other arithmetic: 1.13 us -> 2.69 us
    pallas_call x0 -> x1, Pallas kernels: none -> 25.6 us  [rmatrix(): pl.pallas_call(lambda *refs: rmatrix_kernel(factor, *refs), grid=(width /...]
    dot_general x1 -> x0, matrix products: 16.2 us -> none  [per_device(): jnp.einsum('ekc,kd->ecd', scaled, right_panel, preferred_element_type=jnp...]
    convert_element_type x1 -> x0, local copies, waits for them, and re-layouts: 2.95 us -> none  [per_device(): left_panel[None].astype(jnp.float32)]
    transpose x0 -> x1, local copies, waits for them, and re-layouts: none -> 2.49 us  [per_device(): return rmatrix(weights, left_panel.T, right_panel, factor)]
    select_n x0 -> x1, other arithmetic: none -> 0.96 us  [per_device(): right_panel = jnp.where(lax.axis_index('chan') == holder, piece, other)]
  transfers between devices with their start and end apart: 9 -> 9, of which waited for: 4 -> 4; matrix products, arithmetic and copies ran while one was open for 6% -> 5% of each run, Pallas kernels for 0% -> 0%
where the time goes in v3:
time: 85.9 us; the launch traced here: 85.6 us
  waiting for transfers between devices  26.2 us (31%)
  Pallas kernels  25.6 us (30%)
  starting transfers between devices  11.1 us (13%)
  between operations  8.56 us (10%)
  matrix products  6.4 us (7%)
  local copies, waits for them, and re-layouts  5 us (6%)
  other arithmetic  2.69 us (3%)
    pallas_call x1, Pallas kernels, rmatrix(): pl.pallas_call(lambda *refs: rmatrix_kernel(factor, *refs), grid=(width /...  25.6 us
    ppermute x4, waiting for transfers between devices, per_device(): fwd = lax.ppermute(fwd, 'eig', fwd_pairs)  14.3 us
    ppermute x1, waiting for transfers between devices, per_device(): total = total + lax.ppermute(partial_value, 'basis', shift)  11.9 us
    ppermute x4, starting transfers between devices, per_device(): fwd = lax.ppermute(fwd, 'eig', fwd_pairs)  7.09 us
    dot_general x1, matrix products, per_device(): partial_value = jnp.dot(eigvecs, masked, preferred_element_type=jnp.float32)  6.4 us
    ppermute x1, starting transfers between devices, per_device(): total = total + lax.ppermute(partial_value, 'basis', shift)  3.03 us
    transpose x1, local copies, waits for them, and re-layouts, per_device(): return rmatrix(weights, left_panel.T, right_panel, factor)  2.49 us
  transfers between devices with their start and end apart: 9, of which 4 were waited for; matrix products, arithmetic and copies ran while one was open for 5% of the time, Pallas kernels for 0%

profile of v3, /device:TPU:0, one launch (start us, length us, event | category | flops | bytes accessed | tf_op | source)
XLA Modules:
  0.0 85.6 jit_solution(9445621878929079002)
XLA Ops:
  0.0 0.8 copy.13
  0.8 0.1 reduce
  0.9 0.1 convert_reduce_fusion
  1.1 6.4 %fusion.4 = f32[64,2048]{1,0:T(8,128)S(1)} fusion(bf16[64,2560]{1,0:T(8,128)(2,1)S(1)} %copy-done, bf16[2560,2048]{1,0:T(8,128)(2,1)} %param.9, s32[2048]{0:T(1024)} %param.11, s32[2560]{0:T(1024)S(1)} %convert_reduce_fusion), kind=kOutput, calls=%fused_computation.5 | convolution fusion | flops 681574400 | bytes 11356160 | tf_op jit(solution)/shard_map/dot_general | solution.py:89
  7.5 0.0 copy-start.4
  7.5 0.0 copy-start.1
  7.5 3.0 %collective-permute-start = (f32[64,2048]{1,0:T(8,128)S(1)}, f32[64,2048]{1,0:T(8,128)S(1)}, u32[]{:S(2)}, u32[]{:S(2)}) collective-permute-start(f32[64,2048]{1,0:T(8,128)S(1)} %fusion.4), channel_id=1, source_target_pairs={{0,16},{16,0},{1,17},{17,1},{2,18},{18,2},{3,19},{19,3},{4,20},{20... | collective-permute-start | bytes 1572872 | tf_op jit(solution)/shard_map/ppermute | solution.py:94
  10.5 11.9 %collective-permute-done = f32[64,2048]{1,0:T(8,128)S(1)} collective-permute-done((f32[64,2048]{1,0:T(8,128)S(1)}, f32[64,2048]{1,0:T(8,128)S(1)}, u32[]{:S(2)}, u32[]{:S(2)}) %collective-permute-start) | collective-permute-done | bytes 524320 | tf_op jit(solution)/shard_map/ppermute | solution.py:94
  22.5 0.2 broadcast_in_dim.4
  22.7 0.8 constant_dynamic-update-slice_fusion.7
  23.5 1.8 %collective-permute-start.1 = (bf16[64,2048]{1,0:T(8,128)(2,1)}, bf16[64,2048]{1,0:T(8,128)(2,1)S(1)}, u32[]{:S(2)}, u32[]{:S(2)}) collective-permute-start(bf16[64,2048]{1,0:T(8,128)(2,1)} %get-tuple-element.6), channel_id=1, source_target_pairs={{4,8},{8,12},{12,14},{14,10},{10,6},{6,2},{2,0},{0,4},{5,9},{9,13}... | collective-permute-start | bytes 786440 | tf_op jit(solution)/shard_map/ppermute | solution.py:105
  25.3 0.2 collective-permute-start.2
  25.5 0.6 dynamic_slice.27
  30.2 0.7 fusion.6
  35.2 0.0 collective-permute-done.1
  35.2 1.9 %collective-permute-start.3 = (bf16[64,2048]{1,0:T(8,128)(2,1)S(1)}, bf16[64,2048]{1,0:T(8,128)(2,1)S(1)}, u32[]{:S(2)}, u32[]{:S(2)}) collective-permute-start(bf16[64,2048]{1,0:T(8,128)(2,1)S(1)} %collective-permute-done.1), channel_id=1, source_target_pairs={{4,8},{8,12},{12,14},{14,10},{10,6},{6,2},{2,0},{0,4},{5,9},{9,13}... | collective-permute-start | bytes 786440 | tf_op jit(solution)/shard_map/ppermute | solution.py:105
  37.0 0.0 collective-permute-done.2
  37.0 0.2 collective-permute-start.4
  37.3 0.0 copy-start.2
  37.3 0.0 copy-start.3
  37.3 4.8 %collective-permute-done.3 = bf16[64,2048]{1,0:T(8,128)(2,1)S(1)} collective-permute-done((bf16[64,2048]{1,0:T(8,128)(2,1)S(1)}, bf16[64,2048]{1,0:T(8,128)(2,1)S(1)}, u32[]{:S(2)}, u32[]{:S(2)}) %collective-permute-start.3) | collective-permute-done | bytes 262176 | tf_op jit(solution)/shard_map/ppermute | solution.py:105
  42.1 1.5 %collective-permute-start.5 = (bf16[64,2048]{1,0:T(8,128)(2,1)S(1)}, bf16[64,2048]{1,0:T(8,128)(2,1)S(1)}, u32[]{:S(2)}, u32[]{:S(2)}) collective-permute-start(bf16[64,2048]{1,0:T(8,128)(2,1)S(1)} %collective-permute-done.3), channel_id=1, source_target_pairs={{4,8},{8,12},{12,14},{14,10},{10,6},{6,2},{2,0},{0,4},{5,9},{9,13}... | collective-permute-start | bytes 786440 | tf_op jit(solution)/shard_map/ppermute | solution.py:105
  43.7 0.5 collective-permute-start.6
  44.2 5.0 %collective-permute-done.5 = bf16[64,2048]{1,0:T(8,128)(2,1)S(1)} collective-permute-done((bf16[64,2048]{1,0:T(8,128)(2,1)S(1)}, bf16[64,2048]{1,0:T(8,128)(2,1)S(1)}, u32[]{:S(2)}, u32[]{:S(2)}) %collective-permute-start.5) | collective-permute-done | bytes 262176 | tf_op jit(solution)/shard_map/ppermute | solution.py:105
  49.2 1.8 %collective-permute-start.7 = (bf16[64,2048]{1,0:T(8,128)(2,1)S(1)}, bf16[64,2048]{1,0:T(8,128)(2,1)S(1)}, u32[]{:S(2)}, u32[]{:S(2)}) collective-permute-start(bf16[64,2048]{1,0:T(8,128)(2,1)S(1)} %collective-permute-done.5), channel_id=1, source_target_pairs={{4,8},{8,12},{12,14},{14,10},{10,6},{6,2},{2,0},{0,4},{5,9},{9,13}... | collective-permute-start | bytes 786440 | tf_op jit(solution)/shard_map/ppermute | solution.py:105
  51.1 4.5 %collective-permute-done.7 = bf16[64,2048]{1,0:T(8,128)(2,1)S(1)} collective-permute-done((bf16[64,2048]{1,0:T(8,128)(2,1)S(1)}, bf16[64,2048]{1,0:T(8,128)(2,1)S(1)}, u32[]{:S(2)}, u32[]{:S(2)}) %collective-permute-start.7) | collective-permute-done | bytes 262176 | tf_op jit(solution)/shard_map/ppermute | solution.py:105
  55.7 0.1 collective-permute-start.8
  55.8 0.7 subtract_divide_fusion.refs_0_
  56.5 2.5 %copy.14.refs_1_ = bf16[2048,512]{1,0:T(8,128)(2,1)} copy(bf16[2048,512]{0,1:T(8,128)(2,1)S(1)} %bitcast.19) | data formatting | bytes 4194304 | tf_op jit(solution)/shard_map/transpose | solution.py:125
  58.9 0.0 collective-permute-done.8
  58.9 1.0 %broadcast_select_fusion.refs_2_ = bf16[512,512]{1,0:T(8,128)(2,1)} fusion(bf16[512,512]{1,0:T(8,128)(2,1)S(1)} %collective-permute-done.8, pred[]{:T(512)S(6)} %eq.28, bf16[512,2048]{1,0:T(8,128)(2,1)S(1)} %constant_dynamic-update-slice_fusion, s32[]{:T(128)S(6)} %select_n.129), kind=kLoop, calls=%fused_computation.7 | loop fusion | flops 262144 | bytes 1572869 | tf_op jit(solution)/shard_map/jit(_where)/select_n | solution.py:119
  59.9 25.6 %shard_map.82 = f32[8,2048,512]{2,1,0:T(8,128)} custom-call(f32[8,512]{1,0:T(8,128)} %subtract_divide_fusion.refs_0_, bf16[2048,512]{1,0:T(8,128)(2,1)} %copy.14.refs_1_, bf16[512,512]{1,0:T(8,128)(2,1)} %broadcast_select_fusion.refs_2_), custom_call_target="tpu_custom_call" | custom-call | flops 8589934592 | bytes 36175872 | tf_op jit(solution)/shard_map/pallas_call | solution.py:51
  (18 shorter events, 0.3 us)
Async XLA Ops:
  0.0 1.1 %copy-start = (bf16[64,2560]{1,0:T(8,128)(2,1)S(1)}, bf16[64,2560]{1,0:T(8,128)(2,1)}, u32[]{:S(2)}) copy-start(bf16[64,2560]{1,0:T(8,128)(2,1)} %param.8) | copy-start | bytes 983044
  7.5 18.0 %copy-start.4 = (s32[8]{0:T(128)S(1)}, s32[8]{0:T(128)}, u32[]{:S(2)}) copy-start(s32[8]{0:T(128)} %constant.130.clone) | copy-start | bytes 100
  7.5 22.7 %copy-start.1 = (s32[8]{0:T(128)S(1)}, s32[8]{0:T(128)}, u32[]{:S(2)}) copy-start(s32[8]{0:T(128)} %constant.129.clone) | copy-start | bytes 100
  7.5 15.0 %collective-permute-start = (f32[64,2048]{1,0:T(8,128)S(1)}, f32[64,2048]{1,0:T(8,128)S(1)}, u32[]{:S(2)}, u32[]{:S(2)}) collective-permute-start(f32[64,2048]{1,0:T(8,128)S(1)} %fusion.4), channel_id=1, source_target_pairs={{0,16},{16,0},{1,17},{17,1},{2,18},{18,2},{3,19},{19,3},{4,20},{20... | collective-permute-start | bytes 1572872 | tf_op jit(solution)/shard_map/ppermute | solution.py:94
  23.5 11.7 %collective-permute-start.1 = (bf16[64,2048]{1,0:T(8,128)(2,1)}, bf16[64,2048]{1,0:T(8,128)(2,1)S(1)}, u32[]{:S(2)}, u32[]{:S(2)}) collective-permute-start(bf16[64,2048]{1,0:T(8,128)(2,1)} %get-tuple-element.6), channel_id=1, source_target_pairs={{4,8},{8,12},{12,14},{14,10},{10,6},{6,2},{2,0},{0,4},{5,9},{9,13}... | collective-permute-start | bytes 786440 | tf_op jit(solution)/shard_map/ppermute | solution.py:105
  25.3 11.7 %collective-permute-start.2 = (bf16[64,2048]{1,0:T(8,128)(2,1)}, bf16[64,2048]{1,0:T(8,128)(2,1)S(1)}, u32[]{:S(2)}, u32[]{:S(2)}) collective-permute-start(bf16[64,2048]{1,0:T(8,128)(2,1)} %get-tuple-element.6), channel_id=1, source_target_pairs={{4,0},{8,4},{12,8},{14,12},{10,14},{6,10},{2,6},{0,2},{5,1},{9,5},... | collective-permute-start | bytes 786440 | tf_op jit(solution)/shard_map/ppermute | solution.py:109
  35.2 7.0 %collective-permute-start.3 = (bf16[64,2048]{1,0:T(8,128)(2,1)S(1)}, bf16[64,2048]{1,0:T(8,128)(2,1)S(1)}, u32[]{:S(2)}, u32[]{:S(2)}) collective-permute-start(bf16[64,2048]{1,0:T(8,128)(2,1)S(1)} %collective-permute-done.1), channel_id=1, source_target_pairs={{4,8},{8,12},{12,14},{14,10},{10,6},{6,2},{2,0},{0,4},{5,9},{9,13}... | collective-permute-start | bytes 786440 | tf_op jit(solution)/shard_map/ppermute | solution.py:105
  37.0 6.6 %collective-permute-start.4 = (bf16[64,2048]{1,0:T(8,128)(2,1)S(1)}, bf16[64,2048]{1,0:T(8,128)(2,1)S(1)}, u32[]{:S(2)}, u32[]{:S(2)}) collective-permute-start(bf16[64,2048]{1,0:T(8,128)(2,1)S(1)} %collective-permute-done.2), channel_id=1, source_target_pairs={{4,0},{8,4},{12,8},{14,12},{10,14},{6,10},{2,6},{0,2},{5,1},{9,5},... | collective-permute-start | bytes 786440 | tf_op jit(solution)/shard_map/ppermute | solution.py:109
  37.3 18.5 %copy-start.2 = (f32[512]{0:T(512)S(1)}, f32[512]{0:T(512)}, u32[]{:S(2)}) copy-start(f32[512]{0:T(512)} %param.12) | copy-start | bytes 6148
  37.3 18.5 %copy-start.3 = (f32[8]{0:T(128)S(1)}, f32[8]{0:T(128)}, u32[]{:S(2)}) copy-start(f32[8]{0:T(128)} %param.13) | copy-start | bytes 100
  42.1 7.1 %collective-permute-start.5 = (bf16[64,2048]{1,0:T(8,128)(2,1)S(1)}, bf16[64,2048]{1,0:T(8,128)(2,1)S(1)}, u32[]{:S(2)}, u32[]{:S(2)}) collective-permute-start(bf16[64,2048]{1,0:T(8,128)(2,1)S(1)} %collective-permute-done.3), channel_id=1, source_target_pairs={{4,8},{8,12},{12,14},{14,10},{10,6},{6,2},{2,0},{0,4},{5,9},{9,13}... | collective-permute-start | bytes 786440 | tf_op jit(solution)/shard_map/ppermute | solution.py:105
  43.7 7.4 %collective-permute-start.6 = (bf16[64,2048]{1,0:T(8,128)(2,1)S(1)}, bf16[64,2048]{1,0:T(8,128)(2,1)S(1)}, u32[]{:S(2)}, u32[]{:S(2)}) collective-permute-start(bf16[64,2048]{1,0:T(8,128)(2,1)S(1)} %collective-permute-done.4), channel_id=1, source_target_pairs={{4,0},{8,4},{12,8},{14,12},{10,14},{6,10},{2,6},{0,2},{5,1},{9,5},... | collective-permute-start | bytes 786440 | tf_op jit(solution)/shard_map/ppermute | solution.py:109
  49.2 6.4 %collective-permute-start.7 = (bf16[64,2048]{1,0:T(8,128)(2,1)S(1)}, bf16[64,2048]{1,0:T(8,128)(2,1)S(1)}, u32[]{:S(2)}, u32[]{:S(2)}) collective-permute-start(bf16[64,2048]{1,0:T(8,128)(2,1)S(1)} %collective-permute-done.5), channel_id=1, source_target_pairs={{4,8},{8,12},{12,14},{14,10},{10,6},{6,2},{2,0},{0,4},{5,9},{9,13}... | collective-permute-start | bytes 786440 | tf_op jit(solution)/shard_map/ppermute | solution.py:105
  55.7 3.3 %collective-permute-start.8 = (bf16[512,512]{1,0:T(8,128)(2,1)S(1)}, bf16[512,512]{1,0:T(8,128)(2,1)S(1)}, u32[]{:S(2)}, u32[]{:S(2)}) collective-permute-start(bf16[512,512]{1,0:T(8,128)(2,1)S(1)} %constant_dynamic-slice_fusion), channel_id=1, source_target_pairs={{0,1},{1,0},{2,3},{3,2},{4,5},{5,4},{6,7},{7,6},{8,9},{9,8},{10,11... | collective-permute-start | bytes 1572872 | tf_op jit(solution)/shard_map/ppermute | solution.py:118

commit v4 on v2

--- a/solution.py
+++ b/solution.py
@@ -53,33 +53,51 @@
         owner_of = jnp.sum((block_ends[None, :] <= row_ids[:, None]).astype(jnp.int32), axis=1)
         member = owner_of[:, None] == target_of_channel[None, :]
         masked = jnp.where(member, boundary, jnp.zeros_like(boundary))
-        partial_value = jnp.dot(eigvecs, masked, preferred_element_type=jnp.float32)
         n_basis = lax.axis_size("basis")
-        total = partial_value
-        for s in range(1, n_basis):
-            shift = [(b, (b + s) % n_basis) for b in range(n_basis)]
-            total = total + lax.ppermute(partial_value, "basis", shift)
-        amp = total.astype(jnp.bfloat16)
+        width = masked.shape[1]
+        halves = 2 if width % 256 == 0 else 1
+        step = width // halves
+        amp_parts = []
+        for h in range(halves):
+            part = jnp.dot(eigvecs, masked[:, h * step:(h + 1) * step], preferred_element_type=jnp.float32)
+            total = part
+            for s in range(1, n_basis):
+                shift = [(b, (b + s) % n_basis) for b in range(n_basis)]
+                total = total + lax.ppermute(part, "basis", shift)
+            amp_parts.append(total.astype(jnp.bfloat16))
+        amp = jnp.concatenate(amp_parts, axis=1) if halves > 1 else amp_parts[0]
         eig_index = lax.axis_index("eig")
         cycle_arr = jnp.array(cycle, dtype=jnp.int32)
         pos = jnp.array(position, dtype=jnp.int32)[eig_index]
         k_here = amp.shape[0]
-        left_panel = jnp.zeros((k_here * n_ring, amp.shape[1]), amp.dtype)
-        left_panel = lax.dynamic_update_slice_in_dim(left_panel, amp, eig_index * k_here, 0)
+        col_width = width * n_chan // n_eig
+        ratio = n_eig // n_chan
+        col_first = (eig_index % ratio) * col_width
+        n_e = energies.shape[0]
+        scaled_t = jnp.zeros((n_e, width, k_here * n_ring), jnp.bfloat16)
+        right_rows = []
+
+        def take(slot, block, origin, scaled_t):
+            pole_part = lax.dynamic_slice_in_dim(poles, origin * k_here, k_here)
+            weights = 1.0 / (pole_part[None, :] - energies[:, None])
+            piece = (weights[:, None, :] * block.T[None].astype(jnp.float32)).astype(jnp.bfloat16)
+            scaled_t = scaled_t.at[:, :, slot * k_here:(slot + 1) * k_here].set(piece)
+            right_rows.append(lax.dynamic_slice_in_dim(block, col_first, col_width, 1))
+            return scaled_t
+
+        scaled_t = take(0, amp, eig_index, scaled_t)
+        slot = 1
         fwd, bwd = amp, amp
         for s in range(max(n_fwd, n_bwd)):
             if s < n_fwd:
                 fwd = lax.ppermute(fwd, "eig", fwd_pairs)
-                origin = cycle_arr[(pos - s - 1) % n_ring]
-                left_panel = lax.dynamic_update_slice_in_dim(left_panel, fwd, origin * k_here, 0)
+                scaled_t = take(slot, fwd, cycle_arr[(pos - s - 1) % n_ring], scaled_t)
+                slot += 1
             if s < n_bwd:
                 bwd = lax.ppermute(bwd, "eig", bwd_pairs)
-                origin = cycle_arr[(pos + s + 1) % n_ring]
-                left_panel = lax.dynamic_update_slice_in_dim(left_panel, bwd, origin * k_here, 0)
-        own_width = left_panel.shape[1]
-        col_width = own_width * n_chan // n_eig
-        ratio = n_eig // n_chan
-        piece = lax.dynamic_slice_in_dim(left_panel, (eig_index % ratio) * col_width, col_width, 1)
+                scaled_t = take(slot, bwd, cycle_arr[(pos + s + 1) % n_ring], scaled_t)
+                slot += 1
+        piece = jnp.concatenate(right_rows, axis=0)
         holder = eig_index // ratio
         if n_chan == 2:
             other = lax.ppermute(piece, "chan", [(0, 1), (1, 0)])
@@ -88,9 +106,7 @@
             pieces = lax.all_gather(piece, "chan", axis=0, tiled=False)
             right_panel = lax.dynamic_index_in_dim(pieces, holder, 0, keepdims=False)
         factor = poles.shape[0] ** (-0.5)
-        weights = 1.0 / (poles[None, :] - energies[:, None])
-        scaled = (weights[:, :, None] * left_panel[None].astype(jnp.float32)).astype(jnp.bfloat16)
-        summed = jnp.einsum("ekc,kd->ecd", scaled, right_panel, preferred_element_type=jnp.float32)
+        summed = jnp.einsum("eck,kd->ecd", scaled_t, right_panel, preferred_element_type=jnp.float32)
         return summed * factor
 
     return per_device

time: 75.3 us -> 409 us (5.43); the launches traced: 75 us -> 401 us
  local copies, waits for them, and re-layouts: 5.46 us -> 319 us
  other arithmetic: 1.13 us -> 27.3 us
  waiting for transfers between devices: 26.2 us -> 10.7 us
    scatter x0 -> x8, local copies, waits for them, and re-layouts: none -> 309 us  [take(): scaled_t = scaled_t.at[:, :, slot * k_here:(slot + 1) * k_here].set(piece)]
    convert_element_type x0 -> x17, other arithmetic: none -> 20.1 us  [the longest x8 19.7 us: take(): (weights[:, None, :] * block.T[None].astype(jnp.float32)).astype(jnp.bflo...]
    ppermute x4, waiting for transfers between devices: 14.3 us -> 0.01 us  [per_device(): fwd = lax.ppermute(fwd, 'eig', fwd_pairs)]
    ppermute x1 -> x2, waiting for transfers between devices: 11.9 us -> 0.14 us  [per_device(): total = total + lax.ppermute(part, 'basis', shift)]
    ppermute x3, waiting for transfers between devices: 0.01 us -> 10.5 us  [per_device(): bwd = lax.ppermute(bwd, 'eig', bwd_pairs)]
    select_n x0 -> x1, other arithmetic: none -> 6.77 us  [per_device(): masked = jnp.where(member, boundary, jnp.zeros_like(boundary))]
    unnamed x10 -> x32, local copies, waits for them, and re-layouts: 0.03 us -> 5.31 us
    dot_general x2 -> x3, matrix products: 22.6 us -> 24.2 us  [the longest x1 22.1 us: per_device(): jnp.einsum('eck,kd->ecd', scaled_t, right_panel, preferred_element_type=j...]
  transfers between devices with their start and end apart: 9 -> 10, of which waited for: 4 -> 3; matrix products, arithmetic and copies ran while one was open for 6% -> 81% of each run, Pallas kernels for 0% -> 0%
where the time goes in v4:
time: 409 us; the launch traced here: 401 us
  local copies, waits for them, and re-layouts  319 us (78%)
  other arithmetic  27.3 us (7%)
  matrix products  24.2 us (6%)
  starting transfers between devices  10.9 us (3%)
  waiting for transfers between devices  10.7 us (3%)
  between operations  9.46 us (2%)
    scatter x8, local copies, waits for them, and re-layouts, take(): scaled_t = scaled_t.at[:, :, slot * k_here:(slot + 1) * k_here].set(piece)  309 us
    dot_general x1, matrix products, per_device(): jnp.einsum('eck,kd->ecd', scaled_t, right_panel, preferred_element_type=j...  22.1 us
    convert_element_type x8, other arithmetic, take(): (weights[:, None, :] * block.T[None].astype(jnp.float32)).astype(jnp.bflo...  19.7 us
    ppermute x3, waiting for transfers between devices, per_device(): bwd = lax.ppermute(bwd, 'eig', bwd_pairs)  10.5 us
  transfers between devices with their start and end apart: 10, of which 3 were waited for; matrix products, arithmetic and copies ran while one was open for 81% of the time, Pallas kernels for 0%

profile of v4, /device:TPU:0, one launch (start us, length us, event | category | flops | bytes accessed | tf_op | source)
XLA Modules:
  0.0 401.4 jit_solution(4133889080308708829)
XLA Ops:
  0.0 0.8 copy.27
  1.1 6.8 %compare_select_fusion = bf16[2560,2048]{1,0:T(8,128)(2,1)S(1)} fusion(bf16[2560,2048]{1,0:T(8,128)(2,1)} %param.25, s32[2048]{0:T(1024)} %param.27, s32[2560]{0:T(1024)S(1)} %convert_reduce_fusion), kind=kLoop, calls=%fused_computation | loop fusion | flops 10485760 | bytes 20989952 | tf_op jit(solution)/shard_map/jit(_where)/select_n | solution.py:55
  7.9 1.1 fusion.4
  8.9 3.0 collective-permute-start
  12.0 1.0 fusion.7
  24.0 2.0 collective-permute-start.2
  26.4 0.7 multiply_convert_fusion.7
  27.1 6.0 %scatter.26 = bf16[8,2048,512]{2,1,0:T(8,128)(2,1)} pad(bf16[8,2048,64]{2,1,0:T(8,128)(2,1)S(1)} %multiply_convert_fusion.7, bf16[]{:T(256)} %constant.327.clone.1), padding=0_0x0_0x0_448 | pad | bytes 18874370 | tf_op jit(solution)/shard_map/scatter | solution.py:84
  35.0 2.7 multiply_convert_fusion.6
  37.7 2.0 collective-permute-start.4
  39.7 2.7 multiply_convert_fusion.5
  42.4 46.4 %scatter.29 = bf16[8,2048,512]{2,1,0:T(8,128)(2,1)} dynamic-update-slice(bf16[8,2048,512]{2,1,0:T(8,128)(2,1)} %scatter.26, bf16[8,2048,64]{2,1,0:T(8,128)(2,1)} %multiply_convert_fusion.6, s32[]{:T(128)} %constant.323.clone.1, s32[]{:T(128)} %constant.323.clone.1, s32[]{:T(128)} %constant.322.clone.1) | dynamic-update-slice | bytes 4194308 | tf_op jit(solution)/shard_map/scatter | solution.py:84
  88.8 39.8 %scatter.30 = bf16[8,2048,512]{2,1,0:T(8,128)(2,1)} dynamic-update-slice(bf16[8,2048,512]{2,1,0:T(8,128)(2,1)} %scatter.29, bf16[8,2048,64]{2,1,0:T(8,128)(2,1)} %multiply_convert_fusion.5, s32[]{:T(128)} %constant.323.clone.1, s32[]{:T(128)} %constant.323.clone.1, s32[]{:T(128)} %constant.333.clone.1) | dynamic-update-slice | bytes 4194308 | tf_op jit(solution)/shard_map/scatter | solution.py:84
  128.7 0.8 dynamic-slice_dynamic-update-slice_fusion.6
  129.9 5.3 %collective-permute-done.5 = bf16[64,2048]{1,0:T(8,128)(2,1)S(1)} collective-permute-done((bf16[64,2048]{1,0:T(8,128)(2,1)S(1)}, bf16[64,2048]{1,0:T(8,128)(2,1)S(1)}, u32[]{:S(2)}, u32[]{:S(2)}) %collective-permute-start.5) | collective-permute-done | bytes 262176 | tf_op jit(solution)/shard_map/ppermute | solution.py:97
  135.3 0.7 copy-done.6
  136.4 2.7 multiply_convert_fusion.4
  139.1 1.6 collective-permute-start.6
  140.7 2.7 multiply_convert_fusion.3
  143.4 46.5 %scatter.31 = bf16[8,2048,512]{2,1,0:T(8,128)(2,1)} dynamic-update-slice(bf16[8,2048,512]{2,1,0:T(8,128)(2,1)} %scatter.30, bf16[8,2048,64]{2,1,0:T(8,128)(2,1)} %multiply_convert_fusion.4, s32[]{:T(128)} %constant.323.clone.1, s32[]{:T(128)} %constant.323.clone.1, s32[]{:T(128)} %constant.335.clone.1) | dynamic-update-slice | bytes 4194308 | tf_op jit(solution)/shard_map/scatter | solution.py:84
  189.8 39.8 %scatter.34 = bf16[8,2048,512]{2,1,0:T(8,128)(2,1)} dynamic-update-slice(bf16[8,2048,512]{2,1,0:T(8,128)(2,1)} %scatter.31, bf16[8,2048,64]{2,1,0:T(8,128)(2,1)} %multiply_convert_fusion.3, s32[]{:T(128)} %constant.323.clone.1, s32[]{:T(128)} %constant.323.clone.1, s32[]{:T(128)} %constant.337.clone.1) | dynamic-update-slice | bytes 4194308 | tf_op jit(solution)/shard_map/scatter | solution.py:84
  230.9 5.2 %collective-permute-done.7 = bf16[64,2048]{1,0:T(8,128)(2,1)S(1)} collective-permute-done((bf16[64,2048]{1,0:T(8,128)(2,1)S(1)}, bf16[64,2048]{1,0:T(8,128)(2,1)S(1)}, u32[]{:S(2)}, u32[]{:S(2)}) %collective-permute-start.7) | collective-permute-done | bytes 262176 | tf_op jit(solution)/shard_map/ppermute | solution.py:97
  237.1 2.7 multiply_convert_fusion.2
  239.9 1.6 collective-permute-start.8
  241.5 2.7 multiply_convert_fusion.1
  244.1 46.4 %scatter.35 = bf16[8,2048,512]{2,1,0:T(8,128)(2,1)} dynamic-update-slice(bf16[8,2048,512]{2,1,0:T(8,128)(2,1)} %scatter.34, bf16[8,2048,64]{2,1,0:T(8,128)(2,1)} %multiply_convert_fusion.2, s32[]{:T(128)} %constant.323.clone.1, s32[]{:T(128)} %constant.323.clone.1, s32[]{:T(128)} %constant.339.clone.1) | dynamic-update-slice | bytes 4194308 | tf_op jit(solution)/shard_map/scatter | solution.py:84
  290.5 38.6 %scatter.36 = bf16[8,2048,512]{2,1,0:T(8,128)(2,1)} dynamic-update-slice(bf16[8,2048,512]{2,1,0:T(8,128)(2,1)} %scatter.35, bf16[8,2048,64]{2,1,0:T(8,128)(2,1)} %multiply_convert_fusion.1, s32[]{:T(128)} %constant.323.clone.1, s32[]{:T(128)} %constant.323.clone.1, s32[]{:T(128)} %constant.341.clone.1) | dynamic-update-slice | bytes 4194308 | tf_op jit(solution)/shard_map/scatter | solution.py:84
  329.1 0.8 dynamic-slice_dynamic-update-slice_fusion.2
  329.9 0.8 dynamic-slice_dynamic-update-slice_fusion.1
  331.3 2.7 multiply_convert_fusion
  334.0 45.3 %scatter.39 = bf16[8,2048,512]{2,1,0:T(8,128)(2,1)} dynamic-update-slice(bf16[8,2048,512]{2,1,0:T(8,128)(2,1)} %scatter.36, bf16[8,2048,64]{2,1,0:T(8,128)(2,1)} %multiply_convert_fusion, s32[]{:T(128)} %constant.323.clone.1, s32[]{:T(128)} %constant.323.clone.1, s32[]{:T(128)} %constant.343.clone.1) | dynamic-update-slice | bytes 4194308 | tf_op jit(solution)/shard_map/scatter | solution.py:84
  379.3 22.1 %convolution_multiply_fusion = f32[8,2048,512]{2,1,0:T(8,128)} fusion(bf16[8,2048,512]{2,1,0:T(8,128)(2,1)} %scatter.39, bf16[512,512]{1,0:T(8,128)(2,1)S(1)} %dynamic-slice_dynamic-update-slice_fusion, bf16[512,512]{1,0:T(8,128)(2,1)S(1)} %collective-permute-done.9, pred[]{:T(512)S(6)} %eq.28), kind=kOutput, calls=%fused_computation.1 | convolution fusion | flops 8598585344 | bytes 51380224 | tf_op jit(solution)/shard_map/eck,kd->ecd/dot_general | solution.py:109
  (69 shorter events, 7.7 us)
Async XLA Ops:
  0.0 7.8 %copy-start = (bf16[64,2560]{1,0:T(8,128)(2,1)S(1)}, bf16[64,2560]{1,0:T(8,128)(2,1)}, u32[]{:S(2)}) copy-start(bf16[64,2560]{1,0:T(8,128)(2,1)} %param.24) | copy-start | bytes 983044
  7.8 5.3 %copy-start.12 = (s32[8]{0:T(128)S(1)}, s32[8]{0:T(128)}, u32[]{:S(2)}) copy-start(s32[8]{0:T(128)} %constant.352.clone) | copy-start | bytes 100
  7.9 10.5 %copy-start.9 = (s32[8]{0:T(128)S(1)}, s32[8]{0:T(128)}, u32[]{:S(2)}) copy-start(s32[8]{0:T(128)} %constant.351.clone) | copy-start | bytes 100
  7.9 15.6 %copy-start.10 = (f32[512]{0:T(512)S(1)}, f32[512]{0:T(512)}, u32[]{:S(2)}) copy-start(f32[512]{0:T(512)} %param.28) | copy-start | bytes 6148
  7.9 15.7 %copy-start.11 = (f32[8]{0:T(128)S(1)}, f32[8]{0:T(128)}, u32[]{:S(2)}) copy-start(f32[8]{0:T(128)} %param.29) | copy-start | bytes 100
  8.9 14.8 %collective-permute-start = (f32[64,1024]{1,0:T(8,128)S(1)}, f32[64,1024]{1,0:T(8,128)S(1)}, u32[]{:S(2)}, u32[]{:S(2)}) collective-permute-start(f32[64,1024]{1,0:T(8,128)S(1)} %fusion.4), channel_id=1, source_target_pairs={{0,16},{16,0},{1,17},{17,1},{2,18},{18,2},{3,19},{19,3},{4,20},{20... | collective-permute-start | bytes 786440 | tf_op jit(solution)/shard_map/ppermute | solution.py:66
  13.0 10.9 %collective-permute-start.1 = (f32[64,1024]{1,0:T(8,128)S(1)}, f32[64,1024]{1,0:T(8,128)S(1)}, u32[]{:S(2)}, u32[]{:S(2)}) collective-permute-start(f32[64,1024]{1,0:T(8,128)S(1)} %fusion.7), channel_id=1, source_target_pairs={{0,16},{16,0},{1,17},{17,1},{2,18},{18,2},{3,19},{19,3},{4,20},{20... | collective-permute-start | bytes 786440 | tf_op jit(solution)/shard_map/ppermute | solution.py:66
  24.0 9.2 %collective-permute-start.2 = (bf16[64,2048]{1,0:T(8,128)(2,1)S(1)}, bf16[64,2048]{1,0:T(8,128)(2,1)S(1)}, u32[]{:S(2)}, u32[]{:S(2)}) collective-permute-start(bf16[64,2048]{1,0:T(8,128)(2,1)S(1)} %get-tuple-element.101), channel_id=1, source_target_pairs={{4,8},{8,12},{12,14},{14,10},{10,6},{6,2},{2,0},{0,4},{5,9},{9,13}... | collective-permute-start | bytes 786440 | tf_op jit(solution)/shard_map/ppermute | solution.py:93
  26.0 7.6 %collective-permute-start.3 = (bf16[64,2048]{1,0:T(8,128)(2,1)S(1)}, bf16[64,2048]{1,0:T(8,128)(2,1)S(1)}, u32[]{:S(2)}, u32[]{:S(2)}) collective-permute-start(bf16[64,2048]{1,0:T(8,128)(2,1)S(1)} %get-tuple-element.101), channel_id=1, source_target_pairs={{4,0},{8,4},{12,8},{14,12},{10,14},{6,10},{2,6},{0,2},{5,1},{9,5},... | collective-permute-start | bytes 786440 | tf_op jit(solution)/shard_map/ppermute | solution.py:97
  33.2 0.7 copy-start.5
  33.9 0.7 copy-start.2
  37.7 91.8 %collective-permute-start.4 = (bf16[64,2048]{1,0:T(8,128)(2,1)}, bf16[64,2048]{1,0:T(8,128)(2,1)S(1)}, u32[]{:S(2)}, u32[]{:S(2)}) collective-permute-start(bf16[64,2048]{1,0:T(8,128)(2,1)} %copy-done.5), channel_id=1, source_target_pairs={{4,8},{8,12},{12,14},{14,10},{10,6},{6,2},{2,0},{0,4},{5,9},{9,13}... | collective-permute-start | bytes 786440 | tf_op jit(solution)/shard_map/ppermute | solution.py:93
  42.4 86.3 %copy-start.3 = (bf16[64,2048]{1,0:T(8,128)(2,1)S(1)}, bf16[64,2048]{1,0:T(8,128)(2,1)}, u32[]{:S(2)}) copy-start(bf16[64,2048]{1,0:T(8,128)(2,1)} %copy-done.2) | copy-start | bytes 786436
  128.6 6.6 %collective-permute-start.5 = (bf16[64,2048]{1,0:T(8,128)(2,1)S(1)}, bf16[64,2048]{1,0:T(8,128)(2,1)S(1)}, u32[]{:S(2)}, u32[]{:S(2)}) collective-permute-start(bf16[64,2048]{1,0:T(8,128)(2,1)S(1)} %copy-done.3), channel_id=1, source_target_pairs={{4,0},{8,4},{12,8},{14,12},{10,14},{6,10},{2,6},{0,2},{5,1},{9,5},... | collective-permute-start | bytes 786440 | tf_op jit(solution)/shard_map/ppermute | solution.py:97
  135.3 0.7 copy-start.6
  139.1 91.0 %collective-permute-start.6 = (bf16[64,2048]{1,0:T(8,128)(2,1)S(1)}, bf16[64,2048]{1,0:T(8,128)(2,1)S(1)}, u32[]{:S(2)}, u32[]{:S(2)}) collective-permute-start(bf16[64,2048]{1,0:T(8,128)(2,1)S(1)} %collective-permute-done.4), channel_id=1, source_target_pairs={{4,8},{8,12},{12,14},{14,10},{10,6},{6,2},{2,0},{0,4},{5,9},{9,13}... | collective-permute-start | bytes 786440 | tf_op jit(solution)/shard_map/ppermute | solution.py:93
  143.4 86.3 %copy-start.7 = (bf16[64,2048]{1,0:T(8,128)(2,1)S(1)}, bf16[64,2048]{1,0:T(8,128)(2,1)}, u32[]{:S(2)}) copy-start(bf16[64,2048]{1,0:T(8,128)(2,1)} %copy-done.6) | copy-start | bytes 786436
  229.7 6.4 %collective-permute-start.7 = (bf16[64,2048]{1,0:T(8,128)(2,1)S(1)}, bf16[64,2048]{1,0:T(8,128)(2,1)S(1)}, u32[]{:S(2)}, u32[]{:S(2)}) collective-permute-start(bf16[64,2048]{1,0:T(8,128)(2,1)S(1)} %copy-done.7), channel_id=1, source_target_pairs={{4,0},{8,4},{12,8},{14,12},{10,14},{6,10},{2,6},{0,2},{5,1},{9,5},... | collective-permute-start | bytes 786440 | tf_op jit(solution)/shard_map/ppermute | solution.py:97
  230.2 0.7 copy-start.4
  236.1 0.7 copy-start.8
  239.9 90.9 %collective-permute-start.8 = (bf16[64,2048]{1,0:T(8,128)(2,1)}, bf16[64,2048]{1,0:T(8,128)(2,1)S(1)}, u32[]{:S(2)}, u32[]{:S(2)}) collective-permute-start(bf16[64,2048]{1,0:T(8,128)(2,1)} %copy-done.4), channel_id=1, source_target_pairs={{4,8},{8,12},{12,14},{14,10},{10,6},{6,2},{2,0},{0,4},{5,9},{9,13}... | collective-permute-start | bytes 786440 | tf_op jit(solution)/shard_map/ppermute | solution.py:93
  331.2 48.1 %collective-permute-start.9 = (bf16[512,512]{1,0:T(8,128)(2,1)S(1)}, bf16[512,512]{1,0:T(8,128)(2,1)S(1)}, u32[]{:S(2)}, u32[]{:S(2)}) collective-permute-start(bf16[512,512]{1,0:T(8,128)(2,1)S(1)} %dynamic-slice_dynamic-update-slice_fusion), channel_id=1, source_target_pairs={{0,1},{1,0},{2,3},{3,2},{4,5},{5,4},{6,7},{7,6},{8,9},{9,8},{10,11... | collective-permute-start | bytes 1572872 | tf_op jit(solution)/shard_map/ppermute | solution.py:103
  379.3 22.1 %copy-start.1 = (bf16[64,2560]{1,0:T(8,128)(2,1)S(1)}, bf16[64,2560]{1,0:T(8,128)(2,1)}, u32[]{:S(2)}) copy-start(bf16[64,2560]{1,0:T(8,128)(2,1)} %param.24) | copy-start | bytes 983044

commit v5 on v2

--- a/solution.py
+++ b/solution.py
@@ -34,48 +34,60 @@
         return list(range(n))
 
 
-def make_per_device(cycle):
+def make_per_device(cycle, n_chan):
     n_ring = len(cycle)
     position = [0] * n_ring
     for t, m in enumerate(cycle):
         position[m] = t
-    fwd_pairs = [(cycle[t], cycle[(t + 1) % n_ring]) for t in range(n_ring)]
-    bwd_pairs = [(cycle[t], cycle[(t - 1) % n_ring]) for t in range(n_ring)]
     n_fwd = n_ring // 2
+    long_pairs, short_pairs = [], []
+    for j in range(n_chan):
+        d = 1 if j % 2 == 0 else -1
+        for t in range(n_ring):
+            here = cycle[t] * n_chan + j
+            long_pairs.append((here, cycle[(t + d) % n_ring] * n_chan + j))
+            short_pairs.append((here, cycle[(t - d) % n_ring] * n_chan + j))
     n_bwd = n_ring - 1 - n_fwd
 
     def per_device(eigvecs, boundary, block_sizes, target_of_channel, poles, energies):
         n_eig = lax.axis_size("eig")
-        n_chan = lax.axis_size("chan")
         rows_here = eigvecs.shape[1]
         block_ends = jnp.cumsum(block_sizes)
         row_ids = lax.axis_index("basis") * rows_here + jnp.arange(rows_here, dtype=jnp.int32)
         owner_of = jnp.sum((block_ends[None, :] <= row_ids[:, None]).astype(jnp.int32), axis=1)
-        member = owner_of[:, None] == target_of_channel[None, :]
-        masked = jnp.where(member, boundary, jnp.zeros_like(boundary))
-        partial_value = jnp.dot(eigvecs, masked, preferred_element_type=jnp.float32)
         n_basis = lax.axis_size("basis")
-        total = partial_value
-        for s in range(1, n_basis):
-            shift = [(b, (b + s) % n_basis) for b in range(n_basis)]
-            total = total + lax.ppermute(partial_value, "basis", shift)
-        amp = total.astype(jnp.bfloat16)
+        width = boundary.shape[1]
+        halves = 2 if width % 256 == 0 else 1
+        step = width // halves
+        amp_parts = []
+        for h in range(halves):
+            cols = slice(h * step, (h + 1) * step)
+            member = owner_of[:, None] == target_of_channel[None, cols]
+            masked = jnp.where(member, boundary[:, cols], jnp.zeros_like(boundary[:, cols]))
+            part = jnp.dot(eigvecs, masked, preferred_element_type=jnp.float32)
+            total = part
+            for s in range(1, n_basis):
+                shift = [(b, (b + s) % n_basis) for b in range(n_basis)]
+                total = total + lax.ppermute(part, "basis", shift)
+            amp_parts.append(total.astype(jnp.bfloat16))
+        amp = jnp.concatenate(amp_parts, axis=1) if halves > 1 else amp_parts[0]
         eig_index = lax.axis_index("eig")
         cycle_arr = jnp.array(cycle, dtype=jnp.int32)
         pos = jnp.array(position, dtype=jnp.int32)[eig_index]
         k_here = amp.shape[0]
         left_panel = jnp.zeros((k_here * n_ring, amp.shape[1]), amp.dtype)
         left_panel = lax.dynamic_update_slice_in_dim(left_panel, amp, eig_index * k_here, 0)
-        fwd, bwd = amp, amp
+        sign = 1 - 2 * (lax.axis_index("chan") % 2)
+        long_blk, short_blk = amp, amp
         for s in range(max(n_fwd, n_bwd)):
             if s < n_fwd:
-                fwd = lax.ppermute(fwd, "eig", fwd_pairs)
-                origin = cycle_arr[(pos - s - 1) % n_ring]
-                left_panel = lax.dynamic_update_slice_in_dim(left_panel, fwd, origin * k_here, 0)
+                long_blk = lax.ppermute(long_blk, ("eig", "chan"), long_pairs)
+                origin = cycle_arr[(pos - sign * (s + 1)) % n_ring]
+                left_panel = lax.dynamic_update_slice_in_dim(left_panel, long_blk, origin * k_here, 0)
             if s < n_bwd:
-                bwd = lax.ppermute(bwd, "eig", bwd_pairs)
-                origin = cycle_arr[(pos + s + 1) % n_ring]
-                left_panel = lax.dynamic_update_slice_in_dim(left_panel, bwd, origin * k_here, 0)
+                short_blk = lax.ppermute(short_blk, ("eig", "chan"), short_pairs)
+                origin = cycle_arr[(pos + sign * (s + 1)) % n_ring]
+                left_panel = lax.dynamic_update_slice_in_dim(left_panel, short_blk, origin * k_here, 0)
         own_width = left_panel.shape[1]
         col_width = own_width * n_chan // n_eig
         ratio = n_eig // n_chan
@@ -99,7 +111,7 @@
 def solution(mesh):
     placed = (P("eig", "basis"), P("basis", "chan"), P(), P("chan"), P(), P("basis"))
     return jax.shard_map(
-        make_per_device(ring_order(mesh)),
+        make_per_device(ring_order(mesh), mesh.shape["chan"]),
         mesh=mesh,
         in_specs=placed,
         out_specs=P("basis", "chan", "eig"),

time: 75.3 us -> 75.2 us (level)
  starting transfers between devices: 11.1 us -> 10 us
    ppermute x8 -> x9, starting transfers between devices: 11 us -> 9.92 us  [the longest x4 4.57 us: per_device(): long_blk = lax.ppermute(long_blk, ('eig', 'chan'), long_pairs)]
    dynamic_update_slice x1 -> x0, other arithmetic: 0.79 us -> none  [per_device(): lax.dynamic_update_slice_in_dim(left_panel, amp, eig_index * k_here, 0)]
    ppermute x8 -> x9, waiting for transfers between devices: 26.2 us -> 26.9 us  [the longest x4 14.6 us: per_device(): long_blk = lax.ppermute(long_blk, ('eig', 'chan'), long_pairs)]
    dot_general x1 -> x2, matrix products: 6.4 us -> 5.99 us  [per_device(): part = jnp.dot(eigvecs, masked, preferred_element_type=jnp.float32)]
  transfers between devices with their start and end apart: 9 -> 10, of which waited for: 4 -> 7; matrix products, arithmetic and copies ran while one was open for 6% -> 8% of each run, Pallas kernels for 0% -> 0%
where the time goes in v5:
time: 75.2 us; the launch traced here: 74.9 us
  waiting for transfers between devices  26.9 us (36%)
  matrix products  22.2 us (30%)
  starting transfers between devices  10 us (13%)
  between operations  9.28 us (12%)
  local copies, waits for them, and re-layouts  6.17 us (8%)
    dot_general x1, matrix products, per_device(): jnp.einsum('ekc,kd->ecd', scaled, right_panel, preferred_element_type=jnp...  16.2 us
    ppermute x4, waiting for transfers between devices, per_device(): long_blk = lax.ppermute(long_blk, ('eig', 'chan'), long_pairs)  14.6 us
    ppermute x2, waiting for transfers between devices, per_device(): total = total + lax.ppermute(part, 'basis', shift)  8.67 us
    dot_general x2, matrix products, per_device(): part = jnp.dot(eigvecs, masked, preferred_element_type=jnp.float32)  5.99 us
    ppermute x4, starting transfers between devices, per_device(): long_blk = lax.ppermute(long_blk, ('eig', 'chan'), long_pairs)  4.57 us
    ppermute x2, starting transfers between devices, per_device(): total = total + lax.ppermute(part, 'basis', shift)  4.38 us
    ppermute x3, waiting for transfers between devices, per_device(): short_blk = lax.ppermute(short_blk, ('eig', 'chan'), short_pairs)  3.6 us
    convert_element_type x1, local copies, waits for them, and re-layouts, per_device(): left_panel[None].astype(jnp.float32)  2.96 us
  transfers between devices with their start and end apart: 10, of which 7 were waited for; matrix products, arithmetic and copies ran while one was open for 8% of the time, Pallas kernels for 0%

profile of v5, /device:TPU:0, one launch (start us, length us, event | category | flops | bytes accessed | tf_op | source)
XLA Modules:
  0.0 74.9 jit_solution(7356768008562259680)
XLA Ops:
  0.0 0.8 %copy.13 = s32[16,1]{1,0:T(8,128)S(1)} copy(s32[16,1]{0,1:T(1,128)} %bitcast.18) | data formatting | bytes 128 | tf_op jit(solution)/shard_map/reshape.53
  0.8 0.1 reduce
  0.9 0.7 fusion.19
  1.6 0.1 convert_reduce_fusion
  1.8 4.2 %fusion.13 = f32[64,1024]{1,0:T(8,128)S(1)} fusion(bf16[64,2560]{1,0:T(8,128)(2,1)S(1)} %copy-done, bf16[2560,2048]{1,0:T(8,128)(2,1)} %param.9, s32[1024]{0:T(1024)S(1)} %get-tuple-element.7, s32[2560]{0:T(1024)S(1)} %convert_reduce_fusion), kind=kOutput, calls=%fused_computation.17 | convolution fusion | flops 340787200 | bytes 5847040 | tf_op jit(solution)/shard_map/dot_general | solution.py:67
  6.0 3.0 %collective-permute-start = (f32[64,1024]{1,0:T(8,128)S(1)}, f32[64,1024]{1,0:T(8,128)S(1)}, u32[]{:S(2)}, u32[]{:S(2)}) collective-permute-start(f32[64,1024]{1,0:T(8,128)S(1)} %fusion.13), channel_id=1, source_target_pairs={{0,16},{16,0},{1,17},{17,1},{2,18},{18,2},{3,19},{19,3},{4,20},{20... | collective-permute-start | bytes 786440 | tf_op jit(solution)/shard_map/ppermute | solution.py:71
  9.0 1.8 %fusion.12 = f32[64,1024]{1,0:T(8,128)S(1)} fusion(bf16[64,2560]{1,0:T(8,128)(2,1)S(1)} %copy-done, bf16[2560,2048]{1,0:T(8,128)(2,1)S(1)} %copy-done.4, s32[1024]{0:T(1024)S(1)} %get-tuple-element.8, s32[2560]{0:T(1024)S(1)} %convert_reduce_fusion), kind=kOutput, calls=%fused_computation.16 | convolution fusion | flops 340787200 | bytes 5849088 | tf_op jit(solution)/shard_map/dot_general | solution.py:67
  10.8 0.0 copy-start.5
  10.8 0.0 copy-start.1
  10.8 1.4 %collective-permute-start.1 = (f32[64,1024]{1,0:T(8,128)S(1)}, f32[64,1024]{1,0:T(8,128)S(1)}, u32[]{:S(2)}, u32[]{:S(2)}) collective-permute-start(f32[64,1024]{1,0:T(8,128)S(1)} %fusion.12), channel_id=1, source_target_pairs={{0,16},{16,0},{1,17},{17,1},{2,18},{18,2},{3,19},{19,3},{4,20},{20... | collective-permute-start | bytes 786440 | tf_op jit(solution)/shard_map/ppermute | solution.py:71
  12.2 4.0 %collective-permute-done = f32[64,1024]{1,0:T(8,128)S(1)} collective-permute-done((f32[64,1024]{1,0:T(8,128)S(1)}, f32[64,1024]{1,0:T(8,128)S(1)}, u32[]{:S(2)}, u32[]{:S(2)}) %collective-permute-start) | collective-permute-done | bytes 262176 | tf_op jit(solution)/shard_map/ppermute | solution.py:71
  16.2 0.0 copy-start.3
  16.2 4.7 %collective-permute-done.1 = f32[64,1024]{1,0:T(8,128)S(1)} collective-permute-done((f32[64,1024]{1,0:T(8,128)S(1)}, f32[64,1024]{1,0:T(8,128)S(1)}, u32[]{:S(2)}, u32[]{:S(2)}) %collective-permute-start.1) | collective-permute-done | bytes 262176 | tf_op jit(solution)/shard_map/ppermute | solution.py:71
  20.9 0.2 broadcast_in_dim.2
  21.3 1.9 %collective-permute-start.2 = (bf16[64,2048]{1,0:T(8,128)(2,1)S(1)}, bf16[64,2048]{1,0:T(8,128)(2,1)S(1)}, u32[]{:S(2)}, u32[]{:S(2)}) collective-permute-start(bf16[64,2048]{1,0:T(8,128)(2,1)S(1)} %get-tuple-element.5), channel_id=1, source_target_pairs={{4,8},{8,12},{12,14},{14,10},{10,6},{6,2},{2,0},{0,4},{5,1},{9,5},... | collective-permute-start | bytes 786440 | tf_op jit(solution)/shard_map/ppermute | solution.py:84
  23.1 0.2 collective-permute-start.3
  23.3 0.6 dynamic_slice.27
  28.6 0.7 fusion.20
  33.7 1.9 %collective-permute-start.4 = (bf16[64,2048]{1,0:T(8,128)(2,1)S(1)}, bf16[64,2048]{1,0:T(8,128)(2,1)S(1)}, u32[]{:S(2)}, u32[]{:S(2)}) collective-permute-start(bf16[64,2048]{1,0:T(8,128)(2,1)S(1)} %collective-permute-done.2), channel_id=1, source_target_pairs={{4,8},{8,12},{12,14},{14,10},{10,6},{6,2},{2,0},{0,4},{5,1},{9,5},... | collective-permute-start | bytes 786440 | tf_op jit(solution)/shard_map/ppermute | solution.py:84
  35.6 0.2 collective-permute-start.5
  35.8 6.0 %collective-permute-done.4 = bf16[64,2048]{1,0:T(8,128)(2,1)S(1)} collective-permute-done((bf16[64,2048]{1,0:T(8,128)(2,1)S(1)}, bf16[64,2048]{1,0:T(8,128)(2,1)S(1)}, u32[]{:S(2)}, u32[]{:S(2)}) %collective-permute-start.4) | collective-permute-done | bytes 262176 | tf_op jit(solution)/shard_map/ppermute | solution.py:84
  41.9 0.5 collective-permute-start.6
  42.4 0.9 %collective-permute-done.5 = bf16[64,2048]{1,0:T(8,128)(2,1)S(1)} collective-permute-done((bf16[64,2048]{1,0:T(8,128)(2,1)S(1)}, bf16[64,2048]{1,0:T(8,128)(2,1)S(1)}, u32[]{:S(2)}, u32[]{:S(2)}) %collective-permute-start.5) | collective-permute-done | bytes 262176 | tf_op jit(solution)/shard_map/ppermute | solution.py:88
  43.3 0.6 collective-permute-start.7
  44.0 5.2 %collective-permute-done.6 = bf16[64,2048]{1,0:T(8,128)(2,1)S(1)} collective-permute-done((bf16[64,2048]{1,0:T(8,128)(2,1)S(1)}, bf16[64,2048]{1,0:T(8,128)(2,1)S(1)}, u32[]{:S(2)}, u32[]{:S(2)}) %collective-permute-start.6) | collective-permute-done | bytes 262176 | tf_op jit(solution)/shard_map/ppermute | solution.py:84
  49.1 0.3 collective-permute-start.8
  49.4 2.7 %collective-permute-done.7 = bf16[64,2048]{1,0:T(8,128)(2,1)S(1)} collective-permute-done((bf16[64,2048]{1,0:T(8,128)(2,1)S(1)}, bf16[64,2048]{1,0:T(8,128)(2,1)S(1)}, u32[]{:S(2)}, u32[]{:S(2)}) %collective-permute-start.7) | collective-permute-done | bytes 262176 | tf_op jit(solution)/shard_map/ppermute | solution.py:88
  52.1 3.4 %collective-permute-done.8 = bf16[64,2048]{1,0:T(8,128)(2,1)S(1)} collective-permute-done((bf16[64,2048]{1,0:T(8,128)(2,1)S(1)}, bf16[64,2048]{1,0:T(8,128)(2,1)S(1)}, u32[]{:S(2)}, u32[]{:S(2)}) %collective-permute-start.8) | collective-permute-done | bytes 262176 | tf_op jit(solution)/shard_map/ppermute | solution.py:84
  55.6 0.1 collective-permute-start.9
  55.7 0.1 subtract_divide_fusion
  55.8 3.0 %copy.14 = f32[512,2048]{0,1:T(8,128)} copy(bf16[512,2048]{1,0:T(8,128)(2,1)S(1)} %constant_dynamic-update-slice_fusion) | data formatting | bytes 6291456 | tf_op jit(solution)/shard_map/convert_element_type | solution.py:104
  58.7 16.2 %convolution_multiply_fusion = f32[8,2048,512]{2,1,0:T(8,128)} fusion(f32[512,2048]{0,1:T(8,128)} %copy.14, f32[8,512]{1,0:T(8,128)S(1)} %subtract_divide_fusion, bf16[512,512]{1,0:T(8,128)(2,1)S(1)} %constant_dynamic-slice_fusion, bf16[512,512]{1,0:T(8,128)(2,1)S(1)} %collective-permute-done.9, pred[]{:T(512)S(6)} %eq.42), kind=kOutput, calls=%fused_computation.1 | convolution fusion | flops 8615362560 | bytes 38813696 | tf_op jit(solution)/shard_map/ekc,kd->ecd/dot_general | solution.py:105
  (25 shorter events, 0.4 us)
Async XLA Ops:
  0.0 1.8 %copy-start = (bf16[64,2560]{1,0:T(8,128)(2,1)S(1)}, bf16[64,2560]{1,0:T(8,128)(2,1)}, u32[]{:S(2)}) copy-start(bf16[64,2560]{1,0:T(8,128)(2,1)} %param.8) | copy-start | bytes 983044
  1.8 7.2 %copy-start.4 = (bf16[2560,2048]{1,0:T(8,128)(2,1)S(1)}, bf16[2560,2048]{1,0:T(8,128)(2,1)}, u32[]{:S(2)}) copy-start(bf16[2560,2048]{1,0:T(8,128)(2,1)} %param.9) | copy-start | bytes 31457284
  6.0 10.2 %collective-permute-start = (f32[64,1024]{1,0:T(8,128)S(1)}, f32[64,1024]{1,0:T(8,128)S(1)}, u32[]{:S(2)}, u32[]{:S(2)}) collective-permute-start(f32[64,1024]{1,0:T(8,128)S(1)} %fusion.13), channel_id=1, source_target_pairs={{0,16},{16,0},{1,17},{17,1},{2,18},{18,2},{3,19},{19,3},{4,20},{20... | collective-permute-start | bytes 786440 | tf_op jit(solution)/shard_map/ppermute | solution.py:71
  10.8 12.5 %copy-start.5 = (s32[8]{0:T(128)S(1)}, s32[8]{0:T(128)}, u32[]{:S(2)}) copy-start(s32[8]{0:T(128)} %constant.114.clone) | copy-start | bytes 100
  10.8 17.8 %copy-start.1 = (s32[8]{0:T(128)S(1)}, s32[8]{0:T(128)}, u32[]{:S(2)}) copy-start(s32[8]{0:T(128)} %constant.113.clone) | copy-start | bytes 100
  10.8 10.1 %collective-permute-start.1 = (f32[64,1024]{1,0:T(8,128)S(1)}, f32[64,1024]{1,0:T(8,128)S(1)}, u32[]{:S(2)}, u32[]{:S(2)}) collective-permute-start(f32[64,1024]{1,0:T(8,128)S(1)} %fusion.12), channel_id=1, source_target_pairs={{0,16},{16,0},{1,17},{17,1},{2,18},{18,2},{3,19},{19,3},{4,20},{20... | collective-permute-start | bytes 786440 | tf_op jit(solution)/shard_map/ppermute | solution.py:71
  16.2 39.5 %copy-start.2 = (f32[512]{0:T(512)S(1)}, f32[512]{0:T(512)}, u32[]{:S(2)}) copy-start(f32[512]{0:T(512)} %param.12) | copy-start | bytes 6148
  16.2 39.5 %copy-start.3 = (f32[8]{0:T(128)S(1)}, f32[8]{0:T(128)}, u32[]{:S(2)}) copy-start(f32[8]{0:T(128)} %param.13) | copy-start | bytes 100
  21.3 12.4 %collective-permute-start.2 = (bf16[64,2048]{1,0:T(8,128)(2,1)S(1)}, bf16[64,2048]{1,0:T(8,128)(2,1)S(1)}, u32[]{:S(2)}, u32[]{:S(2)}) collective-permute-start(bf16[64,2048]{1,0:T(8,128)(2,1)S(1)} %get-tuple-element.5), channel_id=1, source_target_pairs={{4,8},{8,12},{12,14},{14,10},{10,6},{6,2},{2,0},{0,4},{5,1},{9,5},... | collective-permute-start | bytes 786440 | tf_op jit(solution)/shard_map/ppermute | solution.py:84
  23.1 12.4 %collective-permute-start.3 = (bf16[64,2048]{1,0:T(8,128)(2,1)S(1)}, bf16[64,2048]{1,0:T(8,128)(2,1)S(1)}, u32[]{:S(2)}, u32[]{:S(2)}) collective-permute-start(bf16[64,2048]{1,0:T(8,128)(2,1)S(1)} %get-tuple-element.5), channel_id=1, source_target_pairs={{4,0},{8,4},{12,8},{14,12},{10,14},{6,10},{2,6},{0,2},{5,9},{9,13}... | collective-permute-start | bytes 786440 | tf_op jit(solution)/shard_map/ppermute | solution.py:88
  33.7 8.2 %collective-permute-start.4 = (bf16[64,2048]{1,0:T(8,128)(2,1)S(1)}, bf16[64,2048]{1,0:T(8,128)(2,1)S(1)}, u32[]{:S(2)}, u32[]{:S(2)}) collective-permute-start(bf16[64,2048]{1,0:T(8,128)(2,1)S(1)} %collective-permute-done.2), channel_id=1, source_target_pairs={{4,8},{8,12},{12,14},{14,10},{10,6},{6,2},{2,0},{0,4},{5,1},{9,5},... | collective-permute-start | bytes 786440 | tf_op jit(solution)/shard_map/ppermute | solution.py:84
  35.6 7.8 %collective-permute-start.5 = (bf16[64,2048]{1,0:T(8,128)(2,1)S(1)}, bf16[64,2048]{1,0:T(8,128)(2,1)S(1)}, u32[]{:S(2)}, u32[]{:S(2)}) collective-permute-start(bf16[64,2048]{1,0:T(8,128)(2,1)S(1)} %collective-permute-done.3), channel_id=1, source_target_pairs={{4,0},{8,4},{12,8},{14,12},{10,14},{6,10},{2,6},{0,2},{5,9},{9,13}... | collective-permute-start | bytes 786440 | tf_op jit(solution)/shard_map/ppermute | solution.py:88
  41.9 7.3 %collective-permute-start.6 = (bf16[64,2048]{1,0:T(8,128)(2,1)S(1)}, bf16[64,2048]{1,0:T(8,128)(2,1)S(1)}, u32[]{:S(2)}, u32[]{:S(2)}) collective-permute-start(bf16[64,2048]{1,0:T(8,128)(2,1)S(1)} %collective-permute-done.4), channel_id=1, source_target_pairs={{4,8},{8,12},{12,14},{14,10},{10,6},{6,2},{2,0},{0,4},{5,1},{9,5},... | collective-permute-start | bytes 786440 | tf_op jit(solution)/shard_map/ppermute | solution.py:84
  43.3 8.8 %collective-permute-start.7 = (bf16[64,2048]{1,0:T(8,128)(2,1)S(1)}, bf16[64,2048]{1,0:T(8,128)(2,1)S(1)}, u32[]{:S(2)}, u32[]{:S(2)}) collective-permute-start(bf16[64,2048]{1,0:T(8,128)(2,1)S(1)} %collective-permute-done.5), channel_id=1, source_target_pairs={{4,0},{8,4},{12,8},{14,12},{10,14},{6,10},{2,6},{0,2},{5,9},{9,13}... | collective-permute-start | bytes 786440 | tf_op jit(solution)/shard_map/ppermute | solution.py:88
  49.1 6.4 %collective-permute-start.8 = (bf16[64,2048]{1,0:T(8,128)(2,1)S(1)}, bf16[64,2048]{1,0:T(8,128)(2,1)S(1)}, u32[]{:S(2)}, u32[]{:S(2)}) collective-permute-start(bf16[64,2048]{1,0:T(8,128)(2,1)S(1)} %collective-permute-done.6), channel_id=1, source_target_pairs={{4,8},{8,12},{12,14},{14,10},{10,6},{6,2},{2,0},{0,4},{5,1},{9,5},... | collective-permute-start | bytes 786440 | tf_op jit(solution)/shard_map/ppermute | solution.py:84
  55.6 3.2 %collective-permute-start.9 = (bf16[512,512]{1,0:T(8,128)(2,1)S(1)}, bf16[512,512]{1,0:T(8,128)(2,1)S(1)}, u32[]{:S(2)}, u32[]{:S(2)}) collective-permute-start(bf16[512,512]{1,0:T(8,128)(2,1)S(1)} %constant_dynamic-slice_fusion), channel_id=1, source_target_pairs={{0,1},{1,0},{2,3},{3,2},{4,5},{5,4},{6,7},{7,6},{8,9},{9,8},{10,11... | collective-permute-start | bytes 1572872 | tf_op jit(solution)/shard_map/ppermute | solution.py:97

commit v6 on v5

--- a/solution.py
+++ b/solution.py
@@ -78,16 +78,21 @@
         left_panel = jnp.zeros((k_here * n_ring, amp.shape[1]), amp.dtype)
         left_panel = lax.dynamic_update_slice_in_dim(left_panel, amp, eig_index * k_here, 0)
         sign = 1 - 2 * (lax.axis_index("chan") % 2)
-        long_blk, short_blk = amp, amp
+        n_split = 2 if amp.shape[1] % 256 == 0 else 1
+        split_w = amp.shape[1] // n_split
+        longs = [amp[:, p * split_w:(p + 1) * split_w] for p in range(n_split)]
+        shorts = list(longs)
         for s in range(max(n_fwd, n_bwd)):
             if s < n_fwd:
-                long_blk = lax.ppermute(long_blk, ("eig", "chan"), long_pairs)
+                longs = [lax.ppermute(x, ("eig", "chan"), long_pairs) for x in longs]
                 origin = cycle_arr[(pos - sign * (s + 1)) % n_ring]
-                left_panel = lax.dynamic_update_slice_in_dim(left_panel, long_blk, origin * k_here, 0)
+                for p, x in enumerate(longs):
+                    left_panel = lax.dynamic_update_slice(left_panel, x, (origin * k_here, p * split_w))
             if s < n_bwd:
-                short_blk = lax.ppermute(short_blk, ("eig", "chan"), short_pairs)
+                shorts = [lax.ppermute(x, ("eig", "chan"), short_pairs) for x in shorts]
                 origin = cycle_arr[(pos + sign * (s + 1)) % n_ring]
-                left_panel = lax.dynamic_update_slice_in_dim(left_panel, short_blk, origin * k_here, 0)
+                for p, x in enumerate(shorts):
+                    left_panel = lax.dynamic_update_slice(left_panel, x, (origin * k_here, p * split_w))
         own_width = left_panel.shape[1]
         col_width = own_width * n_chan // n_eig
         ratio = n_eig // n_chan

time: 75.2 us -> 69.1 us (0.919)
  waiting for transfers between devices: 26.9 us -> 12.6 us
  starting transfers between devices: 10 us -> 17.9 us
    ppermute x2, waiting for transfers between devices: 8.67 us -> 0.01 us  [per_device(): total = total + lax.ppermute(part, 'basis', shift)]
    ppermute x7 -> x14, starting transfers between devices: 5.54 us -> 13.4 us  [the longest x6 8.13 us: per_device(): shorts = [lax.ppermute(x, ('eig', 'chan'), short_pairs) for x in shorts]]
    ppermute x7 -> x14, waiting for transfers between devices: 18.2 us -> 12.6 us  [the longest x8 7.71 us: per_device(): longs = [lax.ppermute(x, ('eig', 'chan'), long_pairs) for x in longs]]
  transfers between devices with their start and end apart: 10 -> 17, of which waited for: 7 -> 10; matrix products, arithmetic and copies ran while one was open for 8% -> 10% of each run, Pallas kernels for 0% -> 0%
where the time goes in v6:
time: 69.1 us; the launch traced here: 68.8 us
  matrix products  22.2 us (32%)
  starting transfers between devices  17.9 us (26%)
  waiting for transfers between devices  12.6 us (18%)
  between operations  9.46 us (14%)
  local copies, waits for them, and re-layouts  6.3 us (9%)
    dot_general x1, matrix products, per_device(): jnp.einsum('ekc,kd->ecd', scaled, right_panel, preferred_element_type=jnp...  16.2 us
    ppermute x6, starting transfers between devices, per_device(): shorts = [lax.ppermute(x, ('eig', 'chan'), short_pairs) for x in shorts]  8.13 us
    ppermute x8, waiting for transfers between devices, per_device(): longs = [lax.ppermute(x, ('eig', 'chan'), long_pairs) for x in longs]  7.71 us
    dot_general x2, matrix products, per_device(): part = jnp.dot(eigvecs, masked, preferred_element_type=jnp.float32)  5.99 us
    ppermute x8, starting transfers between devices, per_device(): longs = [lax.ppermute(x, ('eig', 'chan'), long_pairs) for x in longs]  5.27 us
    ppermute x6, waiting for transfers between devices, per_device(): shorts = [lax.ppermute(x, ('eig', 'chan'), short_pairs) for x in shorts]  4.92 us
    ppermute x2, starting transfers between devices, per_device(): total = total + lax.ppermute(part, 'basis', shift)  4.38 us
    convert_element_type x1, local copies, waits for them, and re-layouts, per_device(): left_panel[None].astype(jnp.float32)  3.01 us
  transfers between devices with their start and end apart: 17, of which 10 were waited for; matrix products, arithmetic and copies ran while one was open for 10% of the time, Pallas kernels for 0%

profile of v6, /device:TPU:0, one launch (start us, length us, event | category | flops | bytes accessed | tf_op | source)
XLA Modules:
  0.0 68.8 jit_solution(1485111663397164476)
XLA Ops:
  0.0 0.8 %copy.13 = s32[16,1]{1,0:T(8,128)S(1)} copy(s32[16,1]{0,1:T(1,128)} %bitcast.18) | data formatting | bytes 128 | tf_op jit(solution)/shard_map/reshape.53
  0.9 0.7 %fusion.19 = (s32[1024]{0:T(1024)S(1)}, s32[1024]{0:T(1024)S(1)}) fusion(s32[2048]{0:T(1024)} %param.11), kind=kLoop, calls=%fused_computation.44 | loop fusion | bytes 16384 | tf_op jit(solution)/shard_map/slice | solution.py:65
  1.8 4.2 %fusion.13 = f32[64,1024]{1,0:T(8,128)S(1)} fusion(bf16[64,2560]{1,0:T(8,128)(2,1)S(1)} %copy-done, bf16[2560,2048]{1,0:T(8,128)(2,1)} %param.9, s32[1024]{0:T(1024)S(1)} %get-tuple-element.5, s32[2560]{0:T(1024)S(1)} %convert_reduce_fusion), kind=kOutput, calls=%fused_computation.17 | convolution fusion | flops 340787200 | bytes 5847040 | tf_op jit(solution)/shard_map/dot_general | solution.py:67
  6.0 3.0 %collective-permute-start = (f32[64,1024]{1,0:T(8,128)S(1)}, f32[64,1024]{1,0:T(8,128)S(1)}, u32[]{:S(2)}, u32[]{:S(2)}) collective-permute-start(f32[64,1024]{1,0:T(8,128)S(1)} %fusion.13), channel_id=1, source_target_pairs={{0,16},{16,0},{1,17},{17,1},{2,18},{18,2},{3,19},{19,3},{4,20},{20... | collective-permute-start | bytes 786440 | tf_op jit(solution)/shard_map/ppermute | solution.py:71
  9.0 1.8 %fusion.12 = f32[64,1024]{1,0:T(8,128)S(1)} fusion(bf16[64,2560]{1,0:T(8,128)(2,1)S(1)} %copy-done, bf16[2560,2048]{1,0:T(8,128)(2,1)S(1)} %copy-done.4, s32[1024]{0:T(1024)S(1)} %get-tuple-element.6, s32[2560]{0:T(1024)S(1)} %convert_reduce_fusion), kind=kOutput, calls=%fused_computation.16 | convolution fusion | flops 340787200 | bytes 5849088 | tf_op jit(solution)/shard_map/dot_general | solution.py:67
  10.8 1.4 %collective-permute-start.1 = (f32[64,1024]{1,0:T(8,128)S(1)}, f32[64,1024]{1,0:T(8,128)S(1)}, u32[]{:S(2)}, u32[]{:S(2)}) collective-permute-start(f32[64,1024]{1,0:T(8,128)S(1)} %fusion.12), channel_id=1, source_target_pairs={{0,16},{16,0},{1,17},{17,1},{2,18},{18,2},{3,19},{19,3},{4,20},{20... | collective-permute-start | bytes 786440 | tf_op jit(solution)/shard_map/ppermute | solution.py:71
  12.2 0.6 dynamic_slice.27
  17.4 0.7 %fusion.20 = (s32[1]{0:T(128)}, s32[1]{0:T(128)}, s32[1]{0:T(128)}, s32[1]{0:T(128)}, s32[1]{0:T(128)}, /*index=5*/s32[1]{0:T(128)}, s32[1]{0:T(128)}) fusion(s32[8]{0:T(128)S(1)} %copy-done.1, s32[]{:T(128)S(6)} %select_n.140, s32[]{:T(128)S(6)} %select_n.134, s32[]{:T(128)S(6)} %select_n.131, s32[]{:T(128)S(6)} %select_n.128, s32[]{:T(128)S(6)} %select_n.125, ...), kind=kLoop, calls=%fused_computation.45 | loop fusion | bytes 84 | tf_op jit(solution)/shard_map/dynamic_slice | solution.py:88
  22.7 1.6 %collective-permute-start.4 = (bf16[64,1024]{1,0:T(8,128)(2,1)S(1)}, bf16[64,1024]{1,0:T(8,128)(2,1)S(1)}, u32[]{:S(2)}, u32[]{:S(2)}) collective-permute-start(bf16[64,1024]{1,0:T(8,128)(2,1)S(1)} %add_convert_fusion.1), channel_id=1, source_target_pairs={{4,0},{8,4},{12,8},{14,12},{10,14},{6,10},{2,6},{0,2},{5,9},{9,13}... | collective-permute-start | bytes 393224 | tf_op jit(solution)/shard_map/ppermute | solution.py:92
  24.3 0.5 collective-permute-start.2
  24.8 1.6 %collective-permute-start.5 = (bf16[64,1024]{1,0:T(8,128)(2,1)S(1)}, bf16[64,1024]{1,0:T(8,128)(2,1)S(1)}, u32[]{:S(2)}, u32[]{:S(2)}) collective-permute-start(bf16[64,1024]{1,0:T(8,128)(2,1)S(1)} %add_convert_fusion), channel_id=1, source_target_pairs={{4,0},{8,4},{12,8},{14,12},{10,14},{6,10},{2,6},{0,2},{5,9},{9,13}... | collective-permute-start | bytes 393224 | tf_op jit(solution)/shard_map/ppermute | solution.py:92
  26.4 0.5 collective-permute-start.3
  26.9 0.2 broadcast_in_dim.2
  27.2 1.9 %collective-permute-done.4 = bf16[64,1024]{1,0:T(8,128)(2,1)S(1)} collective-permute-done((bf16[64,1024]{1,0:T(8,128)(2,1)S(1)}, bf16[64,1024]{1,0:T(8,128)(2,1)S(1)}, u32[]{:S(2)}, u32[]{:S(2)}) %collective-permute-start.4) | collective-permute-done | bytes 131104 | tf_op jit(solution)/shard_map/ppermute | solution.py:92
  29.1 1.5 %collective-permute-start.8 = (bf16[64,1024]{1,0:T(8,128)(2,1)S(1)}, bf16[64,1024]{1,0:T(8,128)(2,1)S(1)}, u32[]{:S(2)}, u32[]{:S(2)}) collective-permute-start(bf16[64,1024]{1,0:T(8,128)(2,1)S(1)} %collective-permute-done.4), channel_id=1, source_target_pairs={{4,0},{8,4},{12,8},{14,12},{10,14},{6,10},{2,6},{0,2},{5,9},{9,13}... | collective-permute-start | bytes 393224 | tf_op jit(solution)/shard_map/ppermute | solution.py:92
  30.6 0.5 collective-permute-start.6
  31.2 0.8 %collective-permute-done.5 = bf16[64,1024]{1,0:T(8,128)(2,1)S(1)} collective-permute-done((bf16[64,1024]{1,0:T(8,128)(2,1)S(1)}, bf16[64,1024]{1,0:T(8,128)(2,1)S(1)}, u32[]{:S(2)}, u32[]{:S(2)}) %collective-permute-start.5) | collective-permute-done | bytes 131104 | tf_op jit(solution)/shard_map/ppermute | solution.py:92
  31.9 0.7 %collective-permute-start.9 = (bf16[64,1024]{1,0:T(8,128)(2,1)S(1)}, bf16[64,1024]{1,0:T(8,128)(2,1)S(1)}, u32[]{:S(2)}, u32[]{:S(2)}) collective-permute-start(bf16[64,1024]{1,0:T(8,128)(2,1)S(1)} %collective-permute-done.5), channel_id=1, source_target_pairs={{4,0},{8,4},{12,8},{14,12},{10,14},{6,10},{2,6},{0,2},{5,9},{9,13}... | collective-permute-start | bytes 393224 | tf_op jit(solution)/shard_map/ppermute | solution.py:92
  32.7 1.3 %collective-permute-start.7 = (bf16[64,1024]{1,0:T(8,128)(2,1)S(1)}, bf16[64,1024]{1,0:T(8,128)(2,1)S(1)}, u32[]{:S(2)}, u32[]{:S(2)}) collective-permute-start(bf16[64,1024]{1,0:T(8,128)(2,1)S(1)} %collective-permute-done.3), channel_id=1, source_target_pairs={{4,8},{8,12},{12,14},{14,10},{10,6},{6,2},{2,0},{0,4},{5,1},{9,5},... | collective-permute-start | bytes 393224 | tf_op jit(solution)/shard_map/ppermute | solution.py:87
  34.1 0.8 %collective-permute-done.8 = bf16[64,1024]{1,0:T(8,128)(2,1)S(1)} collective-permute-done((bf16[64,1024]{1,0:T(8,128)(2,1)S(1)}, bf16[64,1024]{1,0:T(8,128)(2,1)S(1)}, u32[]{:S(2)}, u32[]{:S(2)}) %collective-permute-start.8) | collective-permute-done | bytes 131104 | tf_op jit(solution)/shard_map/ppermute | solution.py:92
  34.8 1.7 %collective-permute-start.12 = (bf16[64,1024]{1,0:T(8,128)(2,1)S(1)}, bf16[64,1024]{1,0:T(8,128)(2,1)S(1)}, u32[]{:S(2)}, u32[]{:S(2)}) collective-permute-start(bf16[64,1024]{1,0:T(8,128)(2,1)S(1)} %collective-permute-done.8), channel_id=1, source_target_pairs={{4,0},{8,4},{12,8},{14,12},{10,14},{6,10},{2,6},{0,2},{5,9},{9,13}... | collective-permute-start | bytes 393224 | tf_op jit(solution)/shard_map/ppermute | solution.py:92
  36.9 1.4 %collective-permute-done.9 = bf16[64,1024]{1,0:T(8,128)(2,1)S(1)} collective-permute-done((bf16[64,1024]{1,0:T(8,128)(2,1)S(1)}, bf16[64,1024]{1,0:T(8,128)(2,1)S(1)}, u32[]{:S(2)}, u32[]{:S(2)}) %collective-permute-start.9) | collective-permute-done | bytes 131104 | tf_op jit(solution)/shard_map/ppermute | solution.py:92
  38.3 1.0 %collective-permute-start.13 = (bf16[64,1024]{1,0:T(8,128)(2,1)S(1)}, bf16[64,1024]{1,0:T(8,128)(2,1)S(1)}, u32[]{:S(2)}, u32[]{:S(2)}) collective-permute-start(bf16[64,1024]{1,0:T(8,128)(2,1)S(1)} %collective-permute-done.9), channel_id=1, source_target_pairs={{4,0},{8,4},{12,8},{14,12},{10,14},{6,10},{2,6},{0,2},{5,9},{9,13}... | collective-permute-start | bytes 393224 | tf_op jit(solution)/shard_map/ppermute | solution.py:92
  39.5 0.9 %collective-permute-start.11 = (bf16[64,1024]{1,0:T(8,128)(2,1)S(1)}, bf16[64,1024]{1,0:T(8,128)(2,1)S(1)}, u32[]{:S(2)}, u32[]{:S(2)}) collective-permute-start(bf16[64,1024]{1,0:T(8,128)(2,1)S(1)} %collective-permute-done.7), channel_id=1, source_target_pairs={{4,8},{8,12},{12,14},{14,10},{10,6},{6,2},{2,0},{0,4},{5,1},{9,5},... | collective-permute-start | bytes 393224 | tf_op jit(solution)/shard_map/ppermute | solution.py:87
  40.4 1.2 %collective-permute-done.10 = bf16[64,1024]{1,0:T(8,128)(2,1)S(1)} collective-permute-done((bf16[64,1024]{1,0:T(8,128)(2,1)S(1)}, bf16[64,1024]{1,0:T(8,128)(2,1)S(1)}, u32[]{:S(2)}, u32[]{:S(2)}) %collective-permute-start.10) | collective-permute-done | bytes 131104 | tf_op jit(solution)/shard_map/ppermute | solution.py:87
  41.6 0.5 collective-permute-start.14
  42.1 2.3 %collective-permute-done.11 = bf16[64,1024]{1,0:T(8,128)(2,1)S(1)} collective-permute-done((bf16[64,1024]{1,0:T(8,128)(2,1)S(1)}, bf16[64,1024]{1,0:T(8,128)(2,1)S(1)}, u32[]{:S(2)}, u32[]{:S(2)}) %collective-permute-start.11) | collective-permute-done | bytes 131104 | tf_op jit(solution)/shard_map/ppermute | solution.py:87
  44.4 0.9 %collective-permute-start.15 = (bf16[64,1024]{1,0:T(8,128)(2,1)S(1)}, bf16[64,1024]{1,0:T(8,128)(2,1)S(1)}, u32[]{:S(2)}, u32[]{:S(2)}) collective-permute-start(bf16[64,1024]{1,0:T(8,128)(2,1)S(1)} %collective-permute-done.11), channel_id=1, source_target_pairs={{4,8},{8,12},{12,14},{14,10},{10,6},{6,2},{2,0},{0,4},{5,1},{9,5},... | collective-permute-start | bytes 393224 | tf_op jit(solution)/shard_map/ppermute | solution.py:87
  45.4 1.2 %collective-permute-done.14 = bf16[64,1024]{1,0:T(8,128)(2,1)S(1)} collective-permute-done((bf16[64,1024]{1,0:T(8,128)(2,1)S(1)}, bf16[64,1024]{1,0:T(8,128)(2,1)S(1)}, u32[]{:S(2)}, u32[]{:S(2)}) %collective-permute-start.14) | collective-permute-done | bytes 131104 | tf_op jit(solution)/shard_map/ppermute | solution.py:87
  46.6 2.8 %collective-permute-done.15 = bf16[64,1024]{1,0:T(8,128)(2,1)S(1)} collective-permute-done((bf16[64,1024]{1,0:T(8,128)(2,1)S(1)}, bf16[64,1024]{1,0:T(8,128)(2,1)S(1)}, u32[]{:S(2)}, u32[]{:S(2)}) %collective-permute-start.15) | collective-permute-done | bytes 131104 | tf_op jit(solution)/shard_map/ppermute | solution.py:87
  49.6 3.0 %copy.14 = f32[512,2048]{0,1:T(8,128)} copy(bf16[512,2048]{1,0:T(8,128)(2,1)S(1)} %constant_dynamic-update-slice_fusion.7) | data formatting | bytes 6291456 | tf_op jit(solution)/shard_map/convert_element_type | solution.py:109
  52.7 16.2 %convolution_multiply_fusion = f32[8,2048,512]{2,1,0:T(8,128)} fusion(f32[512,2048]{0,1:T(8,128)} %copy.14, f32[8,512]{1,0:T(8,128)S(1)} %subtract_divide_fusion, bf16[512,512]{1,0:T(8,128)(2,1)S(1)} %constant_dynamic-slice_fusion, bf16[512,512]{1,0:T(8,128)(2,1)S(1)} %collective-permute-done.16, pred[]{:T(512)S(6)} %eq.42), kind=kOutput, calls=%fused_computation.1 | convolution fusion | flops 8615362560 | bytes 38813696 | tf_op jit(solution)/shard_map/ekc,kd->ecd/dot_general | solution.py:110
  (46 shorter events, 1.3 us)
Async XLA Ops:
  0.0 1.8 %copy-start = (bf16[64,2560]{1,0:T(8,128)(2,1)S(1)}, bf16[64,2560]{1,0:T(8,128)(2,1)}, u32[]{:S(2)}) copy-start(bf16[64,2560]{1,0:T(8,128)(2,1)} %param.8) | copy-start | bytes 983044
  1.8 7.2 %copy-start.4 = (bf16[2560,2048]{1,0:T(8,128)(2,1)S(1)}, bf16[2560,2048]{1,0:T(8,128)(2,1)}, u32[]{:S(2)}) copy-start(bf16[2560,2048]{1,0:T(8,128)(2,1)} %param.9) | copy-start | bytes 31457284
  6.0 16.7 %collective-permute-start = (f32[64,1024]{1,0:T(8,128)S(1)}, f32[64,1024]{1,0:T(8,128)S(1)}, u32[]{:S(2)}, u32[]{:S(2)}) collective-permute-start(f32[64,1024]{1,0:T(8,128)S(1)} %fusion.13), channel_id=1, source_target_pairs={{0,16},{16,0},{1,17},{17,1},{2,18},{18,2},{3,19},{19,3},{4,20},{20... | collective-permute-start | bytes 786440 | tf_op jit(solution)/shard_map/ppermute | solution.py:71
  9.0 3.2 %copy-start.5 = (s32[8]{0:T(128)S(1)}, s32[8]{0:T(128)}, u32[]{:S(2)}) copy-start(s32[8]{0:T(128)} %constant.116.clone) | copy-start | bytes 100
  9.0 8.4 %copy-start.1 = (s32[8]{0:T(128)S(1)}, s32[8]{0:T(128)}, u32[]{:S(2)}) copy-start(s32[8]{0:T(128)} %constant.115.clone) | copy-start | bytes 100
  10.8 14.0 %collective-permute-start.1 = (f32[64,1024]{1,0:T(8,128)S(1)}, f32[64,1024]{1,0:T(8,128)S(1)}, u32[]{:S(2)}, u32[]{:S(2)}) collective-permute-start(f32[64,1024]{1,0:T(8,128)S(1)} %fusion.12), channel_id=1, source_target_pairs={{0,16},{16,0},{1,17},{17,1},{2,18},{18,2},{3,19},{19,3},{4,20},{20... | collective-permute-start | bytes 786440 | tf_op jit(solution)/shard_map/ppermute | solution.py:71
  22.7 6.4 %collective-permute-start.4 = (bf16[64,1024]{1,0:T(8,128)(2,1)S(1)}, bf16[64,1024]{1,0:T(8,128)(2,1)S(1)}, u32[]{:S(2)}, u32[]{:S(2)}) collective-permute-start(bf16[64,1024]{1,0:T(8,128)(2,1)S(1)} %add_convert_fusion.1), channel_id=1, source_target_pairs={{4,0},{8,4},{12,8},{14,12},{10,14},{6,10},{2,6},{0,2},{5,9},{9,13}... | collective-permute-start | bytes 393224 | tf_op jit(solution)/shard_map/ppermute | solution.py:92
  24.3 6.4 %collective-permute-start.2 = (bf16[64,1024]{1,0:T(8,128)(2,1)S(1)}, bf16[64,1024]{1,0:T(8,128)(2,1)S(1)}, u32[]{:S(2)}, u32[]{:S(2)}) collective-permute-start(bf16[64,1024]{1,0:T(8,128)(2,1)S(1)} %add_convert_fusion.1), channel_id=1, source_target_pairs={{4,8},{8,12},{12,14},{14,10},{10,6},{6,2},{2,0},{0,4},{5,1},{9,5},... | collective-permute-start | bytes 393224 | tf_op jit(solution)/shard_map/ppermute | solution.py:87
  24.8 7.1 %collective-permute-start.5 = (bf16[64,1024]{1,0:T(8,128)(2,1)S(1)}, bf16[64,1024]{1,0:T(8,128)(2,1)S(1)}, u32[]{:S(2)}, u32[]{:S(2)}) collective-permute-start(bf16[64,1024]{1,0:T(8,128)(2,1)S(1)} %add_convert_fusion), channel_id=1, source_target_pairs={{4,0},{8,4},{12,8},{14,12},{10,14},{6,10},{2,6},{0,2},{5,9},{9,13}... | collective-permute-start | bytes 393224 | tf_op jit(solution)/shard_map/ppermute | solution.py:92
  26.4 6.3 %collective-permute-start.3 = (bf16[64,1024]{1,0:T(8,128)(2,1)S(1)}, bf16[64,1024]{1,0:T(8,128)(2,1)S(1)}, u32[]{:S(2)}, u32[]{:S(2)}) collective-permute-start(bf16[64,1024]{1,0:T(8,128)(2,1)S(1)} %add_convert_fusion), channel_id=1, source_target_pairs={{4,8},{8,12},{12,14},{14,10},{10,6},{6,2},{2,0},{0,4},{5,1},{9,5},... | collective-permute-start | bytes 393224 | tf_op jit(solution)/shard_map/ppermute | solution.py:87
  29.1 5.7 %collective-permute-start.8 = (bf16[64,1024]{1,0:T(8,128)(2,1)S(1)}, bf16[64,1024]{1,0:T(8,128)(2,1)S(1)}, u32[]{:S(2)}, u32[]{:S(2)}) collective-permute-start(bf16[64,1024]{1,0:T(8,128)(2,1)S(1)} %collective-permute-done.4), channel_id=1, source_target_pairs={{4,0},{8,4},{12,8},{14,12},{10,14},{6,10},{2,6},{0,2},{5,9},{9,13}... | collective-permute-start | bytes 393224 | tf_op jit(solution)/shard_map/ppermute | solution.py:92
  30.6 6.0 %collective-permute-start.6 = (bf16[64,1024]{1,0:T(8,128)(2,1)S(1)}, bf16[64,1024]{1,0:T(8,128)(2,1)S(1)}, u32[]{:S(2)}, u32[]{:S(2)}) collective-permute-start(bf16[64,1024]{1,0:T(8,128)(2,1)S(1)} %collective-permute-done.2), channel_id=1, source_target_pairs={{4,8},{8,12},{12,14},{14,10},{10,6},{6,2},{2,0},{0,4},{5,1},{9,5},... | collective-permute-start | bytes 393224 | tf_op jit(solution)/shard_map/ppermute | solution.py:87
  31.9 6.4 %collective-permute-start.9 = (bf16[64,1024]{1,0:T(8,128)(2,1)S(1)}, bf16[64,1024]{1,0:T(8,128)(2,1)S(1)}, u32[]{:S(2)}, u32[]{:S(2)}) collective-permute-start(bf16[64,1024]{1,0:T(8,128)(2,1)S(1)} %collective-permute-done.5), channel_id=1, source_target_pairs={{4,0},{8,4},{12,8},{14,12},{10,14},{6,10},{2,6},{0,2},{5,9},{9,13}... | collective-permute-start | bytes 393224 | tf_op jit(solution)/shard_map/ppermute | solution.py:92
  32.7 6.8 %collective-permute-start.7 = (bf16[64,1024]{1,0:T(8,128)(2,1)S(1)}, bf16[64,1024]{1,0:T(8,128)(2,1)S(1)}, u32[]{:S(2)}, u32[]{:S(2)}) collective-permute-start(bf16[64,1024]{1,0:T(8,128)(2,1)S(1)} %collective-permute-done.3), channel_id=1, source_target_pairs={{4,8},{8,12},{12,14},{14,10},{10,6},{6,2},{2,0},{0,4},{5,1},{9,5},... | collective-permute-start | bytes 393224 | tf_op jit(solution)/shard_map/ppermute | solution.py:87
  34.0 15.6 %copy-start.2 = (f32[512]{0:T(512)S(1)}, f32[512]{0:T(512)}, u32[]{:S(2)}) copy-start(f32[512]{0:T(512)} %param.12) | copy-start | bytes 6148
  34.0 15.6 %copy-start.3 = (f32[8]{0:T(128)S(1)}, f32[8]{0:T(128)}, u32[]{:S(2)}) copy-start(f32[8]{0:T(128)} %param.13) | copy-start | bytes 100
  34.8 10.5 %collective-permute-start.12 = (bf16[64,1024]{1,0:T(8,128)(2,1)S(1)}, bf16[64,1024]{1,0:T(8,128)(2,1)S(1)}, u32[]{:S(2)}, u32[]{:S(2)}) collective-permute-start(bf16[64,1024]{1,0:T(8,128)(2,1)S(1)} %collective-permute-done.8), channel_id=1, source_target_pairs={{4,0},{8,4},{12,8},{14,12},{10,14},{6,10},{2,6},{0,2},{5,9},{9,13}... | collective-permute-start | bytes 393224 | tf_op jit(solution)/shard_map/ppermute | solution.py:92
  36.6 5.0 %collective-permute-start.10 = (bf16[64,1024]{1,0:T(8,128)(2,1)S(1)}, bf16[64,1024]{1,0:T(8,128)(2,1)S(1)}, u32[]{:S(2)}, u32[]{:S(2)}) collective-permute-start(bf16[64,1024]{1,0:T(8,128)(2,1)S(1)} %collective-permute-done.6), channel_id=1, source_target_pairs={{4,8},{8,12},{12,14},{14,10},{10,6},{6,2},{2,0},{0,4},{5,1},{9,5},... | collective-permute-start | bytes 393224 | tf_op jit(solution)/shard_map/ppermute | solution.py:87
  38.3 7.1 %collective-permute-start.13 = (bf16[64,1024]{1,0:T(8,128)(2,1)S(1)}, bf16[64,1024]{1,0:T(8,128)(2,1)S(1)}, u32[]{:S(2)}, u32[]{:S(2)}) collective-permute-start(bf16[64,1024]{1,0:T(8,128)(2,1)S(1)} %collective-permute-done.9), channel_id=1, source_target_pairs={{4,0},{8,4},{12,8},{14,12},{10,14},{6,10},{2,6},{0,2},{5,9},{9,13}... | collective-permute-start | bytes 393224 | tf_op jit(solution)/shard_map/ppermute | solution.py:92
  39.5 5.0 %collective-permute-start.11 = (bf16[64,1024]{1,0:T(8,128)(2,1)S(1)}, bf16[64,1024]{1,0:T(8,128)(2,1)S(1)}, u32[]{:S(2)}, u32[]{:S(2)}) collective-permute-start(bf16[64,1024]{1,0:T(8,128)(2,1)S(1)} %collective-permute-done.7), channel_id=1, source_target_pairs={{4,8},{8,12},{12,14},{14,10},{10,6},{6,2},{2,0},{0,4},{5,1},{9,5},... | collective-permute-start | bytes 393224 | tf_op jit(solution)/shard_map/ppermute | solution.py:87
  41.6 5.0 %collective-permute-start.14 = (bf16[64,1024]{1,0:T(8,128)(2,1)S(1)}, bf16[64,1024]{1,0:T(8,128)(2,1)S(1)}, u32[]{:S(2)}, u32[]{:S(2)}) collective-permute-start(bf16[64,1024]{1,0:T(8,128)(2,1)S(1)} %collective-permute-done.10), channel_id=1, source_target_pairs={{4,8},{8,12},{12,14},{14,10},{10,6},{6,2},{2,0},{0,4},{5,1},{9,5},... | collective-permute-start | bytes 393224 | tf_op jit(solution)/shard_map/ppermute | solution.py:87
  44.4 5.0 %collective-permute-start.15 = (bf16[64,1024]{1,0:T(8,128)(2,1)S(1)}, bf16[64,1024]{1,0:T(8,128)(2,1)S(1)}, u32[]{:S(2)}, u32[]{:S(2)}) collective-permute-start(bf16[64,1024]{1,0:T(8,128)(2,1)S(1)} %collective-permute-done.11), channel_id=1, source_target_pairs={{4,8},{8,12},{12,14},{14,10},{10,6},{6,2},{2,0},{0,4},{5,1},{9,5},... | collective-permute-start | bytes 393224 | tf_op jit(solution)/shard_map/ppermute | solution.py:87
  49.5 3.2 %collective-permute-start.16 = (bf16[512,512]{1,0:T(8,128)(2,1)S(1)}, bf16[512,512]{1,0:T(8,128)(2,1)S(1)}, u32[]{:S(2)}, u32[]{:S(2)}) collective-permute-start(bf16[512,512]{1,0:T(8,128)(2,1)S(1)} %constant_dynamic-slice_fusion), channel_id=1, source_target_pairs={{0,1},{1,0},{2,3},{3,2},{4,5},{5,4},{6,7},{7,6},{8,9},{9,8},{10,11... | collective-permute-start | bytes 1572872 | tf_op jit(solution)/shard_map/ppermute | solution.py:102

commit v7 on v6

--- a/solution.py
+++ b/solution.py
@@ -57,7 +57,7 @@
         owner_of = jnp.sum((block_ends[None, :] <= row_ids[:, None]).astype(jnp.int32), axis=1)
         n_basis = lax.axis_size("basis")
         width = boundary.shape[1]
-        halves = 2 if width % 256 == 0 else 1
+        halves = 4 if width % 512 == 0 else 1
         step = width // halves
         amp_parts = []
         for h in range(halves):
@@ -70,18 +70,17 @@
                 shift = [(b, (b + s) % n_basis) for b in range(n_basis)]
                 total = total + lax.ppermute(part, "basis", shift)
             amp_parts.append(total.astype(jnp.bfloat16))
-        amp = jnp.concatenate(amp_parts, axis=1) if halves > 1 else amp_parts[0]
         eig_index = lax.axis_index("eig")
         cycle_arr = jnp.array(cycle, dtype=jnp.int32)
         pos = jnp.array(position, dtype=jnp.int32)[eig_index]
-        k_here = amp.shape[0]
-        left_panel = jnp.zeros((k_here * n_ring, amp.shape[1]), amp.dtype)
-        left_panel = lax.dynamic_update_slice_in_dim(left_panel, amp, eig_index * k_here, 0)
+        k_here = amp_parts[0].shape[0]
+        left_panel = jnp.zeros((k_here * n_ring, width), jnp.bfloat16)
+        for p, x in enumerate(amp_parts):
+            left_panel = lax.dynamic_update_slice(left_panel, x, (eig_index * k_here, p * step))
         sign = 1 - 2 * (lax.axis_index("chan") % 2)
-        n_split = 2 if amp.shape[1] % 256 == 0 else 1
-        split_w = amp.shape[1] // n_split
-        longs = [amp[:, p * split_w:(p + 1) * split_w] for p in range(n_split)]
-        shorts = list(longs)
+        split_w = step
+        longs = list(amp_parts)
+        shorts = list(amp_parts)
         for s in range(max(n_fwd, n_bwd)):
             if s < n_fwd:
                 longs = [lax.ppermute(x, ("eig", "chan"), long_pairs) for x in longs]

time: 69.1 us -> 101 us (1.46)
  starting transfers between devices: 17.9 us -> 37.3 us
  waiting for transfers between devices: 12.6 us -> 22.8 us
  matrix products: 22.2 us -> 24 us
    ppermute x8 -> x16, starting transfers between devices: 5.27 us -> 22.9 us  [per_device(): longs = [lax.ppermute(x, ('eig', 'chan'), long_pairs) for x in longs]]
    ppermute x8 -> x16, waiting for transfers between devices: 7.71 us -> 14 us  [per_device(): longs = [lax.ppermute(x, ('eig', 'chan'), long_pairs) for x in longs]]
    ppermute x6 -> x12, waiting for transfers between devices: 4.92 us -> 8.8 us  [per_device(): shorts = [lax.ppermute(x, ('eig', 'chan'), short_pairs) for x in shorts]]
    dot_general x2 -> x4, matrix products: 5.99 us -> 7.85 us  [per_device(): part = jnp.dot(eigvecs, masked, preferred_element_type=jnp.float32)]
    ppermute x2 -> x4, starting transfers between devices: 4.38 us -> 5.95 us  [per_device(): total = total + lax.ppermute(part, 'basis', shift)]
    ppermute x6 -> x12, starting transfers between devices: 8.13 us -> 8.35 us  [per_device(): shorts = [lax.ppermute(x, ('eig', 'chan'), short_pairs) for x in shorts]]
  transfers between devices with their start and end apart: 17 -> 33, of which waited for: 10 -> 9; matrix products, arithmetic and copies ran while one was open for 10% -> 10% of each run, Pallas kernels for 0% -> 0%
where the time goes in v7:
time: 101 us; the launch traced here: 100 us
  starting transfers between devices  37.3 us (37%)
  matrix products  24 us (24%)
  waiting for transfers between devices  22.8 us (23%)
  between operations  9.49 us (9%)
  local copies, waits for them, and re-layouts  6.35 us (6%)
    ppermute x16, starting transfers between devices, per_device(): longs = [lax.ppermute(x, ('eig', 'chan'), long_pairs) for x in longs]  22.9 us
    dot_general x1, matrix products, per_device(): jnp.einsum('ekc,kd->ecd', scaled, right_panel, preferred_element_type=jnp...  16.2 us
    ppermute x16, waiting for transfers between devices, per_device(): longs = [lax.ppermute(x, ('eig', 'chan'), long_pairs) for x in longs]  14 us
    ppermute x12, waiting for transfers between devices, per_device(): shorts = [lax.ppermute(x, ('eig', 'chan'), short_pairs) for x in shorts]  8.8 us
    ppermute x12, starting transfers between devices, per_device(): shorts = [lax.ppermute(x, ('eig', 'chan'), short_pairs) for x in shorts]  8.35 us
    dot_general x4, matrix products, per_device(): part = jnp.dot(eigvecs, masked, preferred_element_type=jnp.float32)  7.85 us
    ppermute x4, starting transfers between devices, per_device(): total = total + lax.ppermute(part, 'basis', shift)  5.95 us
    convert_element_type x1, local copies, waits for them, and re-layouts, per_device(): left_panel[None].astype(jnp.float32)  2.97 us
  transfers between devices with their start and end apart: 33, of which 9 were waited for; matrix products, arithmetic and copies ran while one was open for 10% of the time, Pallas kernels for 0%

profile of v7, /device:TPU:0, one launch (start us, length us, event | category | flops | bytes accessed | tf_op | source)
XLA Modules:
  0.0 100.3 jit_solution(8025743835808933813)
XLA Ops:
  1.8 3.0 %fusion.25 = f32[64,512]{1,0:T(8,128)S(1)} fusion(bf16[64,2560]{1,0:T(8,128)(2,1)S(1)} %copy-done, bf16[2560,2048]{1,0:T(8,128)(2,1)} %param.9, s32[512]{0:T(512)S(1)} %get-tuple-element.15, s32[2560]{0:T(1024)S(1)} %convert_reduce_fusion), kind=kOutput, calls=%fused_computation.31 | convolution fusion | flops 170393600 | bytes 3092480 | tf_op jit(solution)/shard_map/dot_general | solution.py:67
  4.9 3.0 %collective-permute-start = (f32[64,512]{1,0:T(8,128)S(1)}, f32[64,512]{1,0:T(8,128)S(1)}, u32[]{:S(2)}, u32[]{:S(2)}) collective-permute-start(f32[64,512]{1,0:T(8,128)S(1)} %fusion.25), channel_id=1, source_target_pairs={{0,16},{16,0},{1,17},{17,1},{2,18},{18,2},{3,19},{19,3},{4,20},{20... | collective-permute-start | bytes 393224 | tf_op jit(solution)/shard_map/ppermute | solution.py:71
  7.9 2.8 %fusion.22 = f32[64,512]{1,0:T(8,128)S(1)} fusion(bf16[64,2560]{1,0:T(8,128)(2,1)S(1)} %copy-done, bf16[2560,2048]{1,0:T(8,128)(2,1)} %param.9, s32[512]{0:T(512)S(1)} %get-tuple-element.13, s32[2560]{0:T(1024)S(1)} %convert_reduce_fusion), kind=kOutput, calls=%fused_computation.28 | convolution fusion | flops 170393600 | bytes 3092480 | tf_op jit(solution)/shard_map/dot_general | solution.py:67
  12.5 1.4 %collective-permute-start.2 = (f32[64,512]{1,0:T(8,128)S(1)}, f32[64,512]{1,0:T(8,128)S(1)}, u32[]{:S(2)}, u32[]{:S(2)}) collective-permute-start(f32[64,512]{1,0:T(8,128)S(1)} %fusion.23), channel_id=1, source_target_pairs={{0,16},{16,0},{1,17},{17,1},{2,18},{18,2},{3,19},{19,3},{4,20},{20... | collective-permute-start | bytes 393224 | tf_op jit(solution)/shard_map/ppermute | solution.py:71
  26.3 1.6 %collective-permute-start.4 = (bf16[64,512]{1,0:T(8,128)(2,1)S(1)}, bf16[64,512]{1,0:T(8,128)(2,1)S(1)}, u32[]{:S(2)}, u32[]{:S(2)}) collective-permute-start(bf16[64,512]{1,0:T(8,128)(2,1)S(1)} %get-tuple-element.12), channel_id=1, source_target_pairs={{4,8},{8,12},{12,14},{14,10},{10,6},{6,2},{2,0},{0,4},{5,1},{9,5},... | collective-permute-start | bytes 196616 | tf_op jit(solution)/shard_map/ppermute | solution.py:86
  28.0 1.6 %collective-permute-start.7 = (bf16[64,512]{1,0:T(8,128)(2,1)S(1)}, bf16[64,512]{1,0:T(8,128)(2,1)S(1)}, u32[]{:S(2)}, u32[]{:S(2)}) collective-permute-start(bf16[64,512]{1,0:T(8,128)(2,1)S(1)} %get-tuple-element.6), channel_id=1, source_target_pairs={{4,8},{8,12},{12,14},{14,10},{10,6},{6,2},{2,0},{0,4},{5,1},{9,5},... | collective-permute-start | bytes 196616 | tf_op jit(solution)/shard_map/ppermute | solution.py:86
  30.1 1.6 %collective-permute-start.6 = (bf16[64,512]{1,0:T(8,128)(2,1)S(1)}, bf16[64,512]{1,0:T(8,128)(2,1)S(1)}, u32[]{:S(2)}, u32[]{:S(2)}) collective-permute-start(bf16[64,512]{1,0:T(8,128)(2,1)S(1)} %get-tuple-element.8), channel_id=1, source_target_pairs={{4,8},{8,12},{12,14},{14,10},{10,6},{6,2},{2,0},{0,4},{5,1},{9,5},... | collective-permute-start | bytes 196616 | tf_op jit(solution)/shard_map/ppermute | solution.py:86
  32.1 1.6 %collective-permute-start.5 = (bf16[64,512]{1,0:T(8,128)(2,1)S(1)}, bf16[64,512]{1,0:T(8,128)(2,1)S(1)}, u32[]{:S(2)}, u32[]{:S(2)}) collective-permute-start(bf16[64,512]{1,0:T(8,128)(2,1)S(1)} %get-tuple-element.10), channel_id=1, source_target_pairs={{4,8},{8,12},{12,14},{14,10},{10,6},{6,2},{2,0},{0,4},{5,1},{9,5},... | collective-permute-start | bytes 196616 | tf_op jit(solution)/shard_map/ppermute | solution.py:86
  33.7 3.0 %collective-permute-done.5 = bf16[64,512]{1,0:T(8,128)(2,1)S(1)} collective-permute-done((bf16[64,512]{1,0:T(8,128)(2,1)S(1)}, bf16[64,512]{1,0:T(8,128)(2,1)S(1)}, u32[]{:S(2)}, u32[]{:S(2)}) %collective-permute-start.5) | collective-permute-done | bytes 65568 | tf_op jit(solution)/shard_map/ppermute | solution.py:86
  36.9 1.6 %collective-permute-start.8 = (bf16[64,512]{1,0:T(8,128)(2,1)S(1)}, bf16[64,512]{1,0:T(8,128)(2,1)S(1)}, u32[]{:S(2)}, u32[]{:S(2)}) collective-permute-start(bf16[64,512]{1,0:T(8,128)(2,1)S(1)} %get-tuple-element.12), channel_id=1, source_target_pairs={{4,0},{8,4},{12,8},{14,12},{10,14},{6,10},{2,6},{0,2},{5,9},{9,13}... | collective-permute-start | bytes 196616 | tf_op jit(solution)/shard_map/ppermute | solution.py:91
  39.0 4.0 %collective-permute-done.8 = bf16[64,512]{1,0:T(8,128)(2,1)S(1)} collective-permute-done((bf16[64,512]{1,0:T(8,128)(2,1)S(1)}, bf16[64,512]{1,0:T(8,128)(2,1)S(1)}, u32[]{:S(2)}, u32[]{:S(2)}) %collective-permute-start.8) | collective-permute-done | bytes 65568 | tf_op jit(solution)/shard_map/ppermute | solution.py:91
  43.0 1.0 %collective-permute-start.14 = (bf16[64,512]{1,0:T(8,128)(2,1)S(1)}, bf16[64,512]{1,0:T(8,128)(2,1)S(1)}, u32[]{:S(2)}, u32[]{:S(2)}) collective-permute-start(bf16[64,512]{1,0:T(8,128)(2,1)S(1)} %collective-permute-done.6), channel_id=1, source_target_pairs={{4,8},{8,12},{12,14},{14,10},{10,6},{6,2},{2,0},{0,4},{5,1},{9,5},... | collective-permute-start | bytes 196616 | tf_op jit(solution)/shard_map/ppermute | solution.py:86
  44.1 1.5 %collective-permute-start.12 = (bf16[64,512]{1,0:T(8,128)(2,1)S(1)}, bf16[64,512]{1,0:T(8,128)(2,1)S(1)}, u32[]{:S(2)}, u32[]{:S(2)}) collective-permute-start(bf16[64,512]{1,0:T(8,128)(2,1)S(1)} %collective-permute-done.4), channel_id=1, source_target_pairs={{4,8},{8,12},{12,14},{14,10},{10,6},{6,2},{2,0},{0,4},{5,1},{9,5},... | collective-permute-start | bytes 196616 | tf_op jit(solution)/shard_map/ppermute | solution.py:86
  47.2 1.2 %collective-permute-done.12 = bf16[64,512]{1,0:T(8,128)(2,1)S(1)} collective-permute-done((bf16[64,512]{1,0:T(8,128)(2,1)S(1)}, bf16[64,512]{1,0:T(8,128)(2,1)S(1)}, u32[]{:S(2)}, u32[]{:S(2)}) %collective-permute-start.12) | collective-permute-done | bytes 65568 | tf_op jit(solution)/shard_map/ppermute | solution.py:86
  48.4 2.0 %collective-permute-start.13 = (bf16[64,512]{1,0:T(8,128)(2,1)S(1)}, bf16[64,512]{1,0:T(8,128)(2,1)S(1)}, u32[]{:S(2)}, u32[]{:S(2)}) collective-permute-start(bf16[64,512]{1,0:T(8,128)(2,1)S(1)} %collective-permute-done.5), channel_id=1, source_target_pairs={{4,8},{8,12},{12,14},{14,10},{10,6},{6,2},{2,0},{0,4},{5,1},{9,5},... | collective-permute-start | bytes 196616 | tf_op jit(solution)/shard_map/ppermute | solution.py:86
  50.4 2.3 %collective-permute-done.13 = bf16[64,512]{1,0:T(8,128)(2,1)S(1)} collective-permute-done((bf16[64,512]{1,0:T(8,128)(2,1)S(1)}, bf16[64,512]{1,0:T(8,128)(2,1)S(1)}, u32[]{:S(2)}, u32[]{:S(2)}) %collective-permute-start.13) | collective-permute-done | bytes 65568 | tf_op jit(solution)/shard_map/ppermute | solution.py:86
  52.7 1.1 %collective-permute-start.17 = (bf16[64,512]{1,0:T(8,128)(2,1)S(1)}, bf16[64,512]{1,0:T(8,128)(2,1)S(1)}, u32[]{:S(2)}, u32[]{:S(2)}) collective-permute-start(bf16[64,512]{1,0:T(8,128)(2,1)S(1)} %collective-permute-done.9), channel_id=1, source_target_pairs={{4,0},{8,4},{12,8},{14,12},{10,14},{6,10},{2,6},{0,2},{5,9},{9,13}... | collective-permute-start | bytes 196616 | tf_op jit(solution)/shard_map/ppermute | solution.py:91
  54.1 1.8 %collective-permute-start.23 = (bf16[64,512]{1,0:T(8,128)(2,1)S(1)}, bf16[64,512]{1,0:T(8,128)(2,1)S(1)}, u32[]{:S(2)}, u32[]{:S(2)}) collective-permute-start(bf16[64,512]{1,0:T(8,128)(2,1)S(1)} %collective-permute-done.15), channel_id=1, source_target_pairs={{4,8},{8,12},{12,14},{14,10},{10,6},{6,2},{2,0},{0,4},{5,1},{9,5},... | collective-permute-start | bytes 196616 | tf_op jit(solution)/shard_map/ppermute | solution.py:86
  55.9 2.4 %collective-permute-done.16 = bf16[64,512]{1,0:T(8,128)(2,1)S(1)} collective-permute-done((bf16[64,512]{1,0:T(8,128)(2,1)S(1)}, bf16[64,512]{1,0:T(8,128)(2,1)S(1)}, u32[]{:S(2)}, u32[]{:S(2)}) %collective-permute-start.16) | collective-permute-done | bytes 65568 | tf_op jit(solution)/shard_map/ppermute | solution.py:91
  58.3 1.6 %collective-permute-start.22 = (bf16[64,512]{1,0:T(8,128)(2,1)S(1)}, bf16[64,512]{1,0:T(8,128)(2,1)S(1)}, u32[]{:S(2)}, u32[]{:S(2)}) collective-permute-start(bf16[64,512]{1,0:T(8,128)(2,1)S(1)} %collective-permute-done.14), channel_id=1, source_target_pairs={{4,8},{8,12},{12,14},{14,10},{10,6},{6,2},{2,0},{0,4},{5,1},{9,5},... | collective-permute-start | bytes 196616 | tf_op jit(solution)/shard_map/ppermute | solution.py:86
  59.9 1.4 %collective-permute-start.20 = (bf16[64,512]{1,0:T(8,128)(2,1)S(1)}, bf16[64,512]{1,0:T(8,128)(2,1)S(1)}, u32[]{:S(2)}, u32[]{:S(2)}) collective-permute-start(bf16[64,512]{1,0:T(8,128)(2,1)S(1)} %collective-permute-done.12), channel_id=1, source_target_pairs={{4,8},{8,12},{12,14},{14,10},{10,6},{6,2},{2,0},{0,4},{5,1},{9,5},... | collective-permute-start | bytes 196616 | tf_op jit(solution)/shard_map/ppermute | solution.py:86
  62.5 1.7 %collective-permute-done.20 = bf16[64,512]{1,0:T(8,128)(2,1)S(1)} collective-permute-done((bf16[64,512]{1,0:T(8,128)(2,1)S(1)}, bf16[64,512]{1,0:T(8,128)(2,1)S(1)}, u32[]{:S(2)}, u32[]{:S(2)}) %collective-permute-start.20) | collective-permute-done | bytes 65568 | tf_op jit(solution)/shard_map/ppermute | solution.py:86
  64.2 1.4 %collective-permute-start.21 = (bf16[64,512]{1,0:T(8,128)(2,1)S(1)}, bf16[64,512]{1,0:T(8,128)(2,1)S(1)}, u32[]{:S(2)}, u32[]{:S(2)}) collective-permute-start(bf16[64,512]{1,0:T(8,128)(2,1)S(1)} %collective-permute-done.13), channel_id=1, source_target_pairs={{4,8},{8,12},{12,14},{14,10},{10,6},{6,2},{2,0},{0,4},{5,1},{9,5},... | collective-permute-start | bytes 196616 | tf_op jit(solution)/shard_map/ppermute | solution.py:86
  65.6 2.9 %collective-permute-done.21 = bf16[64,512]{1,0:T(8,128)(2,1)S(1)} collective-permute-done((bf16[64,512]{1,0:T(8,128)(2,1)S(1)}, bf16[64,512]{1,0:T(8,128)(2,1)S(1)}, u32[]{:S(2)}, u32[]{:S(2)}) %collective-permute-start.21) | collective-permute-done | bytes 65568 | tf_op jit(solution)/shard_map/ppermute | solution.py:86
  69.0 1.2 %collective-permute-start.24 = (bf16[64,512]{1,0:T(8,128)(2,1)S(1)}, bf16[64,512]{1,0:T(8,128)(2,1)S(1)}, u32[]{:S(2)}, u32[]{:S(2)}) collective-permute-start(bf16[64,512]{1,0:T(8,128)(2,1)S(1)} %collective-permute-done.16), channel_id=1, source_target_pairs={{4,0},{8,4},{12,8},{14,12},{10,14},{6,10},{2,6},{0,2},{5,9},{9,13}... | collective-permute-start | bytes 196616 | tf_op jit(solution)/shard_map/ppermute | solution.py:91
  71.1 2.4 %collective-permute-done.24 = bf16[64,512]{1,0:T(8,128)(2,1)S(1)} collective-permute-done((bf16[64,512]{1,0:T(8,128)(2,1)S(1)}, bf16[64,512]{1,0:T(8,128)(2,1)S(1)}, u32[]{:S(2)}, u32[]{:S(2)}) %collective-permute-start.24) | collective-permute-done | bytes 65568 | tf_op jit(solution)/shard_map/ppermute | solution.py:91
  73.5 1.4 %collective-permute-start.30 = (bf16[64,512]{1,0:T(8,128)(2,1)S(1)}, bf16[64,512]{1,0:T(8,128)(2,1)S(1)}, u32[]{:S(2)}, u32[]{:S(2)}) collective-permute-start(bf16[64,512]{1,0:T(8,128)(2,1)S(1)} %collective-permute-done.22), channel_id=1, source_target_pairs={{4,8},{8,12},{12,14},{14,10},{10,6},{6,2},{2,0},{0,4},{5,1},{9,5},... | collective-permute-start | bytes 196616 | tf_op jit(solution)/shard_map/ppermute | solution.py:86
  74.9 1.6 %collective-permute-start.29 = (bf16[64,512]{1,0:T(8,128)(2,1)S(1)}, bf16[64,512]{1,0:T(8,128)(2,1)S(1)}, u32[]{:S(2)}, u32[]{:S(2)}) collective-permute-start(bf16[64,512]{1,0:T(8,128)(2,1)S(1)} %collective-permute-done.21), channel_id=1, source_target_pairs={{4,8},{8,12},{12,14},{14,10},{10,6},{6,2},{2,0},{0,4},{5,1},{9,5},... | collective-permute-start | bytes 196616 | tf_op jit(solution)/shard_map/ppermute | solution.py:86
  76.5 1.5 %collective-permute-start.28 = (bf16[64,512]{1,0:T(8,128)(2,1)S(1)}, bf16[64,512]{1,0:T(8,128)(2,1)S(1)}, u32[]{:S(2)}, u32[]{:S(2)}) collective-permute-start(bf16[64,512]{1,0:T(8,128)(2,1)S(1)} %collective-permute-done.20), channel_id=1, source_target_pairs={{4,8},{8,12},{12,14},{14,10},{10,6},{6,2},{2,0},{0,4},{5,1},{9,5},... | collective-permute-start | bytes 196616 | tf_op jit(solution)/shard_map/ppermute | solution.py:86
  78.0 2.8 %collective-permute-done.28 = bf16[64,512]{1,0:T(8,128)(2,1)S(1)} collective-permute-done((bf16[64,512]{1,0:T(8,128)(2,1)S(1)}, bf16[64,512]{1,0:T(8,128)(2,1)S(1)}, u32[]{:S(2)}, u32[]{:S(2)}) %collective-permute-start.28) | collective-permute-done | bytes 65568 | tf_op jit(solution)/shard_map/ppermute | solution.py:86
  81.2 3.0 %copy.14 = f32[512,2048]{0,1:T(8,128)} copy(bf16[512,2048]{1,0:T(8,128)(2,1)S(1)} %constant_dynamic-update-slice_fusion) | data formatting | bytes 6291456 | tf_op jit(solution)/shard_map/convert_element_type | solution.py:108
  84.1 16.2 %convolution_multiply_fusion = f32[8,2048,512]{2,1,0:T(8,128)} fusion(f32[512,2048]{0,1:T(8,128)} %copy.14, f32[8,512]{1,0:T(8,128)S(1)} %subtract_divide_fusion, bf16[512,512]{1,0:T(8,128)(2,1)S(1)} %constant_dynamic-slice_fusion, bf16[512,512]{1,0:T(8,128)(2,1)S(1)} %collective-permute-done.32, pred[]{:T(512)S(6)} %eq.68), kind=kOutput, calls=%fused_computation.1 | convolution fusion | flops 8615362560 | bytes 38813696 | tf_op jit(solution)/shard_map/ekc,kd->ecd/dot_general | solution.py:109
  (95 shorter events, 13.3 us)
Async XLA Ops:
  4.9 21.1 %collective-permute-start = (f32[64,512]{1,0:T(8,128)S(1)}, f32[64,512]{1,0:T(8,128)S(1)}, u32[]{:S(2)}, u32[]{:S(2)}) collective-permute-start(f32[64,512]{1,0:T(8,128)S(1)} %fusion.25), channel_id=1, source_target_pairs={{0,16},{16,0},{1,17},{17,1},{2,18},{18,2},{3,19},{19,3},{4,20},{20... | collective-permute-start | bytes 393224 | tf_op jit(solution)/shard_map/ppermute | solution.py:71
  10.7 17.2 %collective-permute-start.3 = (f32[64,512]{1,0:T(8,128)S(1)}, f32[64,512]{1,0:T(8,128)S(1)}, u32[]{:S(2)}, u32[]{:S(2)}) collective-permute-start(f32[64,512]{1,0:T(8,128)S(1)} %fusion.22), channel_id=1, source_target_pairs={{0,16},{16,0},{1,17},{17,1},{2,18},{18,2},{3,19},{19,3},{4,20},{20... | collective-permute-start | bytes 393224 | tf_op jit(solution)/shard_map/ppermute | solution.py:71
  12.5 15.4 %collective-permute-start.2 = (f32[64,512]{1,0:T(8,128)S(1)}, f32[64,512]{1,0:T(8,128)S(1)}, u32[]{:S(2)}, u32[]{:S(2)}) collective-permute-start(f32[64,512]{1,0:T(8,128)S(1)} %fusion.23), channel_id=1, source_target_pairs={{0,16},{16,0},{1,17},{17,1},{2,18},{18,2},{3,19},{19,3},{4,20},{20... | collective-permute-start | bytes 393224 | tf_op jit(solution)/shard_map/ppermute | solution.py:71
  14.9 13.0 %collective-permute-start.1 = (f32[64,512]{1,0:T(8,128)S(1)}, f32[64,512]{1,0:T(8,128)S(1)}, u32[]{:S(2)}, u32[]{:S(2)}) collective-permute-start(f32[64,512]{1,0:T(8,128)S(1)} %fusion.24), channel_id=1, source_target_pairs={{0,16},{16,0},{1,17},{17,1},{2,18},{18,2},{3,19},{19,3},{4,20},{20... | collective-permute-start | bytes 393224 | tf_op jit(solution)/shard_map/ppermute | solution.py:71
  26.3 5.8 %collective-permute-start.4 = (bf16[64,512]{1,0:T(8,128)(2,1)S(1)}, bf16[64,512]{1,0:T(8,128)(2,1)S(1)}, u32[]{:S(2)}, u32[]{:S(2)}) collective-permute-start(bf16[64,512]{1,0:T(8,128)(2,1)S(1)} %get-tuple-element.12), channel_id=1, source_target_pairs={{4,8},{8,12},{12,14},{14,10},{10,6},{6,2},{2,0},{0,4},{5,1},{9,5},... | collective-permute-start | bytes 196616 | tf_op jit(solution)/shard_map/ppermute | solution.py:86
  28.0 8.8 %collective-permute-start.7 = (bf16[64,512]{1,0:T(8,128)(2,1)S(1)}, bf16[64,512]{1,0:T(8,128)(2,1)S(1)}, u32[]{:S(2)}, u32[]{:S(2)}) collective-permute-start(bf16[64,512]{1,0:T(8,128)(2,1)S(1)} %get-tuple-element.6), channel_id=1, source_target_pairs={{4,8},{8,12},{12,14},{14,10},{10,6},{6,2},{2,0},{0,4},{5,1},{9,5},... | collective-permute-start | bytes 196616 | tf_op jit(solution)/shard_map/ppermute | solution.py:86
  29.7 14.4 %collective-permute-start.11 = (bf16[64,512]{1,0:T(8,128)(2,1)S(1)}, bf16[64,512]{1,0:T(8,128)(2,1)S(1)}, u32[]{:S(2)}, u32[]{:S(2)}) collective-permute-start(bf16[64,512]{1,0:T(8,128)(2,1)S(1)} %get-tuple-element.6), channel_id=1, source_target_pairs={{4,0},{8,4},{12,8},{14,12},{10,14},{6,10},{2,6},{0,2},{5,9},{9,13}... | collective-permute-start | bytes 196616 | tf_op jit(solution)/shard_map/ppermute | solution.py:91
  30.1 8.3 %collective-permute-start.6 = (bf16[64,512]{1,0:T(8,128)(2,1)S(1)}, bf16[64,512]{1,0:T(8,128)(2,1)S(1)}, u32[]{:S(2)}, u32[]{:S(2)}) collective-permute-start(bf16[64,512]{1,0:T(8,128)(2,1)S(1)} %get-tuple-element.8), channel_id=1, source_target_pairs={{4,8},{8,12},{12,14},{14,10},{10,6},{6,2},{2,0},{0,4},{5,1},{9,5},... | collective-permute-start | bytes 196616 | tf_op jit(solution)/shard_map/ppermute | solution.py:86
  31.7 13.9 %collective-permute-start.10 = (bf16[64,512]{1,0:T(8,128)(2,1)S(1)}, bf16[64,512]{1,0:T(8,128)(2,1)S(1)}, u32[]{:S(2)}, u32[]{:S(2)}) collective-permute-start(bf16[64,512]{1,0:T(8,128)(2,1)S(1)} %get-tuple-element.8), channel_id=1, source_target_pairs={{4,0},{8,4},{12,8},{14,12},{10,14},{6,10},{2,6},{0,2},{5,9},{9,13}... | collective-permute-start | bytes 196616 | tf_op jit(solution)/shard_map/ppermute | solution.py:91
  32.1 4.6 %collective-permute-start.5 = (bf16[64,512]{1,0:T(8,128)(2,1)S(1)}, bf16[64,512]{1,0:T(8,128)(2,1)S(1)}, u32[]{:S(2)}, u32[]{:S(2)}) collective-permute-start(bf16[64,512]{1,0:T(8,128)(2,1)S(1)} %get-tuple-element.10), channel_id=1, source_target_pairs={{4,8},{8,12},{12,14},{14,10},{10,6},{6,2},{2,0},{0,4},{5,1},{9,5},... | collective-permute-start | bytes 196616 | tf_op jit(solution)/shard_map/ppermute | solution.py:86
  36.8 9.4 %collective-permute-start.9 = (bf16[64,512]{1,0:T(8,128)(2,1)S(1)}, bf16[64,512]{1,0:T(8,128)(2,1)S(1)}, u32[]{:S(2)}, u32[]{:S(2)}) collective-permute-start(bf16[64,512]{1,0:T(8,128)(2,1)S(1)} %get-tuple-element.10), channel_id=1, source_target_pairs={{4,0},{8,4},{12,8},{14,12},{10,14},{6,10},{2,6},{0,2},{5,9},{9,13}... | collective-permute-start | bytes 196616 | tf_op jit(solution)/shard_map/ppermute | solution.py:91
  36.9 6.2 %collective-permute-start.8 = (bf16[64,512]{1,0:T(8,128)(2,1)S(1)}, bf16[64,512]{1,0:T(8,128)(2,1)S(1)}, u32[]{:S(2)}, u32[]{:S(2)}) collective-permute-start(bf16[64,512]{1,0:T(8,128)(2,1)S(1)} %get-tuple-element.12), channel_id=1, source_target_pairs={{4,0},{8,4},{12,8},{14,12},{10,14},{6,10},{2,6},{0,2},{5,9},{9,13}... | collective-permute-start | bytes 196616 | tf_op jit(solution)/shard_map/ppermute | solution.py:91
  38.4 15.4 %collective-permute-start.15 = (bf16[64,512]{1,0:T(8,128)(2,1)S(1)}, bf16[64,512]{1,0:T(8,128)(2,1)S(1)}, u32[]{:S(2)}, u32[]{:S(2)}) collective-permute-start(bf16[64,512]{1,0:T(8,128)(2,1)S(1)} %collective-permute-done.7), channel_id=1, source_target_pairs={{4,8},{8,12},{12,14},{14,10},{10,6},{6,2},{2,0},{0,4},{5,1},{9,5},... | collective-permute-start | bytes 196616 | tf_op jit(solution)/shard_map/ppermute | solution.py:86
  43.0 11.1 %collective-permute-start.14 = (bf16[64,512]{1,0:T(8,128)(2,1)S(1)}, bf16[64,512]{1,0:T(8,128)(2,1)S(1)}, u32[]{:S(2)}, u32[]{:S(2)}) collective-permute-start(bf16[64,512]{1,0:T(8,128)(2,1)S(1)} %collective-permute-done.6), channel_id=1, source_target_pairs={{4,8},{8,12},{12,14},{14,10},{10,6},{6,2},{2,0},{0,4},{5,1},{9,5},... | collective-permute-start | bytes 196616 | tf_op jit(solution)/shard_map/ppermute | solution.py:86
  44.1 4.3 %collective-permute-start.12 = (bf16[64,512]{1,0:T(8,128)(2,1)S(1)}, bf16[64,512]{1,0:T(8,128)(2,1)S(1)}, u32[]{:S(2)}, u32[]{:S(2)}) collective-permute-start(bf16[64,512]{1,0:T(8,128)(2,1)S(1)} %collective-permute-done.4), channel_id=1, source_target_pairs={{4,8},{8,12},{12,14},{14,10},{10,6},{6,2},{2,0},{0,4},{5,1},{9,5},... | collective-permute-start | bytes 196616 | tf_op jit(solution)/shard_map/ppermute | solution.py:86
  45.6 14.3 %collective-permute-start.19 = (bf16[64,512]{1,0:T(8,128)(2,1)S(1)}, bf16[64,512]{1,0:T(8,128)(2,1)S(1)}, u32[]{:S(2)}, u32[]{:S(2)}) collective-permute-start(bf16[64,512]{1,0:T(8,128)(2,1)S(1)} %collective-permute-done.11), channel_id=1, source_target_pairs={{4,0},{8,4},{12,8},{14,12},{10,14},{6,10},{2,6},{0,2},{5,9},{9,13}... | collective-permute-start | bytes 196616 | tf_op jit(solution)/shard_map/ppermute | solution.py:91
  46.2 15.2 %collective-permute-start.18 = (bf16[64,512]{1,0:T(8,128)(2,1)S(1)}, bf16[64,512]{1,0:T(8,128)(2,1)S(1)}, u32[]{:S(2)}, u32[]{:S(2)}) collective-permute-start(bf16[64,512]{1,0:T(8,128)(2,1)S(1)} %collective-permute-done.10), channel_id=1, source_target_pairs={{4,0},{8,4},{12,8},{14,12},{10,14},{6,10},{2,6},{0,2},{5,9},{9,13}... | collective-permute-start | bytes 196616 | tf_op jit(solution)/shard_map/ppermute | solution.py:91
  48.4 4.3 %collective-permute-start.13 = (bf16[64,512]{1,0:T(8,128)(2,1)S(1)}, bf16[64,512]{1,0:T(8,128)(2,1)S(1)}, u32[]{:S(2)}, u32[]{:S(2)}) collective-permute-start(bf16[64,512]{1,0:T(8,128)(2,1)S(1)} %collective-permute-done.5), channel_id=1, source_target_pairs={{4,8},{8,12},{12,14},{14,10},{10,6},{6,2},{2,0},{0,4},{5,1},{9,5},... | collective-permute-start | bytes 196616 | tf_op jit(solution)/shard_map/ppermute | solution.py:86
  52.7 9.3 %collective-permute-start.17 = (bf16[64,512]{1,0:T(8,128)(2,1)S(1)}, bf16[64,512]{1,0:T(8,128)(2,1)S(1)}, u32[]{:S(2)}, u32[]{:S(2)}) collective-permute-start(bf16[64,512]{1,0:T(8,128)(2,1)S(1)} %collective-permute-done.9), channel_id=1, source_target_pairs={{4,0},{8,4},{12,8},{14,12},{10,14},{6,10},{2,6},{0,2},{5,9},{9,13}... | collective-permute-start | bytes 196616 | tf_op jit(solution)/shard_map/ppermute | solution.py:91
  53.8 4.5 %collective-permute-start.16 = (bf16[64,512]{1,0:T(8,128)(2,1)S(1)}, bf16[64,512]{1,0:T(8,128)(2,1)S(1)}, u32[]{:S(2)}, u32[]{:S(2)}) collective-permute-start(bf16[64,512]{1,0:T(8,128)(2,1)S(1)} %collective-permute-done.8), channel_id=1, source_target_pairs={{4,0},{8,4},{12,8},{14,12},{10,14},{6,10},{2,6},{0,2},{5,9},{9,13}... | collective-permute-start | bytes 196616 | tf_op jit(solution)/shard_map/ppermute | solution.py:91
  54.1 14.9 %collective-permute-start.23 = (bf16[64,512]{1,0:T(8,128)(2,1)S(1)}, bf16[64,512]{1,0:T(8,128)(2,1)S(1)}, u32[]{:S(2)}, u32[]{:S(2)}) collective-permute-start(bf16[64,512]{1,0:T(8,128)(2,1)S(1)} %collective-permute-done.15), channel_id=1, source_target_pairs={{4,8},{8,12},{12,14},{14,10},{10,6},{6,2},{2,0},{0,4},{5,1},{9,5},... | collective-permute-start | bytes 196616 | tf_op jit(solution)/shard_map/ppermute | solution.py:86
  58.3 11.8 %collective-permute-start.22 = (bf16[64,512]{1,0:T(8,128)(2,1)S(1)}, bf16[64,512]{1,0:T(8,128)(2,1)S(1)}, u32[]{:S(2)}, u32[]{:S(2)}) collective-permute-start(bf16[64,512]{1,0:T(8,128)(2,1)S(1)} %collective-permute-done.14), channel_id=1, source_target_pairs={{4,8},{8,12},{12,14},{14,10},{10,6},{6,2},{2,0},{0,4},{5,1},{9,5},... | collective-permute-start | bytes 196616 | tf_op jit(solution)/shard_map/ppermute | solution.py:86
  59.9 4.3 %collective-permute-start.20 = (bf16[64,512]{1,0:T(8,128)(2,1)S(1)}, bf16[64,512]{1,0:T(8,128)(2,1)S(1)}, u32[]{:S(2)}, u32[]{:S(2)}) collective-permute-start(bf16[64,512]{1,0:T(8,128)(2,1)S(1)} %collective-permute-done.12), channel_id=1, source_target_pairs={{4,8},{8,12},{12,14},{14,10},{10,6},{6,2},{2,0},{0,4},{5,1},{9,5},... | collective-permute-start | bytes 196616 | tf_op jit(solution)/shard_map/ppermute | solution.py:86
  61.3 16.6 %collective-permute-start.27 = (bf16[64,512]{1,0:T(8,128)(2,1)S(1)}, bf16[64,512]{1,0:T(8,128)(2,1)S(1)}, u32[]{:S(2)}, u32[]{:S(2)}) collective-permute-start(bf16[64,512]{1,0:T(8,128)(2,1)S(1)} %collective-permute-done.19), channel_id=1, source_target_pairs={{4,0},{8,4},{12,8},{14,12},{10,14},{6,10},{2,6},{0,2},{5,9},{9,13}... | collective-permute-start | bytes 196616 | tf_op jit(solution)/shard_map/ppermute | solution.py:91
  62.0 14.5 %collective-permute-start.26 = (bf16[64,512]{1,0:T(8,128)(2,1)S(1)}, bf16[64,512]{1,0:T(8,128)(2,1)S(1)}, u32[]{:S(2)}, u32[]{:S(2)}) collective-permute-start(bf16[64,512]{1,0:T(8,128)(2,1)S(1)} %collective-permute-done.18), channel_id=1, source_target_pairs={{4,0},{8,4},{12,8},{14,12},{10,14},{6,10},{2,6},{0,2},{5,9},{9,13}... | collective-permute-start | bytes 196616 | tf_op jit(solution)/shard_map/ppermute | solution.py:91
  64.2 4.3 %collective-permute-start.21 = (bf16[64,512]{1,0:T(8,128)(2,1)S(1)}, bf16[64,512]{1,0:T(8,128)(2,1)S(1)}, u32[]{:S(2)}, u32[]{:S(2)}) collective-permute-start(bf16[64,512]{1,0:T(8,128)(2,1)S(1)} %collective-permute-done.13), channel_id=1, source_target_pairs={{4,8},{8,12},{12,14},{14,10},{10,6},{6,2},{2,0},{0,4},{5,1},{9,5},... | collective-permute-start | bytes 196616 | tf_op jit(solution)/shard_map/ppermute | solution.py:86
  68.5 6.4 %collective-permute-start.25 = (bf16[64,512]{1,0:T(8,128)(2,1)S(1)}, bf16[64,512]{1,0:T(8,128)(2,1)S(1)}, u32[]{:S(2)}, u32[]{:S(2)}) collective-permute-start(bf16[64,512]{1,0:T(8,128)(2,1)S(1)} %collective-permute-done.17), channel_id=1, source_target_pairs={{4,0},{8,4},{12,8},{14,12},{10,14},{6,10},{2,6},{0,2},{5,9},{9,13}... | collective-permute-start | bytes 196616 | tf_op jit(solution)/shard_map/ppermute | solution.py:91
  69.0 4.5 %collective-permute-start.24 = (bf16[64,512]{1,0:T(8,128)(2,1)S(1)}, bf16[64,512]{1,0:T(8,128)(2,1)S(1)}, u32[]{:S(2)}, u32[]{:S(2)}) collective-permute-start(bf16[64,512]{1,0:T(8,128)(2,1)S(1)} %collective-permute-done.16), channel_id=1, source_target_pairs={{4,0},{8,4},{12,8},{14,12},{10,14},{6,10},{2,6},{0,2},{5,9},{9,13}... | collective-permute-start | bytes 196616 | tf_op jit(solution)/shard_map/ppermute | solution.py:91
  70.2 10.7 %collective-permute-start.31 = (bf16[64,512]{1,0:T(8,128)(2,1)S(1)}, bf16[64,512]{1,0:T(8,128)(2,1)S(1)}, u32[]{:S(2)}, u32[]{:S(2)}) collective-permute-start(bf16[64,512]{1,0:T(8,128)(2,1)S(1)} %collective-permute-done.23), channel_id=1, source_target_pairs={{4,8},{8,12},{12,14},{14,10},{10,6},{6,2},{2,0},{0,4},{5,1},{9,5},... | collective-permute-start | bytes 196616 | tf_op jit(solution)/shard_map/ppermute | solution.py:86
  73.5 7.4 %collective-permute-start.30 = (bf16[64,512]{1,0:T(8,128)(2,1)S(1)}, bf16[64,512]{1,0:T(8,128)(2,1)S(1)}, u32[]{:S(2)}, u32[]{:S(2)}) collective-permute-start(bf16[64,512]{1,0:T(8,128)(2,1)S(1)} %collective-permute-done.22), channel_id=1, source_target_pairs={{4,8},{8,12},{12,14},{14,10},{10,6},{6,2},{2,0},{0,4},{5,1},{9,5},... | collective-permute-start | bytes 196616 | tf_op jit(solution)/shard_map/ppermute | solution.py:86
  74.9 5.9 %collective-permute-start.29 = (bf16[64,512]{1,0:T(8,128)(2,1)S(1)}, bf16[64,512]{1,0:T(8,128)(2,1)S(1)}, u32[]{:S(2)}, u32[]{:S(2)}) collective-permute-start(bf16[64,512]{1,0:T(8,128)(2,1)S(1)} %collective-permute-done.21), channel_id=1, source_target_pairs={{4,8},{8,12},{12,14},{14,10},{10,6},{6,2},{2,0},{0,4},{5,1},{9,5},... | collective-permute-start | bytes 196616 | tf_op jit(solution)/shard_map/ppermute | solution.py:86
  76.5 4.3 %collective-permute-start.28 = (bf16[64,512]{1,0:T(8,128)(2,1)S(1)}, bf16[64,512]{1,0:T(8,128)(2,1)S(1)}, u32[]{:S(2)}, u32[]{:S(2)}) collective-permute-start(bf16[64,512]{1,0:T(8,128)(2,1)S(1)} %collective-permute-done.20), channel_id=1, source_target_pairs={{4,8},{8,12},{12,14},{14,10},{10,6},{6,2},{2,0},{0,4},{5,1},{9,5},... | collective-permute-start | bytes 196616 | tf_op jit(solution)/shard_map/ppermute | solution.py:86
  (7 other events, 107.7 us)

commit v8 on v5

--- a/solution.py
+++ b/solution.py
@@ -57,37 +57,72 @@
         owner_of = jnp.sum((block_ends[None, :] <= row_ids[:, None]).astype(jnp.int32), axis=1)
         n_basis = lax.axis_size("basis")
         width = boundary.shape[1]
+        eig_index = lax.axis_index("eig")
+        cycle_arr = jnp.array(cycle, dtype=jnp.int32)
+        pos = jnp.array(position, dtype=jnp.int32)[eig_index]
+        sign = 1 - 2 * (lax.axis_index("chan") % 2)
+        k_here = eigvecs.shape[0]
+        left_panel = jnp.zeros((k_here * n_ring, width), jnp.bfloat16)
         halves = 2 if width % 256 == 0 else 1
         step = width // halves
-        amp_parts = []
+        parts = []
         for h in range(halves):
             cols = slice(h * step, (h + 1) * step)
             member = owner_of[:, None] == target_of_channel[None, cols]
             masked = jnp.where(member, boundary[:, cols], jnp.zeros_like(boundary[:, cols]))
-            part = jnp.dot(eigvecs, masked, preferred_element_type=jnp.float32)
-            total = part
-            for s in range(1, n_basis):
-                shift = [(b, (b + s) % n_basis) for b in range(n_basis)]
-                total = total + lax.ppermute(part, "basis", shift)
-            amp_parts.append(total.astype(jnp.bfloat16))
-        amp = jnp.concatenate(amp_parts, axis=1) if halves > 1 else amp_parts[0]
-        eig_index = lax.axis_index("eig")
-        cycle_arr = jnp.array(cycle, dtype=jnp.int32)
-        pos = jnp.array(position, dtype=jnp.int32)[eig_index]
-        k_here = amp.shape[0]
-        left_panel = jnp.zeros((k_here * n_ring, amp.shape[1]), amp.dtype)
-        left_panel = lax.dynamic_update_slice_in_dim(left_panel, amp, eig_index * k_here, 0)
-        sign = 1 - 2 * (lax.axis_index("chan") % 2)
-        long_blk, short_blk = amp, amp
-        for s in range(max(n_fwd, n_bwd)):
-            if s < n_fwd:
-                long_blk = lax.ppermute(long_blk, ("eig", "chan"), long_pairs)
-                origin = cycle_arr[(pos - sign * (s + 1)) % n_ring]
-                left_panel = lax.dynamic_update_slice_in_dim(left_panel, long_blk, origin * k_here, 0)
-            if s < n_bwd:
-                short_blk = lax.ppermute(short_blk, ("eig", "chan"), short_pairs)
-                origin = cycle_arr[(pos + sign * (s + 1)) % n_ring]
-                left_panel = lax.dynamic_update_slice_in_dim(left_panel, short_blk, origin * k_here, 0)
+            parts.append(jnp.dot(eigvecs, masked, preferred_element_type=jnp.float32))
+        if n_basis == 2 and halves == 2:
+            mine = lax.axis_index("basis")
+            swap = [(0, 1), (1, 0)]
+            keep = jnp.where(mine == 0, parts[0], parts[1])
+            give = jnp.where(mine == 0, parts[1], parts[0])
+            amp_mine = (keep + lax.ppermute(give, "basis", swap)).astype(jnp.bfloat16)
+            own_col = mine * step
+            other_col = (1 - mine) * step
+            left_panel = lax.dynamic_update_slice(left_panel, amp_mine, (eig_index * k_here, own_col))
+            got = lax.ppermute(amp_mine, "basis", swap)
+            left_panel = lax.dynamic_update_slice(left_panel, got, (eig_index * k_here, other_col))
+            long_blk, short_blk = amp_mine, amp_mine
+            for s in range(max(n_fwd, n_bwd)):
+                new_blocks = []
+                if s < n_fwd:
+                    long_blk = lax.ppermute(long_blk, ("eig", "chan"), long_pairs)
+                    origin = cycle_arr[(pos - sign * (s + 1)) % n_ring]
+                    left_panel = lax.dynamic_update_slice(left_panel, long_blk, (origin * k_here, own_col))
+                    new_blocks.append((long_blk, origin))
+                if s < n_bwd:
+                    short_blk = lax.ppermute(short_blk, ("eig", "chan"), short_pairs)
+                    origin = cycle_arr[(pos + sign * (s + 1)) % n_ring]
+                    left_panel = lax.dynamic_update_slice(left_panel, short_blk, (origin * k_here, own_col))
+                    new_blocks.append((short_blk, origin))
+                sent = jnp.concatenate([b for b, _ in new_blocks], axis=0)
+                got = lax.ppermute(sent, "basis", swap)
+                for i, (_, origin) in enumerate(new_blocks):
+                    piece_i = got[i * k_here:(i + 1) * k_here]
+                    left_panel = lax.dynamic_update_slice(left_panel, piece_i, (origin * k_here, other_col))
+        else:
+            amp_parts = []
+            for part in parts:
+                total = part
+                for s in range(1, n_basis):
+                    shift = [(b, (b + s) % n_basis) for b in range(n_basis)]
+                    total = total + lax.ppermute(part, "basis", shift)
+                amp_parts.append(total.astype(jnp.bfloat16))
+            for p, x in enumerate(amp_parts):
+                left_panel = lax.dynamic_update_slice(left_panel, x, (eig_index * k_here, p * step))
+            longs = list(amp_parts)
+            shorts = list(amp_parts)
+            for s in range(max(n_fwd, n_bwd)):
+                if s < n_fwd:
+                    longs = [lax.ppermute(x, ("eig", "chan"), long_pairs) for x in longs]
+                    origin = cycle_arr[(pos - sign * (s + 1)) % n_ring]
+                    for p, x in enumerate(longs):
+                        left_panel = lax.dynamic_update_slice(left_panel, x, (origin * k_here, p * step))
+                if s < n_bwd:
+                    shorts = [lax.ppermute(x, ("eig", "chan"), short_pairs) for x in shorts]
+                    origin = cycle_arr[(pos + sign * (s + 1)) % n_ring]
+                    for p, x in enumerate(shorts):
+                        left_panel = lax.dynamic_update_slice(left_panel, x, (origin * k_here, p * step))
         own_width = left_panel.shape[1]
         col_width = own_width * n_chan // n_eig
         ratio = n_eig // n_chan

time: 75.2 us -> 93.3 us (1.24)
  local copies, waits for them, and re-layouts: 6.17 us -> 30.2 us
  waiting for transfers between devices: 26.9 us -> 15.5 us
  starting transfers between devices: 10 us -> 14.1 us
  other arithmetic: 0.45 us -> 1.84 us
    dynamic_update_slice x7 -> x15, local copies, waits for them, and re-layouts: 0.15 us -> 22.8 us  [the longest x4 10.1 us: per_device(): lax.dynamic_update_slice(left_panel, long_blk, (origin * k_here, own_col))]
    ppermute x4, waiting for transfers between devices: 14.6 us -> 4.28 us  [per_device(): long_blk = lax.ppermute(long_blk, ('eig', 'chan'), long_pairs)]
    ppermute x2 -> x6, starting transfers between devices: 4.38 us -> 7.29 us  [the longest x1 3.03 us: per_device(): amp_mine = (keep + lax.ppermute(give, 'basis', swap)).astype(jnp.bfloat16)]
    ppermute x3, waiting for transfers between devices: 3.6 us -> 1.86 us  [per_device(): short_blk = lax.ppermute(short_blk, ('eig', 'chan'), short_pairs)]
    ppermute x4, starting transfers between devices: 4.57 us -> 6.26 us  [per_device(): long_blk = lax.ppermute(long_blk, ('eig', 'chan'), long_pairs)]
    unnamed x12, local copies, waits for them, and re-layouts: 0.04 us -> 1.38 us
    ppermute x2 -> x6, waiting for transfers between devices: 8.67 us -> 9.36 us  [the longest x1 6.31 us: per_device(): amp_mine = (keep + lax.ppermute(give, 'basis', swap)).astype(jnp.bfloat16)]
  transfers between devices with their start and end apart: 10 -> 14, of which waited for: 7 -> 6; matrix products, arithmetic and copies ran while one was open for 8% -> 29% of each run, Pallas kernels for 0% -> 0%
where the time goes in v8:
time: 93.3 us; the launch traced here: 92.9 us
  local copies, waits for them, and re-layouts  30.2 us (32%)
  matrix products  22.1 us (24%)
  waiting for transfers between devices  15.5 us (17%)
  starting transfers between devices  14.1 us (15%)
  between operations  9.11 us (10%)
  other arithmetic  1.84 us (2%)
    dot_general x1, matrix products, per_device(): jnp.einsum('ekc,kd->ecd', scaled, right_panel, preferred_element_type=jnp...  16.2 us
    dynamic_update_slice x4, local copies, waits for them, and re-layouts, per_device(): lax.dynamic_update_slice(left_panel, long_blk, (origin * k_here, own_col))  10.1 us
    dynamic_update_slice x3, local copies, waits for them, and re-layouts, per_device(): lax.dynamic_update_slice(left_panel, short_blk, (origin * k_here, own_col))  8.29 us
    ppermute x1, waiting for transfers between devices, per_device(): amp_mine = (keep + lax.ppermute(give, 'basis', swap)).astype(jnp.bfloat16)  6.31 us
    ppermute x4, starting transfers between devices, per_device(): long_blk = lax.ppermute(long_blk, ('eig', 'chan'), long_pairs)  6.26 us
    dot_general x2, matrix products, per_device(): parts.append(jnp.dot(eigvecs, masked, preferred_element_type=jnp.float32))  5.99 us
    ppermute x4, waiting for transfers between devices, per_device(): long_blk = lax.ppermute(long_blk, ('eig', 'chan'), long_pairs)  4.28 us
    ppermute x4, waiting for transfers between devices, per_device(): got = lax.ppermute(sent, 'basis', swap)  3.05 us
  transfers between devices with their start and end apart: 14, of which 6 were waited for; matrix products, arithmetic and copies ran while one was open for 29% of the time, Pallas kernels for 0%

profile of v8, /device:TPU:0, one launch (start us, length us, event | category | flops | bytes accessed | tf_op | source)
XLA Modules:
  0.0 92.9 jit_solution(18301352296621384735)
XLA Ops:
  0.0 0.8 copy.13
  0.9 0.7 fusion.20
  1.8 4.2 %fusion.3 = f32[1024,64]{0,1:T(8,128)S(1)} fusion(bf16[64,2560]{1,0:T(8,128)(2,1)S(1)} %copy-done, bf16[2560,2048]{1,0:T(8,128)(2,1)} %param.9, s32[1024]{0:T(1024)S(1)} %get-tuple-element.8, s32[2560]{0:T(1024)S(1)} %convert_reduce_fusion), kind=kOutput, calls=%fused_computation.7 | convolution fusion | flops 340787200 | bytes 5847040 | tf_op jit(solution)/shard_map/dot_general | solution.py:73
  6.0 1.3 %copy-done.4 = bf16[2560,2048]{1,0:T(8,128)(2,1)S(1)} copy-done((bf16[2560,2048]{1,0:T(8,128)(2,1)S(1)}, bf16[2560,2048]{1,0:T(8,128)(2,1)}, u32[]{:S(2)}) %copy-start.4) | copy-done | bytes 10485784
  7.3 1.8 %fusion.2 = f32[1024,64]{0,1:T(8,128)S(1)} fusion(bf16[64,2560]{1,0:T(8,128)(2,1)S(1)} %copy-done, bf16[2560,2048]{1,0:T(8,128)(2,1)S(1)} %copy-done.4, s32[1024]{0:T(1024)S(1)} %get-tuple-element.7, s32[2560]{0:T(1024)S(1)} %convert_reduce_fusion), kind=kOutput, calls=%fused_computation.6 | convolution fusion | flops 340787200 | bytes 5849088 | tf_op jit(solution)/shard_map/dot_general | solution.py:73
  9.2 3.0 %collective-permute-start = (f32[64,1024]{1,0:T(8,128)S(1)}, f32[64,1024]{1,0:T(8,128)S(1)}, u32[]{:S(2)}, u32[]{:S(2)}) collective-permute-start(f32[64,1024]{1,0:T(8,128)S(1)} %select_bitcast_fusion), channel_id=1, source_target_pairs={{0,16},{16,0},{1,17},{17,1},{2,18},{18,2},{3,19},{19,3},{4,20},{20... | collective-permute-start | bytes 786440 | tf_op jit(solution)/shard_map/ppermute | solution.py:79
  12.2 6.3 %collective-permute-done = f32[64,1024]{1,0:T(8,128)S(1)} collective-permute-done((f32[64,1024]{1,0:T(8,128)S(1)}, f32[64,1024]{1,0:T(8,128)S(1)}, u32[]{:S(2)}, u32[]{:S(2)}) %collective-permute-start) | collective-permute-done | bytes 262176 | tf_op jit(solution)/shard_map/ppermute | solution.py:79
  18.8 0.7 fusion.18
  19.5 1.8 %collective-permute-start.2 = (bf16[64,1024]{1,0:T(8,128)(2,1)}, bf16[64,1024]{1,0:T(8,128)(2,1)S(1)}, u32[]{:S(2)}, u32[]{:S(2)}) collective-permute-start(bf16[64,1024]{1,0:T(8,128)(2,1)} %get-tuple-element.6), channel_id=1, source_target_pairs={{4,8},{8,12},{12,14},{14,10},{10,6},{6,2},{2,0},{0,4},{5,1},{9,5},... | collective-permute-start | bytes 393224 | tf_op jit(solution)/shard_map/ppermute | solution.py:89
  21.5 4.1 %collective-permute-done.2 = bf16[64,1024]{1,0:T(8,128)(2,1)S(1)} collective-permute-done((bf16[64,1024]{1,0:T(8,128)(2,1)}, bf16[64,1024]{1,0:T(8,128)(2,1)S(1)}, u32[]{:S(2)}, u32[]{:S(2)}) %collective-permute-start.2) | collective-permute-done | bytes 131104 | tf_op jit(solution)/shard_map/ppermute | solution.py:89
  25.6 0.9 collective-permute-start.5
  26.5 1.1 %collective-permute-done.3 = bf16[64,1024]{1,0:T(8,128)(2,1)S(1)} collective-permute-done((bf16[64,1024]{1,0:T(8,128)(2,1)}, bf16[64,1024]{1,0:T(8,128)(2,1)S(1)}, u32[]{:S(2)}, u32[]{:S(2)}) %collective-permute-start.3) | collective-permute-done | bytes 131104 | tf_op jit(solution)/shard_map/ppermute | solution.py:94
  27.6 1.5 %collective-permute-start.1 = (bf16[64,1024]{1,0:T(8,128)(2,1)}, bf16[64,1024]{1,0:T(8,128)(2,1)}, u32[]{:S(2)}, u32[]{:S(2)}) collective-permute-start(bf16[64,1024]{1,0:T(8,128)(2,1)} %get-tuple-element.6), channel_id=1, source_target_pairs={{0,16},{16,0},{1,17},{17,1},{2,18},{18,2},{3,19},{19,3},{4,20},{20... | collective-permute-start | bytes 393224 | tf_op jit(solution)/shard_map/ppermute | solution.py:83
  29.1 0.7 pad_maximum_fusion
  30.6 1.8 %collective-permute-start.8 = (bf16[64,1024]{1,0:T(8,128)(2,1)S(1)}, bf16[64,1024]{1,0:T(8,128)(2,1)S(1)}, u32[]{:S(2)}, u32[]{:S(2)}) collective-permute-start(bf16[64,1024]{1,0:T(8,128)(2,1)S(1)} %collective-permute-done.5), channel_id=1, source_target_pairs={{4,8},{8,12},{12,14},{14,10},{10,6},{6,2},{2,0},{0,4},{5,1},{9,5},... | collective-permute-start | bytes 393224 | tf_op jit(solution)/shard_map/ppermute | solution.py:89
  32.4 0.7 collective-permute-done.6
  33.5 0.6 dynamic_slice.27
  38.5 0.7 fusion.21
  43.6 3.0 %dynamic_update_slice.49 = bf16[512,2048]{1,0:T(8,128)(2,1)S(1)} dynamic-update-slice(bf16[512,2048]{1,0:T(8,128)(2,1)S(1)} %get-tuple-element.5, bf16[64,1024]{1,0:T(8,128)(2,1)} %collective-permute-done.1, s32[]{:T(128)S(6)} %select_n.162, s32[]{:T(128)S(6)} %select_n.164) | dynamic-update-slice | bytes 262148 | tf_op jit(solution)/shard_map/dynamic_update_slice | solution.py:84
  46.5 2.8 %dynamic_update_slice.50 = bf16[512,2048]{1,0:T(8,128)(2,1)S(1)} dynamic-update-slice(bf16[512,2048]{1,0:T(8,128)(2,1)S(1)} %dynamic_update_slice.49, bf16[64,1024]{1,0:T(8,128)(2,1)S(1)} %collective-permute-done.2, s32[]{:T(128)S(6)} %select_n.169, s32[]{:T(128)S(6)} %select_n.163) | dynamic-update-slice | bytes 262148 | tf_op jit(solution)/shard_map/dynamic_update_slice | solution.py:91
  49.3 2.8 %dynamic_update_slice.51 = bf16[512,2048]{1,0:T(8,128)(2,1)S(1)} dynamic-update-slice(bf16[512,2048]{1,0:T(8,128)(2,1)S(1)} %dynamic_update_slice.50, bf16[64,1024]{1,0:T(8,128)(2,1)S(1)} %collective-permute-done.3, s32[]{:T(128)S(6)} %select_n.172, s32[]{:T(128)S(6)} %select_n.163) | dynamic-update-slice | bytes 262148 | tf_op jit(solution)/shard_map/dynamic_update_slice | solution.py:96
  52.6 1.7 %collective-permute-start.10 = (bf16[128,1024]{1,0:T(8,128)(2,1)S(1)}, bf16[128,1024]{1,0:T(8,128)(2,1)S(1)}, u32[]{:S(2)}, u32[]{:S(2)}) collective-permute-start(bf16[128,1024]{1,0:T(8,128)(2,1)S(1)} %pad_maximum_fusion.2), channel_id=1, source_target_pairs={{0,16},{16,0},{1,17},{17,1},{2,18},{18,2},{3,19},{19,3},{4,20},{20... | collective-permute-start | bytes 786440 | tf_op jit(solution)/shard_map/ppermute | solution.py:99
  54.3 1.7 %collective-permute-start.11 = (bf16[64,1024]{1,0:T(8,128)(2,1)S(1)}, bf16[64,1024]{1,0:T(8,128)(2,1)S(1)}, u32[]{:S(2)}, u32[]{:S(2)}) collective-permute-start(bf16[64,1024]{1,0:T(8,128)(2,1)S(1)} %collective-permute-done.8), channel_id=1, source_target_pairs={{4,8},{8,12},{12,14},{14,10},{10,6},{6,2},{2,0},{0,4},{5,1},{9,5},... | collective-permute-start | bytes 393224 | tf_op jit(solution)/shard_map/ppermute | solution.py:89
  56.1 2.8 %dynamic_update_slice.54 = bf16[512,2048]{1,0:T(8,128)(2,1)S(1)} dynamic-update-slice(bf16[512,2048]{1,0:T(8,128)(2,1)S(1)} %slice_dynamic-update-slice_fusion.4, bf16[64,1024]{1,0:T(8,128)(2,1)S(1)} %collective-permute-done.5, s32[]{:T(128)S(6)} %select_n.175, s32[]{:T(128)S(6)} %select_n.163) | dynamic-update-slice | bytes 262148 | tf_op jit(solution)/shard_map/dynamic_update_slice | solution.py:91
  58.8 2.8 %dynamic_update_slice.55 = bf16[512,2048]{1,0:T(8,128)(2,1)S(1)} dynamic-update-slice(bf16[512,2048]{1,0:T(8,128)(2,1)S(1)} %dynamic_update_slice.54, bf16[64,1024]{1,0:T(8,128)(2,1)S(1)} %collective-permute-done.6, s32[]{:T(128)S(6)} %select_n.178, s32[]{:T(128)S(6)} %select_n.163) | dynamic-update-slice | bytes 262148 | tf_op jit(solution)/shard_map/dynamic_update_slice | solution.py:96
  61.7 2.8 %dynamic_update_slice.58 = bf16[512,2048]{1,0:T(8,128)(2,1)S(1)} dynamic-update-slice(bf16[512,2048]{1,0:T(8,128)(2,1)S(1)} %slice_dynamic-update-slice_fusion.2, bf16[64,1024]{1,0:T(8,128)(2,1)S(1)} %collective-permute-done.8, s32[]{:T(128)S(6)} %select_n.181, s32[]{:T(128)S(6)} %select_n.163) | dynamic-update-slice | bytes 262148 | tf_op jit(solution)/shard_map/dynamic_update_slice | solution.py:91
  64.4 2.8 %dynamic_update_slice.59 = bf16[512,2048]{1,0:T(8,128)(2,1)S(1)} dynamic-update-slice(bf16[512,2048]{1,0:T(8,128)(2,1)S(1)} %dynamic_update_slice.58, bf16[64,1024]{1,0:T(8,128)(2,1)S(1)} %collective-permute-done.9, s32[]{:T(128)S(6)} %select_n.184, s32[]{:T(128)S(6)} %select_n.163) | dynamic-update-slice | bytes 262148 | tf_op jit(solution)/shard_map/dynamic_update_slice | solution.py:96
  67.4 1.8 %dynamic_update_slice.62 = bf16[512,2048]{1,0:T(8,128)(2,1)S(1)} dynamic-update-slice(bf16[512,2048]{1,0:T(8,128)(2,1)S(1)} %slice_dynamic-update-slice_fusion, bf16[64,1024]{1,0:T(8,128)(2,1)S(1)} %collective-permute-done.11, s32[]{:T(128)S(6)} %select_n.187, s32[]{:T(128)S(6)} %select_n.163) | dynamic-update-slice | bytes 262148 | tf_op jit(solution)/shard_map/dynamic_update_slice | solution.py:91
  69.2 3.0 %collective-permute-done.12 = bf16[64,1024]{1,0:T(8,128)(2,1)S(1)} collective-permute-done((bf16[64,1024]{1,0:T(8,128)(2,1)S(1)}, bf16[64,1024]{1,0:T(8,128)(2,1)S(1)}, u32[]{:S(2)}, u32[]{:S(2)}) %collective-permute-start.12) | collective-permute-done | bytes 131104 | tf_op jit(solution)/shard_map/ppermute | solution.py:99
  72.3 1.3 %dynamic_update_slice.63 = bf16[512,2048]{1,0:T(8,128)(2,1)S(1)} dynamic-update-slice(bf16[512,2048]{1,0:T(8,128)(2,1)S(1)} %dynamic_update_slice.62, bf16[64,1024]{1,0:T(8,128)(2,1)S(1)} %collective-permute-done.12, s32[]{:T(128)S(6)} %select_n.187, s32[]{:T(128)S(6)} %select_n.164) | dynamic-update-slice | bytes 262148 | tf_op jit(solution)/shard_map/dynamic_update_slice | solution.py:102
  73.8 3.0 %copy.14 = f32[512,2048]{0,1:T(8,128)} copy(bf16[512,2048]{1,0:T(8,128)(2,1)S(1)} %dynamic_update_slice.63) | data formatting | bytes 6291456 | tf_op jit(solution)/shard_map/convert_element_type | solution.py:139
  76.8 16.2 %convolution_multiply_fusion = f32[8,2048,512]{2,1,0:T(8,128)} fusion(f32[512,2048]{0,1:T(8,128)} %copy.14, f32[8,512]{1,0:T(8,128)S(1)} %subtract_divide_fusion, bf16[512,512]{1,0:T(8,128)(2,1)S(1)} %constant_dynamic-slice_fusion, bf16[512,512]{1,0:T(8,128)(2,1)S(1)} %collective-permute-done.13, pred[]{:T(512)S(6)} %eq.47), kind=kOutput, calls=%fused_computation.1 | convolution fusion | flops 8615362560 | bytes 38813696 | tf_op jit(solution)/shard_map/ekc,kd->ecd/dot_general | solution.py:140
  (43 shorter events, 2.7 us)
Async XLA Ops:
  0.0 1.8 %copy-start = (bf16[64,2560]{1,0:T(8,128)(2,1)S(1)}, bf16[64,2560]{1,0:T(8,128)(2,1)}, u32[]{:S(2)}) copy-start(bf16[64,2560]{1,0:T(8,128)(2,1)} %param.8) | copy-start | bytes 983044
  1.8 5.5 %copy-start.4 = (bf16[2560,2048]{1,0:T(8,128)(2,1)S(1)}, bf16[2560,2048]{1,0:T(8,128)(2,1)}, u32[]{:S(2)}) copy-start(bf16[2560,2048]{1,0:T(8,128)(2,1)} %param.9) | copy-start | bytes 31457284
  9.1 24.3 %copy-start.5 = (s32[8]{0:T(128)S(1)}, s32[8]{0:T(128)}, u32[]{:S(2)}) copy-start(s32[8]{0:T(128)} %constant.116.clone) | copy-start | bytes 100
  9.2 29.3 %copy-start.1 = (s32[8]{0:T(128)S(1)}, s32[8]{0:T(128)}, u32[]{:S(2)}) copy-start(s32[8]{0:T(128)} %constant.115.clone) | copy-start | bytes 100
  9.2 9.3 %collective-permute-start = (f32[64,1024]{1,0:T(8,128)S(1)}, f32[64,1024]{1,0:T(8,128)S(1)}, u32[]{:S(2)}, u32[]{:S(2)}) collective-permute-start(f32[64,1024]{1,0:T(8,128)S(1)} %select_bitcast_fusion), channel_id=1, source_target_pairs={{0,16},{16,0},{1,17},{17,1},{2,18},{18,2},{3,19},{19,3},{4,20},{20... | collective-permute-start | bytes 786440 | tf_op jit(solution)/shard_map/ppermute | solution.py:79
  19.5 6.1 %collective-permute-start.2 = (bf16[64,1024]{1,0:T(8,128)(2,1)}, bf16[64,1024]{1,0:T(8,128)(2,1)S(1)}, u32[]{:S(2)}, u32[]{:S(2)}) collective-permute-start(bf16[64,1024]{1,0:T(8,128)(2,1)} %get-tuple-element.6), channel_id=1, source_target_pairs={{4,8},{8,12},{12,14},{14,10},{10,6},{6,2},{2,0},{0,4},{5,1},{9,5},... | collective-permute-start | bytes 393224 | tf_op jit(solution)/shard_map/ppermute | solution.py:89
  21.3 6.3 %collective-permute-start.3 = (bf16[64,1024]{1,0:T(8,128)(2,1)}, bf16[64,1024]{1,0:T(8,128)(2,1)S(1)}, u32[]{:S(2)}, u32[]{:S(2)}) collective-permute-start(bf16[64,1024]{1,0:T(8,128)(2,1)} %get-tuple-element.6), channel_id=1, source_target_pairs={{4,0},{8,4},{12,8},{14,12},{10,14},{6,10},{2,6},{0,2},{5,9},{9,13}... | collective-permute-start | bytes 393224 | tf_op jit(solution)/shard_map/ppermute | solution.py:94
  25.6 5.0 %collective-permute-start.5 = (bf16[64,1024]{1,0:T(8,128)(2,1)S(1)}, bf16[64,1024]{1,0:T(8,128)(2,1)S(1)}, u32[]{:S(2)}, u32[]{:S(2)}) collective-permute-start(bf16[64,1024]{1,0:T(8,128)(2,1)S(1)} %collective-permute-done.2), channel_id=1, source_target_pairs={{4,8},{8,12},{12,14},{14,10},{10,6},{6,2},{2,0},{0,4},{5,1},{9,5},... | collective-permute-start | bytes 393224 | tf_op jit(solution)/shard_map/ppermute | solution.py:89
  27.6 5.5 %collective-permute-start.6 = (bf16[64,1024]{1,0:T(8,128)(2,1)S(1)}, bf16[64,1024]{1,0:T(8,128)(2,1)S(1)}, u32[]{:S(2)}, u32[]{:S(2)}) collective-permute-start(bf16[64,1024]{1,0:T(8,128)(2,1)S(1)} %collective-permute-done.3), channel_id=1, source_target_pairs={{4,0},{8,4},{12,8},{14,12},{10,14},{6,10},{2,6},{0,2},{5,9},{9,13}... | collective-permute-start | bytes 393224 | tf_op jit(solution)/shard_map/ppermute | solution.py:94
  27.6 15.9 %collective-permute-start.1 = (bf16[64,1024]{1,0:T(8,128)(2,1)}, bf16[64,1024]{1,0:T(8,128)(2,1)}, u32[]{:S(2)}, u32[]{:S(2)}) collective-permute-start(bf16[64,1024]{1,0:T(8,128)(2,1)} %get-tuple-element.6), channel_id=1, source_target_pairs={{0,16},{16,0},{1,17},{17,1},{2,18},{18,2},{3,19},{19,3},{4,20},{20... | collective-permute-start | bytes 393224 | tf_op jit(solution)/shard_map/ppermute | solution.py:83
  29.9 26.1 %collective-permute-start.4 = (bf16[128,1024]{1,0:T(8,128)(2,1)}, bf16[128,1024]{1,0:T(8,128)(2,1)S(1)}, u32[]{:S(2)}, u32[]{:S(2)}) collective-permute-start(bf16[128,1024]{1,0:T(8,128)(2,1)} %pad_maximum_fusion), channel_id=1, source_target_pairs={{0,16},{16,0},{1,17},{17,1},{2,18},{18,2},{3,19},{19,3},{4,20},{20... | collective-permute-start | bytes 786440 | tf_op jit(solution)/shard_map/ppermute | solution.py:99
  30.6 22.0 %collective-permute-start.8 = (bf16[64,1024]{1,0:T(8,128)(2,1)S(1)}, bf16[64,1024]{1,0:T(8,128)(2,1)S(1)}, u32[]{:S(2)}, u32[]{:S(2)}) collective-permute-start(bf16[64,1024]{1,0:T(8,128)(2,1)S(1)} %collective-permute-done.5), channel_id=1, source_target_pairs={{4,8},{8,12},{12,14},{14,10},{10,6},{6,2},{2,0},{0,4},{5,1},{9,5},... | collective-permute-start | bytes 393224 | tf_op jit(solution)/shard_map/ppermute | solution.py:89
  33.1 19.4 %collective-permute-start.9 = (bf16[64,1024]{1,0:T(8,128)(2,1)S(1)}, bf16[64,1024]{1,0:T(8,128)(2,1)S(1)}, u32[]{:S(2)}, u32[]{:S(2)}) collective-permute-start(bf16[64,1024]{1,0:T(8,128)(2,1)S(1)} %collective-permute-done.6), channel_id=1, source_target_pairs={{4,0},{8,4},{12,8},{14,12},{10,14},{6,10},{2,6},{0,2},{5,9},{9,13}... | collective-permute-start | bytes 393224 | tf_op jit(solution)/shard_map/ppermute | solution.py:94
  52.1 9.5 %collective-permute-start.7 = (bf16[128,1024]{1,0:T(8,128)(2,1)S(1)}, bf16[128,1024]{1,0:T(8,128)(2,1)S(1)}, u32[]{:S(2)}, u32[]{:S(2)}) collective-permute-start(bf16[128,1024]{1,0:T(8,128)(2,1)S(1)} %pad_maximum_fusion.1), channel_id=1, source_target_pairs={{0,16},{16,0},{1,17},{17,1},{2,18},{18,2},{3,19},{19,3},{4,20},{20... | collective-permute-start | bytes 786440 | tf_op jit(solution)/shard_map/ppermute | solution.py:99
  52.6 21.1 %copy-start.2 = (f32[512]{0:T(512)S(1)}, f32[512]{0:T(512)}, u32[]{:S(2)}) copy-start(f32[512]{0:T(512)} %param.12) | copy-start | bytes 6148
  52.6 21.1 %copy-start.3 = (f32[8]{0:T(128)S(1)}, f32[8]{0:T(128)}, u32[]{:S(2)}) copy-start(f32[8]{0:T(128)} %param.13) | copy-start | bytes 100
  52.6 14.7 %collective-permute-start.10 = (bf16[128,1024]{1,0:T(8,128)(2,1)S(1)}, bf16[128,1024]{1,0:T(8,128)(2,1)S(1)}, u32[]{:S(2)}, u32[]{:S(2)}) collective-permute-start(bf16[128,1024]{1,0:T(8,128)(2,1)S(1)} %pad_maximum_fusion.2), channel_id=1, source_target_pairs={{0,16},{16,0},{1,17},{17,1},{2,18},{18,2},{3,19},{19,3},{4,20},{20... | collective-permute-start | bytes 786440 | tf_op jit(solution)/shard_map/ppermute | solution.py:99
  54.3 12.9 %collective-permute-start.11 = (bf16[64,1024]{1,0:T(8,128)(2,1)S(1)}, bf16[64,1024]{1,0:T(8,128)(2,1)S(1)}, u32[]{:S(2)}, u32[]{:S(2)}) collective-permute-start(bf16[64,1024]{1,0:T(8,128)(2,1)S(1)} %collective-permute-done.8), channel_id=1, source_target_pairs={{4,8},{8,12},{12,14},{14,10},{10,6},{6,2},{2,0},{0,4},{5,1},{9,5},... | collective-permute-start | bytes 393224 | tf_op jit(solution)/shard_map/ppermute | solution.py:89
  67.2 5.0 %collective-permute-start.12 = (bf16[64,1024]{1,0:T(8,128)(2,1)S(1)}, bf16[64,1024]{1,0:T(8,128)(2,1)S(1)}, u32[]{:S(2)}, u32[]{:S(2)}) collective-permute-start(bf16[64,1024]{1,0:T(8,128)(2,1)S(1)} %collective-permute-done.11), channel_id=1, source_target_pairs={{0,16},{16,0},{1,17},{17,1},{2,18},{18,2},{3,19},{19,3},{4,20},{20... | collective-permute-start | bytes 393224 | tf_op jit(solution)/shard_map/ppermute | solution.py:99
  73.6 3.2 %collective-permute-start.13 = (bf16[512,512]{1,0:T(8,128)(2,1)S(1)}, bf16[512,512]{1,0:T(8,128)(2,1)S(1)}, u32[]{:S(2)}, u32[]{:S(2)}) collective-permute-start(bf16[512,512]{1,0:T(8,128)(2,1)S(1)} %constant_dynamic-slice_fusion), channel_id=1, source_target_pairs={{0,1},{1,0},{2,3},{3,2},{4,5},{5,4},{6,7},{7,6},{8,9},{9,8},{10,11... | collective-permute-start | bytes 1572872 | tf_op jit(solution)/shard_map/ppermute | solution.py:132

commit v9 on v8

--- a/solution.py
+++ b/solution.py
@@ -77,29 +77,33 @@
             keep = jnp.where(mine == 0, parts[0], parts[1])
             give = jnp.where(mine == 0, parts[1], parts[0])
             amp_mine = (keep + lax.ppermute(give, "basis", swap)).astype(jnp.bfloat16)
-            own_col = mine * step
-            other_col = (1 - mine) * step
-            left_panel = lax.dynamic_update_slice(left_panel, amp_mine, (eig_index * k_here, own_col))
+            own_half = jnp.zeros((k_here * n_ring, step), jnp.bfloat16)
+            other_half = jnp.zeros((k_here * n_ring, step), jnp.bfloat16)
+            own_half = lax.dynamic_update_slice_in_dim(own_half, amp_mine, eig_index * k_here, 0)
             got = lax.ppermute(amp_mine, "basis", swap)
-            left_panel = lax.dynamic_update_slice(left_panel, got, (eig_index * k_here, other_col))
+            other_half = lax.dynamic_update_slice_in_dim(other_half, got, eig_index * k_here, 0)
             long_blk, short_blk = amp_mine, amp_mine
             for s in range(max(n_fwd, n_bwd)):
                 new_blocks = []
                 if s < n_fwd:
                     long_blk = lax.ppermute(long_blk, ("eig", "chan"), long_pairs)
                     origin = cycle_arr[(pos - sign * (s + 1)) % n_ring]
-                    left_panel = lax.dynamic_update_slice(left_panel, long_blk, (origin * k_here, own_col))
+                    own_half = lax.dynamic_update_slice_in_dim(own_half, long_blk, origin * k_here, 0)
                     new_blocks.append((long_blk, origin))
                 if s < n_bwd:
                     short_blk = lax.ppermute(short_blk, ("eig", "chan"), short_pairs)
                     origin = cycle_arr[(pos + sign * (s + 1)) % n_ring]
-                    left_panel = lax.dynamic_update_slice(left_panel, short_blk, (origin * k_here, own_col))
+                    own_half = lax.dynamic_update_slice_in_dim(own_half, short_blk, origin * k_here, 0)
                     new_blocks.append((short_blk, origin))
-                sent = jnp.concatenate([b for b, _ in new_blocks], axis=0)
+                sent = jnp.concatenate([blk for blk, _ in new_blocks], axis=0)
                 got = lax.ppermute(sent, "basis", swap)
                 for i, (_, origin) in enumerate(new_blocks):
                     piece_i = got[i * k_here:(i + 1) * k_here]
-                    left_panel = lax.dynamic_update_slice(left_panel, piece_i, (origin * k_here, other_col))
+                    other_half = lax.dynamic_update_slice_in_dim(other_half, piece_i, origin * k_here, 0)
+            first = mine == 0
+            left_panel = jnp.concatenate(
+                [jnp.where(first, own_half, other_half), jnp.where(first, other_half, own_half)], axis=1
+            )
         else:
             amp_parts = []
             for part in parts:

time: 93.3 us -> 84.8 us (0.909)
  local copies, waits for them, and re-layouts: 30.2 us -> 9.97 us
  waiting for transfers between devices: 15.5 us -> 23.5 us
  starting transfers between devices: 14.1 us -> 15.9 us
  other arithmetic: 1.84 us -> 3.51 us
    dynamic_update_slice x15, local copies, waits for them, and re-layouts: 22.8 us -> 0.23 us  [the longest x7 0.11 us: per_device(): lax.dynamic_update_slice_in_dim(other_half, piece_i, origin * k_here, 0)]
    ppermute x4, starting transfers between devices: 6.26 us -> 0.53 us  [per_device(): long_blk = lax.ppermute(long_blk, ('eig', 'chan'), long_pairs)]
    ppermute x3, starting transfers between devices: 0.52 us -> 6.25 us  [per_device(): short_blk = lax.ppermute(short_blk, ('eig', 'chan'), short_pairs)]
    ppermute x4, waiting for transfers between devices: 4.28 us -> 8.59 us  [per_device(): long_blk = lax.ppermute(long_blk, ('eig', 'chan'), long_pairs)]
    convert_element_type x0 -> x1, other arithmetic: none -> 2.55 us  [per_device(): left_panel[None].astype(jnp.float32)]
    convert_element_type x1, local copies, waits for them, and re-layouts: 2.98 us -> 5.37 us  [per_device(): left_panel[None].astype(jnp.float32)]
    ppermute x1, waiting for transfers between devices: 0.01 us -> 2.18 us  [per_device(): got = lax.ppermute(amp_mine, 'basis', swap)]
    ppermute x3, waiting for transfers between devices: 1.86 us -> 3.47 us  [per_device(): short_blk = lax.ppermute(short_blk, ('eig', 'chan'), short_pairs)]
  transfers between devices with their start and end apart: 14 -> 14, of which waited for: 6 -> 8; matrix products, arithmetic and copies ran while one was open for 29% -> 11% of each run, Pallas kernels for 0% -> 0%
where the time goes in v9:
time: 84.8 us; the launch traced here: 84.5 us
  waiting for transfers between devices  23.5 us (28%)
  matrix products  22.2 us (26%)
  starting transfers between devices  15.9 us (19%)
  local copies, waits for them, and re-layouts  9.97 us (12%)
  between operations  9.39 us (11%)
  other arithmetic  3.51 us (4%)
    dot_general x1, matrix products, per_device(): jnp.einsum('ekc,kd->ecd', scaled, right_panel, preferred_element_type=jnp...  16.2 us
    ppermute x4, waiting for transfers between devices, per_device(): long_blk = lax.ppermute(long_blk, ('eig', 'chan'), long_pairs)  8.59 us
    ppermute x1, waiting for transfers between devices, per_device(): amp_mine = (keep + lax.ppermute(give, 'basis', swap)).astype(jnp.bfloat16)  6.31 us
    ppermute x3, starting transfers between devices, per_device(): short_blk = lax.ppermute(short_blk, ('eig', 'chan'), short_pairs)  6.25 us
    dot_general x2, matrix products, per_device(): parts.append(jnp.dot(eigvecs, masked, preferred_element_type=jnp.float32))  6 us
    convert_element_type x1, local copies, waits for them, and re-layouts, per_device(): left_panel[None].astype(jnp.float32)  5.37 us
    ppermute x4, starting transfers between devices, per_device(): got = lax.ppermute(sent, 'basis', swap)  4.26 us
    ppermute x3, waiting for transfers between devices, per_device(): short_blk = lax.ppermute(short_blk, ('eig', 'chan'), short_pairs)  3.47 us
  transfers between devices with their start and end apart: 14, of which 8 were waited for; matrix products, arithmetic and copies ran while one was open for 11% of the time, Pallas kernels for 0%

profile of v9, /device:TPU:0, one launch (start us, length us, event | category | flops | bytes accessed | tf_op | source)
XLA Modules:
  0.0 84.5 jit_solution(9170397434683355656)
XLA Ops:
  0.0 0.8 copy.13
  0.8 0.1 reduce
  0.9 0.7 fusion.21
  1.8 4.2 %fusion.3 = f32[1024,64]{0,1:T(8,128)S(1)} fusion(bf16[64,2560]{1,0:T(8,128)(2,1)S(1)} %copy-done, bf16[2560,2048]{1,0:T(8,128)(2,1)} %param.9, s32[1024]{0:T(1024)S(1)} %get-tuple-element.10, s32[2560]{0:T(1024)S(1)} %convert_reduce_fusion), kind=kOutput, calls=%fused_computation.7 | convolution fusion | flops 340787200 | bytes 5847040 | tf_op jit(solution)/shard_map/dot_general | solution.py:73
  6.0 1.4 %copy-done.4 = bf16[2560,2048]{1,0:T(8,128)(2,1)S(1)} copy-done((bf16[2560,2048]{1,0:T(8,128)(2,1)S(1)}, bf16[2560,2048]{1,0:T(8,128)(2,1)}, u32[]{:S(2)}) %copy-start.4) | copy-done | bytes 10485784
  7.3 1.8 %fusion.2 = f32[1024,64]{0,1:T(8,128)S(1)} fusion(bf16[64,2560]{1,0:T(8,128)(2,1)S(1)} %copy-done, bf16[2560,2048]{1,0:T(8,128)(2,1)S(1)} %copy-done.4, s32[1024]{0:T(1024)S(1)} %get-tuple-element.9, s32[2560]{0:T(1024)S(1)} %convert_reduce_fusion), kind=kOutput, calls=%fused_computation.6 | convolution fusion | flops 340787200 | bytes 5849088 | tf_op jit(solution)/shard_map/dot_general | solution.py:73
  9.2 3.0 %collective-permute-start = (f32[64,1024]{1,0:T(8,128)S(1)}, f32[64,1024]{1,0:T(8,128)S(1)}, u32[]{:S(2)}, u32[]{:S(2)}) collective-permute-start(f32[64,1024]{1,0:T(8,128)S(1)} %select_bitcast_fusion), channel_id=1, source_target_pairs={{0,16},{16,0},{1,17},{17,1},{2,18},{18,2},{3,19},{19,3},{4,20},{20... | collective-permute-start | bytes 786440 | tf_op jit(solution)/shard_map/ppermute | solution.py:79
  12.2 6.3 %collective-permute-done = f32[64,1024]{1,0:T(8,128)S(1)} collective-permute-done((f32[64,1024]{1,0:T(8,128)S(1)}, f32[64,1024]{1,0:T(8,128)S(1)}, u32[]{:S(2)}, u32[]{:S(2)}) %collective-permute-start) | collective-permute-done | bytes 262176 | tf_op jit(solution)/shard_map/ppermute | solution.py:79
  18.7 1.8 %collective-permute-start.2 = (bf16[64,1024]{1,0:T(8,128)(2,1)S(1)}, bf16[64,1024]{1,0:T(8,128)(2,1)S(1)}, u32[]{:S(2)}, u32[]{:S(2)}) collective-permute-start(bf16[64,1024]{1,0:T(8,128)(2,1)S(1)} %get-tuple-element.6), channel_id=1, source_target_pairs={{4,0},{8,4},{12,8},{14,12},{10,14},{6,10},{2,6},{0,2},{5,9},{9,13}... | collective-permute-start | bytes 393224 | tf_op jit(solution)/shard_map/ppermute | solution.py:94
  20.5 0.3 collective-permute-start.1
  20.8 0.6 dynamic_slice.27
  26.1 0.7 fusion.22
  31.2 1.8 %collective-permute-start.8 = (bf16[64,1024]{1,0:T(8,128)(2,1)S(1)}, bf16[64,1024]{1,0:T(8,128)(2,1)S(1)}, u32[]{:S(2)}, u32[]{:S(2)}) collective-permute-start(bf16[64,1024]{1,0:T(8,128)(2,1)S(1)} %get-tuple-element.6), channel_id=1, source_target_pairs={{0,16},{16,0},{1,17},{17,1},{2,18},{18,2},{3,19},{19,3},{4,20},{20... | collective-permute-start | bytes 393224 | tf_op jit(solution)/shard_map/ppermute | solution.py:83
  33.0 0.4 collective-permute-start.9
  33.4 1.8 %collective-permute-start.4 = (bf16[64,1024]{1,0:T(8,128)(2,1)S(1)}, bf16[64,1024]{1,0:T(8,128)(2,1)S(1)}, u32[]{:S(2)}, u32[]{:S(2)}) collective-permute-start(bf16[64,1024]{1,0:T(8,128)(2,1)S(1)} %collective-permute-done.2), channel_id=1, source_target_pairs={{4,0},{8,4},{12,8},{14,12},{10,14},{6,10},{2,6},{0,2},{5,9},{9,13}... | collective-permute-start | bytes 393224 | tf_op jit(solution)/shard_map/ppermute | solution.py:94
  35.2 0.3 collective-permute-start.3
  35.5 2.2 %collective-permute-done.8 = bf16[64,1024]{1,0:T(8,128)(2,1)S(1)} collective-permute-done((bf16[64,1024]{1,0:T(8,128)(2,1)S(1)}, bf16[64,1024]{1,0:T(8,128)(2,1)S(1)}, u32[]{:S(2)}, u32[]{:S(2)}) %collective-permute-start.8) | collective-permute-done | bytes 131104 | tf_op jit(solution)/shard_map/ppermute | solution.py:83
  37.8 0.6 collective-permute-done.4
  38.4 1.8 %collective-permute-done.3 = bf16[64,1024]{1,0:T(8,128)(2,1)S(1)} collective-permute-done((bf16[64,1024]{1,0:T(8,128)(2,1)S(1)}, bf16[64,1024]{1,0:T(8,128)(2,1)S(1)}, u32[]{:S(2)}, u32[]{:S(2)}) %collective-permute-start.3) | collective-permute-done | bytes 131104 | tf_op jit(solution)/shard_map/ppermute | solution.py:89
  40.2 1.8 %collective-permute-start.10 = (bf16[128,1024]{1,0:T(8,128)(2,1)S(1)}, bf16[128,1024]{1,0:T(8,128)(2,1)S(1)}, u32[]{:S(2)}, u32[]{:S(2)}) collective-permute-start(bf16[128,1024]{1,0:T(8,128)(2,1)S(1)} %pad_maximum_fusion.2), channel_id=1, source_target_pairs={{0,16},{16,0},{1,17},{17,1},{2,18},{18,2},{3,19},{19,3},{4,20},{20... | collective-permute-start | bytes 786440 | tf_op jit(solution)/shard_map/ppermute | solution.py:99
  42.0 2.7 %collective-permute-start.6 = (bf16[64,1024]{1,0:T(8,128)(2,1)S(1)}, bf16[64,1024]{1,0:T(8,128)(2,1)S(1)}, u32[]{:S(2)}, u32[]{:S(2)}) collective-permute-start(bf16[64,1024]{1,0:T(8,128)(2,1)S(1)} %collective-permute-done.4), channel_id=1, source_target_pairs={{4,0},{8,4},{12,8},{14,12},{10,14},{6,10},{2,6},{0,2},{5,9},{9,13}... | collective-permute-start | bytes 393224 | tf_op jit(solution)/shard_map/ppermute | solution.py:94
  44.7 2.9 %collective-permute-done.6 = bf16[64,1024]{1,0:T(8,128)(2,1)S(1)} collective-permute-done((bf16[64,1024]{1,0:T(8,128)(2,1)S(1)}, bf16[64,1024]{1,0:T(8,128)(2,1)S(1)}, u32[]{:S(2)}, u32[]{:S(2)}) %collective-permute-start.6) | collective-permute-done | bytes 131104 | tf_op jit(solution)/shard_map/ppermute | solution.py:94
  47.6 2.0 %collective-permute-done.5 = bf16[64,1024]{1,0:T(8,128)(2,1)S(1)} collective-permute-done((bf16[64,1024]{1,0:T(8,128)(2,1)S(1)}, bf16[64,1024]{1,0:T(8,128)(2,1)S(1)}, u32[]{:S(2)}, u32[]{:S(2)}) %collective-permute-start.5) | collective-permute-done | bytes 131104 | tf_op jit(solution)/shard_map/ppermute | solution.py:89
  49.6 0.1 collective-permute-start.11
  50.0 4.8 %collective-permute-done.7 = bf16[64,1024]{1,0:T(8,128)(2,1)S(1)} collective-permute-done((bf16[64,1024]{1,0:T(8,128)(2,1)S(1)}, bf16[64,1024]{1,0:T(8,128)(2,1)S(1)}, u32[]{:S(2)}, u32[]{:S(2)}) %collective-permute-start.7) | collective-permute-done | bytes 131104 | tf_op jit(solution)/shard_map/ppermute | solution.py:89
  54.7 2.0 %collective-permute-start.12 = (bf16[64,1024]{1,0:T(8,128)(2,1)S(1)}, bf16[64,1024]{1,0:T(8,128)(2,1)S(1)}, u32[]{:S(2)}, u32[]{:S(2)}) collective-permute-start(bf16[64,1024]{1,0:T(8,128)(2,1)S(1)} %collective-permute-done.7), channel_id=1, source_target_pairs={{0,16},{16,0},{1,17},{17,1},{2,18},{18,2},{3,19},{19,3},{4,20},{20... | collective-permute-start | bytes 393224 | tf_op jit(solution)/shard_map/ppermute | solution.py:99
  56.8 2.9 %collective-permute-done.12 = bf16[64,1024]{1,0:T(8,128)(2,1)S(1)} collective-permute-done((bf16[64,1024]{1,0:T(8,128)(2,1)S(1)}, bf16[64,1024]{1,0:T(8,128)(2,1)S(1)}, u32[]{:S(2)}, u32[]{:S(2)}) %collective-permute-start.12) | collective-permute-done | bytes 131104 | tf_op jit(solution)/shard_map/ppermute | solution.py:99
  59.7 0.1 broadcast_select_fusion.1
  59.9 0.3 fusion.13
  60.4 2.6 %fusion.12 = f32[512,2048]{1,0:T(8,128)} fusion(bf16[512,1024]{1,0:T(8,128)(2,1)S(1)} %get-tuple-element.8, bf16[512,1024]{1,0:T(8,128)(2,1)S(1)} %get-tuple-element.7), kind=kLoop, calls=%fused_computation.19 | loop fusion | flops 4194304 | bytes 6291456 | tf_op jit(solution)/shard_map/convert_element_type | solution.py:143
  62.9 5.4 %copy.14 = f32[512,2048]{0,1:T(8,128)} copy(f32[512,2048]{1,0:T(8,128)} %fusion.12) | data formatting | bytes 8388608 | tf_op jit(solution)/shard_map/convert_element_type | solution.py:143
  68.3 16.2 %convolution_multiply_fusion = f32[8,2048,512]{2,1,0:T(8,128)} fusion(f32[512,2048]{0,1:T(8,128)} %copy.14, f32[8,512]{1,0:T(8,128)S(1)} %subtract_divide_fusion, bf16[512,512]{1,0:T(8,128)(2,1)S(1)} %fusion.13, bf16[512,512]{1,0:T(8,128)(2,1)S(1)} %collective-permute-done.13, pred[]{:T(512)S(6)} %eq.48), kind=kOutput, calls=%fused_computation.1 | convolution fusion | flops 8615362560 | bytes 38813696 | tf_op jit(solution)/shard_map/ekc,kd->ecd/dot_general | solution.py:144
  (46 shorter events, 1.0 us)
Async XLA Ops:
  0.0 1.8 %copy-start = (bf16[64,2560]{1,0:T(8,128)(2,1)S(1)}, bf16[64,2560]{1,0:T(8,128)(2,1)}, u32[]{:S(2)}) copy-start(bf16[64,2560]{1,0:T(8,128)(2,1)} %param.8) | copy-start | bytes 983044
  1.8 5.5 %copy-start.4 = (bf16[2560,2048]{1,0:T(8,128)(2,1)S(1)}, bf16[2560,2048]{1,0:T(8,128)(2,1)}, u32[]{:S(2)}) copy-start(bf16[2560,2048]{1,0:T(8,128)(2,1)} %param.9) | copy-start | bytes 31457284
  7.3 13.5 %copy-start.5 = (s32[8]{0:T(128)S(1)}, s32[8]{0:T(128)}, u32[]{:S(2)}) copy-start(s32[8]{0:T(128)} %constant.114.clone) | copy-start | bytes 100
  7.3 18.7 %copy-start.1 = (s32[8]{0:T(128)S(1)}, s32[8]{0:T(128)}, u32[]{:S(2)}) copy-start(s32[8]{0:T(128)} %constant.113.clone) | copy-start | bytes 100
  9.2 9.3 %collective-permute-start = (f32[64,1024]{1,0:T(8,128)S(1)}, f32[64,1024]{1,0:T(8,128)S(1)}, u32[]{:S(2)}, u32[]{:S(2)}) collective-permute-start(f32[64,1024]{1,0:T(8,128)S(1)} %select_bitcast_fusion), channel_id=1, source_target_pairs={{0,16},{16,0},{1,17},{17,1},{2,18},{18,2},{3,19},{19,3},{4,20},{20... | collective-permute-start | bytes 786440 | tf_op jit(solution)/shard_map/ppermute | solution.py:79
  18.7 14.3 %collective-permute-start.2 = (bf16[64,1024]{1,0:T(8,128)(2,1)S(1)}, bf16[64,1024]{1,0:T(8,128)(2,1)S(1)}, u32[]{:S(2)}, u32[]{:S(2)}) collective-permute-start(bf16[64,1024]{1,0:T(8,128)(2,1)S(1)} %get-tuple-element.6), channel_id=1, source_target_pairs={{4,0},{8,4},{12,8},{14,12},{10,14},{6,10},{2,6},{0,2},{5,9},{9,13}... | collective-permute-start | bytes 393224 | tf_op jit(solution)/shard_map/ppermute | solution.py:94
  20.5 12.5 %collective-permute-start.1 = (bf16[64,1024]{1,0:T(8,128)(2,1)S(1)}, bf16[64,1024]{1,0:T(8,128)(2,1)S(1)}, u32[]{:S(2)}, u32[]{:S(2)}) collective-permute-start(bf16[64,1024]{1,0:T(8,128)(2,1)S(1)} %get-tuple-element.6), channel_id=1, source_target_pairs={{4,8},{8,12},{12,14},{14,10},{10,6},{6,2},{2,0},{0,4},{5,1},{9,5},... | collective-permute-start | bytes 393224 | tf_op jit(solution)/shard_map/ppermute | solution.py:89
  31.2 6.4 %collective-permute-start.8 = (bf16[64,1024]{1,0:T(8,128)(2,1)S(1)}, bf16[64,1024]{1,0:T(8,128)(2,1)S(1)}, u32[]{:S(2)}, u32[]{:S(2)}) collective-permute-start(bf16[64,1024]{1,0:T(8,128)(2,1)S(1)} %get-tuple-element.6), channel_id=1, source_target_pairs={{0,16},{16,0},{1,17},{17,1},{2,18},{18,2},{3,19},{19,3},{4,20},{20... | collective-permute-start | bytes 393224 | tf_op jit(solution)/shard_map/ppermute | solution.py:83
  33.0 16.8 %collective-permute-start.9 = (bf16[128,1024]{1,0:T(8,128)(2,1)S(1)}, bf16[128,1024]{1,0:T(8,128)(2,1)S(1)}, u32[]{:S(2)}, u32[]{:S(2)}) collective-permute-start(bf16[128,1024]{1,0:T(8,128)(2,1)S(1)} %pad_maximum_fusion.1), channel_id=1, source_target_pairs={{0,16},{16,0},{1,17},{17,1},{2,18},{18,2},{3,19},{19,3},{4,20},{20... | collective-permute-start | bytes 786440 | tf_op jit(solution)/shard_map/ppermute | solution.py:99
  33.4 5.0 %collective-permute-start.4 = (bf16[64,1024]{1,0:T(8,128)(2,1)S(1)}, bf16[64,1024]{1,0:T(8,128)(2,1)S(1)}, u32[]{:S(2)}, u32[]{:S(2)}) collective-permute-start(bf16[64,1024]{1,0:T(8,128)(2,1)S(1)} %collective-permute-done.2), channel_id=1, source_target_pairs={{4,0},{8,4},{12,8},{14,12},{10,14},{6,10},{2,6},{0,2},{5,9},{9,13}... | collective-permute-start | bytes 393224 | tf_op jit(solution)/shard_map/ppermute | solution.py:94
  35.2 5.0 %collective-permute-start.3 = (bf16[64,1024]{1,0:T(8,128)(2,1)S(1)}, bf16[64,1024]{1,0:T(8,128)(2,1)S(1)}, u32[]{:S(2)}, u32[]{:S(2)}) collective-permute-start(bf16[64,1024]{1,0:T(8,128)(2,1)S(1)} %collective-permute-done.1), channel_id=1, source_target_pairs={{4,8},{8,12},{12,14},{14,10},{10,6},{6,2},{2,0},{0,4},{5,1},{9,5},... | collective-permute-start | bytes 393224 | tf_op jit(solution)/shard_map/ppermute | solution.py:89
  40.1 20.1 %copy-start.2 = (f32[512]{0:T(512)S(1)}, f32[512]{0:T(512)}, u32[]{:S(2)}) copy-start(f32[512]{0:T(512)} %param.12) | copy-start | bytes 6148
  40.2 20.1 %copy-start.3 = (f32[8]{0:T(128)S(1)}, f32[8]{0:T(128)}, u32[]{:S(2)}) copy-start(f32[8]{0:T(128)} %param.13) | copy-start | bytes 100
  40.2 9.7 %collective-permute-start.10 = (bf16[128,1024]{1,0:T(8,128)(2,1)S(1)}, bf16[128,1024]{1,0:T(8,128)(2,1)S(1)}, u32[]{:S(2)}, u32[]{:S(2)}) collective-permute-start(bf16[128,1024]{1,0:T(8,128)(2,1)S(1)} %pad_maximum_fusion.2), channel_id=1, source_target_pairs={{0,16},{16,0},{1,17},{17,1},{2,18},{18,2},{3,19},{19,3},{4,20},{20... | collective-permute-start | bytes 786440 | tf_op jit(solution)/shard_map/ppermute | solution.py:99
  42.0 5.6 %collective-permute-start.6 = (bf16[64,1024]{1,0:T(8,128)(2,1)S(1)}, bf16[64,1024]{1,0:T(8,128)(2,1)S(1)}, u32[]{:S(2)}, u32[]{:S(2)}) collective-permute-start(bf16[64,1024]{1,0:T(8,128)(2,1)S(1)} %collective-permute-done.4), channel_id=1, source_target_pairs={{4,0},{8,4},{12,8},{14,12},{10,14},{6,10},{2,6},{0,2},{5,9},{9,13}... | collective-permute-start | bytes 393224 | tf_op jit(solution)/shard_map/ppermute | solution.py:94
  44.7 5.0 %collective-permute-start.5 = (bf16[64,1024]{1,0:T(8,128)(2,1)S(1)}, bf16[64,1024]{1,0:T(8,128)(2,1)S(1)}, u32[]{:S(2)}, u32[]{:S(2)}) collective-permute-start(bf16[64,1024]{1,0:T(8,128)(2,1)S(1)} %collective-permute-done.3), channel_id=1, source_target_pairs={{4,8},{8,12},{12,14},{14,10},{10,6},{6,2},{2,0},{0,4},{5,1},{9,5},... | collective-permute-start | bytes 393224 | tf_op jit(solution)/shard_map/ppermute | solution.py:89
  49.6 7.1 %collective-permute-start.11 = (bf16[128,1024]{1,0:T(8,128)(2,1)S(1)}, bf16[128,1024]{1,0:T(8,128)(2,1)S(1)}, u32[]{:S(2)}, u32[]{:S(2)}) collective-permute-start(bf16[128,1024]{1,0:T(8,128)(2,1)S(1)} %pad_maximum_fusion.3), channel_id=1, source_target_pairs={{0,16},{16,0},{1,17},{17,1},{2,18},{18,2},{3,19},{19,3},{4,20},{20... | collective-permute-start | bytes 786440 | tf_op jit(solution)/shard_map/ppermute | solution.py:99
  49.8 5.0 %collective-permute-start.7 = (bf16[64,1024]{1,0:T(8,128)(2,1)S(1)}, bf16[64,1024]{1,0:T(8,128)(2,1)S(1)}, u32[]{:S(2)}, u32[]{:S(2)}) collective-permute-start(bf16[64,1024]{1,0:T(8,128)(2,1)S(1)} %collective-permute-done.5), channel_id=1, source_target_pairs={{4,8},{8,12},{12,14},{14,10},{10,6},{6,2},{2,0},{0,4},{5,1},{9,5},... | collective-permute-start | bytes 393224 | tf_op jit(solution)/shard_map/ppermute | solution.py:89
  54.7 5.0 %collective-permute-start.12 = (bf16[64,1024]{1,0:T(8,128)(2,1)S(1)}, bf16[64,1024]{1,0:T(8,128)(2,1)S(1)}, u32[]{:S(2)}, u32[]{:S(2)}) collective-permute-start(bf16[64,1024]{1,0:T(8,128)(2,1)S(1)} %collective-permute-done.7), channel_id=1, source_target_pairs={{0,16},{16,0},{1,17},{17,1},{2,18},{18,2},{3,19},{19,3},{4,20},{20... | collective-permute-start | bytes 393224 | tf_op jit(solution)/shard_map/ppermute | solution.py:99
  60.2 8.1 %collective-permute-start.13 = (bf16[512,512]{1,0:T(8,128)(2,1)S(1)}, bf16[512,512]{1,0:T(8,128)(2,1)S(1)}, u32[]{:S(2)}, u32[]{:S(2)}) collective-permute-start(bf16[512,512]{1,0:T(8,128)(2,1)S(1)} %fusion.13), channel_id=1, source_target_pairs={{0,1},{1,0},{2,3},{3,2},{4,5},{5,4},{6,7},{7,6},{8,9},{9,8},{10,11... | collective-permute-start | bytes 1572872 | tf_op jit(solution)/shard_map/ppermute | solution.py:136

commit v10 on v6

--- a/solution.py
+++ b/solution.py
@@ -52,7 +52,9 @@
     def per_device(eigvecs, boundary, block_sizes, target_of_channel, poles, energies):
         n_eig = lax.axis_size("eig")
         rows_here = eigvecs.shape[1]
-        block_ends = jnp.cumsum(block_sizes)
+        n_blocks = block_sizes.shape[0]
+        upto = jnp.arange(n_blocks)[:, None] >= jnp.arange(n_blocks)[None, :]
+        block_ends = jnp.sum(jnp.where(upto, block_sizes[None, :], 0), axis=1)
         row_ids = lax.axis_index("basis") * rows_here + jnp.arange(rows_here, dtype=jnp.int32)
         owner_of = jnp.sum((block_ends[None, :] <= row_ids[:, None]).astype(jnp.int32), axis=1)
         n_basis = lax.axis_size("basis")

time: 69.1 us -> 69.1 us (level)
  local copies, waits for them, and re-layouts: 6.3 us -> 5.52 us
    reduce_sum x0 -> x1, other arithmetic: none -> 0.82 us  [per_device(): block_ends = jnp.sum(jnp.where(upto, block_sizes[None, :], 0), axis=1)]
    another operation x1 -> x0, local copies, waits for them, and re-layouts: 0.78 us -> none
where the time goes in v10:
time: 69.1 us; the launch traced here: 68.8 us
  matrix products  22.1 us (32%)
  starting transfers between devices  17.9 us (26%)
  waiting for transfers between devices  12.6 us (18%)
  between operations  9.52 us (14%)
  local copies, waits for them, and re-layouts  5.52 us (8%)
  other arithmetic  1.09 us (2%)
    dot_general x1, matrix products, per_device(): jnp.einsum('ekc,kd->ecd', scaled, right_panel, preferred_element_type=jnp...  16.2 us
    ppermute x6, starting transfers between devices, per_device(): shorts = [lax.ppermute(x, ('eig', 'chan'), short_pairs) for x in shorts]  8.14 us
    ppermute x8, waiting for transfers between devices, per_device(): longs = [lax.ppermute(x, ('eig', 'chan'), long_pairs) for x in longs]  7.71 us
    dot_general x2, matrix products, per_device(): part = jnp.dot(eigvecs, masked, preferred_element_type=jnp.float32)  5.99 us
    ppermute x8, starting transfers between devices, per_device(): longs = [lax.ppermute(x, ('eig', 'chan'), long_pairs) for x in longs]  5.26 us
    ppermute x6, waiting for transfers between devices, per_device(): shorts = [lax.ppermute(x, ('eig', 'chan'), short_pairs) for x in shorts]  4.92 us
    ppermute x2, starting transfers between devices, per_device(): total = total + lax.ppermute(part, 'basis', shift)  4.38 us
    convert_element_type x1, local copies, waits for them, and re-layouts, per_device(): left_panel[None].astype(jnp.float32)  2.99 us
  transfers between devices with their start and end apart: 17, of which 10 were waited for; matrix products, arithmetic and copies ran while one was open for 10% of the time, Pallas kernels for 0%

profile of v10, /device:TPU:0, one launch (start us, length us, event | category | flops | bytes accessed | tf_op | source)
XLA Modules:
  0.0 68.8 jit_solution(15007490963290120973)
XLA Ops:
  0.0 0.8 %select_reduce_fusion = s32[16]{0:T(128)S(1)} fusion(s32[16]{0:T(128)} %param.10), kind=kLoop, calls=%fused_computation.27 | loop fusion | flops 752 | bytes 128 | tf_op jit(solution)/shard_map/reduce_sum | solution.py:57
  0.8 0.7 %fusion.19 = (s32[1024]{0:T(1024)S(1)}, s32[1024]{0:T(1024)S(1)}) fusion(s32[2048]{0:T(1024)} %param.11), kind=kLoop, calls=%fused_computation.46 | loop fusion | bytes 16384 | tf_op jit(solution)/shard_map/slice | solution.py:67
  1.7 4.2 %fusion.13 = f32[64,1024]{1,0:T(8,128)S(1)} fusion(bf16[64,2560]{1,0:T(8,128)(2,1)S(1)} %copy-done, bf16[2560,2048]{1,0:T(8,128)(2,1)} %param.9, s32[1024]{0:T(1024)S(1)} %get-tuple-element.5, s32[2560]{0:T(1024)S(1)} %convert_reduce_fusion), kind=kOutput, calls=%fused_computation.17 | convolution fusion | flops 340787200 | bytes 5847040 | tf_op jit(solution)/shard_map/dot_general | solution.py:69
  5.8 3.0 %collective-permute-start = (f32[64,1024]{1,0:T(8,128)S(1)}, f32[64,1024]{1,0:T(8,128)S(1)}, u32[]{:S(2)}, u32[]{:S(2)}) collective-permute-start(f32[64,1024]{1,0:T(8,128)S(1)} %fusion.13), channel_id=1, source_target_pairs={{0,16},{16,0},{1,17},{17,1},{2,18},{18,2},{3,19},{19,3},{4,20},{20... | collective-permute-start | bytes 786440 | tf_op jit(solution)/shard_map/ppermute | solution.py:73
  8.9 1.8 %fusion.12 = f32[64,1024]{1,0:T(8,128)S(1)} fusion(bf16[64,2560]{1,0:T(8,128)(2,1)S(1)} %copy-done, bf16[2560,2048]{1,0:T(8,128)(2,1)S(1)} %copy-done.4, s32[1024]{0:T(1024)S(1)} %get-tuple-element.6, s32[2560]{0:T(1024)S(1)} %convert_reduce_fusion), kind=kOutput, calls=%fused_computation.16 | convolution fusion | flops 340787200 | bytes 5849088 | tf_op jit(solution)/shard_map/dot_general | solution.py:69
  10.7 1.4 %collective-permute-start.1 = (f32[64,1024]{1,0:T(8,128)S(1)}, f32[64,1024]{1,0:T(8,128)S(1)}, u32[]{:S(2)}, u32[]{:S(2)}) collective-permute-start(f32[64,1024]{1,0:T(8,128)S(1)} %fusion.12), channel_id=1, source_target_pairs={{0,16},{16,0},{1,17},{17,1},{2,18},{18,2},{3,19},{19,3},{4,20},{20... | collective-permute-start | bytes 786440 | tf_op jit(solution)/shard_map/ppermute | solution.py:73
  12.1 0.6 dynamic_slice.27
  17.3 0.7 %fusion.20 = (s32[1]{0:T(128)}, s32[1]{0:T(128)}, s32[1]{0:T(128)}, s32[1]{0:T(128)}, s32[1]{0:T(128)}, /*index=5*/s32[1]{0:T(128)}, s32[1]{0:T(128)}) fusion(s32[8]{0:T(128)S(1)} %copy-done.1, s32[]{:T(128)S(6)} %select_n.145, s32[]{:T(128)S(6)} %select_n.139, s32[]{:T(128)S(6)} %select_n.136, s32[]{:T(128)S(6)} %select_n.133, s32[]{:T(128)S(6)} %select_n.130, ...), kind=kLoop, calls=%fused_computation.47 | loop fusion | bytes 84 | tf_op jit(solution)/shard_map/dynamic_slice | solution.py:90
  22.7 1.6 %collective-permute-start.4 = (bf16[64,1024]{1,0:T(8,128)(2,1)S(1)}, bf16[64,1024]{1,0:T(8,128)(2,1)S(1)}, u32[]{:S(2)}, u32[]{:S(2)}) collective-permute-start(bf16[64,1024]{1,0:T(8,128)(2,1)S(1)} %add_convert_fusion.1), channel_id=1, source_target_pairs={{4,0},{8,4},{12,8},{14,12},{10,14},{6,10},{2,6},{0,2},{5,9},{9,13}... | collective-permute-start | bytes 393224 | tf_op jit(solution)/shard_map/ppermute | solution.py:94
  24.2 0.5 collective-permute-start.2
  24.8 1.6 %collective-permute-start.5 = (bf16[64,1024]{1,0:T(8,128)(2,1)S(1)}, bf16[64,1024]{1,0:T(8,128)(2,1)S(1)}, u32[]{:S(2)}, u32[]{:S(2)}) collective-permute-start(bf16[64,1024]{1,0:T(8,128)(2,1)S(1)} %add_convert_fusion), channel_id=1, source_target_pairs={{4,0},{8,4},{12,8},{14,12},{10,14},{6,10},{2,6},{0,2},{5,9},{9,13}... | collective-permute-start | bytes 393224 | tf_op jit(solution)/shard_map/ppermute | solution.py:94
  26.3 0.5 collective-permute-start.3
  26.8 0.2 broadcast_in_dim.14
  27.1 1.9 %collective-permute-done.4 = bf16[64,1024]{1,0:T(8,128)(2,1)S(1)} collective-permute-done((bf16[64,1024]{1,0:T(8,128)(2,1)S(1)}, bf16[64,1024]{1,0:T(8,128)(2,1)S(1)}, u32[]{:S(2)}, u32[]{:S(2)}) %collective-permute-start.4) | collective-permute-done | bytes 131104 | tf_op jit(solution)/shard_map/ppermute | solution.py:94
  29.1 1.5 %collective-permute-start.8 = (bf16[64,1024]{1,0:T(8,128)(2,1)S(1)}, bf16[64,1024]{1,0:T(8,128)(2,1)S(1)}, u32[]{:S(2)}, u32[]{:S(2)}) collective-permute-start(bf16[64,1024]{1,0:T(8,128)(2,1)S(1)} %collective-permute-done.4), channel_id=1, source_target_pairs={{4,0},{8,4},{12,8},{14,12},{10,14},{6,10},{2,6},{0,2},{5,9},{9,13}... | collective-permute-start | bytes 393224 | tf_op jit(solution)/shard_map/ppermute | solution.py:94
  30.6 0.5 collective-permute-start.6
  31.1 0.8 %collective-permute-done.5 = bf16[64,1024]{1,0:T(8,128)(2,1)S(1)} collective-permute-done((bf16[64,1024]{1,0:T(8,128)(2,1)S(1)}, bf16[64,1024]{1,0:T(8,128)(2,1)S(1)}, u32[]{:S(2)}, u32[]{:S(2)}) %collective-permute-start.5) | collective-permute-done | bytes 131104 | tf_op jit(solution)/shard_map/ppermute | solution.py:94
  31.9 0.7 %collective-permute-start.9 = (bf16[64,1024]{1,0:T(8,128)(2,1)S(1)}, bf16[64,1024]{1,0:T(8,128)(2,1)S(1)}, u32[]{:S(2)}, u32[]{:S(2)}) collective-permute-start(bf16[64,1024]{1,0:T(8,128)(2,1)S(1)} %collective-permute-done.5), channel_id=1, source_target_pairs={{4,0},{8,4},{12,8},{14,12},{10,14},{6,10},{2,6},{0,2},{5,9},{9,13}... | collective-permute-start | bytes 393224 | tf_op jit(solution)/shard_map/ppermute | solution.py:94
  32.6 1.3 %collective-permute-start.7 = (bf16[64,1024]{1,0:T(8,128)(2,1)S(1)}, bf16[64,1024]{1,0:T(8,128)(2,1)S(1)}, u32[]{:S(2)}, u32[]{:S(2)}) collective-permute-start(bf16[64,1024]{1,0:T(8,128)(2,1)S(1)} %collective-permute-done.3), channel_id=1, source_target_pairs={{4,8},{8,12},{12,14},{14,10},{10,6},{6,2},{2,0},{0,4},{5,1},{9,5},... | collective-permute-start | bytes 393224 | tf_op jit(solution)/shard_map/ppermute | solution.py:89
  34.0 0.8 %collective-permute-done.8 = bf16[64,1024]{1,0:T(8,128)(2,1)S(1)} collective-permute-done((bf16[64,1024]{1,0:T(8,128)(2,1)S(1)}, bf16[64,1024]{1,0:T(8,128)(2,1)S(1)}, u32[]{:S(2)}, u32[]{:S(2)}) %collective-permute-start.8) | collective-permute-done | bytes 131104 | tf_op jit(solution)/shard_map/ppermute | solution.py:94
  34.8 1.7 %collective-permute-start.12 = (bf16[64,1024]{1,0:T(8,128)(2,1)S(1)}, bf16[64,1024]{1,0:T(8,128)(2,1)S(1)}, u32[]{:S(2)}, u32[]{:S(2)}) collective-permute-start(bf16[64,1024]{1,0:T(8,128)(2,1)S(1)} %collective-permute-done.8), channel_id=1, source_target_pairs={{4,0},{8,4},{12,8},{14,12},{10,14},{6,10},{2,6},{0,2},{5,9},{9,13}... | collective-permute-start | bytes 393224 | tf_op jit(solution)/shard_map/ppermute | solution.py:94
  36.8 1.4 %collective-permute-done.9 = bf16[64,1024]{1,0:T(8,128)(2,1)S(1)} collective-permute-done((bf16[64,1024]{1,0:T(8,128)(2,1)S(1)}, bf16[64,1024]{1,0:T(8,128)(2,1)S(1)}, u32[]{:S(2)}, u32[]{:S(2)}) %collective-permute-start.9) | collective-permute-done | bytes 131104 | tf_op jit(solution)/shard_map/ppermute | solution.py:94
  38.3 1.0 %collective-permute-start.13 = (bf16[64,1024]{1,0:T(8,128)(2,1)S(1)}, bf16[64,1024]{1,0:T(8,128)(2,1)S(1)}, u32[]{:S(2)}, u32[]{:S(2)}) collective-permute-start(bf16[64,1024]{1,0:T(8,128)(2,1)S(1)} %collective-permute-done.9), channel_id=1, source_target_pairs={{4,0},{8,4},{12,8},{14,12},{10,14},{6,10},{2,6},{0,2},{5,9},{9,13}... | collective-permute-start | bytes 393224 | tf_op jit(solution)/shard_map/ppermute | solution.py:94
  39.4 0.9 %collective-permute-start.11 = (bf16[64,1024]{1,0:T(8,128)(2,1)S(1)}, bf16[64,1024]{1,0:T(8,128)(2,1)S(1)}, u32[]{:S(2)}, u32[]{:S(2)}) collective-permute-start(bf16[64,1024]{1,0:T(8,128)(2,1)S(1)} %collective-permute-done.7), channel_id=1, source_target_pairs={{4,8},{8,12},{12,14},{14,10},{10,6},{6,2},{2,0},{0,4},{5,1},{9,5},... | collective-permute-start | bytes 393224 | tf_op jit(solution)/shard_map/ppermute | solution.py:89
  40.4 1.2 %collective-permute-done.10 = bf16[64,1024]{1,0:T(8,128)(2,1)S(1)} collective-permute-done((bf16[64,1024]{1,0:T(8,128)(2,1)S(1)}, bf16[64,1024]{1,0:T(8,128)(2,1)S(1)}, u32[]{:S(2)}, u32[]{:S(2)}) %collective-permute-start.10) | collective-permute-done | bytes 131104 | tf_op jit(solution)/shard_map/ppermute | solution.py:89
  41.6 0.5 collective-permute-start.14
  42.0 2.3 %collective-permute-done.11 = bf16[64,1024]{1,0:T(8,128)(2,1)S(1)} collective-permute-done((bf16[64,1024]{1,0:T(8,128)(2,1)S(1)}, bf16[64,1024]{1,0:T(8,128)(2,1)S(1)}, u32[]{:S(2)}, u32[]{:S(2)}) %collective-permute-start.11) | collective-permute-done | bytes 131104 | tf_op jit(solution)/shard_map/ppermute | solution.py:89
  44.4 0.9 %collective-permute-start.15 = (bf16[64,1024]{1,0:T(8,128)(2,1)S(1)}, bf16[64,1024]{1,0:T(8,128)(2,1)S(1)}, u32[]{:S(2)}, u32[]{:S(2)}) collective-permute-start(bf16[64,1024]{1,0:T(8,128)(2,1)S(1)} %collective-permute-done.11), channel_id=1, source_target_pairs={{4,8},{8,12},{12,14},{14,10},{10,6},{6,2},{2,0},{0,4},{5,1},{9,5},... | collective-permute-start | bytes 393224 | tf_op jit(solution)/shard_map/ppermute | solution.py:89
  45.4 1.2 %collective-permute-done.14 = bf16[64,1024]{1,0:T(8,128)(2,1)S(1)} collective-permute-done((bf16[64,1024]{1,0:T(8,128)(2,1)S(1)}, bf16[64,1024]{1,0:T(8,128)(2,1)S(1)}, u32[]{:S(2)}, u32[]{:S(2)}) %collective-permute-start.14) | collective-permute-done | bytes 131104 | tf_op jit(solution)/shard_map/ppermute | solution.py:89
  46.5 2.8 %collective-permute-done.15 = bf16[64,1024]{1,0:T(8,128)(2,1)S(1)} collective-permute-done((bf16[64,1024]{1,0:T(8,128)(2,1)S(1)}, bf16[64,1024]{1,0:T(8,128)(2,1)S(1)}, u32[]{:S(2)}, u32[]{:S(2)}) %collective-permute-start.15) | collective-permute-done | bytes 131104 | tf_op jit(solution)/shard_map/ppermute | solution.py:89
  49.6 3.0 %copy.10 = f32[512,2048]{0,1:T(8,128)} copy(bf16[512,2048]{1,0:T(8,128)(2,1)S(1)} %constant_dynamic-update-slice_fusion.7) | data formatting | bytes 6291456 | tf_op jit(solution)/shard_map/convert_element_type | solution.py:111
  52.6 16.2 %convolution_multiply_fusion = f32[8,2048,512]{2,1,0:T(8,128)} fusion(f32[512,2048]{0,1:T(8,128)} %copy.10, f32[8,512]{1,0:T(8,128)S(1)} %subtract_divide_fusion, bf16[512,512]{1,0:T(8,128)(2,1)S(1)} %constant_dynamic-slice_fusion, bf16[512,512]{1,0:T(8,128)(2,1)S(1)} %collective-permute-done.16, pred[]{:T(512)S(6)} %eq.42), kind=kOutput, calls=%fused_computation.1 | convolution fusion | flops 8615362560 | bytes 38813696 | tf_op jit(solution)/shard_map/ekc,kd->ecd/dot_general | solution.py:112
  (44 shorter events, 1.1 us)
Async XLA Ops:
  0.0 1.6 %copy-start = (bf16[64,2560]{1,0:T(8,128)(2,1)S(1)}, bf16[64,2560]{1,0:T(8,128)(2,1)}, u32[]{:S(2)}) copy-start(bf16[64,2560]{1,0:T(8,128)(2,1)} %param.8) | copy-start | bytes 983044
  1.7 7.2 %copy-start.4 = (bf16[2560,2048]{1,0:T(8,128)(2,1)S(1)}, bf16[2560,2048]{1,0:T(8,128)(2,1)}, u32[]{:S(2)}) copy-start(bf16[2560,2048]{1,0:T(8,128)(2,1)} %param.9) | copy-start | bytes 31457284
  5.8 16.8 %collective-permute-start = (f32[64,1024]{1,0:T(8,128)S(1)}, f32[64,1024]{1,0:T(8,128)S(1)}, u32[]{:S(2)}, u32[]{:S(2)}) collective-permute-start(f32[64,1024]{1,0:T(8,128)S(1)} %fusion.13), channel_id=1, source_target_pairs={{0,16},{16,0},{1,17},{17,1},{2,18},{18,2},{3,19},{19,3},{4,20},{20... | collective-permute-start | bytes 786440 | tf_op jit(solution)/shard_map/ppermute | solution.py:73
  8.9 3.2 %copy-start.5 = (s32[8]{0:T(128)S(1)}, s32[8]{0:T(128)}, u32[]{:S(2)}) copy-start(s32[8]{0:T(128)} %constant.113.clone) | copy-start | bytes 100
  8.9 8.4 %copy-start.1 = (s32[8]{0:T(128)S(1)}, s32[8]{0:T(128)}, u32[]{:S(2)}) copy-start(s32[8]{0:T(128)} %constant.112.clone) | copy-start | bytes 100
  10.7 14.0 %collective-permute-start.1 = (f32[64,1024]{1,0:T(8,128)S(1)}, f32[64,1024]{1,0:T(8,128)S(1)}, u32[]{:S(2)}, u32[]{:S(2)}) collective-permute-start(f32[64,1024]{1,0:T(8,128)S(1)} %fusion.12), channel_id=1, source_target_pairs={{0,16},{16,0},{1,17},{17,1},{2,18},{18,2},{3,19},{19,3},{4,20},{20... | collective-permute-start | bytes 786440 | tf_op jit(solution)/shard_map/ppermute | solution.py:73
  22.7 6.4 %collective-permute-start.4 = (bf16[64,1024]{1,0:T(8,128)(2,1)S(1)}, bf16[64,1024]{1,0:T(8,128)(2,1)S(1)}, u32[]{:S(2)}, u32[]{:S(2)}) collective-permute-start(bf16[64,1024]{1,0:T(8,128)(2,1)S(1)} %add_convert_fusion.1), channel_id=1, source_target_pairs={{4,0},{8,4},{12,8},{14,12},{10,14},{6,10},{2,6},{0,2},{5,9},{9,13}... | collective-permute-start | bytes 393224 | tf_op jit(solution)/shard_map/ppermute | solution.py:94
  24.2 6.4 %collective-permute-start.2 = (bf16[64,1024]{1,0:T(8,128)(2,1)S(1)}, bf16[64,1024]{1,0:T(8,128)(2,1)S(1)}, u32[]{:S(2)}, u32[]{:S(2)}) collective-permute-start(bf16[64,1024]{1,0:T(8,128)(2,1)S(1)} %add_convert_fusion.1), channel_id=1, source_target_pairs={{4,8},{8,12},{12,14},{14,10},{10,6},{6,2},{2,0},{0,4},{5,1},{9,5},... | collective-permute-start | bytes 393224 | tf_op jit(solution)/shard_map/ppermute | solution.py:89
  24.8 7.1 %collective-permute-start.5 = (bf16[64,1024]{1,0:T(8,128)(2,1)S(1)}, bf16[64,1024]{1,0:T(8,128)(2,1)S(1)}, u32[]{:S(2)}, u32[]{:S(2)}) collective-permute-start(bf16[64,1024]{1,0:T(8,128)(2,1)S(1)} %add_convert_fusion), channel_id=1, source_target_pairs={{4,0},{8,4},{12,8},{14,12},{10,14},{6,10},{2,6},{0,2},{5,9},{9,13}... | collective-permute-start | bytes 393224 | tf_op jit(solution)/shard_map/ppermute | solution.py:94
  26.3 6.3 %collective-permute-start.3 = (bf16[64,1024]{1,0:T(8,128)(2,1)S(1)}, bf16[64,1024]{1,0:T(8,128)(2,1)S(1)}, u32[]{:S(2)}, u32[]{:S(2)}) collective-permute-start(bf16[64,1024]{1,0:T(8,128)(2,1)S(1)} %add_convert_fusion), channel_id=1, source_target_pairs={{4,8},{8,12},{12,14},{14,10},{10,6},{6,2},{2,0},{0,4},{5,1},{9,5},... | collective-permute-start | bytes 393224 | tf_op jit(solution)/shard_map/ppermute | solution.py:89
  29.1 5.7 %collective-permute-start.8 = (bf16[64,1024]{1,0:T(8,128)(2,1)S(1)}, bf16[64,1024]{1,0:T(8,128)(2,1)S(1)}, u32[]{:S(2)}, u32[]{:S(2)}) collective-permute-start(bf16[64,1024]{1,0:T(8,128)(2,1)S(1)} %collective-permute-done.4), channel_id=1, source_target_pairs={{4,0},{8,4},{12,8},{14,12},{10,14},{6,10},{2,6},{0,2},{5,9},{9,13}... | collective-permute-start | bytes 393224 | tf_op jit(solution)/shard_map/ppermute | solution.py:94
  30.6 6.0 %collective-permute-start.6 = (bf16[64,1024]{1,0:T(8,128)(2,1)S(1)}, bf16[64,1024]{1,0:T(8,128)(2,1)S(1)}, u32[]{:S(2)}, u32[]{:S(2)}) collective-permute-start(bf16[64,1024]{1,0:T(8,128)(2,1)S(1)} %collective-permute-done.2), channel_id=1, source_target_pairs={{4,8},{8,12},{12,14},{14,10},{10,6},{6,2},{2,0},{0,4},{5,1},{9,5},... | collective-permute-start | bytes 393224 | tf_op jit(solution)/shard_map/ppermute | solution.py:89
  31.9 6.4 %collective-permute-start.9 = (bf16[64,1024]{1,0:T(8,128)(2,1)S(1)}, bf16[64,1024]{1,0:T(8,128)(2,1)S(1)}, u32[]{:S(2)}, u32[]{:S(2)}) collective-permute-start(bf16[64,1024]{1,0:T(8,128)(2,1)S(1)} %collective-permute-done.5), channel_id=1, source_target_pairs={{4,0},{8,4},{12,8},{14,12},{10,14},{6,10},{2,6},{0,2},{5,9},{9,13}... | collective-permute-start | bytes 393224 | tf_op jit(solution)/shard_map/ppermute | solution.py:94
  32.6 6.8 %collective-permute-start.7 = (bf16[64,1024]{1,0:T(8,128)(2,1)S(1)}, bf16[64,1024]{1,0:T(8,128)(2,1)S(1)}, u32[]{:S(2)}, u32[]{:S(2)}) collective-permute-start(bf16[64,1024]{1,0:T(8,128)(2,1)S(1)} %collective-permute-done.3), channel_id=1, source_target_pairs={{4,8},{8,12},{12,14},{14,10},{10,6},{6,2},{2,0},{0,4},{5,1},{9,5},... | collective-permute-start | bytes 393224 | tf_op jit(solution)/shard_map/ppermute | solution.py:89
  34.0 15.6 %copy-start.2 = (f32[512]{0:T(512)S(1)}, f32[512]{0:T(512)}, u32[]{:S(2)}) copy-start(f32[512]{0:T(512)} %param.12) | copy-start | bytes 6148
  34.0 15.6 %copy-start.3 = (f32[8]{0:T(128)S(1)}, f32[8]{0:T(128)}, u32[]{:S(2)}) copy-start(f32[8]{0:T(128)} %param.13) | copy-start | bytes 100
  34.8 10.5 %collective-permute-start.12 = (bf16[64,1024]{1,0:T(8,128)(2,1)S(1)}, bf16[64,1024]{1,0:T(8,128)(2,1)S(1)}, u32[]{:S(2)}, u32[]{:S(2)}) collective-permute-start(bf16[64,1024]{1,0:T(8,128)(2,1)S(1)} %collective-permute-done.8), channel_id=1, source_target_pairs={{4,0},{8,4},{12,8},{14,12},{10,14},{6,10},{2,6},{0,2},{5,9},{9,13}... | collective-permute-start | bytes 393224 | tf_op jit(solution)/shard_map/ppermute | solution.py:94
  36.6 5.0 %collective-permute-start.10 = (bf16[64,1024]{1,0:T(8,128)(2,1)S(1)}, bf16[64,1024]{1,0:T(8,128)(2,1)S(1)}, u32[]{:S(2)}, u32[]{:S(2)}) collective-permute-start(bf16[64,1024]{1,0:T(8,128)(2,1)S(1)} %collective-permute-done.6), channel_id=1, source_target_pairs={{4,8},{8,12},{12,14},{14,10},{10,6},{6,2},{2,0},{0,4},{5,1},{9,5},... | collective-permute-start | bytes 393224 | tf_op jit(solution)/shard_map/ppermute | solution.py:89
  38.3 7.1 %collective-permute-start.13 = (bf16[64,1024]{1,0:T(8,128)(2,1)S(1)}, bf16[64,1024]{1,0:T(8,128)(2,1)S(1)}, u32[]{:S(2)}, u32[]{:S(2)}) collective-permute-start(bf16[64,1024]{1,0:T(8,128)(2,1)S(1)} %collective-permute-done.9), channel_id=1, source_target_pairs={{4,0},{8,4},{12,8},{14,12},{10,14},{6,10},{2,6},{0,2},{5,9},{9,13}... | collective-permute-start | bytes 393224 | tf_op jit(solution)/shard_map/ppermute | solution.py:94
  39.4 5.0 %collective-permute-start.11 = (bf16[64,1024]{1,0:T(8,128)(2,1)S(1)}, bf16[64,1024]{1,0:T(8,128)(2,1)S(1)}, u32[]{:S(2)}, u32[]{:S(2)}) collective-permute-start(bf16[64,1024]{1,0:T(8,128)(2,1)S(1)} %collective-permute-done.7), channel_id=1, source_target_pairs={{4,8},{8,12},{12,14},{14,10},{10,6},{6,2},{2,0},{0,4},{5,1},{9,5},... | collective-permute-start | bytes 393224 | tf_op jit(solution)/shard_map/ppermute | solution.py:89
  41.6 5.0 %collective-permute-start.14 = (bf16[64,1024]{1,0:T(8,128)(2,1)S(1)}, bf16[64,1024]{1,0:T(8,128)(2,1)S(1)}, u32[]{:S(2)}, u32[]{:S(2)}) collective-permute-start(bf16[64,1024]{1,0:T(8,128)(2,1)S(1)} %collective-permute-done.10), channel_id=1, source_target_pairs={{4,8},{8,12},{12,14},{14,10},{10,6},{6,2},{2,0},{0,4},{5,1},{9,5},... | collective-permute-start | bytes 393224 | tf_op jit(solution)/shard_map/ppermute | solution.py:89
  44.4 5.0 %collective-permute-start.15 = (bf16[64,1024]{1,0:T(8,128)(2,1)S(1)}, bf16[64,1024]{1,0:T(8,128)(2,1)S(1)}, u32[]{:S(2)}, u32[]{:S(2)}) collective-permute-start(bf16[64,1024]{1,0:T(8,128)(2,1)S(1)} %collective-permute-done.11), channel_id=1, source_target_pairs={{4,8},{8,12},{12,14},{14,10},{10,6},{6,2},{2,0},{0,4},{5,1},{9,5},... | collective-permute-start | bytes 393224 | tf_op jit(solution)/shard_map/ppermute | solution.py:89
  49.4 3.2 %collective-permute-start.16 = (bf16[512,512]{1,0:T(8,128)(2,1)S(1)}, bf16[512,512]{1,0:T(8,128)(2,1)S(1)}, u32[]{:S(2)}, u32[]{:S(2)}) collective-permute-start(bf16[512,512]{1,0:T(8,128)(2,1)S(1)} %constant_dynamic-slice_fusion), channel_id=1, source_target_pairs={{0,1},{1,0},{2,3},{3,2},{4,5},{5,4},{6,7},{7,6},{8,9},{9,8},{10,11... | collective-permute-start | bytes 1572872 | tf_op jit(solution)/shard_map/ppermute | solution.py:104

commit v11 on v7

--- a/solution.py
+++ b/solution.py
@@ -52,12 +52,14 @@
     def per_device(eigvecs, boundary, block_sizes, target_of_channel, poles, energies):
         n_eig = lax.axis_size("eig")
         rows_here = eigvecs.shape[1]
-        block_ends = jnp.cumsum(block_sizes)
+        n_blocks = block_sizes.shape[0]
+        upto = jnp.arange(n_blocks)[:, None] >= jnp.arange(n_blocks)[None, :]
+        block_ends = jnp.sum(jnp.where(upto, block_sizes[None, :], 0), axis=1)
         row_ids = lax.axis_index("basis") * rows_here + jnp.arange(rows_here, dtype=jnp.int32)
         owner_of = jnp.sum((block_ends[None, :] <= row_ids[:, None]).astype(jnp.int32), axis=1)
         n_basis = lax.axis_size("basis")
         width = boundary.shape[1]
-        halves = 4 if width % 512 == 0 else 1
+        halves = 2 if width % 256 == 0 else 1
         step = width // halves
         amp_parts = []
         for h in range(halves):
@@ -75,8 +77,7 @@
         pos = jnp.array(position, dtype=jnp.int32)[eig_index]
         k_here = amp_parts[0].shape[0]
         left_panel = jnp.zeros((k_here * n_ring, width), jnp.bfloat16)
-        for p, x in enumerate(amp_parts):
-            left_panel = lax.dynamic_update_slice(left_panel, x, (eig_index * k_here, p * step))
+        left_panel = lax.dynamic_update_slice(left_panel, amp_parts[0], (eig_index * k_here, 0))
         sign = 1 - 2 * (lax.axis_index("chan") % 2)
         split_w = step
         longs = list(amp_parts)
@@ -92,6 +93,8 @@
                 origin = cycle_arr[(pos + sign * (s + 1)) % n_ring]
                 for p, x in enumerate(shorts):
                     left_panel = lax.dynamic_update_slice(left_panel, x, (origin * k_here, p * split_w))
+        for p, x in enumerate(amp_parts[1:]):
+            left_panel = lax.dynamic_update_slice(left_panel, x, (eig_index * k_here, (p + 1) * step))
         own_width = left_panel.shape[1]
         col_width = own_width * n_chan // n_eig
         ratio = n_eig // n_chan

time: 101 us -> 74.3 us (0.74)
  starting transfers between devices: 37.3 us -> 20.5 us
  waiting for transfers between devices: 22.8 us -> 15.4 us
  matrix products: 24 us -> 22.2 us
    ppermute x16 -> x8, starting transfers between devices: 22.9 us -> 11.2 us  [per_device(): longs = [lax.ppermute(x, ('eig', 'chan'), long_pairs) for x in longs]]
    ppermute x16 -> x8, waiting for transfers between devices: 14 us -> 3.56 us  [per_device(): longs = [lax.ppermute(x, ('eig', 'chan'), long_pairs) for x in longs]]
    ppermute x4 -> x2, waiting for transfers between devices: 0.01 us -> 6.47 us  [per_device(): total = total + lax.ppermute(part, 'basis', shift)]
    ppermute x12 -> x6, starting transfers between devices: 8.35 us -> 4.86 us  [per_device(): shorts = [lax.ppermute(x, ('eig', 'chan'), short_pairs) for x in shorts]]
    ppermute x12 -> x6, waiting for transfers between devices: 8.8 us -> 5.38 us  [per_device(): shorts = [lax.ppermute(x, ('eig', 'chan'), short_pairs) for x in shorts]]
    dot_general x4 -> x2, matrix products: 7.85 us -> 5.99 us  [per_device(): part = jnp.dot(eigvecs, masked, preferred_element_type=jnp.float32)]
    ppermute x4 -> x2, starting transfers between devices: 5.95 us -> 4.38 us  [per_device(): total = total + lax.ppermute(part, 'basis', shift)]
  transfers between devices with their start and end apart: 33 -> 17, of which waited for: 9 -> 7; matrix products, arithmetic and copies ran while one was open for 10% -> 9% of each run, Pallas kernels for 0% -> 0%
where the time goes in v11:
time: 74.3 us; the launch traced here: 74 us
  matrix products  22.2 us (30%)
  starting transfers between devices  20.5 us (28%)
  waiting for transfers between devices  15.4 us (21%)
  between operations  9.33 us (13%)
  local copies, waits for them, and re-layouts  5.51 us (7%)
  other arithmetic  1.07 us (1%)
    dot_general x1, matrix products, per_device(): jnp.einsum('ekc,kd->ecd', scaled, right_panel, preferred_element_type=jnp...  16.2 us
    ppermute x8, starting transfers between devices, per_device(): longs = [lax.ppermute(x, ('eig', 'chan'), long_pairs) for x in longs]  11.2 us
    ppermute x2, waiting for transfers between devices, per_device(): total = total + lax.ppermute(part, 'basis', shift)  6.47 us
    dot_general x2, matrix products, per_device(): part = jnp.dot(eigvecs, masked, preferred_element_type=jnp.float32)  5.99 us
    ppermute x6, waiting for transfers between devices, per_device(): shorts = [lax.ppermute(x, ('eig', 'chan'), short_pairs) for x in shorts]  5.38 us
    ppermute x6, starting transfers between devices, per_device(): shorts = [lax.ppermute(x, ('eig', 'chan'), short_pairs) for x in shorts]  4.86 us
    ppermute x2, starting transfers between devices, per_device(): total = total + lax.ppermute(part, 'basis', shift)  4.38 us
    ppermute x8, waiting for transfers between devices, per_device(): longs = [lax.ppermute(x, ('eig', 'chan'), long_pairs) for x in longs]  3.56 us
  transfers between devices with their start and end apart: 17, of which 7 were waited for; matrix products, arithmetic and copies ran while one was open for 9% of the time, Pallas kernels for 0%

profile of v11, /device:TPU:0, one launch (start us, length us, event | category | flops | bytes accessed | tf_op | source)
XLA Modules:
  0.0 74.0 jit_solution(18360632661983762281)
XLA Ops:
  0.0 0.8 %select_reduce_fusion = s32[16]{0:T(128)S(1)} fusion(s32[16]{0:T(128)} %param.10), kind=kLoop, calls=%fused_computation.26 | loop fusion | flops 752 | bytes 128 | tf_op jit(solution)/shard_map/reduce_sum | solution.py:57
  0.8 0.7 fusion.19
  1.5 0.1 convert_reduce_fusion
  1.7 4.2 %fusion.12 = f32[64,1024]{1,0:T(8,128)S(1)} fusion(bf16[64,2560]{1,0:T(8,128)(2,1)S(1)} %copy-done, bf16[2560,2048]{1,0:T(8,128)(2,1)} %param.9, s32[1024]{0:T(1024)S(1)} %get-tuple-element.7, s32[2560]{0:T(1024)S(1)} %convert_reduce_fusion), kind=kOutput, calls=%fused_computation.16 | convolution fusion | flops 340787200 | bytes 5847040 | tf_op jit(solution)/shard_map/dot_general | solution.py:69
  5.8 3.0 %collective-permute-start.2 = (f32[64,1024]{1,0:T(8,128)S(1)}, f32[64,1024]{1,0:T(8,128)S(1)}, u32[]{:S(2)}, u32[]{:S(2)}) collective-permute-start(f32[64,1024]{1,0:T(8,128)S(1)} %fusion.12), channel_id=1, source_target_pairs={{0,16},{16,0},{1,17},{17,1},{2,18},{18,2},{3,19},{19,3},{4,20},{20... | collective-permute-start | bytes 786440 | tf_op jit(solution)/shard_map/ppermute | solution.py:73
  8.9 1.8 %fusion.13 = f32[64,1024]{1,0:T(8,128)S(1)} fusion(bf16[64,2560]{1,0:T(8,128)(2,1)S(1)} %copy-done, bf16[2560,2048]{1,0:T(8,128)(2,1)S(1)} %copy-done.4, s32[1024]{0:T(1024)S(1)} %get-tuple-element.8, s32[2560]{0:T(1024)S(1)} %convert_reduce_fusion), kind=kOutput, calls=%fused_computation.17 | convolution fusion | flops 340787200 | bytes 5849088 | tf_op jit(solution)/shard_map/dot_general | solution.py:69
  10.7 1.4 %collective-permute-start = (f32[64,1024]{1,0:T(8,128)S(1)}, f32[64,1024]{1,0:T(8,128)S(1)}, u32[]{:S(2)}, u32[]{:S(2)}) collective-permute-start(f32[64,1024]{1,0:T(8,128)S(1)} %fusion.13), channel_id=1, source_target_pairs={{0,16},{16,0},{1,17},{17,1},{2,18},{18,2},{3,19},{19,3},{4,20},{20... | collective-permute-start | bytes 786440 | tf_op jit(solution)/shard_map/ppermute | solution.py:73
  12.1 4.0 %collective-permute-done.2 = f32[64,1024]{1,0:T(8,128)S(1)} collective-permute-done((f32[64,1024]{1,0:T(8,128)S(1)}, f32[64,1024]{1,0:T(8,128)S(1)}, u32[]{:S(2)}, u32[]{:S(2)}) %collective-permute-start.2) | collective-permute-done | bytes 262176 | tf_op jit(solution)/shard_map/ppermute | solution.py:73
  16.1 2.1 %collective-permute-start.5 = (bf16[64,1024]{1,0:T(8,128)(2,1)S(1)}, bf16[64,1024]{1,0:T(8,128)(2,1)S(1)}, u32[]{:S(2)}, u32[]{:S(2)}) collective-permute-start(bf16[64,1024]{1,0:T(8,128)(2,1)S(1)} %add_convert_fusion), channel_id=1, source_target_pairs={{4,0},{8,4},{12,8},{14,12},{10,14},{6,10},{2,6},{0,2},{5,9},{9,13}... | collective-permute-start | bytes 393224 | tf_op jit(solution)/shard_map/ppermute | solution.py:92
  18.2 0.1 collective-permute-start.3
  18.3 2.5 %collective-permute-done = f32[64,1024]{1,0:T(8,128)S(1)} collective-permute-done((f32[64,1024]{1,0:T(8,128)S(1)}, f32[64,1024]{1,0:T(8,128)S(1)}, u32[]{:S(2)}, u32[]{:S(2)}) %collective-permute-start) | collective-permute-done | bytes 262176 | tf_op jit(solution)/shard_map/ppermute | solution.py:73
  20.8 0.2 broadcast_in_dim.14
  21.1 1.9 %collective-permute-start.1 = (bf16[64,1024]{1,0:T(8,128)(2,1)S(1)}, bf16[64,1024]{1,0:T(8,128)(2,1)S(1)}, u32[]{:S(2)}, u32[]{:S(2)}) collective-permute-start(bf16[64,1024]{1,0:T(8,128)(2,1)S(1)} %get-tuple-element.6), channel_id=1, source_target_pairs={{4,8},{8,12},{12,14},{14,10},{10,6},{6,2},{2,0},{0,4},{5,1},{9,5},... | collective-permute-start | bytes 393224 | tf_op jit(solution)/shard_map/ppermute | solution.py:87
  23.0 0.6 dynamic_slice.27
  28.2 0.7 fusion.20
  33.3 0.3 collective-permute-start.4
  33.6 1.8 %collective-permute-start.9 = (bf16[64,1024]{1,0:T(8,128)(2,1)S(1)}, bf16[64,1024]{1,0:T(8,128)(2,1)S(1)}, u32[]{:S(2)}, u32[]{:S(2)}) collective-permute-start(bf16[64,1024]{1,0:T(8,128)(2,1)S(1)} %collective-permute-done.5), channel_id=1, source_target_pairs={{4,0},{8,4},{12,8},{14,12},{10,14},{6,10},{2,6},{0,2},{5,9},{9,13}... | collective-permute-start | bytes 393224 | tf_op jit(solution)/shard_map/ppermute | solution.py:92
  35.3 0.3 collective-permute-start.7
  35.6 1.8 %collective-permute-start.6 = (bf16[64,1024]{1,0:T(8,128)(2,1)S(1)}, bf16[64,1024]{1,0:T(8,128)(2,1)S(1)}, u32[]{:S(2)}, u32[]{:S(2)}) collective-permute-start(bf16[64,1024]{1,0:T(8,128)(2,1)S(1)} %collective-permute-done.1), channel_id=1, source_target_pairs={{4,8},{8,12},{12,14},{14,10},{10,6},{6,2},{2,0},{0,4},{5,1},{9,5},... | collective-permute-start | bytes 393224 | tf_op jit(solution)/shard_map/ppermute | solution.py:87
  37.5 2.3 %collective-permute-done.4 = bf16[64,1024]{1,0:T(8,128)(2,1)S(1)} collective-permute-done((bf16[64,1024]{1,0:T(8,128)(2,1)S(1)}, bf16[64,1024]{1,0:T(8,128)(2,1)S(1)}, u32[]{:S(2)}, u32[]{:S(2)}) %collective-permute-start.4) | collective-permute-done | bytes 131104 | tf_op jit(solution)/shard_map/ppermute | solution.py:92
  39.7 0.2 collective-permute-start.8
  40.0 2.5 %collective-permute-done.9 = bf16[64,1024]{1,0:T(8,128)(2,1)S(1)} collective-permute-done((bf16[64,1024]{1,0:T(8,128)(2,1)S(1)}, bf16[64,1024]{1,0:T(8,128)(2,1)S(1)}, u32[]{:S(2)}, u32[]{:S(2)}) %collective-permute-start.9) | collective-permute-done | bytes 131104 | tf_op jit(solution)/shard_map/ppermute | solution.py:92
  42.6 2.0 %collective-permute-start.11 = (bf16[64,1024]{1,0:T(8,128)(2,1)S(1)}, bf16[64,1024]{1,0:T(8,128)(2,1)S(1)}, u32[]{:S(2)}, u32[]{:S(2)}) collective-permute-start(bf16[64,1024]{1,0:T(8,128)(2,1)S(1)} %collective-permute-done.7), channel_id=1, source_target_pairs={{4,8},{8,12},{12,14},{14,10},{10,6},{6,2},{2,0},{0,4},{5,1},{9,5},... | collective-permute-start | bytes 393224 | tf_op jit(solution)/shard_map/ppermute | solution.py:87
  44.6 1.6 %collective-permute-start.10 = (bf16[64,1024]{1,0:T(8,128)(2,1)S(1)}, bf16[64,1024]{1,0:T(8,128)(2,1)S(1)}, u32[]{:S(2)}, u32[]{:S(2)}) collective-permute-start(bf16[64,1024]{1,0:T(8,128)(2,1)S(1)} %collective-permute-done.6), channel_id=1, source_target_pairs={{4,8},{8,12},{12,14},{14,10},{10,6},{6,2},{2,0},{0,4},{5,1},{9,5},... | collective-permute-start | bytes 393224 | tf_op jit(solution)/shard_map/ppermute | solution.py:87
  46.2 0.5 collective-permute-start.12
  46.8 0.8 %collective-permute-done.11 = bf16[64,1024]{1,0:T(8,128)(2,1)S(1)} collective-permute-done((bf16[64,1024]{1,0:T(8,128)(2,1)S(1)}, bf16[64,1024]{1,0:T(8,128)(2,1)S(1)}, u32[]{:S(2)}, u32[]{:S(2)}) %collective-permute-start.11) | collective-permute-done | bytes 131104 | tf_op jit(solution)/shard_map/ppermute | solution.py:87
  47.6 2.0 %collective-permute-start.15 = (bf16[64,1024]{1,0:T(8,128)(2,1)S(1)}, bf16[64,1024]{1,0:T(8,128)(2,1)S(1)}, u32[]{:S(2)}, u32[]{:S(2)}) collective-permute-start(bf16[64,1024]{1,0:T(8,128)(2,1)S(1)} %collective-permute-done.11), channel_id=1, source_target_pairs={{4,8},{8,12},{12,14},{14,10},{10,6},{6,2},{2,0},{0,4},{5,1},{9,5},... | collective-permute-start | bytes 393224 | tf_op jit(solution)/shard_map/ppermute | solution.py:87
  49.6 1.6 %collective-permute-start.14 = (bf16[64,1024]{1,0:T(8,128)(2,1)S(1)}, bf16[64,1024]{1,0:T(8,128)(2,1)S(1)}, u32[]{:S(2)}, u32[]{:S(2)}) collective-permute-start(bf16[64,1024]{1,0:T(8,128)(2,1)S(1)} %collective-permute-done.10), channel_id=1, source_target_pairs={{4,8},{8,12},{12,14},{14,10},{10,6},{6,2},{2,0},{0,4},{5,1},{9,5},... | collective-permute-start | bytes 393224 | tf_op jit(solution)/shard_map/ppermute | solution.py:87
  51.2 0.6 collective-permute-done.12
  51.8 2.7 %collective-permute-done.14 = bf16[64,1024]{1,0:T(8,128)(2,1)S(1)} collective-permute-done((bf16[64,1024]{1,0:T(8,128)(2,1)S(1)}, bf16[64,1024]{1,0:T(8,128)(2,1)S(1)}, u32[]{:S(2)}, u32[]{:S(2)}) %collective-permute-start.14) | collective-permute-done | bytes 131104 | tf_op jit(solution)/shard_map/ppermute | solution.py:87
  54.8 3.0 %copy.10 = f32[512,2048]{0,1:T(8,128)} copy(bf16[512,2048]{1,0:T(8,128)(2,1)S(1)} %constant_dynamic-update-slice_fusion) | data formatting | bytes 6291456 | tf_op jit(solution)/shard_map/convert_element_type | solution.py:111
  57.8 16.2 %convolution_multiply_fusion = f32[8,2048,512]{2,1,0:T(8,128)} fusion(f32[512,2048]{0,1:T(8,128)} %copy.10, f32[8,512]{1,0:T(8,128)S(1)} %subtract_divide_fusion, bf16[512,512]{1,0:T(8,128)(2,1)S(1)} %constant_dynamic-slice_fusion, bf16[512,512]{1,0:T(8,128)(2,1)S(1)} %collective-permute-done.16, pred[]{:T(512)S(6)} %eq.42), kind=kOutput, calls=%fused_computation.1 | convolution fusion | flops 8615362560 | bytes 38813696 | tf_op jit(solution)/shard_map/ekc,kd->ecd/dot_general | solution.py:112
  (44 shorter events, 0.6 us)
Async XLA Ops:
  0.0 1.6 %copy-start = (bf16[64,2560]{1,0:T(8,128)(2,1)S(1)}, bf16[64,2560]{1,0:T(8,128)(2,1)}, u32[]{:S(2)}) copy-start(bf16[64,2560]{1,0:T(8,128)(2,1)} %param.8) | copy-start | bytes 983044
  1.7 7.2 %copy-start.4 = (bf16[2560,2048]{1,0:T(8,128)(2,1)S(1)}, bf16[2560,2048]{1,0:T(8,128)(2,1)}, u32[]{:S(2)}) copy-start(bf16[2560,2048]{1,0:T(8,128)(2,1)} %param.9) | copy-start | bytes 31457284
  5.8 10.2 %collective-permute-start.2 = (f32[64,1024]{1,0:T(8,128)S(1)}, f32[64,1024]{1,0:T(8,128)S(1)}, u32[]{:S(2)}, u32[]{:S(2)}) collective-permute-start(f32[64,1024]{1,0:T(8,128)S(1)} %fusion.12), channel_id=1, source_target_pairs={{0,16},{16,0},{1,17},{17,1},{2,18},{18,2},{3,19},{19,3},{4,20},{20... | collective-permute-start | bytes 786440 | tf_op jit(solution)/shard_map/ppermute | solution.py:73
  10.7 12.3 %copy-start.5 = (s32[8]{0:T(128)S(1)}, s32[8]{0:T(128)}, u32[]{:S(2)}) copy-start(s32[8]{0:T(128)} %constant.113.clone) | copy-start | bytes 100
  10.7 17.5 %copy-start.1 = (s32[8]{0:T(128)S(1)}, s32[8]{0:T(128)}, u32[]{:S(2)}) copy-start(s32[8]{0:T(128)} %constant.112.clone) | copy-start | bytes 100
  10.7 10.1 %collective-permute-start = (f32[64,1024]{1,0:T(8,128)S(1)}, f32[64,1024]{1,0:T(8,128)S(1)}, u32[]{:S(2)}, u32[]{:S(2)}) collective-permute-start(f32[64,1024]{1,0:T(8,128)S(1)} %fusion.13), channel_id=1, source_target_pairs={{0,16},{16,0},{1,17},{17,1},{2,18},{18,2},{3,19},{19,3},{4,20},{20... | collective-permute-start | bytes 786440 | tf_op jit(solution)/shard_map/ppermute | solution.py:73
  16.1 17.5 %collective-permute-start.5 = (bf16[64,1024]{1,0:T(8,128)(2,1)S(1)}, bf16[64,1024]{1,0:T(8,128)(2,1)S(1)}, u32[]{:S(2)}, u32[]{:S(2)}) collective-permute-start(bf16[64,1024]{1,0:T(8,128)(2,1)S(1)} %add_convert_fusion), channel_id=1, source_target_pairs={{4,0},{8,4},{12,8},{14,12},{10,14},{6,10},{2,6},{0,2},{5,9},{9,13}... | collective-permute-start | bytes 393224 | tf_op jit(solution)/shard_map/ppermute | solution.py:92
  18.2 17.2 %collective-permute-start.3 = (bf16[64,1024]{1,0:T(8,128)(2,1)S(1)}, bf16[64,1024]{1,0:T(8,128)(2,1)S(1)}, u32[]{:S(2)}, u32[]{:S(2)}) collective-permute-start(bf16[64,1024]{1,0:T(8,128)(2,1)S(1)} %add_convert_fusion), channel_id=1, source_target_pairs={{4,8},{8,12},{12,14},{14,10},{10,6},{6,2},{2,0},{0,4},{5,1},{9,5},... | collective-permute-start | bytes 393224 | tf_op jit(solution)/shard_map/ppermute | solution.py:87
  21.1 14.5 %collective-permute-start.1 = (bf16[64,1024]{1,0:T(8,128)(2,1)S(1)}, bf16[64,1024]{1,0:T(8,128)(2,1)S(1)}, u32[]{:S(2)}, u32[]{:S(2)}) collective-permute-start(bf16[64,1024]{1,0:T(8,128)(2,1)S(1)} %get-tuple-element.6), channel_id=1, source_target_pairs={{4,8},{8,12},{12,14},{14,10},{10,6},{6,2},{2,0},{0,4},{5,1},{9,5},... | collective-permute-start | bytes 393224 | tf_op jit(solution)/shard_map/ppermute | solution.py:87
  33.3 6.4 %collective-permute-start.4 = (bf16[64,1024]{1,0:T(8,128)(2,1)S(1)}, bf16[64,1024]{1,0:T(8,128)(2,1)S(1)}, u32[]{:S(2)}, u32[]{:S(2)}) collective-permute-start(bf16[64,1024]{1,0:T(8,128)(2,1)S(1)} %get-tuple-element.6), channel_id=1, source_target_pairs={{4,0},{8,4},{12,8},{14,12},{10,14},{6,10},{2,6},{0,2},{5,9},{9,13}... | collective-permute-start | bytes 393224 | tf_op jit(solution)/shard_map/ppermute | solution.py:92
  33.6 9.0 %collective-permute-start.9 = (bf16[64,1024]{1,0:T(8,128)(2,1)S(1)}, bf16[64,1024]{1,0:T(8,128)(2,1)S(1)}, u32[]{:S(2)}, u32[]{:S(2)}) collective-permute-start(bf16[64,1024]{1,0:T(8,128)(2,1)S(1)} %collective-permute-done.5), channel_id=1, source_target_pairs={{4,0},{8,4},{12,8},{14,12},{10,14},{6,10},{2,6},{0,2},{5,9},{9,13}... | collective-permute-start | bytes 393224 | tf_op jit(solution)/shard_map/ppermute | solution.py:92
  35.3 7.2 %collective-permute-start.7 = (bf16[64,1024]{1,0:T(8,128)(2,1)S(1)}, bf16[64,1024]{1,0:T(8,128)(2,1)S(1)}, u32[]{:S(2)}, u32[]{:S(2)}) collective-permute-start(bf16[64,1024]{1,0:T(8,128)(2,1)S(1)} %collective-permute-done.3), channel_id=1, source_target_pairs={{4,8},{8,12},{12,14},{14,10},{10,6},{6,2},{2,0},{0,4},{5,1},{9,5},... | collective-permute-start | bytes 393224 | tf_op jit(solution)/shard_map/ppermute | solution.py:87
  35.6 9.0 %collective-permute-start.6 = (bf16[64,1024]{1,0:T(8,128)(2,1)S(1)}, bf16[64,1024]{1,0:T(8,128)(2,1)S(1)}, u32[]{:S(2)}, u32[]{:S(2)}) collective-permute-start(bf16[64,1024]{1,0:T(8,128)(2,1)S(1)} %collective-permute-done.1), channel_id=1, source_target_pairs={{4,8},{8,12},{12,14},{14,10},{10,6},{6,2},{2,0},{0,4},{5,1},{9,5},... | collective-permute-start | bytes 393224 | tf_op jit(solution)/shard_map/ppermute | solution.py:87
  39.7 6.5 %collective-permute-start.8 = (bf16[64,1024]{1,0:T(8,128)(2,1)S(1)}, bf16[64,1024]{1,0:T(8,128)(2,1)S(1)}, u32[]{:S(2)}, u32[]{:S(2)}) collective-permute-start(bf16[64,1024]{1,0:T(8,128)(2,1)S(1)} %collective-permute-done.4), channel_id=1, source_target_pairs={{4,0},{8,4},{12,8},{14,12},{10,14},{6,10},{2,6},{0,2},{5,9},{9,13}... | collective-permute-start | bytes 393224 | tf_op jit(solution)/shard_map/ppermute | solution.py:92
  40.0 14.8 %copy-start.2 = (f32[512]{0:T(512)S(1)}, f32[512]{0:T(512)}, u32[]{:S(2)}) copy-start(f32[512]{0:T(512)} %param.12) | copy-start | bytes 6148
  40.0 14.8 %copy-start.3 = (f32[8]{0:T(128)S(1)}, f32[8]{0:T(128)}, u32[]{:S(2)}) copy-start(f32[8]{0:T(128)} %param.13) | copy-start | bytes 100
  42.6 9.2 %collective-permute-start.13 = (bf16[64,1024]{1,0:T(8,128)(2,1)S(1)}, bf16[64,1024]{1,0:T(8,128)(2,1)S(1)}, u32[]{:S(2)}, u32[]{:S(2)}) collective-permute-start(bf16[64,1024]{1,0:T(8,128)(2,1)S(1)} %collective-permute-done.9), channel_id=1, source_target_pairs={{4,0},{8,4},{12,8},{14,12},{10,14},{6,10},{2,6},{0,2},{5,9},{9,13}... | collective-permute-start | bytes 393224 | tf_op jit(solution)/shard_map/ppermute | solution.py:92
  42.6 5.0 %collective-permute-start.11 = (bf16[64,1024]{1,0:T(8,128)(2,1)S(1)}, bf16[64,1024]{1,0:T(8,128)(2,1)S(1)}, u32[]{:S(2)}, u32[]{:S(2)}) collective-permute-start(bf16[64,1024]{1,0:T(8,128)(2,1)S(1)} %collective-permute-done.7), channel_id=1, source_target_pairs={{4,8},{8,12},{12,14},{14,10},{10,6},{6,2},{2,0},{0,4},{5,1},{9,5},... | collective-permute-start | bytes 393224 | tf_op jit(solution)/shard_map/ppermute | solution.py:87
  44.6 5.0 %collective-permute-start.10 = (bf16[64,1024]{1,0:T(8,128)(2,1)S(1)}, bf16[64,1024]{1,0:T(8,128)(2,1)S(1)}, u32[]{:S(2)}, u32[]{:S(2)}) collective-permute-start(bf16[64,1024]{1,0:T(8,128)(2,1)S(1)} %collective-permute-done.6), channel_id=1, source_target_pairs={{4,8},{8,12},{12,14},{14,10},{10,6},{6,2},{2,0},{0,4},{5,1},{9,5},... | collective-permute-start | bytes 393224 | tf_op jit(solution)/shard_map/ppermute | solution.py:87
  46.2 5.5 %collective-permute-start.12 = (bf16[64,1024]{1,0:T(8,128)(2,1)S(1)}, bf16[64,1024]{1,0:T(8,128)(2,1)S(1)}, u32[]{:S(2)}, u32[]{:S(2)}) collective-permute-start(bf16[64,1024]{1,0:T(8,128)(2,1)S(1)} %collective-permute-done.8), channel_id=1, source_target_pairs={{4,0},{8,4},{12,8},{14,12},{10,14},{6,10},{2,6},{0,2},{5,9},{9,13}... | collective-permute-start | bytes 393224 | tf_op jit(solution)/shard_map/ppermute | solution.py:92
  47.6 7.0 %collective-permute-start.15 = (bf16[64,1024]{1,0:T(8,128)(2,1)S(1)}, bf16[64,1024]{1,0:T(8,128)(2,1)S(1)}, u32[]{:S(2)}, u32[]{:S(2)}) collective-permute-start(bf16[64,1024]{1,0:T(8,128)(2,1)S(1)} %collective-permute-done.11), channel_id=1, source_target_pairs={{4,8},{8,12},{12,14},{14,10},{10,6},{6,2},{2,0},{0,4},{5,1},{9,5},... | collective-permute-start | bytes 393224 | tf_op jit(solution)/shard_map/ppermute | solution.py:87
  49.6 5.0 %collective-permute-start.14 = (bf16[64,1024]{1,0:T(8,128)(2,1)S(1)}, bf16[64,1024]{1,0:T(8,128)(2,1)S(1)}, u32[]{:S(2)}, u32[]{:S(2)}) collective-permute-start(bf16[64,1024]{1,0:T(8,128)(2,1)S(1)} %collective-permute-done.10), channel_id=1, source_target_pairs={{4,8},{8,12},{12,14},{14,10},{10,6},{6,2},{2,0},{0,4},{5,1},{9,5},... | collective-permute-start | bytes 393224 | tf_op jit(solution)/shard_map/ppermute | solution.py:87
  54.7 3.2 %collective-permute-start.16 = (bf16[512,512]{1,0:T(8,128)(2,1)S(1)}, bf16[512,512]{1,0:T(8,128)(2,1)S(1)}, u32[]{:S(2)}, u32[]{:S(2)}) collective-permute-start(bf16[512,512]{1,0:T(8,128)(2,1)S(1)} %constant_dynamic-slice_fusion), channel_id=1, source_target_pairs={{0,1},{1,0},{2,3},{3,2},{4,5},{5,4},{6,7},{7,6},{8,9},{9,8},{10,11... | collective-permute-start | bytes 1572872 | tf_op jit(solution)/shard_map/ppermute | solution.py:104

commit v12 on v10

--- a/solution.py
+++ b/solution.py
@@ -67,6 +67,18 @@
             member = owner_of[:, None] == target_of_channel[None, cols]
             masked = jnp.where(member, boundary[:, cols], jnp.zeros_like(boundary[:, cols]))
             part = jnp.dot(eigvecs, masked, preferred_element_type=jnp.float32)
+            if n_basis == 2 and part.shape[0] % 16 == 0:
+                rows = part.shape[0] // 2
+                mine = lax.axis_index("basis")
+                keep = lax.dynamic_slice_in_dim(part, mine * rows, rows, 0)
+                give = lax.dynamic_slice_in_dim(part, (1 - mine) * rows, rows, 0)
+                summed = (keep + lax.ppermute(give, "basis", [(0, 1), (1, 0)])).astype(jnp.bfloat16)
+                other = lax.ppermute(summed, "basis", [(0, 1), (1, 0)])
+                first = mine == 0
+                upper = jnp.where(first, summed, other)
+                lower = jnp.where(first, other, summed)
+                amp_parts.append(jnp.concatenate([upper, lower], axis=0))
+                continue
             total = part
             for s in range(1, n_basis):
                 shift = [(b, (b + s) % n_basis) for b in range(n_basis)]

time: 69.1 us -> 72.2 us (1.045)
  starting transfers between devices: 17.9 us -> 19.8 us
  waiting for transfers between devices: 12.6 us -> 13.7 us
    ppermute x6, starting transfers between devices: 8.14 us -> 3.06 us  [per_device(): shorts = [lax.ppermute(x, ('eig', 'chan'), short_pairs) for x in shorts]]
    ppermute x8, starting transfers between devices: 5.26 us -> 10.2 us  [per_device(): longs = [lax.ppermute(x, ('eig', 'chan'), long_pairs) for x in longs]]
    ppermute x6, waiting for transfers between devices: 4.92 us -> 2.59 us  [per_device(): shorts = [lax.ppermute(x, ('eig', 'chan'), short_pairs) for x in shorts]]
    ppermute x2 -> x4, waiting for transfers between devices: 0.01 us -> 2.16 us  [the longest x2 2.15 us: per_device(): other = lax.ppermute(summed, 'basis', [(0, 1), (1, 0)])]
    ppermute x2 -> x4, starting transfers between devices: 4.38 us -> 6.51 us  [the longest x2 4.35 us: per_device(): lax.ppermute(give, 'basis', [(0, 1), (1, 0)])]
    ppermute x8, waiting for transfers between devices: 7.71 us -> 8.99 us  [per_device(): longs = [lax.ppermute(x, ('eig', 'chan'), long_pairs) for x in longs]]
  transfers between devices with their start and end apart: 17 -> 19, of which waited for: 10 -> 13; matrix products, arithmetic and copies ran while one was open for 10% -> 9% of each run, Pallas kernels for 0% -> 0%
where the time goes in v12:
time: 72.2 us; the launch traced here: 71.9 us
  matrix products  22.2 us (31%)
  starting transfers between devices  19.8 us (27%)
  waiting for transfers between devices  13.7 us (19%)
  between operations  9.55 us (13%)
  local copies, waits for them, and re-layouts  5.49 us (8%)
  other arithmetic  1.12 us (2%)
    dot_general x1, matrix products, per_device(): jnp.einsum('ekc,kd->ecd', scaled, right_panel, preferred_element_type=jnp...  16.2 us
    ppermute x8, starting transfers between devices, per_device(): longs = [lax.ppermute(x, ('eig', 'chan'), long_pairs) for x in longs]  10.2 us
    ppermute x8, waiting for transfers between devices, per_device(): longs = [lax.ppermute(x, ('eig', 'chan'), long_pairs) for x in longs]  8.99 us
    dot_general x2, matrix products, per_device(): part = jnp.dot(eigvecs, masked, preferred_element_type=jnp.float32)  6 us
    ppermute x2, starting transfers between devices, per_device(): lax.ppermute(give, 'basis', [(0, 1), (1, 0)])  4.35 us
    ppermute x6, starting transfers between devices, per_device(): shorts = [lax.ppermute(x, ('eig', 'chan'), short_pairs) for x in shorts]  3.06 us
    convert_element_type x1, local copies, waits for them, and re-layouts, per_device(): left_panel[None].astype(jnp.float32)  2.95 us
    ppermute x6, waiting for transfers between devices, per_device(): shorts = [lax.ppermute(x, ('eig', 'chan'), short_pairs) for x in shorts]  2.59 us
  transfers between devices with their start and end apart: 19, of which 13 were waited for; matrix products, arithmetic and copies ran while one was open for 9% of the time, Pallas kernels for 0%

profile of v12, /device:TPU:0, one launch (start us, length us, event | category | flops | bytes accessed | tf_op | source)
XLA Modules:
  0.0 71.9 jit_solution(9680999120575648268)
XLA Ops:
  0.0 0.8 %select_reduce_fusion = s32[16]{0:T(128)S(1)} fusion(s32[16]{0:T(128)} %param.10), kind=kLoop, calls=%fused_computation.35 | loop fusion | flops 752 | bytes 128 | tf_op jit(solution)/shard_map/reduce_sum | solution.py:57
  0.8 0.7 fusion.19
  1.7 4.2 %fusion.3 = f32[1024,64]{0,1:T(8,128)S(1)} fusion(bf16[64,2560]{1,0:T(8,128)(2,1)S(1)} %copy-done, bf16[2560,2048]{1,0:T(8,128)(2,1)} %param.9, s32[1024]{0:T(1024)S(1)} %get-tuple-element.10, s32[2560]{0:T(1024)S(1)} %convert_reduce_fusion), kind=kOutput, calls=%fused_computation.7 | convolution fusion | flops 340787200 | bytes 5847040 | tf_op jit(solution)/shard_map/dot_general | solution.py:69
  5.9 3.0 %collective-permute-start.2 = (f32[32,1024]{1,0:T(8,128)S(1)}, f32[32,1024]{1,0:T(8,128)S(1)}, u32[]{:S(2)}, u32[]{:S(2)}) collective-permute-start(f32[32,1024]{1,0:T(8,128)S(1)} %dynamic-slice_bitcast_fusion), channel_id=1, source_target_pairs={{0,16},{16,0},{1,17},{17,1},{2,18},{18,2},{3,19},{19,3},{4,20},{20... | collective-permute-start | bytes 393224 | tf_op jit(solution)/shard_map/ppermute | solution.py:75
  8.9 1.8 %fusion.2 = f32[1024,64]{0,1:T(8,128)S(1)} fusion(bf16[64,2560]{1,0:T(8,128)(2,1)S(1)} %copy-done, bf16[2560,2048]{1,0:T(8,128)(2,1)S(1)} %copy-done.4, s32[1024]{0:T(1024)S(1)} %get-tuple-element.9, s32[2560]{0:T(1024)S(1)} %convert_reduce_fusion), kind=kOutput, calls=%fused_computation.6 | convolution fusion | flops 340787200 | bytes 5849088 | tf_op jit(solution)/shard_map/dot_general | solution.py:69
  10.8 1.3 %collective-permute-start = (f32[32,1024]{1,0:T(8,128)S(1)}, f32[32,1024]{1,0:T(8,128)S(1)}, u32[]{:S(2)}, u32[]{:S(2)}) collective-permute-start(f32[32,1024]{1,0:T(8,128)S(1)} %dynamic-slice_bitcast_fusion.1), channel_id=1, source_target_pairs={{0,16},{16,0},{1,17},{17,1},{2,18},{18,2},{3,19},{19,3},{4,20},{20... | collective-permute-start | bytes 393224 | tf_op jit(solution)/shard_map/ppermute | solution.py:75
  12.1 0.6 dynamic_slice.43
  17.3 0.7 fusion.20
  22.7 0.8 %collective-permute-start.3 = (bf16[32,1024]{1,0:T(8,128)(2,1)S(1)}, bf16[32,1024]{1,0:T(8,128)(2,1)S(1)}, u32[]{:S(2)}, u32[]{:S(2)}) collective-permute-start(bf16[32,1024]{1,0:T(8,128)(2,1)S(1)} %fusion.15), channel_id=1, source_target_pairs={{0,16},{16,0},{1,17},{17,1},{2,18},{18,2},{3,19},{19,3},{4,20},{20... | collective-permute-start | bytes 196616 | tf_op jit(solution)/shard_map/ppermute | solution.py:76
  23.5 1.3 %collective-permute-start.1 = (bf16[32,1024]{1,0:T(8,128)(2,1)S(1)}, bf16[32,1024]{1,0:T(8,128)(2,1)S(1)}, u32[]{:S(2)}, u32[]{:S(2)}) collective-permute-start(bf16[32,1024]{1,0:T(8,128)(2,1)S(1)} %fusion.16), channel_id=1, source_target_pairs={{0,16},{16,0},{1,17},{17,1},{2,18},{18,2},{3,19},{19,3},{4,20},{20... | collective-permute-start | bytes 196616 | tf_op jit(solution)/shard_map/ppermute | solution.py:76
  24.8 2.1 %collective-permute-done.3 = bf16[32,1024]{1,0:T(8,128)(2,1)S(1)} collective-permute-done((bf16[32,1024]{1,0:T(8,128)(2,1)S(1)}, bf16[32,1024]{1,0:T(8,128)(2,1)S(1)}, u32[]{:S(2)}, u32[]{:S(2)}) %collective-permute-start.3) | collective-permute-done | bytes 65568 | tf_op jit(solution)/shard_map/ppermute | solution.py:76
  27.0 1.6 %collective-permute-start.5 = (bf16[64,1024]{1,0:T(8,128)(2,1)S(1)}, bf16[64,1024]{1,0:T(8,128)(2,1)S(1)}, u32[]{:S(2)}, u32[]{:S(2)}) collective-permute-start(bf16[64,1024]{1,0:T(8,128)(2,1)S(1)} %pad_maximum_fusion.1), channel_id=1, source_target_pairs={{4,8},{8,12},{12,14},{14,10},{10,6},{6,2},{2,0},{0,4},{5,1},{9,5},... | collective-permute-start | bytes 393224 | tf_op jit(solution)/shard_map/ppermute | solution.py:101
  29.1 1.6 %collective-permute-start.4 = (bf16[64,1024]{1,0:T(8,128)(2,1)S(1)}, bf16[64,1024]{1,0:T(8,128)(2,1)S(1)}, u32[]{:S(2)}, u32[]{:S(2)}) collective-permute-start(bf16[64,1024]{1,0:T(8,128)(2,1)S(1)} %pad_maximum_fusion), channel_id=1, source_target_pairs={{4,8},{8,12},{12,14},{14,10},{10,6},{6,2},{2,0},{0,4},{5,1},{9,5},... | collective-permute-start | bytes 393224 | tf_op jit(solution)/shard_map/ppermute | solution.py:101
  31.5 1.9 %collective-permute-done.5 = bf16[64,1024]{1,0:T(8,128)(2,1)S(1)} collective-permute-done((bf16[64,1024]{1,0:T(8,128)(2,1)S(1)}, bf16[64,1024]{1,0:T(8,128)(2,1)S(1)}, u32[]{:S(2)}, u32[]{:S(2)}) %collective-permute-start.5) | collective-permute-done | bytes 131104 | tf_op jit(solution)/shard_map/ppermute | solution.py:101
  33.4 1.2 %collective-permute-start.9 = (bf16[64,1024]{1,0:T(8,128)(2,1)S(1)}, bf16[64,1024]{1,0:T(8,128)(2,1)S(1)}, u32[]{:S(2)}, u32[]{:S(2)}) collective-permute-start(bf16[64,1024]{1,0:T(8,128)(2,1)S(1)} %collective-permute-done.5), channel_id=1, source_target_pairs={{4,8},{8,12},{12,14},{14,10},{10,6},{6,2},{2,0},{0,4},{5,1},{9,5},... | collective-permute-start | bytes 393224 | tf_op jit(solution)/shard_map/ppermute | solution.py:101
  35.4 0.8 %collective-permute-done.4 = bf16[64,1024]{1,0:T(8,128)(2,1)S(1)} collective-permute-done((bf16[64,1024]{1,0:T(8,128)(2,1)S(1)}, bf16[64,1024]{1,0:T(8,128)(2,1)S(1)}, u32[]{:S(2)}, u32[]{:S(2)}) %collective-permute-start.4) | collective-permute-done | bytes 131104 | tf_op jit(solution)/shard_map/ppermute | solution.py:101
  36.2 1.1 %collective-permute-start.8 = (bf16[64,1024]{1,0:T(8,128)(2,1)S(1)}, bf16[64,1024]{1,0:T(8,128)(2,1)S(1)}, u32[]{:S(2)}, u32[]{:S(2)}) collective-permute-start(bf16[64,1024]{1,0:T(8,128)(2,1)S(1)} %collective-permute-done.4), channel_id=1, source_target_pairs={{4,8},{8,12},{12,14},{14,10},{10,6},{6,2},{2,0},{0,4},{5,1},{9,5},... | collective-permute-start | bytes 393224 | tf_op jit(solution)/shard_map/ppermute | solution.py:101
  37.3 0.5 collective-permute-done.6
  38.3 1.0 %collective-permute-done.9 = bf16[64,1024]{1,0:T(8,128)(2,1)S(1)} collective-permute-done((bf16[64,1024]{1,0:T(8,128)(2,1)S(1)}, bf16[64,1024]{1,0:T(8,128)(2,1)S(1)}, u32[]{:S(2)}, u32[]{:S(2)}) %collective-permute-start.9) | collective-permute-done | bytes 131104 | tf_op jit(solution)/shard_map/ppermute | solution.py:101
  39.3 0.9 %collective-permute-start.13 = (bf16[64,1024]{1,0:T(8,128)(2,1)S(1)}, bf16[64,1024]{1,0:T(8,128)(2,1)S(1)}, u32[]{:S(2)}, u32[]{:S(2)}) collective-permute-start(bf16[64,1024]{1,0:T(8,128)(2,1)S(1)} %collective-permute-done.9), channel_id=1, source_target_pairs={{4,8},{8,12},{12,14},{14,10},{10,6},{6,2},{2,0},{0,4},{5,1},{9,5},... | collective-permute-start | bytes 393224 | tf_op jit(solution)/shard_map/ppermute | solution.py:101
  40.3 0.5 collective-permute-done.11
  40.7 1.0 %collective-permute-start.15 = (bf16[64,1024]{1,0:T(8,128)(2,1)S(1)}, bf16[64,1024]{1,0:T(8,128)(2,1)S(1)}, u32[]{:S(2)}, u32[]{:S(2)}) collective-permute-start(bf16[64,1024]{1,0:T(8,128)(2,1)S(1)} %collective-permute-done.11), channel_id=1, source_target_pairs={{4,0},{8,4},{12,8},{14,12},{10,14},{6,10},{2,6},{0,2},{5,9},{9,13}... | collective-permute-start | bytes 393224 | tf_op jit(solution)/shard_map/ppermute | solution.py:106
  41.8 0.8 %collective-permute-done.8 = bf16[64,1024]{1,0:T(8,128)(2,1)S(1)} collective-permute-done((bf16[64,1024]{1,0:T(8,128)(2,1)S(1)}, bf16[64,1024]{1,0:T(8,128)(2,1)S(1)}, u32[]{:S(2)}, u32[]{:S(2)}) %collective-permute-start.8) | collective-permute-done | bytes 131104 | tf_op jit(solution)/shard_map/ppermute | solution.py:101
  42.5 1.0 %collective-permute-start.12 = (bf16[64,1024]{1,0:T(8,128)(2,1)S(1)}, bf16[64,1024]{1,0:T(8,128)(2,1)S(1)}, u32[]{:S(2)}, u32[]{:S(2)}) collective-permute-start(bf16[64,1024]{1,0:T(8,128)(2,1)S(1)} %collective-permute-done.8), channel_id=1, source_target_pairs={{4,8},{8,12},{12,14},{14,10},{10,6},{6,2},{2,0},{0,4},{5,1},{9,5},... | collective-permute-start | bytes 393224 | tf_op jit(solution)/shard_map/ppermute | solution.py:101
  43.6 0.6 collective-permute-done.10
  44.8 1.6 %collective-permute-start.17 = (bf16[64,1024]{1,0:T(8,128)(2,1)S(1)}, bf16[64,1024]{1,0:T(8,128)(2,1)S(1)}, u32[]{:S(2)}, u32[]{:S(2)}) collective-permute-start(bf16[64,1024]{1,0:T(8,128)(2,1)S(1)} %collective-permute-done.13), channel_id=1, source_target_pairs={{4,8},{8,12},{12,14},{14,10},{10,6},{6,2},{2,0},{0,4},{5,1},{9,5},... | collective-permute-start | bytes 393224 | tf_op jit(solution)/shard_map/ppermute | solution.py:101
  46.4 1.1 %collective-permute-done.12 = bf16[64,1024]{1,0:T(8,128)(2,1)S(1)} collective-permute-done((bf16[64,1024]{1,0:T(8,128)(2,1)S(1)}, bf16[64,1024]{1,0:T(8,128)(2,1)S(1)}, u32[]{:S(2)}, u32[]{:S(2)}) %collective-permute-start.12) | collective-permute-done | bytes 131104 | tf_op jit(solution)/shard_map/ppermute | solution.py:101
  47.5 1.0 %collective-permute-start.16 = (bf16[64,1024]{1,0:T(8,128)(2,1)S(1)}, bf16[64,1024]{1,0:T(8,128)(2,1)S(1)}, u32[]{:S(2)}, u32[]{:S(2)}) collective-permute-start(bf16[64,1024]{1,0:T(8,128)(2,1)S(1)} %collective-permute-done.12), channel_id=1, source_target_pairs={{4,8},{8,12},{12,14},{14,10},{10,6},{6,2},{2,0},{0,4},{5,1},{9,5},... | collective-permute-start | bytes 393224 | tf_op jit(solution)/shard_map/ppermute | solution.py:101
  48.6 0.6 collective-permute-done.14
  49.2 3.3 %collective-permute-done.16 = bf16[64,1024]{1,0:T(8,128)(2,1)S(1)} collective-permute-done((bf16[64,1024]{1,0:T(8,128)(2,1)S(1)}, bf16[64,1024]{1,0:T(8,128)(2,1)S(1)}, u32[]{:S(2)}, u32[]{:S(2)}) %collective-permute-start.16) | collective-permute-done | bytes 131104 | tf_op jit(solution)/shard_map/ppermute | solution.py:101
  52.8 2.9 %copy.10 = f32[512,2048]{0,1:T(8,128)} copy(bf16[512,2048]{1,0:T(8,128)(2,1)S(1)} %constant_dynamic-update-slice_fusion.7) | data formatting | bytes 6291456 | tf_op jit(solution)/shard_map/convert_element_type | solution.py:123
  55.7 16.2 %convolution_multiply_fusion = f32[8,2048,512]{2,1,0:T(8,128)} fusion(f32[512,2048]{0,1:T(8,128)} %copy.10, f32[8,512]{1,0:T(8,128)S(1)} %subtract_divide_fusion, bf16[512,512]{1,0:T(8,128)(2,1)S(1)} %constant_dynamic-slice_fusion, bf16[512,512]{1,0:T(8,128)(2,1)S(1)} %collective-permute-done.18, pred[]{:T(512)S(6)} %eq.47), kind=kOutput, calls=%fused_computation.1 | convolution fusion | flops 8615362560 | bytes 38813696 | tf_op jit(solution)/shard_map/ekc,kd->ecd/dot_general | solution.py:124
  (54 shorter events, 3.6 us)
Async XLA Ops:
  0.0 1.6 %copy-start = (bf16[64,2560]{1,0:T(8,128)(2,1)S(1)}, bf16[64,2560]{1,0:T(8,128)(2,1)}, u32[]{:S(2)}) copy-start(bf16[64,2560]{1,0:T(8,128)(2,1)} %param.8) | copy-start | bytes 983044
  1.7 7.3 %copy-start.4 = (bf16[2560,2048]{1,0:T(8,128)(2,1)S(1)}, bf16[2560,2048]{1,0:T(8,128)(2,1)}, u32[]{:S(2)}) copy-start(bf16[2560,2048]{1,0:T(8,128)(2,1)} %param.9) | copy-start | bytes 31457284
  5.9 16.7 %collective-permute-start.2 = (f32[32,1024]{1,0:T(8,128)S(1)}, f32[32,1024]{1,0:T(8,128)S(1)}, u32[]{:S(2)}, u32[]{:S(2)}) collective-permute-start(f32[32,1024]{1,0:T(8,128)S(1)} %dynamic-slice_bitcast_fusion), channel_id=1, source_target_pairs={{0,16},{16,0},{1,17},{17,1},{2,18},{18,2},{3,19},{19,3},{4,20},{20... | collective-permute-start | bytes 393224 | tf_op jit(solution)/shard_map/ppermute | solution.py:75
  8.9 3.2 %copy-start.5 = (s32[8]{0:T(128)S(1)}, s32[8]{0:T(128)}, u32[]{:S(2)}) copy-start(s32[8]{0:T(128)} %constant.115.clone) | copy-start | bytes 100
  8.9 8.4 %copy-start.1 = (s32[8]{0:T(128)S(1)}, s32[8]{0:T(128)}, u32[]{:S(2)}) copy-start(s32[8]{0:T(128)} %constant.114.clone) | copy-start | bytes 100
  10.8 12.7 %collective-permute-start = (f32[32,1024]{1,0:T(8,128)S(1)}, f32[32,1024]{1,0:T(8,128)S(1)}, u32[]{:S(2)}, u32[]{:S(2)}) collective-permute-start(f32[32,1024]{1,0:T(8,128)S(1)} %dynamic-slice_bitcast_fusion.1), channel_id=1, source_target_pairs={{0,16},{16,0},{1,17},{17,1},{2,18},{18,2},{3,19},{19,3},{4,20},{20... | collective-permute-start | bytes 393224 | tf_op jit(solution)/shard_map/ppermute | solution.py:75
  22.7 4.3 %collective-permute-start.3 = (bf16[32,1024]{1,0:T(8,128)(2,1)S(1)}, bf16[32,1024]{1,0:T(8,128)(2,1)S(1)}, u32[]{:S(2)}, u32[]{:S(2)}) collective-permute-start(bf16[32,1024]{1,0:T(8,128)(2,1)S(1)} %fusion.15), channel_id=1, source_target_pairs={{0,16},{16,0},{1,17},{17,1},{2,18},{18,2},{3,19},{19,3},{4,20},{20... | collective-permute-start | bytes 196616 | tf_op jit(solution)/shard_map/ppermute | solution.py:76
  23.5 5.6 %collective-permute-start.1 = (bf16[32,1024]{1,0:T(8,128)(2,1)S(1)}, bf16[32,1024]{1,0:T(8,128)(2,1)S(1)}, u32[]{:S(2)}, u32[]{:S(2)}) collective-permute-start(bf16[32,1024]{1,0:T(8,128)(2,1)S(1)} %fusion.16), channel_id=1, source_target_pairs={{0,16},{16,0},{1,17},{17,1},{2,18},{18,2},{3,19},{19,3},{4,20},{20... | collective-permute-start | bytes 196616 | tf_op jit(solution)/shard_map/ppermute | solution.py:76
  27.0 6.3 %collective-permute-start.5 = (bf16[64,1024]{1,0:T(8,128)(2,1)S(1)}, bf16[64,1024]{1,0:T(8,128)(2,1)S(1)}, u32[]{:S(2)}, u32[]{:S(2)}) collective-permute-start(bf16[64,1024]{1,0:T(8,128)(2,1)S(1)} %pad_maximum_fusion.1), channel_id=1, source_target_pairs={{4,8},{8,12},{12,14},{14,10},{10,6},{6,2},{2,0},{0,4},{5,1},{9,5},... | collective-permute-start | bytes 393224 | tf_op jit(solution)/shard_map/ppermute | solution.py:101
  28.7 6.4 %collective-permute-start.7 = (bf16[64,1024]{1,0:T(8,128)(2,1)S(1)}, bf16[64,1024]{1,0:T(8,128)(2,1)S(1)}, u32[]{:S(2)}, u32[]{:S(2)}) collective-permute-start(bf16[64,1024]{1,0:T(8,128)(2,1)S(1)} %pad_maximum_fusion.1), channel_id=1, source_target_pairs={{4,0},{8,4},{12,8},{14,12},{10,14},{6,10},{2,6},{0,2},{5,9},{9,13}... | collective-permute-start | bytes 393224 | tf_op jit(solution)/shard_map/ppermute | solution.py:106
  29.1 7.0 %collective-permute-start.4 = (bf16[64,1024]{1,0:T(8,128)(2,1)S(1)}, bf16[64,1024]{1,0:T(8,128)(2,1)S(1)}, u32[]{:S(2)}, u32[]{:S(2)}) collective-permute-start(bf16[64,1024]{1,0:T(8,128)(2,1)S(1)} %pad_maximum_fusion), channel_id=1, source_target_pairs={{4,8},{8,12},{12,14},{14,10},{10,6},{6,2},{2,0},{0,4},{5,1},{9,5},... | collective-permute-start | bytes 393224 | tf_op jit(solution)/shard_map/ppermute | solution.py:101
  30.8 7.1 %collective-permute-start.6 = (bf16[64,1024]{1,0:T(8,128)(2,1)S(1)}, bf16[64,1024]{1,0:T(8,128)(2,1)S(1)}, u32[]{:S(2)}, u32[]{:S(2)}) collective-permute-start(bf16[64,1024]{1,0:T(8,128)(2,1)S(1)} %pad_maximum_fusion), channel_id=1, source_target_pairs={{4,0},{8,4},{12,8},{14,12},{10,14},{6,10},{2,6},{0,2},{5,9},{9,13}... | collective-permute-start | bytes 393224 | tf_op jit(solution)/shard_map/ppermute | solution.py:106
  33.4 6.0 %collective-permute-start.9 = (bf16[64,1024]{1,0:T(8,128)(2,1)S(1)}, bf16[64,1024]{1,0:T(8,128)(2,1)S(1)}, u32[]{:S(2)}, u32[]{:S(2)}) collective-permute-start(bf16[64,1024]{1,0:T(8,128)(2,1)S(1)} %collective-permute-done.5), channel_id=1, source_target_pairs={{4,8},{8,12},{12,14},{14,10},{10,6},{6,2},{2,0},{0,4},{5,1},{9,5},... | collective-permute-start | bytes 393224 | tf_op jit(solution)/shard_map/ppermute | solution.py:101
  35.0 5.7 %collective-permute-start.11 = (bf16[64,1024]{1,0:T(8,128)(2,1)S(1)}, bf16[64,1024]{1,0:T(8,128)(2,1)S(1)}, u32[]{:S(2)}, u32[]{:S(2)}) collective-permute-start(bf16[64,1024]{1,0:T(8,128)(2,1)S(1)} %collective-permute-done.7), channel_id=1, source_target_pairs={{4,0},{8,4},{12,8},{14,12},{10,14},{6,10},{2,6},{0,2},{5,9},{9,13}... | collective-permute-start | bytes 393224 | tf_op jit(solution)/shard_map/ppermute | solution.py:106
  36.2 6.4 %collective-permute-start.8 = (bf16[64,1024]{1,0:T(8,128)(2,1)S(1)}, bf16[64,1024]{1,0:T(8,128)(2,1)S(1)}, u32[]{:S(2)}, u32[]{:S(2)}) collective-permute-start(bf16[64,1024]{1,0:T(8,128)(2,1)S(1)} %collective-permute-done.4), channel_id=1, source_target_pairs={{4,8},{8,12},{12,14},{14,10},{10,6},{6,2},{2,0},{0,4},{5,1},{9,5},... | collective-permute-start | bytes 393224 | tf_op jit(solution)/shard_map/ppermute | solution.py:101
  37.8 6.4 %collective-permute-start.10 = (bf16[64,1024]{1,0:T(8,128)(2,1)S(1)}, bf16[64,1024]{1,0:T(8,128)(2,1)S(1)}, u32[]{:S(2)}, u32[]{:S(2)}) collective-permute-start(bf16[64,1024]{1,0:T(8,128)(2,1)S(1)} %collective-permute-done.6), channel_id=1, source_target_pairs={{4,0},{8,4},{12,8},{14,12},{10,14},{6,10},{2,6},{0,2},{5,9},{9,13}... | collective-permute-start | bytes 393224 | tf_op jit(solution)/shard_map/ppermute | solution.py:106
  38.2 14.4 %copy-start.2 = (f32[512]{0:T(512)S(1)}, f32[512]{0:T(512)}, u32[]{:S(2)}) copy-start(f32[512]{0:T(512)} %param.12) | copy-start | bytes 6148
  38.3 14.4 %copy-start.3 = (f32[8]{0:T(128)S(1)}, f32[8]{0:T(128)}, u32[]{:S(2)}) copy-start(f32[8]{0:T(128)} %param.13) | copy-start | bytes 100
  39.3 5.5 %collective-permute-start.13 = (bf16[64,1024]{1,0:T(8,128)(2,1)S(1)}, bf16[64,1024]{1,0:T(8,128)(2,1)S(1)}, u32[]{:S(2)}, u32[]{:S(2)}) collective-permute-start(bf16[64,1024]{1,0:T(8,128)(2,1)S(1)} %collective-permute-done.9), channel_id=1, source_target_pairs={{4,8},{8,12},{12,14},{14,10},{10,6},{6,2},{2,0},{0,4},{5,1},{9,5},... | collective-permute-start | bytes 393224 | tf_op jit(solution)/shard_map/ppermute | solution.py:101
  40.7 8.4 %collective-permute-start.15 = (bf16[64,1024]{1,0:T(8,128)(2,1)S(1)}, bf16[64,1024]{1,0:T(8,128)(2,1)S(1)}, u32[]{:S(2)}, u32[]{:S(2)}) collective-permute-start(bf16[64,1024]{1,0:T(8,128)(2,1)S(1)} %collective-permute-done.11), channel_id=1, source_target_pairs={{4,0},{8,4},{12,8},{14,12},{10,14},{6,10},{2,6},{0,2},{5,9},{9,13}... | collective-permute-start | bytes 393224 | tf_op jit(solution)/shard_map/ppermute | solution.py:106
  42.5 5.0 %collective-permute-start.12 = (bf16[64,1024]{1,0:T(8,128)(2,1)S(1)}, bf16[64,1024]{1,0:T(8,128)(2,1)S(1)}, u32[]{:S(2)}, u32[]{:S(2)}) collective-permute-start(bf16[64,1024]{1,0:T(8,128)(2,1)S(1)} %collective-permute-done.8), channel_id=1, source_target_pairs={{4,8},{8,12},{12,14},{14,10},{10,6},{6,2},{2,0},{0,4},{5,1},{9,5},... | collective-permute-start | bytes 393224 | tf_op jit(solution)/shard_map/ppermute | solution.py:101
  44.2 5.0 %collective-permute-start.14 = (bf16[64,1024]{1,0:T(8,128)(2,1)S(1)}, bf16[64,1024]{1,0:T(8,128)(2,1)S(1)}, u32[]{:S(2)}, u32[]{:S(2)}) collective-permute-start(bf16[64,1024]{1,0:T(8,128)(2,1)S(1)} %collective-permute-done.10), channel_id=1, source_target_pairs={{4,0},{8,4},{12,8},{14,12},{10,14},{6,10},{2,6},{0,2},{5,9},{9,13}... | collective-permute-start | bytes 393224 | tf_op jit(solution)/shard_map/ppermute | solution.py:106
  44.8 7.7 %collective-permute-start.17 = (bf16[64,1024]{1,0:T(8,128)(2,1)S(1)}, bf16[64,1024]{1,0:T(8,128)(2,1)S(1)}, u32[]{:S(2)}, u32[]{:S(2)}) collective-permute-start(bf16[64,1024]{1,0:T(8,128)(2,1)S(1)} %collective-permute-done.13), channel_id=1, source_target_pairs={{4,8},{8,12},{12,14},{14,10},{10,6},{6,2},{2,0},{0,4},{5,1},{9,5},... | collective-permute-start | bytes 393224 | tf_op jit(solution)/shard_map/ppermute | solution.py:101
  47.5 5.0 %collective-permute-start.16 = (bf16[64,1024]{1,0:T(8,128)(2,1)S(1)}, bf16[64,1024]{1,0:T(8,128)(2,1)S(1)}, u32[]{:S(2)}, u32[]{:S(2)}) collective-permute-start(bf16[64,1024]{1,0:T(8,128)(2,1)S(1)} %collective-permute-done.12), channel_id=1, source_target_pairs={{4,8},{8,12},{12,14},{14,10},{10,6},{6,2},{2,0},{0,4},{5,1},{9,5},... | collective-permute-start | bytes 393224 | tf_op jit(solution)/shard_map/ppermute | solution.py:101
  52.6 3.1 %collective-permute-start.18 = (bf16[512,512]{1,0:T(8,128)(2,1)S(1)}, bf16[512,512]{1,0:T(8,128)(2,1)S(1)}, u32[]{:S(2)}, u32[]{:S(2)}) collective-permute-start(bf16[512,512]{1,0:T(8,128)(2,1)S(1)} %constant_dynamic-slice_fusion), channel_id=1, source_target_pairs={{0,1},{1,0},{2,3},{3,2},{4,5},{5,4},{6,7},{7,6},{8,9},{9,8},{10,11... | collective-permute-start | bytes 1572872 | tf_op jit(solution)/shard_map/ppermute | solution.py:116

commit v13 on v10

--- a/solution.py
+++ b/solution.py
@@ -82,17 +82,20 @@
         sign = 1 - 2 * (lax.axis_index("chan") % 2)
         n_split = 2 if amp.shape[1] % 256 == 0 else 1
         split_w = amp.shape[1] // n_split
+        tag = jnp.full((8, 128), eig_index, jnp.float32)
+        long_from = lax.ppermute(tag, ("eig", "chan"), long_pairs)[0, 0].astype(jnp.int32)
+        short_from = lax.ppermute(tag, ("eig", "chan"), short_pairs)[0, 0].astype(jnp.int32)
         longs = [amp[:, p * split_w:(p + 1) * split_w] for p in range(n_split)]
         shorts = list(longs)
         for s in range(max(n_fwd, n_bwd)):
             if s < n_fwd:
                 longs = [lax.ppermute(x, ("eig", "chan"), long_pairs) for x in longs]
-                origin = cycle_arr[(pos - sign * (s + 1)) % n_ring]
+                origin = long_from if s == 0 else cycle_arr[(pos - sign * (s + 1)) % n_ring]
                 for p, x in enumerate(longs):
                     left_panel = lax.dynamic_update_slice(left_panel, x, (origin * k_here, p * split_w))
             if s < n_bwd:
                 shorts = [lax.ppermute(x, ("eig", "chan"), short_pairs) for x in shorts]
-                origin = cycle_arr[(pos + sign * (s + 1)) % n_ring]
+                origin = short_from if s == 0 else cycle_arr[(pos + sign * (s + 1)) % n_ring]
                 for p, x in enumerate(shorts):
                     left_panel = lax.dynamic_update_slice(left_panel, x, (origin * k_here, p * split_w))
         own_width = left_panel.shape[1]

time: 69.1 us -> 70.9 us (1.026)
  starting transfers between devices: 17.9 us -> 19.6 us
  between operations: 9.52 us -> 8.2 us
  local copies, waits for them, and re-layouts: 5.52 us -> 6.49 us
    ppermute x0 -> x2, starting transfers between devices: none -> 2.03 us  [the longest x1 1.52 us: per_device(): lax.ppermute(tag, ('eig', 'chan'), short_pairs)[0, 0].astype(jnp.int32)]
    slice x0 -> x2, local copies, waits for them, and re-layouts: none -> 1.03 us  [the longest x1 0.51 us: per_device(): lax.ppermute(tag, ('eig', 'chan'), short_pairs)[0, 0].astype(jnp.int32)]
    ppermute x8, starting transfers between devices: 5.26 us -> 4.49 us  [per_device(): longs = [lax.ppermute(x, ('eig', 'chan'), long_pairs) for x in longs]]
  transfers between devices with their start and end apart: 17 -> 19, of which waited for: 10 -> 9; matrix products, arithmetic and copies ran while one was open for 10% -> 11% of each run, Pallas kernels for 0% -> 0%
where the time goes in v13:
time: 70.9 us; the launch traced here: 70.6 us
  matrix products  22.1 us (31%)
  starting transfers between devices  19.6 us (28%)
  waiting for transfers between devices  13 us (18%)
  between operations  8.2 us (12%)
  local copies, waits for them, and re-layouts  6.49 us (9%)
  other arithmetic  1.09 us (2%)
    dot_general x1, matrix products, per_device(): jnp.einsum('ekc,kd->ecd', scaled, right_panel, preferred_element_type=jnp...  16.2 us
    ppermute x6, starting transfers between devices, per_device(): shorts = [lax.ppermute(x, ('eig', 'chan'), short_pairs) for x in shorts]  8.67 us
    ppermute x8, waiting for transfers between devices, per_device(): longs = [lax.ppermute(x, ('eig', 'chan'), long_pairs) for x in longs]  8.16 us
    dot_general x2, matrix products, per_device(): part = jnp.dot(eigvecs, masked, preferred_element_type=jnp.float32)  5.99 us
    ppermute x6, waiting for transfers between devices, per_device(): shorts = [lax.ppermute(x, ('eig', 'chan'), short_pairs) for x in shorts]  4.86 us
    ppermute x8, starting transfers between devices, per_device(): longs = [lax.ppermute(x, ('eig', 'chan'), long_pairs) for x in longs]  4.49 us
    ppermute x2, starting transfers between devices, per_device(): total = total + lax.ppermute(part, 'basis', shift)  4.38 us
    convert_element_type x1, local copies, waits for them, and re-layouts, per_device(): left_panel[None].astype(jnp.float32)  2.97 us
  transfers between devices with their start and end apart: 19, of which 9 were waited for; matrix products, arithmetic and copies ran while one was open for 11% of the time, Pallas kernels for 0%

profile of v13, /device:TPU:0, one launch (start us, length us, event | category | flops | bytes accessed | tf_op | source)
XLA Modules:
  0.0 70.6 jit_solution(11642019599522312887)
XLA Ops:
  0.0 0.8 %select_reduce_fusion = s32[16]{0:T(128)S(1)} fusion(s32[16]{0:T(128)} %param.10), kind=kLoop, calls=%fused_computation.27 | loop fusion | flops 752 | bytes 128 | tf_op jit(solution)/shard_map/reduce_sum | solution.py:57
  0.8 0.7 %fusion.19 = (s32[1024]{0:T(1024)S(1)}, s32[1024]{0:T(1024)S(1)}) fusion(s32[2048]{0:T(1024)} %param.11), kind=kLoop, calls=%fused_computation.46 | loop fusion | bytes 16384 | tf_op jit(solution)/shard_map/slice | solution.py:67
  1.7 4.2 %fusion.13 = f32[64,1024]{1,0:T(8,128)S(1)} fusion(bf16[64,2560]{1,0:T(8,128)(2,1)S(1)} %copy-done, bf16[2560,2048]{1,0:T(8,128)(2,1)} %param.9, s32[1024]{0:T(1024)S(1)} %get-tuple-element.5, s32[2560]{0:T(1024)S(1)} %convert_reduce_fusion), kind=kOutput, calls=%fused_computation.17 | convolution fusion | flops 340787200 | bytes 5847040 | tf_op jit(solution)/shard_map/dot_general | solution.py:69
  5.8 3.0 %collective-permute-start = (f32[64,1024]{1,0:T(8,128)S(1)}, f32[64,1024]{1,0:T(8,128)S(1)}, u32[]{:S(2)}, u32[]{:S(2)}) collective-permute-start(f32[64,1024]{1,0:T(8,128)S(1)} %fusion.13), channel_id=1, source_target_pairs={{0,16},{16,0},{1,17},{17,1},{2,18},{18,2},{3,19},{19,3},{4,20},{20... | collective-permute-start | bytes 786440 | tf_op jit(solution)/shard_map/ppermute | solution.py:73
  8.9 1.8 %fusion.12 = f32[64,1024]{1,0:T(8,128)S(1)} fusion(bf16[64,2560]{1,0:T(8,128)(2,1)S(1)} %copy-done, bf16[2560,2048]{1,0:T(8,128)(2,1)S(1)} %copy-done.4, s32[1024]{0:T(1024)S(1)} %get-tuple-element.6, s32[2560]{0:T(1024)S(1)} %convert_reduce_fusion), kind=kOutput, calls=%fused_computation.16 | convolution fusion | flops 340787200 | bytes 5849088 | tf_op jit(solution)/shard_map/dot_general | solution.py:69
  10.7 1.4 %collective-permute-start.1 = (f32[64,1024]{1,0:T(8,128)S(1)}, f32[64,1024]{1,0:T(8,128)S(1)}, u32[]{:S(2)}, u32[]{:S(2)}) collective-permute-start(f32[64,1024]{1,0:T(8,128)S(1)} %fusion.12), channel_id=1, source_target_pairs={{0,16},{16,0},{1,17},{17,1},{2,18},{18,2},{3,19},{19,3},{4,20},{20... | collective-permute-start | bytes 786440 | tf_op jit(solution)/shard_map/ppermute | solution.py:73
  12.1 1.5 %collective-permute-start.6 = (f32[8,128]{1,0:T(8,128)S(1)}, f32[8,128]{1,0:T(8,128)S(1)}, u32[]{:S(2)}, u32[]{:S(2)}) collective-permute-start(f32[8,128]{1,0:T(8,128)S(1)} %broadcast_in_dim.19), channel_id=1, source_target_pairs={{4,0},{8,4},{12,8},{14,12},{10,14},{6,10},{2,6},{0,2},{5,9},{9,13}... | collective-permute-start | bytes 12296 | tf_op jit(solution)/shard_map/ppermute | solution.py:87
  13.6 0.5 collective-permute-start.3
  14.1 0.6 dynamic_slice.21
  18.0 0.7 fusion.20
  22.0 0.5 slice.23
  23.1 0.5 slice.22
  24.4 1.6 %collective-permute-start.5 = (bf16[64,1024]{1,0:T(8,128)(2,1)S(1)}, bf16[64,1024]{1,0:T(8,128)(2,1)S(1)}, u32[]{:S(2)}, u32[]{:S(2)}) collective-permute-start(bf16[64,1024]{1,0:T(8,128)(2,1)S(1)} %add_convert_fusion.1), channel_id=1, source_target_pairs={{4,0},{8,4},{12,8},{14,12},{10,14},{6,10},{2,6},{0,2},{5,9},{9,13}... | collective-permute-start | bytes 393224 | tf_op jit(solution)/shard_map/ppermute | solution.py:97
  26.5 1.6 %collective-permute-start.7 = (bf16[64,1024]{1,0:T(8,128)(2,1)S(1)}, bf16[64,1024]{1,0:T(8,128)(2,1)S(1)}, u32[]{:S(2)}, u32[]{:S(2)}) collective-permute-start(bf16[64,1024]{1,0:T(8,128)(2,1)S(1)} %add_convert_fusion), channel_id=1, source_target_pairs={{4,0},{8,4},{12,8},{14,12},{10,14},{6,10},{2,6},{0,2},{5,9},{9,13}... | collective-permute-start | bytes 393224 | tf_op jit(solution)/shard_map/ppermute | solution.py:97
  28.8 1.9 %collective-permute-done.5 = bf16[64,1024]{1,0:T(8,128)(2,1)S(1)} collective-permute-done((bf16[64,1024]{1,0:T(8,128)(2,1)S(1)}, bf16[64,1024]{1,0:T(8,128)(2,1)S(1)}, u32[]{:S(2)}, u32[]{:S(2)}) %collective-permute-start.5) | collective-permute-done | bytes 131104 | tf_op jit(solution)/shard_map/ppermute | solution.py:97
  30.8 1.3 %collective-permute-start.10 = (bf16[64,1024]{1,0:T(8,128)(2,1)S(1)}, bf16[64,1024]{1,0:T(8,128)(2,1)S(1)}, u32[]{:S(2)}, u32[]{:S(2)}) collective-permute-start(bf16[64,1024]{1,0:T(8,128)(2,1)S(1)} %collective-permute-done.5), channel_id=1, source_target_pairs={{4,0},{8,4},{12,8},{14,12},{10,14},{6,10},{2,6},{0,2},{5,9},{9,13}... | collective-permute-start | bytes 393224 | tf_op jit(solution)/shard_map/ppermute | solution.py:97
  32.1 0.7 collective-permute-start.8
  32.8 0.8 %collective-permute-done.7 = bf16[64,1024]{1,0:T(8,128)(2,1)S(1)} collective-permute-done((bf16[64,1024]{1,0:T(8,128)(2,1)S(1)}, bf16[64,1024]{1,0:T(8,128)(2,1)S(1)}, u32[]{:S(2)}, u32[]{:S(2)}) %collective-permute-start.7) | collective-permute-done | bytes 131104 | tf_op jit(solution)/shard_map/ppermute | solution.py:97
  33.6 1.0 %collective-permute-start.11 = (bf16[64,1024]{1,0:T(8,128)(2,1)S(1)}, bf16[64,1024]{1,0:T(8,128)(2,1)S(1)}, u32[]{:S(2)}, u32[]{:S(2)}) collective-permute-start(bf16[64,1024]{1,0:T(8,128)(2,1)S(1)} %collective-permute-done.7), channel_id=1, source_target_pairs={{4,0},{8,4},{12,8},{14,12},{10,14},{6,10},{2,6},{0,2},{5,9},{9,13}... | collective-permute-start | bytes 393224 | tf_op jit(solution)/shard_map/ppermute | solution.py:97
  34.8 0.8 %collective-permute-start.9 = (bf16[64,1024]{1,0:T(8,128)(2,1)S(1)}, bf16[64,1024]{1,0:T(8,128)(2,1)S(1)}, u32[]{:S(2)}, u32[]{:S(2)}) collective-permute-start(bf16[64,1024]{1,0:T(8,128)(2,1)S(1)} %collective-permute-done.4), channel_id=1, source_target_pairs={{4,8},{8,12},{12,14},{14,10},{10,6},{6,2},{2,0},{0,4},{5,1},{9,5},... | collective-permute-start | bytes 393224 | tf_op jit(solution)/shard_map/ppermute | solution.py:92
  35.7 0.8 %collective-permute-done.10 = bf16[64,1024]{1,0:T(8,128)(2,1)S(1)} collective-permute-done((bf16[64,1024]{1,0:T(8,128)(2,1)S(1)}, bf16[64,1024]{1,0:T(8,128)(2,1)S(1)}, u32[]{:S(2)}, u32[]{:S(2)}) %collective-permute-start.10) | collective-permute-done | bytes 131104 | tf_op jit(solution)/shard_map/ppermute | solution.py:97
  36.6 1.9 %collective-permute-start.14 = (bf16[64,1024]{1,0:T(8,128)(2,1)S(1)}, bf16[64,1024]{1,0:T(8,128)(2,1)S(1)}, u32[]{:S(2)}, u32[]{:S(2)}) collective-permute-start(bf16[64,1024]{1,0:T(8,128)(2,1)S(1)} %collective-permute-done.10), channel_id=1, source_target_pairs={{4,0},{8,4},{12,8},{14,12},{10,14},{6,10},{2,6},{0,2},{5,9},{9,13}... | collective-permute-start | bytes 393224 | tf_op jit(solution)/shard_map/ppermute | solution.py:97
  38.7 1.3 %collective-permute-done.11 = bf16[64,1024]{1,0:T(8,128)(2,1)S(1)} collective-permute-done((bf16[64,1024]{1,0:T(8,128)(2,1)S(1)}, bf16[64,1024]{1,0:T(8,128)(2,1)S(1)}, u32[]{:S(2)}, u32[]{:S(2)}) %collective-permute-start.11) | collective-permute-done | bytes 131104 | tf_op jit(solution)/shard_map/ppermute | solution.py:97
  40.0 1.3 %collective-permute-start.15 = (bf16[64,1024]{1,0:T(8,128)(2,1)S(1)}, bf16[64,1024]{1,0:T(8,128)(2,1)S(1)}, u32[]{:S(2)}, u32[]{:S(2)}) collective-permute-start(bf16[64,1024]{1,0:T(8,128)(2,1)S(1)} %collective-permute-done.11), channel_id=1, source_target_pairs={{4,0},{8,4},{12,8},{14,12},{10,14},{6,10},{2,6},{0,2},{5,9},{9,13}... | collective-permute-start | bytes 393224 | tf_op jit(solution)/shard_map/ppermute | solution.py:97
  41.3 0.7 %collective-permute-start.13 = (bf16[64,1024]{1,0:T(8,128)(2,1)S(1)}, bf16[64,1024]{1,0:T(8,128)(2,1)S(1)}, u32[]{:S(2)}, u32[]{:S(2)}) collective-permute-start(bf16[64,1024]{1,0:T(8,128)(2,1)S(1)} %collective-permute-done.9), channel_id=1, source_target_pairs={{4,8},{8,12},{12,14},{14,10},{10,6},{6,2},{2,0},{0,4},{5,1},{9,5},... | collective-permute-start | bytes 393224 | tf_op jit(solution)/shard_map/ppermute | solution.py:92
  42.1 1.4 %collective-permute-done.12 = bf16[64,1024]{1,0:T(8,128)(2,1)S(1)} collective-permute-done((bf16[64,1024]{1,0:T(8,128)(2,1)S(1)}, bf16[64,1024]{1,0:T(8,128)(2,1)S(1)}, u32[]{:S(2)}, u32[]{:S(2)}) %collective-permute-start.12) | collective-permute-done | bytes 131104 | tf_op jit(solution)/shard_map/ppermute | solution.py:92
  43.7 2.5 %collective-permute-done.13 = bf16[64,1024]{1,0:T(8,128)(2,1)S(1)} collective-permute-done((bf16[64,1024]{1,0:T(8,128)(2,1)S(1)}, bf16[64,1024]{1,0:T(8,128)(2,1)S(1)}, u32[]{:S(2)}, u32[]{:S(2)}) %collective-permute-start.13) | collective-permute-done | bytes 131104 | tf_op jit(solution)/shard_map/ppermute | solution.py:92
  46.2 0.7 %collective-permute-start.17 = (bf16[64,1024]{1,0:T(8,128)(2,1)S(1)}, bf16[64,1024]{1,0:T(8,128)(2,1)S(1)}, u32[]{:S(2)}, u32[]{:S(2)}) collective-permute-start(bf16[64,1024]{1,0:T(8,128)(2,1)S(1)} %collective-permute-done.13), channel_id=1, source_target_pairs={{4,8},{8,12},{12,14},{14,10},{10,6},{6,2},{2,0},{0,4},{5,1},{9,5},... | collective-permute-start | bytes 393224 | tf_op jit(solution)/shard_map/ppermute | solution.py:92
  47.1 1.3 %collective-permute-done.16 = bf16[64,1024]{1,0:T(8,128)(2,1)S(1)} collective-permute-done((bf16[64,1024]{1,0:T(8,128)(2,1)S(1)}, bf16[64,1024]{1,0:T(8,128)(2,1)S(1)}, u32[]{:S(2)}, u32[]{:S(2)}) %collective-permute-start.16) | collective-permute-done | bytes 131104 | tf_op jit(solution)/shard_map/ppermute | solution.py:92
  48.4 2.8 %collective-permute-done.17 = bf16[64,1024]{1,0:T(8,128)(2,1)S(1)} collective-permute-done((bf16[64,1024]{1,0:T(8,128)(2,1)S(1)}, bf16[64,1024]{1,0:T(8,128)(2,1)S(1)}, u32[]{:S(2)}, u32[]{:S(2)}) %collective-permute-start.17) | collective-permute-done | bytes 131104 | tf_op jit(solution)/shard_map/ppermute | solution.py:92
  51.5 3.0 %copy.10 = f32[512,2048]{0,1:T(8,128)} copy(bf16[512,2048]{1,0:T(8,128)(2,1)S(1)} %constant_dynamic-update-slice_fusion.7) | data formatting | bytes 6291456 | tf_op jit(solution)/shard_map/convert_element_type | solution.py:114
  54.4 16.2 %convolution_multiply_fusion = f32[8,2048,512]{2,1,0:T(8,128)} fusion(f32[512,2048]{0,1:T(8,128)} %copy.10, f32[8,512]{1,0:T(8,128)S(1)} %subtract_divide_fusion, bf16[512,512]{1,0:T(8,128)(2,1)S(1)} %constant_dynamic-slice_fusion, bf16[512,512]{1,0:T(8,128)(2,1)S(1)} %collective-permute-done.18, pred[]{:T(512)S(6)} %eq.40), kind=kOutput, calls=%fused_computation.1 | convolution fusion | flops 8615362560 | bytes 38813696 | tf_op jit(solution)/shard_map/ekc,kd->ecd/dot_general | solution.py:115
  (51 shorter events, 2.6 us)
Async XLA Ops:
  0.0 1.6 %copy-start = (bf16[64,2560]{1,0:T(8,128)(2,1)S(1)}, bf16[64,2560]{1,0:T(8,128)(2,1)}, u32[]{:S(2)}) copy-start(bf16[64,2560]{1,0:T(8,128)(2,1)} %param.8) | copy-start | bytes 983044
  1.7 7.2 %copy-start.4 = (bf16[2560,2048]{1,0:T(8,128)(2,1)S(1)}, bf16[2560,2048]{1,0:T(8,128)(2,1)}, u32[]{:S(2)}) copy-start(bf16[2560,2048]{1,0:T(8,128)(2,1)} %param.9) | copy-start | bytes 31457284
  5.8 18.5 %collective-permute-start = (f32[64,1024]{1,0:T(8,128)S(1)}, f32[64,1024]{1,0:T(8,128)S(1)}, u32[]{:S(2)}, u32[]{:S(2)}) collective-permute-start(f32[64,1024]{1,0:T(8,128)S(1)} %fusion.13), channel_id=1, source_target_pairs={{0,16},{16,0},{1,17},{17,1},{2,18},{18,2},{3,19},{19,3},{4,20},{20... | collective-permute-start | bytes 786440 | tf_op jit(solution)/shard_map/ppermute | solution.py:73
  8.9 5.2 %copy-start.5 = (s32[8]{0:T(128)S(1)}, s32[8]{0:T(128)}, u32[]{:S(2)}) copy-start(s32[8]{0:T(128)} %constant.106.clone) | copy-start | bytes 100
  8.9 9.1 %copy-start.1 = (s32[8]{0:T(128)S(1)}, s32[8]{0:T(128)}, u32[]{:S(2)}) copy-start(s32[8]{0:T(128)} %constant.105.clone) | copy-start | bytes 100
  10.7 15.7 %collective-permute-start.1 = (f32[64,1024]{1,0:T(8,128)S(1)}, f32[64,1024]{1,0:T(8,128)S(1)}, u32[]{:S(2)}, u32[]{:S(2)}) collective-permute-start(f32[64,1024]{1,0:T(8,128)S(1)} %fusion.12), channel_id=1, source_target_pairs={{0,16},{16,0},{1,17},{17,1},{2,18},{18,2},{3,19},{19,3},{4,20},{20... | collective-permute-start | bytes 786440 | tf_op jit(solution)/shard_map/ppermute | solution.py:73
  12.1 9.9 %collective-permute-start.6 = (f32[8,128]{1,0:T(8,128)S(1)}, f32[8,128]{1,0:T(8,128)S(1)}, u32[]{:S(2)}, u32[]{:S(2)}) collective-permute-start(f32[8,128]{1,0:T(8,128)S(1)} %broadcast_in_dim.19), channel_id=1, source_target_pairs={{4,0},{8,4},{12,8},{14,12},{10,14},{6,10},{2,6},{0,2},{5,9},{9,13}... | collective-permute-start | bytes 12296 | tf_op jit(solution)/shard_map/ppermute | solution.py:87
  13.6 9.6 %collective-permute-start.3 = (f32[8,128]{1,0:T(8,128)S(1)}, f32[8,128]{1,0:T(8,128)S(1)}, u32[]{:S(2)}, u32[]{:S(2)}) collective-permute-start(f32[8,128]{1,0:T(8,128)S(1)} %broadcast_in_dim.19), channel_id=1, source_target_pairs={{4,8},{8,12},{12,14},{14,10},{10,6},{6,2},{2,0},{0,4},{5,1},{9,5},... | collective-permute-start | bytes 12296 | tf_op jit(solution)/shard_map/ppermute | solution.py:86
  24.4 6.4 %collective-permute-start.5 = (bf16[64,1024]{1,0:T(8,128)(2,1)S(1)}, bf16[64,1024]{1,0:T(8,128)(2,1)S(1)}, u32[]{:S(2)}, u32[]{:S(2)}) collective-permute-start(bf16[64,1024]{1,0:T(8,128)(2,1)S(1)} %add_convert_fusion.1), channel_id=1, source_target_pairs={{4,0},{8,4},{12,8},{14,12},{10,14},{6,10},{2,6},{0,2},{5,9},{9,13}... | collective-permute-start | bytes 393224 | tf_op jit(solution)/shard_map/ppermute | solution.py:97
  25.9 6.2 %collective-permute-start.2 = (bf16[64,1024]{1,0:T(8,128)(2,1)S(1)}, bf16[64,1024]{1,0:T(8,128)(2,1)S(1)}, u32[]{:S(2)}, u32[]{:S(2)}) collective-permute-start(bf16[64,1024]{1,0:T(8,128)(2,1)S(1)} %add_convert_fusion.1), channel_id=1, source_target_pairs={{4,8},{8,12},{12,14},{14,10},{10,6},{6,2},{2,0},{0,4},{5,1},{9,5},... | collective-permute-start | bytes 393224 | tf_op jit(solution)/shard_map/ppermute | solution.py:92
  26.5 7.1 %collective-permute-start.7 = (bf16[64,1024]{1,0:T(8,128)(2,1)S(1)}, bf16[64,1024]{1,0:T(8,128)(2,1)S(1)}, u32[]{:S(2)}, u32[]{:S(2)}) collective-permute-start(bf16[64,1024]{1,0:T(8,128)(2,1)S(1)} %add_convert_fusion), channel_id=1, source_target_pairs={{4,0},{8,4},{12,8},{14,12},{10,14},{6,10},{2,6},{0,2},{5,9},{9,13}... | collective-permute-start | bytes 393224 | tf_op jit(solution)/shard_map/ppermute | solution.py:97
  28.1 6.7 %collective-permute-start.4 = (bf16[64,1024]{1,0:T(8,128)(2,1)S(1)}, bf16[64,1024]{1,0:T(8,128)(2,1)S(1)}, u32[]{:S(2)}, u32[]{:S(2)}) collective-permute-start(bf16[64,1024]{1,0:T(8,128)(2,1)S(1)} %add_convert_fusion), channel_id=1, source_target_pairs={{4,8},{8,12},{12,14},{14,10},{10,6},{6,2},{2,0},{0,4},{5,1},{9,5},... | collective-permute-start | bytes 393224 | tf_op jit(solution)/shard_map/ppermute | solution.py:92
  30.8 5.8 %collective-permute-start.10 = (bf16[64,1024]{1,0:T(8,128)(2,1)S(1)}, bf16[64,1024]{1,0:T(8,128)(2,1)S(1)}, u32[]{:S(2)}, u32[]{:S(2)}) collective-permute-start(bf16[64,1024]{1,0:T(8,128)(2,1)S(1)} %collective-permute-done.5), channel_id=1, source_target_pairs={{4,0},{8,4},{12,8},{14,12},{10,14},{6,10},{2,6},{0,2},{5,9},{9,13}... | collective-permute-start | bytes 393224 | tf_op jit(solution)/shard_map/ppermute | solution.py:97
  32.1 6.3 %collective-permute-start.8 = (bf16[64,1024]{1,0:T(8,128)(2,1)S(1)}, bf16[64,1024]{1,0:T(8,128)(2,1)S(1)}, u32[]{:S(2)}, u32[]{:S(2)}) collective-permute-start(bf16[64,1024]{1,0:T(8,128)(2,1)S(1)} %collective-permute-done.2), channel_id=1, source_target_pairs={{4,8},{8,12},{12,14},{14,10},{10,6},{6,2},{2,0},{0,4},{5,1},{9,5},... | collective-permute-start | bytes 393224 | tf_op jit(solution)/shard_map/ppermute | solution.py:92
  33.6 6.4 %collective-permute-start.11 = (bf16[64,1024]{1,0:T(8,128)(2,1)S(1)}, bf16[64,1024]{1,0:T(8,128)(2,1)S(1)}, u32[]{:S(2)}, u32[]{:S(2)}) collective-permute-start(bf16[64,1024]{1,0:T(8,128)(2,1)S(1)} %collective-permute-done.7), channel_id=1, source_target_pairs={{4,0},{8,4},{12,8},{14,12},{10,14},{6,10},{2,6},{0,2},{5,9},{9,13}... | collective-permute-start | bytes 393224 | tf_op jit(solution)/shard_map/ppermute | solution.py:97
  34.8 6.5 %collective-permute-start.9 = (bf16[64,1024]{1,0:T(8,128)(2,1)S(1)}, bf16[64,1024]{1,0:T(8,128)(2,1)S(1)}, u32[]{:S(2)}, u32[]{:S(2)}) collective-permute-start(bf16[64,1024]{1,0:T(8,128)(2,1)S(1)} %collective-permute-done.4), channel_id=1, source_target_pairs={{4,8},{8,12},{12,14},{14,10},{10,6},{6,2},{2,0},{0,4},{5,1},{9,5},... | collective-permute-start | bytes 393224 | tf_op jit(solution)/shard_map/ppermute | solution.py:92
  35.7 15.7 %copy-start.2 = (f32[512]{0:T(512)S(1)}, f32[512]{0:T(512)}, u32[]{:S(2)}) copy-start(f32[512]{0:T(512)} %param.12) | copy-start | bytes 6148
  35.7 15.7 %copy-start.3 = (f32[8]{0:T(128)S(1)}, f32[8]{0:T(128)}, u32[]{:S(2)}) copy-start(f32[8]{0:T(128)} %param.13) | copy-start | bytes 100
  36.6 10.5 %collective-permute-start.14 = (bf16[64,1024]{1,0:T(8,128)(2,1)S(1)}, bf16[64,1024]{1,0:T(8,128)(2,1)S(1)}, u32[]{:S(2)}, u32[]{:S(2)}) collective-permute-start(bf16[64,1024]{1,0:T(8,128)(2,1)S(1)} %collective-permute-done.10), channel_id=1, source_target_pairs={{4,0},{8,4},{12,8},{14,12},{10,14},{6,10},{2,6},{0,2},{5,9},{9,13}... | collective-permute-start | bytes 393224 | tf_op jit(solution)/shard_map/ppermute | solution.py:97
  38.5 5.0 %collective-permute-start.12 = (bf16[64,1024]{1,0:T(8,128)(2,1)S(1)}, bf16[64,1024]{1,0:T(8,128)(2,1)S(1)}, u32[]{:S(2)}, u32[]{:S(2)}) collective-permute-start(bf16[64,1024]{1,0:T(8,128)(2,1)S(1)} %collective-permute-done.8), channel_id=1, source_target_pairs={{4,8},{8,12},{12,14},{14,10},{10,6},{6,2},{2,0},{0,4},{5,1},{9,5},... | collective-permute-start | bytes 393224 | tf_op jit(solution)/shard_map/ppermute | solution.py:92
  40.0 7.1 %collective-permute-start.15 = (bf16[64,1024]{1,0:T(8,128)(2,1)S(1)}, bf16[64,1024]{1,0:T(8,128)(2,1)S(1)}, u32[]{:S(2)}, u32[]{:S(2)}) collective-permute-start(bf16[64,1024]{1,0:T(8,128)(2,1)S(1)} %collective-permute-done.11), channel_id=1, source_target_pairs={{4,0},{8,4},{12,8},{14,12},{10,14},{6,10},{2,6},{0,2},{5,9},{9,13}... | collective-permute-start | bytes 393224 | tf_op jit(solution)/shard_map/ppermute | solution.py:97
  41.3 5.0 %collective-permute-start.13 = (bf16[64,1024]{1,0:T(8,128)(2,1)S(1)}, bf16[64,1024]{1,0:T(8,128)(2,1)S(1)}, u32[]{:S(2)}, u32[]{:S(2)}) collective-permute-start(bf16[64,1024]{1,0:T(8,128)(2,1)S(1)} %collective-permute-done.9), channel_id=1, source_target_pairs={{4,8},{8,12},{12,14},{14,10},{10,6},{6,2},{2,0},{0,4},{5,1},{9,5},... | collective-permute-start | bytes 393224 | tf_op jit(solution)/shard_map/ppermute | solution.py:92
  43.4 5.0 %collective-permute-start.16 = (bf16[64,1024]{1,0:T(8,128)(2,1)S(1)}, bf16[64,1024]{1,0:T(8,128)(2,1)S(1)}, u32[]{:S(2)}, u32[]{:S(2)}) collective-permute-start(bf16[64,1024]{1,0:T(8,128)(2,1)S(1)} %collective-permute-done.12), channel_id=1, source_target_pairs={{4,8},{8,12},{12,14},{14,10},{10,6},{6,2},{2,0},{0,4},{5,1},{9,5},... | collective-permute-start | bytes 393224 | tf_op jit(solution)/shard_map/ppermute | solution.py:92
  46.2 5.0 %collective-permute-start.17 = (bf16[64,1024]{1,0:T(8,128)(2,1)S(1)}, bf16[64,1024]{1,0:T(8,128)(2,1)S(1)}, u32[]{:S(2)}, u32[]{:S(2)}) collective-permute-start(bf16[64,1024]{1,0:T(8,128)(2,1)S(1)} %collective-permute-done.13), channel_id=1, source_target_pairs={{4,8},{8,12},{12,14},{14,10},{10,6},{6,2},{2,0},{0,4},{5,1},{9,5},... | collective-permute-start | bytes 393224 | tf_op jit(solution)/shard_map/ppermute | solution.py:92
  51.3 3.2 %collective-permute-start.18 = (bf16[512,512]{1,0:T(8,128)(2,1)S(1)}, bf16[512,512]{1,0:T(8,128)(2,1)S(1)}, u32[]{:S(2)}, u32[]{:S(2)}) collective-permute-start(bf16[512,512]{1,0:T(8,128)(2,1)S(1)} %constant_dynamic-slice_fusion), channel_id=1, source_target_pairs={{0,1},{1,0},{2,3},{3,2},{4,5},{5,4},{6,7},{7,6},{8,9},{9,8},{10,11... | collective-permute-start | bytes 1572872 | tf_op jit(solution)/shard_map/ppermute | solution.py:107

commit v14 on v10

--- a/solution.py
+++ b/solution.py
@@ -83,7 +83,7 @@
         n_split = 2 if amp.shape[1] % 256 == 0 else 1
         split_w = amp.shape[1] // n_split
         longs = [amp[:, p * split_w:(p + 1) * split_w] for p in range(n_split)]
-        shorts = list(longs)
+        shorts = [amp]
         for s in range(max(n_fwd, n_bwd)):
             if s < n_fwd:
                 longs = [lax.ppermute(x, ("eig", "chan"), long_pairs) for x in longs]
@@ -93,8 +93,8 @@
             if s < n_bwd:
                 shorts = [lax.ppermute(x, ("eig", "chan"), short_pairs) for x in shorts]
                 origin = cycle_arr[(pos + sign * (s + 1)) % n_ring]
-                for p, x in enumerate(shorts):
-                    left_panel = lax.dynamic_update_slice(left_panel, x, (origin * k_here, p * split_w))
+                for x in shorts:
+                    left_panel = lax.dynamic_update_slice(left_panel, x, (origin * k_here, 0))
         own_width = left_panel.shape[1]
         col_width = own_width * n_chan // n_eig
         ratio = n_eig // n_chan

time: 69.1 us -> 74.7 us (1.081)
  waiting for transfers between devices: 12.6 us -> 16.7 us
  starting transfers between devices: 17.9 us -> 19.7 us
    ppermute x8, starting transfers between devices: 5.26 us -> 13 us  [per_device(): longs = [lax.ppermute(x, ('eig', 'chan'), long_pairs) for x in longs]]
    ppermute x2, waiting for transfers between devices: 0.01 us -> 6.55 us  [per_device(): total = total + lax.ppermute(part, 'basis', shift)]
    ppermute x6 -> x3, starting transfers between devices: 8.14 us -> 2.19 us  [per_device(): shorts = [lax.ppermute(x, ('eig', 'chan'), short_pairs) for x in shorts]]
    ppermute x8, waiting for transfers between devices: 7.71 us -> 4.81 us  [per_device(): longs = [lax.ppermute(x, ('eig', 'chan'), long_pairs) for x in longs]]
    ppermute x6 -> x3, waiting for transfers between devices: 4.92 us -> 5.33 us  [per_device(): shorts = [lax.ppermute(x, ('eig', 'chan'), short_pairs) for x in shorts]]
  transfers between devices with their start and end apart: 17 -> 14, of which waited for: 10 -> 7; matrix products, arithmetic and copies ran while one was open for 10% -> 9% of each run, Pallas kernels for 0% -> 0%
where the time goes in v14:
time: 74.7 us; the launch traced here: 74.4 us
  matrix products  22.1 us (30%)
  starting transfers between devices  19.7 us (26%)
  waiting for transfers between devices  16.7 us (22%)
  between operations  9.28 us (12%)
  local copies, waits for them, and re-layouts  5.49 us (7%)
  other arithmetic  1.11 us (1%)
    dot_general x1, matrix products, per_device(): jnp.einsum('ekc,kd->ecd', scaled, right_panel, preferred_element_type=jnp...  16.2 us
    ppermute x8, starting transfers between devices, per_device(): longs = [lax.ppermute(x, ('eig', 'chan'), long_pairs) for x in longs]  13 us
    ppermute x2, waiting for transfers between devices, per_device(): total = total + lax.ppermute(part, 'basis', shift)  6.55 us
    dot_general x2, matrix products, per_device(): part = jnp.dot(eigvecs, masked, preferred_element_type=jnp.float32)  5.99 us
    ppermute x3, waiting for transfers between devices, per_device(): shorts = [lax.ppermute(x, ('eig', 'chan'), short_pairs) for x in shorts]  5.33 us
    ppermute x8, waiting for transfers between devices, per_device(): longs = [lax.ppermute(x, ('eig', 'chan'), long_pairs) for x in longs]  4.81 us
    ppermute x2, starting transfers between devices, per_device(): total = total + lax.ppermute(part, 'basis', shift)  4.38 us
    convert_element_type x1, local copies, waits for them, and re-layouts, per_device(): left_panel[None].astype(jnp.float32)  3 us
  transfers between devices with their start and end apart: 14, of which 7 were waited for; matrix products, arithmetic and copies ran while one was open for 9% of the time, Pallas kernels for 0%

profile of v14, /device:TPU:0, one launch (start us, length us, event | category | flops | bytes accessed | tf_op | source)
XLA Modules:
  0.0 74.4 jit_solution(7034322486331630144)
XLA Ops:
  0.0 0.8 %select_reduce_fusion = s32[16]{0:T(128)S(1)} fusion(s32[16]{0:T(128)} %param.10), kind=kLoop, calls=%fused_computation.27 | loop fusion | flops 752 | bytes 128 | tf_op jit(solution)/shard_map/reduce_sum | solution.py:57
  0.8 0.7 fusion.19
  1.5 0.1 convert_reduce_fusion
  1.7 4.2 %fusion.13 = f32[64,1024]{1,0:T(8,128)S(1)} fusion(bf16[64,2560]{1,0:T(8,128)(2,1)S(1)} %copy-done, bf16[2560,2048]{1,0:T(8,128)(2,1)} %param.9, s32[1024]{0:T(1024)S(1)} %get-tuple-element.7, s32[2560]{0:T(1024)S(1)} %convert_reduce_fusion), kind=kOutput, calls=%fused_computation.17 | convolution fusion | flops 340787200 | bytes 5847040 | tf_op jit(solution)/shard_map/dot_general | solution.py:69
  5.8 3.0 %collective-permute-start = (f32[64,1024]{1,0:T(8,128)S(1)}, f32[64,1024]{1,0:T(8,128)S(1)}, u32[]{:S(2)}, u32[]{:S(2)}) collective-permute-start(f32[64,1024]{1,0:T(8,128)S(1)} %fusion.13), channel_id=1, source_target_pairs={{0,16},{16,0},{1,17},{17,1},{2,18},{18,2},{3,19},{19,3},{4,20},{20... | collective-permute-start | bytes 786440 | tf_op jit(solution)/shard_map/ppermute | solution.py:73
  8.9 1.8 %fusion.12 = f32[64,1024]{1,0:T(8,128)S(1)} fusion(bf16[64,2560]{1,0:T(8,128)(2,1)S(1)} %copy-done, bf16[2560,2048]{1,0:T(8,128)(2,1)S(1)} %copy-done.4, s32[1024]{0:T(1024)S(1)} %get-tuple-element.8, s32[2560]{0:T(1024)S(1)} %convert_reduce_fusion), kind=kOutput, calls=%fused_computation.16 | convolution fusion | flops 340787200 | bytes 5849088 | tf_op jit(solution)/shard_map/dot_general | solution.py:69
  10.7 1.4 %collective-permute-start.1 = (f32[64,1024]{1,0:T(8,128)S(1)}, f32[64,1024]{1,0:T(8,128)S(1)}, u32[]{:S(2)}, u32[]{:S(2)}) collective-permute-start(f32[64,1024]{1,0:T(8,128)S(1)} %fusion.12), channel_id=1, source_target_pairs={{0,16},{16,0},{1,17},{17,1},{2,18},{18,2},{3,19},{19,3},{4,20},{20... | collective-permute-start | bytes 786440 | tf_op jit(solution)/shard_map/ppermute | solution.py:73
  12.1 4.0 %collective-permute-done = f32[64,1024]{1,0:T(8,128)S(1)} collective-permute-done((f32[64,1024]{1,0:T(8,128)S(1)}, f32[64,1024]{1,0:T(8,128)S(1)}, u32[]{:S(2)}, u32[]{:S(2)}) %collective-permute-start) | collective-permute-done | bytes 262176 | tf_op jit(solution)/shard_map/ppermute | solution.py:73
  16.1 2.2 %collective-permute-start.2 = (bf16[64,1024]{1,0:T(8,128)(2,1)S(1)}, bf16[64,1024]{1,0:T(8,128)(2,1)S(1)}, u32[]{:S(2)}, u32[]{:S(2)}) collective-permute-start(bf16[64,1024]{1,0:T(8,128)(2,1)S(1)} %add_convert_fusion.1), channel_id=1, source_target_pairs={{4,8},{8,12},{12,14},{14,10},{10,6},{6,2},{2,0},{0,4},{5,1},{9,5},... | collective-permute-start | bytes 393224 | tf_op jit(solution)/shard_map/ppermute | solution.py:89
  18.2 2.6 %collective-permute-done.1 = f32[64,1024]{1,0:T(8,128)S(1)} collective-permute-done((f32[64,1024]{1,0:T(8,128)S(1)}, f32[64,1024]{1,0:T(8,128)S(1)}, u32[]{:S(2)}, u32[]{:S(2)}) %collective-permute-start.1) | collective-permute-done | bytes 262176 | tf_op jit(solution)/shard_map/ppermute | solution.py:73
  20.8 1.9 %collective-permute-start.3 = (bf16[64,1024]{1,0:T(8,128)(2,1)S(1)}, bf16[64,1024]{1,0:T(8,128)(2,1)S(1)}, u32[]{:S(2)}, u32[]{:S(2)}) collective-permute-start(bf16[64,1024]{1,0:T(8,128)(2,1)S(1)} %add_convert_fusion), channel_id=1, source_target_pairs={{4,8},{8,12},{12,14},{14,10},{10,6},{6,2},{2,0},{0,4},{5,1},{9,5},... | collective-permute-start | bytes 393224 | tf_op jit(solution)/shard_map/ppermute | solution.py:89
  22.7 0.2 broadcast_in_dim.14
  23.0 0.3 collective-permute-start.4
  23.3 0.6 dynamic_slice.27
  28.5 0.7 fusion.20
  33.6 1.9 %collective-permute-start.5 = (bf16[64,1024]{1,0:T(8,128)(2,1)S(1)}, bf16[64,1024]{1,0:T(8,128)(2,1)S(1)}, u32[]{:S(2)}, u32[]{:S(2)}) collective-permute-start(bf16[64,1024]{1,0:T(8,128)(2,1)S(1)} %collective-permute-done.2), channel_id=1, source_target_pairs={{4,8},{8,12},{12,14},{14,10},{10,6},{6,2},{2,0},{0,4},{5,1},{9,5},... | collective-permute-start | bytes 393224 | tf_op jit(solution)/shard_map/ppermute | solution.py:89
  35.5 1.6 %collective-permute-start.6 = (bf16[64,1024]{1,0:T(8,128)(2,1)S(1)}, bf16[64,1024]{1,0:T(8,128)(2,1)S(1)}, u32[]{:S(2)}, u32[]{:S(2)}) collective-permute-start(bf16[64,1024]{1,0:T(8,128)(2,1)S(1)} %collective-permute-done.3), channel_id=1, source_target_pairs={{4,8},{8,12},{12,14},{14,10},{10,6},{6,2},{2,0},{0,4},{5,1},{9,5},... | collective-permute-start | bytes 393224 | tf_op jit(solution)/shard_map/ppermute | solution.py:89
  37.1 1.5 %collective-permute-done.5 = bf16[64,1024]{1,0:T(8,128)(2,1)S(1)} collective-permute-done((bf16[64,1024]{1,0:T(8,128)(2,1)S(1)}, bf16[64,1024]{1,0:T(8,128)(2,1)S(1)}, u32[]{:S(2)}, u32[]{:S(2)}) %collective-permute-start.5) | collective-permute-done | bytes 131104 | tf_op jit(solution)/shard_map/ppermute | solution.py:89
  38.6 1.8 %collective-permute-start.8 = (bf16[64,1024]{1,0:T(8,128)(2,1)S(1)}, bf16[64,1024]{1,0:T(8,128)(2,1)S(1)}, u32[]{:S(2)}, u32[]{:S(2)}) collective-permute-start(bf16[64,1024]{1,0:T(8,128)(2,1)S(1)} %collective-permute-done.5), channel_id=1, source_target_pairs={{4,8},{8,12},{12,14},{14,10},{10,6},{6,2},{2,0},{0,4},{5,1},{9,5},... | collective-permute-start | bytes 393224 | tf_op jit(solution)/shard_map/ppermute | solution.py:89
  40.5 1.6 %collective-permute-start.9 = (bf16[64,1024]{1,0:T(8,128)(2,1)S(1)}, bf16[64,1024]{1,0:T(8,128)(2,1)S(1)}, u32[]{:S(2)}, u32[]{:S(2)}) collective-permute-start(bf16[64,1024]{1,0:T(8,128)(2,1)S(1)} %collective-permute-done.6), channel_id=1, source_target_pairs={{4,8},{8,12},{12,14},{14,10},{10,6},{6,2},{2,0},{0,4},{5,1},{9,5},... | collective-permute-start | bytes 393224 | tf_op jit(solution)/shard_map/ppermute | solution.py:89
  42.0 0.4 collective-permute-start.7
  42.6 2.4 %collective-permute-done.8 = bf16[64,1024]{1,0:T(8,128)(2,1)S(1)} collective-permute-done((bf16[64,1024]{1,0:T(8,128)(2,1)S(1)}, bf16[64,1024]{1,0:T(8,128)(2,1)S(1)}, u32[]{:S(2)}, u32[]{:S(2)}) %collective-permute-start.8) | collective-permute-done | bytes 131104 | tf_op jit(solution)/shard_map/ppermute | solution.py:89
  45.0 1.4 %collective-permute-start.11 = (bf16[64,1024]{1,0:T(8,128)(2,1)S(1)}, bf16[64,1024]{1,0:T(8,128)(2,1)S(1)}, u32[]{:S(2)}, u32[]{:S(2)}) collective-permute-start(bf16[64,1024]{1,0:T(8,128)(2,1)S(1)} %collective-permute-done.8), channel_id=1, source_target_pairs={{4,8},{8,12},{12,14},{14,10},{10,6},{6,2},{2,0},{0,4},{5,1},{9,5},... | collective-permute-start | bytes 393224 | tf_op jit(solution)/shard_map/ppermute | solution.py:89
  46.4 0.9 %collective-permute-done.9 = bf16[64,1024]{1,0:T(8,128)(2,1)S(1)} collective-permute-done((bf16[64,1024]{1,0:T(8,128)(2,1)S(1)}, bf16[64,1024]{1,0:T(8,128)(2,1)S(1)}, u32[]{:S(2)}, u32[]{:S(2)}) %collective-permute-start.9) | collective-permute-done | bytes 131104 | tf_op jit(solution)/shard_map/ppermute | solution.py:89
  47.3 0.7 collective-permute-start.12
  48.0 0.5 collective-permute-done.7
  48.5 1.5 %collective-permute-start.10 = (bf16[64,2048]{1,0:T(8,128)(2,1)S(1)}, bf16[64,2048]{1,0:T(8,128)(2,1)S(1)}, u32[]{:S(2)}, u32[]{:S(2)}) collective-permute-start(bf16[64,2048]{1,0:T(8,128)(2,1)S(1)} %collective-permute-done.7), channel_id=1, source_target_pairs={{4,0},{8,4},{12,8},{14,12},{10,14},{6,10},{2,6},{0,2},{5,9},{9,13}... | collective-permute-start | bytes 786440 | tf_op jit(solution)/shard_map/ppermute | solution.py:94
  50.1 4.8 %collective-permute-done.10 = bf16[64,2048]{1,0:T(8,128)(2,1)S(1)} collective-permute-done((bf16[64,2048]{1,0:T(8,128)(2,1)S(1)}, bf16[64,2048]{1,0:T(8,128)(2,1)S(1)}, u32[]{:S(2)}, u32[]{:S(2)}) %collective-permute-start.10) | collective-permute-done | bytes 262176 | tf_op jit(solution)/shard_map/ppermute | solution.py:94
  55.0 0.1 collective-permute-start.13
  55.1 0.1 subtract_divide_fusion
  55.2 3.0 %copy.10 = f32[512,2048]{0,1:T(8,128)} copy(bf16[512,2048]{1,0:T(8,128)(2,1)S(1)} %constant_dynamic-update-slice_fusion.8) | data formatting | bytes 6291456 | tf_op jit(solution)/shard_map/convert_element_type | solution.py:111
  58.2 16.2 %convolution_multiply_fusion = f32[8,2048,512]{2,1,0:T(8,128)} fusion(f32[512,2048]{0,1:T(8,128)} %copy.10, f32[8,512]{1,0:T(8,128)S(1)} %subtract_divide_fusion, bf16[512,512]{1,0:T(8,128)(2,1)S(1)} %constant_dynamic-slice_fusion, bf16[512,512]{1,0:T(8,128)(2,1)S(1)} %collective-permute-done.13, pred[]{:T(512)S(6)} %eq.42), kind=kOutput, calls=%fused_computation.1 | convolution fusion | flops 8615362560 | bytes 38813696 | tf_op jit(solution)/shard_map/ekc,kd->ecd/dot_general | solution.py:112
  (35 shorter events, 0.4 us)
Async XLA Ops:
  0.0 1.6 %copy-start = (bf16[64,2560]{1,0:T(8,128)(2,1)S(1)}, bf16[64,2560]{1,0:T(8,128)(2,1)}, u32[]{:S(2)}) copy-start(bf16[64,2560]{1,0:T(8,128)(2,1)} %param.8) | copy-start | bytes 983044
  1.7 7.2 %copy-start.4 = (bf16[2560,2048]{1,0:T(8,128)(2,1)S(1)}, bf16[2560,2048]{1,0:T(8,128)(2,1)}, u32[]{:S(2)}) copy-start(bf16[2560,2048]{1,0:T(8,128)(2,1)} %param.9) | copy-start | bytes 31457284
  5.8 10.2 %collective-permute-start = (f32[64,1024]{1,0:T(8,128)S(1)}, f32[64,1024]{1,0:T(8,128)S(1)}, u32[]{:S(2)}, u32[]{:S(2)}) collective-permute-start(f32[64,1024]{1,0:T(8,128)S(1)} %fusion.13), channel_id=1, source_target_pairs={{0,16},{16,0},{1,17},{17,1},{2,18},{18,2},{3,19},{19,3},{4,20},{20... | collective-permute-start | bytes 786440 | tf_op jit(solution)/shard_map/ppermute | solution.py:73
  10.7 10.1 %collective-permute-start.1 = (f32[64,1024]{1,0:T(8,128)S(1)}, f32[64,1024]{1,0:T(8,128)S(1)}, u32[]{:S(2)}, u32[]{:S(2)}) collective-permute-start(f32[64,1024]{1,0:T(8,128)S(1)} %fusion.12), channel_id=1, source_target_pairs={{0,16},{16,0},{1,17},{17,1},{2,18},{18,2},{3,19},{19,3},{4,20},{20... | collective-permute-start | bytes 786440 | tf_op jit(solution)/shard_map/ppermute | solution.py:73
  12.1 11.2 %copy-start.5 = (s32[8]{0:T(128)S(1)}, s32[8]{0:T(128)}, u32[]{:S(2)}) copy-start(s32[8]{0:T(128)} %constant.113.clone) | copy-start | bytes 100
  12.1 16.5 %copy-start.1 = (s32[8]{0:T(128)S(1)}, s32[8]{0:T(128)}, u32[]{:S(2)}) copy-start(s32[8]{0:T(128)} %constant.112.clone) | copy-start | bytes 100
  16.1 17.5 %collective-permute-start.2 = (bf16[64,1024]{1,0:T(8,128)(2,1)S(1)}, bf16[64,1024]{1,0:T(8,128)(2,1)S(1)}, u32[]{:S(2)}, u32[]{:S(2)}) collective-permute-start(bf16[64,1024]{1,0:T(8,128)(2,1)S(1)} %add_convert_fusion.1), channel_id=1, source_target_pairs={{4,8},{8,12},{12,14},{14,10},{10,6},{6,2},{2,0},{0,4},{5,1},{9,5},... | collective-permute-start | bytes 393224 | tf_op jit(solution)/shard_map/ppermute | solution.py:89
  20.8 14.7 %collective-permute-start.3 = (bf16[64,1024]{1,0:T(8,128)(2,1)S(1)}, bf16[64,1024]{1,0:T(8,128)(2,1)S(1)}, u32[]{:S(2)}, u32[]{:S(2)}) collective-permute-start(bf16[64,1024]{1,0:T(8,128)(2,1)S(1)} %add_convert_fusion), channel_id=1, source_target_pairs={{4,8},{8,12},{12,14},{14,10},{10,6},{6,2},{2,0},{0,4},{5,1},{9,5},... | collective-permute-start | bytes 393224 | tf_op jit(solution)/shard_map/ppermute | solution.py:89
  23.0 19.0 %collective-permute-start.4 = (bf16[64,2048]{1,0:T(8,128)(2,1)S(1)}, bf16[64,2048]{1,0:T(8,128)(2,1)S(1)}, u32[]{:S(2)}, u32[]{:S(2)}) collective-permute-start(bf16[64,2048]{1,0:T(8,128)(2,1)S(1)} %get-tuple-element.5), channel_id=1, source_target_pairs={{4,0},{8,4},{12,8},{14,12},{10,14},{6,10},{2,6},{0,2},{5,9},{9,13}... | collective-permute-start | bytes 786440 | tf_op jit(solution)/shard_map/ppermute | solution.py:94
  33.6 5.0 %collective-permute-start.5 = (bf16[64,1024]{1,0:T(8,128)(2,1)S(1)}, bf16[64,1024]{1,0:T(8,128)(2,1)S(1)}, u32[]{:S(2)}, u32[]{:S(2)}) collective-permute-start(bf16[64,1024]{1,0:T(8,128)(2,1)S(1)} %collective-permute-done.2), channel_id=1, source_target_pairs={{4,8},{8,12},{12,14},{14,10},{10,6},{6,2},{2,0},{0,4},{5,1},{9,5},... | collective-permute-start | bytes 393224 | tf_op jit(solution)/shard_map/ppermute | solution.py:89
  35.5 5.0 %collective-permute-start.6 = (bf16[64,1024]{1,0:T(8,128)(2,1)S(1)}, bf16[64,1024]{1,0:T(8,128)(2,1)S(1)}, u32[]{:S(2)}, u32[]{:S(2)}) collective-permute-start(bf16[64,1024]{1,0:T(8,128)(2,1)S(1)} %collective-permute-done.3), channel_id=1, source_target_pairs={{4,8},{8,12},{12,14},{14,10},{10,6},{6,2},{2,0},{0,4},{5,1},{9,5},... | collective-permute-start | bytes 393224 | tf_op jit(solution)/shard_map/ppermute | solution.py:89
  37.1 18.0 %copy-start.2 = (f32[512]{0:T(512)S(1)}, f32[512]{0:T(512)}, u32[]{:S(2)}) copy-start(f32[512]{0:T(512)} %param.12) | copy-start | bytes 6148
  37.1 18.0 %copy-start.3 = (f32[8]{0:T(128)S(1)}, f32[8]{0:T(128)}, u32[]{:S(2)}) copy-start(f32[8]{0:T(128)} %param.13) | copy-start | bytes 100
  38.6 6.4 %collective-permute-start.8 = (bf16[64,1024]{1,0:T(8,128)(2,1)S(1)}, bf16[64,1024]{1,0:T(8,128)(2,1)S(1)}, u32[]{:S(2)}, u32[]{:S(2)}) collective-permute-start(bf16[64,1024]{1,0:T(8,128)(2,1)S(1)} %collective-permute-done.5), channel_id=1, source_target_pairs={{4,8},{8,12},{12,14},{14,10},{10,6},{6,2},{2,0},{0,4},{5,1},{9,5},... | collective-permute-start | bytes 393224 | tf_op jit(solution)/shard_map/ppermute | solution.py:89
  40.5 6.8 %collective-permute-start.9 = (bf16[64,1024]{1,0:T(8,128)(2,1)S(1)}, bf16[64,1024]{1,0:T(8,128)(2,1)S(1)}, u32[]{:S(2)}, u32[]{:S(2)}) collective-permute-start(bf16[64,1024]{1,0:T(8,128)(2,1)S(1)} %collective-permute-done.6), channel_id=1, source_target_pairs={{4,8},{8,12},{12,14},{14,10},{10,6},{6,2},{2,0},{0,4},{5,1},{9,5},... | collective-permute-start | bytes 393224 | tf_op jit(solution)/shard_map/ppermute | solution.py:89
  42.0 6.5 %collective-permute-start.7 = (bf16[64,2048]{1,0:T(8,128)(2,1)S(1)}, bf16[64,2048]{1,0:T(8,128)(2,1)S(1)}, u32[]{:S(2)}, u32[]{:S(2)}) collective-permute-start(bf16[64,2048]{1,0:T(8,128)(2,1)S(1)} %collective-permute-done.4), channel_id=1, source_target_pairs={{4,0},{8,4},{12,8},{14,12},{10,14},{6,10},{2,6},{0,2},{5,9},{9,13}... | collective-permute-start | bytes 786440 | tf_op jit(solution)/shard_map/ppermute | solution.py:94
  45.0 9.9 %collective-permute-start.11 = (bf16[64,1024]{1,0:T(8,128)(2,1)S(1)}, bf16[64,1024]{1,0:T(8,128)(2,1)S(1)}, u32[]{:S(2)}, u32[]{:S(2)}) collective-permute-start(bf16[64,1024]{1,0:T(8,128)(2,1)S(1)} %collective-permute-done.8), channel_id=1, source_target_pairs={{4,8},{8,12},{12,14},{14,10},{10,6},{6,2},{2,0},{0,4},{5,1},{9,5},... | collective-permute-start | bytes 393224 | tf_op jit(solution)/shard_map/ppermute | solution.py:89
  47.3 7.6 %collective-permute-start.12 = (bf16[64,1024]{1,0:T(8,128)(2,1)S(1)}, bf16[64,1024]{1,0:T(8,128)(2,1)S(1)}, u32[]{:S(2)}, u32[]{:S(2)}) collective-permute-start(bf16[64,1024]{1,0:T(8,128)(2,1)S(1)} %collective-permute-done.9), channel_id=1, source_target_pairs={{4,8},{8,12},{12,14},{14,10},{10,6},{6,2},{2,0},{0,4},{5,1},{9,5},... | collective-permute-start | bytes 393224 | tf_op jit(solution)/shard_map/ppermute | solution.py:89
  48.5 6.4 %collective-permute-start.10 = (bf16[64,2048]{1,0:T(8,128)(2,1)S(1)}, bf16[64,2048]{1,0:T(8,128)(2,1)S(1)}, u32[]{:S(2)}, u32[]{:S(2)}) collective-permute-start(bf16[64,2048]{1,0:T(8,128)(2,1)S(1)} %collective-permute-done.7), channel_id=1, source_target_pairs={{4,0},{8,4},{12,8},{14,12},{10,14},{6,10},{2,6},{0,2},{5,9},{9,13}... | collective-permute-start | bytes 786440 | tf_op jit(solution)/shard_map/ppermute | solution.py:94
  55.0 3.2 %collective-permute-start.13 = (bf16[512,512]{1,0:T(8,128)(2,1)S(1)}, bf16[512,512]{1,0:T(8,128)(2,1)S(1)}, u32[]{:S(2)}, u32[]{:S(2)}) collective-permute-start(bf16[512,512]{1,0:T(8,128)(2,1)S(1)} %constant_dynamic-slice_fusion), channel_id=1, source_target_pairs={{0,1},{1,0},{2,3},{3,2},{4,5},{5,4},{6,7},{7,6},{8,9},{9,8},{10,11... | collective-permute-start | bytes 1572872 | tf_op jit(solution)/shard_map/ppermute | solution.py:104
